TPU v7x, 32 devices: a whole 2x2x4 slice. The times are simulated.
32 devices in a mesh: req: 8 (over z, y), tp: 4 (over x, core).
Axes of the slice: x: 2, y: 2, z: 4, core: 2. Of those that a mesh axis runs over, the one named last changes fastest.
Arguments:
- hidden_in: bfloat16 [192, 1536], P('req', 'tp'), may hold values from -12 to 12
- queries: bfloat16 [192, 1536], P('req', 'tp'), may hold values from -6 to 6
- fresh_key_value: bfloat16 [192, 2, 256], P('req'), may hold values from -120 to 120
- positions: int32 [192], P('req'), may hold values from 0 to 4095
- lengths: int32 [8, 24], P('req'), may hold values from 1 to 2048, 3072 in all within a row
- cache: bfloat16 [24576, 2, 2, 128], P(('req', 'tp')), may hold values from -160 to 160
- out_proj: bfloat16 [1536, 1536], P('tp'), may hold values from -0.59765625 to 0.59765625
- norm_gain: float32 [1536], replicated, may hold values from 0.1 to 1.9
- expert_ids: int32 [192, 4], P('req'), may hold values from 0 to 31, all different within a row; in each aligned block of 24 rows (0 to 23, 24 to 47, ...) at most 8 rows name the same one
- router_weights: float32 [192, 4], P('req'), may hold values from 0.05 to 0.5
- gate_up: bfloat16 [32, 2, 1536, 768], P('req', None, None, 'tp'), may hold values from -0.15625 to 0.15625
- down: bfloat16 [32, 768, 1536], P('req', 'tp'), may hold values from -0.21875 to 0.21875
Outputs:
- layer_out: bfloat16 [192, 1536], P('req', 'tp')
Inputs may be any that keep to these rules, and one draw needn't show every extreme that they name: `lengths`: each row sums to 3072. `expert_ids`: each row names 4 different experts; among the 24 aligned rows of one request group no expert is named by more than 8 rows, a bound that some block reaches.
All inputs are finite; a program needn't handle non-finite values.
Results may differ from a plain program's by a relative error of at most 0.012.
The roundings to bfloat16 on the way count: a program that leaves them out, or rounds other values in their place, can miss the bound.
Values may be sent and summed in bfloat16 or wider, within the bound.
No kernel may reach another device: no remote copies, remote signals or barrier semaphores. Data moves between devices by JAX's collectives and lax.ppermute only.
A program may use at most 64 MiB of HBM per device.

v0:
```python
import math

import jax
import jax.numpy as jnp
from jax import lax
from jax.sharding import PartitionSpec as P

EXPERTS = 32
CAP = 8


rope_base = 1000000.0
norm_eps = 1e-06
neg_floor = -1e30


def combined_all(value, axis, join):
    pieces = jax.tree.map(lambda part: lax.all_gather(part, axis), value)
    head = jax.tree.map(lambda part: part[0], pieces)
    tail = jax.tree.map(lambda part: part[1:], pieces)
    so_far, _ = lax.scan(lambda so_far, piece: (join(so_far, piece), None), head, tail)
    return so_far


def apply_rotary_heads(values, positions, head_size):
    half_size = head_size // 2
    exponents = jnp.arange(half_size, dtype=jnp.float32) * (2.0 / head_size)
    inverse_freq = jnp.power(jnp.float32(rope_base), -exponents)
    angles = positions.astype(jnp.float32)[:, None] * inverse_freq[None, :]
    cosine = jnp.cos(angles)[:, None, :]
    sine = jnp.sin(angles)[:, None, :]
    first_half = values[..., :half_size]
    second_half = values[..., half_size:]
    return jnp.concatenate(
        [first_half * cosine - second_half * sine, second_half * cosine + first_half * sine],
        axis=-1,
    )


def per_device(
    hidden_in,
    queries,
    fresh_key_value,
    positions,
    lengths,
    cache,
    out_proj,
    norm_gain,
    expert_ids,
    router_weights,
    gate_up,
    down,
):
    tp_count = lax.axis_size("tp")
    req_count = lax.axis_size("req")
    tp_index = lax.axis_index("tp")
    row_count = hidden_in.shape[0]
    head_size = cache.shape[3]
    kv_count = cache.shape[2]
    own_heads = queries.shape[1] // head_size
    head_count = own_heads * tp_count
    request_group_size = head_count // kv_count
    score_scaling = head_size ** (-0.5)
    model_width = norm_gain.shape[0]
    own_width = hidden_in.shape[1]
    first_head = tp_index * own_heads
    q_local = apply_rotary_heads(
        queries.reshape(row_count, own_heads, head_size).astype(jnp.float32), positions, head_size
    ).astype(jnp.bfloat16)
    q_all = lax.all_gather(
        q_local.reshape(row_count, own_heads * head_size), "tp", axis=1, tiled=True
    )
    k_new = apply_rotary_heads(
        fresh_key_value[:, 0].reshape(row_count, kv_count, head_size).astype(jnp.float32),
        positions,
        head_size,
    ).astype(jnp.bfloat16)
    value_fresh = fresh_key_value[:, 1].reshape(row_count, kv_count, head_size)
    own_score = (
        jnp.einsum(
            "tsjp,tsp->tsj",
            q_all.reshape(row_count, kv_count, request_group_size, head_size),
            k_new,
            preferred_element_type=jnp.float32,
        ).reshape(row_count, head_count)
        * score_scaling
    )
    span_rows = cache.shape[0]
    block_rows = math.gcd(span_rows, 512)
    block_count = span_rows // block_rows
    segment_ends = jnp.cumsum(lengths[0], dtype=jnp.int32)
    cache_spots = tp_index * span_rows + jnp.arange(span_rows, dtype=jnp.int32)
    owners = jnp.sum((cache_spots[:, None] >= segment_ends[None, :]).astype(jnp.int32), axis=1)
    owner_blocks = owners.reshape(block_count, block_rows)
    cache_blocks = cache.reshape(block_count, block_rows, 2, kv_count, head_size)

    def score_block(carried, pieces):
        block_owners, stored_entries = pieces
        selected_experts = q_all[block_owners].reshape(
            block_rows, kv_count, request_group_size, head_size
        )
        values = jnp.einsum(
            "zynx,zyx->zyn",
            selected_experts,
            stored_entries[:, 0],
            preferred_element_type=jnp.float32,
        )
        return (carried, values.reshape(block_rows, head_count) * score_scaling)

    unused, scores = lax.scan(score_block, jnp.zeros((), jnp.float32), (owner_blocks, cache_blocks))
    scores = scores.reshape(span_rows, head_count)
    highest_local = jnp.maximum(jax.ops.segment_max(scores, owners, row_count), neg_floor)
    weights_local = jnp.exp(scores - highest_local[owners])
    totals_local = jax.ops.segment_sum(weights_local, owners, row_count)

    def value_block(accumulated, pieces):
        block_owners, stored_entries, block_weights = pieces
        weighted = (
            block_weights.reshape(block_rows, kv_count, request_group_size, 1)
            * stored_entries[:, 1][:, :, None, :]
        )
        return (
            accumulated
            + jax.ops.segment_sum(
                weighted.reshape(block_rows, head_count * head_size), block_owners, row_count
            ),
            None,
        )

    sums_local, unused = lax.scan(
        value_block,
        jnp.zeros((row_count, head_count * head_size), jnp.float32),
        (owner_blocks, cache_blocks, weights_local.reshape(block_count, block_rows, head_count)),
    )
    sums_local = sums_local.reshape(row_count, head_count, head_size)

    def join_states(earlier, later):
        highest = jnp.maximum(earlier[0], later[0])
        early_factor = jnp.exp(earlier[0] - highest)
        late_factor = jnp.exp(later[0] - highest)
        return (
            highest,
            earlier[1] * early_factor + later[1] * late_factor,
            earlier[2] * early_factor[:, :, None] + later[2] * late_factor[:, :, None],
        )

    highest, totals, summed = combined_all(
        (highest_local, totals_local, sums_local), "tp", join_states
    )
    highest = lax.dynamic_slice_in_dim(highest, first_head, own_heads, 1)
    totals = lax.dynamic_slice_in_dim(totals, first_head, own_heads, 1)
    summed = lax.dynamic_slice_in_dim(summed, first_head, own_heads, 1)
    own_slice = lax.dynamic_slice_in_dim(own_score, first_head, own_heads, 1)
    top_score = jnp.maximum(highest, own_slice)
    retained = jnp.exp(highest - top_score)
    own_part = jnp.exp(own_slice - top_score)
    head_kv = (first_head + jnp.arange(own_heads, dtype=jnp.int32)) // request_group_size
    own_values = jnp.take(value_fresh, head_kv, axis=1).astype(jnp.float32)
    attention_output = (summed * retained[:, :, None] + own_values * own_part[:, :, None]) / (
        totals * retained + own_part
    )[:, :, None]
    attention_output = attention_output.astype(jnp.bfloat16).reshape(
        row_count, own_heads * head_size
    )
    partial_proj = jnp.dot(attention_output, out_proj, preferred_element_type=jnp.float32)
    projected = lax.psum_scatter(
        partial_proj.astype(jnp.bfloat16), "tp", scatter_dimension=1, tiled=True
    ).astype(jnp.float32)
    residual = hidden_in.astype(jnp.float32) + projected
    squares = lax.psum(jnp.sum(residual * residual, axis=1), "tp")
    inverse_norm = lax.rsqrt(squares / model_width + norm_eps)
    gain_local = lax.dynamic_slice_in_dim(norm_gain, tp_index * own_width, own_width, 0)
    normed_local = (residual * inverse_norm[:, None] * gain_local[None, :]).astype(jnp.bfloat16)
    normed = lax.all_gather(normed_local, "tp", axis=1, tiled=True)
    expert_range = jnp.arange(EXPERTS, dtype=jnp.int32)
    member = jnp.any(expert_ids[:, :, None] == expert_range[None, None, :], axis=1)
    member_int = member.astype(jnp.int32)
    slot_of = jnp.cumsum(member_int, axis=0, dtype=jnp.int32) - member_int
    slot_range = jnp.arange(CAP, dtype=jnp.int32)
    matches = member.T[:, None, :] & (slot_of.T[:, None, :] == slot_range[None, :, None])
    row_range = jnp.arange(row_count, dtype=jnp.int32)
    slot_rows = jnp.sum(jnp.where(matches, row_range[None, None, :], 0), axis=2)
    slot_live = jnp.any(matches, axis=2)
    split_count = max(1, req_count // EXPERTS)
    per_replica = CAP // split_count
    order_rows = jnp.transpose(slot_rows.reshape(EXPERTS, per_replica, split_count), (2, 0, 1))
    order_live = jnp.transpose(slot_live.reshape(EXPERTS, per_replica, split_count), (2, 0, 1))
    outgoing = jnp.where(order_live[..., None], normed[order_rows], jnp.zeros((), jnp.bfloat16))
    outgoing = outgoing.reshape(split_count * EXPERTS, per_replica, model_width)
    local_count = gate_up.shape[0]
    arrived_rows = lax.all_to_all(outgoing, "req", split_axis=0, concat_axis=0, tiled=True)
    item_count = arrived_rows.shape[1]
    grouped_rows = arrived_rows.reshape(req_count, local_count, item_count, model_width)
    results_list = []
    for local_block in range(local_count):
        flat_rows = grouped_rows[:, local_block].reshape(req_count * item_count, model_width)
        gate_part = jnp.dot(flat_rows, gate_up[local_block, 0], preferred_element_type=jnp.float32)
        up_part = jnp.dot(flat_rows, gate_up[local_block, 1], preferred_element_type=jnp.float32)
        activation = (jnp.maximum(gate_part, 0.0) * up_part).astype(jnp.bfloat16)
        produced_block = jnp.dot(activation, down[local_block], preferred_element_type=jnp.float32)
        results_list.append(produced_block.reshape(req_count, item_count, model_width))
    produced = jnp.stack(results_list, axis=1).reshape(
        req_count * local_count, item_count, model_width
    )
    returned_rows = lax.all_to_all(
        produced.astype(jnp.bfloat16), "req", split_axis=0, concat_axis=0, tiled=True
    )
    arrived = returned_rows.reshape(split_count, EXPERTS, per_replica, returned_rows.shape[2])
    slot_taken = jnp.take_along_axis(slot_of, expert_ids, axis=1)
    picked_rows = arrived[slot_taken % split_count, expert_ids, slot_taken // split_count]
    mixed = jnp.sum(router_weights[:, :, None] * picked_rows.astype(jnp.float32), axis=1)
    mixed = lax.psum_scatter(
        mixed.astype(jnp.bfloat16), "tp", scatter_dimension=1, tiled=True
    ).astype(jnp.float32)
    return (residual + mixed).astype(jnp.bfloat16)


def solution(mesh):
    placed = (
        P("req", "tp"),
        P("req", "tp"),
        P("req", None, None),
        P("req"),
        P("req", None),
        P(("req", "tp"), None, None, None),
        P("tp", None),
        P(),
        P("req", None),
        P("req", None),
        P("req", None, None, "tp"),
        P("req", "tp", None),
    )
    return jax.shard_map(
        per_device, mesh=mesh, in_specs=placed, out_specs=P("req", "tp"), check_vma=False
    )
```

profile of v0, /device:TPU:0, one launch (start us, length us, event | category | flops | bytes accessed | tf_op | source)
XLA Modules:
  0.0 220.3 jit_solution(14795943301095957744)
XLA Ops:
  9.5 6.3 %all_gather.21 = bf16[24,1536]{1,0:T(8,128)(2,1)S(1)} all-gather(bf16[24,384]{1,0:T(8,128)(2,1)S(1)} %bitcast.254), channel_id=1, replica_groups=mesh['req'=8,'tp'=4] {'tp'}, dimensions={1}, use_global_device_ids=true | all-gather | bytes 92160 | tf_op jit(solution)/shard_map/all_gather | solution.py:70
  15.8 2.1 copy.156
  18.0 10.0 %while.34 = (s32[]{:T(128)}, f32[3,256,12]{1,2,0:T(8,128)S(1)}, s32[3,256]{1,0:T(4,128)S(1)}, bf16[24,1536]{1,0:T(8,128)(2,1)S(1)}, bf16[3,256,2,2,128]{4,1,0,3,2:T(8,128)(2,1)}, /*index=5*/s32[]{:T(128)}) while((s32[]{:T(128)}, f32[3,256,12]{1,2,0:T(8,128)S(1)}, s32[3,256]{1,0:T(4,128)S(1)}, bf16[24,1536]{1,0:T(8,128)(2,1)S(1)}, ...), condition=%wide.region_3.4_spmd, body=%wide.region_2.3_spmd.sunk | while | flops 1246978 | bytes 6262873 | solution.py:110
  18.0 1.0 constant_dynamic-slice_fusion.10
  19.5 1.3 gather_fusion
  21.3 1.0 constant_dynamic-slice_fusion.10
  22.8 1.3 gather_fusion
  24.6 1.0 constant_dynamic-slice_fusion.10
  26.1 1.3 gather_fusion
  28.1 7.1 %scatter_custom_fusion.1 = f32[24,12]{1,0:T(8,128)S(1)} fusion(s32[768]{0:T(1024)S(1)} %convert_reduce_fusion, f32[768,12]{1,0:T(8,128)S(1)} %bitcast.244, f32[]{:T(128)} %constant.86.clone.1), kind=kCustom, calls=%fused_computation.135 | custom fusion | flops 9216 | bytes 1156 | tf_op jit(solution)/shard_map/scatter-max | solution.py:112
  35.4 5.5 %all-gather.2 = f32[4,24,12]{1,2,0:T(8,128)S(1)} all-gather(f32[1,24,12]{1,2,0:T(8,128)S(1)} %copy.159), channel_id=2, replica_groups=mesh['req'=8,'tp'=4] {'tp'}, dimensions={0}, use_global_device_ids=true | all-gather | bytes 5760 | tf_op jit(solution)/shard_map/all_gather | solution.py:18
  40.9 1.6 gather_fusion.1
  42.4 7.3 %scatter_custom_fusion.2 = f32[24,12]{1,0:T(8,128)S(1)} fusion(s32[768]{0:T(1024)S(1)} %convert_reduce_fusion, f32[768,12]{1,0:T(8,128)S(1)} %bitcast.245, f32[768,12]{1,0:T(8,128)S(1)} %gather_fusion.1, f32[]{:T(128)} %constant.89.clone.1), kind=kCustom, calls=%fused_computation.86 | custom fusion | flops 18432 | bytes 787588 | tf_op jit(solution)/shard_map/scatter-add | solution.py:114
  49.8 5.3 %all-gather.3 = f32[4,24,12]{1,2,0:T(8,128)S(1)} all-gather(f32[1,24,12]{1,2,0:T(8,128)S(1)} %copy.160), channel_id=3, replica_groups=mesh['req'=8,'tp'=4] {'tp'}, dimensions={0}, use_global_device_ids=true | all-gather | bytes 5760 | tf_op jit(solution)/shard_map/all_gather | solution.py:18
  55.7 20.8 %while.35 = (s32[]{:T(128)}, f32[24,1536]{1,0:T(8,128)S(1)}, s32[3,256]{1,0:T(4,128)S(1)}, f32[3,256,12]{1,2,0:T(8,128)S(1)}, bf16[3,256,2,2,128]{4,1,0,3,2:T(8,128)(2,1)}, /*index=5*/s32[]{:T(128)}) while((s32[]{:T(128)}, f32[24,1536]{1,0:T(8,128)S(1)}, s32[3,256]{1,0:T(4,128)S(1)}, f32[3,256,12]{1,2,0:T(8,128)S(1)}, ...), condition=%wide.region_8.9_spmd, body=%wide.region_6.8_spmd.sunk | while | flops 851970 | bytes 11205721 | solution.py:130
  55.7 1.0 constant_dynamic-slice_fusion.12
  57.0 1.6 copy.225
  58.6 3.9 %scatter_fusion = f32[24,1536]{1,0:T(8,128)S(1)} fusion(f32[24,1536]{1,0:T(8,128)S(1)} %get-tuple-element.389, s32[256]{0:T(256)S(1)} %bitcast.250, f32[256,1536]{1,0:T(8,128)} %copy.225), kind=kCustom, calls=%fused_computation.6.clone.1 | custom fusion | flops 393216 | bytes 4719616 | tf_op jit(solution)/shard_map/while/body/eval_jaxpr/scatter-add | solution.py:124
  62.6 1.0 constant_dynamic-slice_fusion.12
  63.9 1.6 copy.225
  65.6 3.9 %scatter_fusion = f32[24,1536]{1,0:T(8,128)S(1)} fusion(f32[24,1536]{1,0:T(8,128)S(1)} %get-tuple-element.389, s32[256]{0:T(256)S(1)} %bitcast.250, f32[256,1536]{1,0:T(8,128)} %copy.225), kind=kCustom, calls=%fused_computation.6.clone.1 | custom fusion | flops 393216 | bytes 4719616 | tf_op jit(solution)/shard_map/while/body/eval_jaxpr/scatter-add | solution.py:124
  69.6 1.0 constant_dynamic-slice_fusion.12
  70.9 1.6 copy.225
  72.5 3.9 %scatter_fusion = f32[24,1536]{1,0:T(8,128)S(1)} fusion(f32[24,1536]{1,0:T(8,128)S(1)} %get-tuple-element.389, s32[256]{0:T(256)S(1)} %bitcast.250, f32[256,1536]{1,0:T(8,128)} %copy.225), kind=kCustom, calls=%fused_computation.6.clone.1 | custom fusion | flops 393216 | bytes 4719616 | tf_op jit(solution)/shard_map/while/body/eval_jaxpr/scatter-add | solution.py:124
  76.6 8.0 %all_gather.26 = f32[4,24,12,128]{3,1,2,0:T(8,128)S(1)} all-gather(f32[1,24,12,128]{3,1,2,0:T(8,128)S(1)} %copy.163), channel_id=1, replica_groups=mesh['req'=8,'tp'=4] {'tp'}, dimensions={0}, use_global_device_ids=true | all-gather | bytes 737280 | tf_op jit(solution)/shard_map/all_gather | solution.py:18
  85.3 1.3 while.36
  87.6 0.9 copy.185
  89.9 21.0 %reduce-scatter.7.cloned.1.call-done = bf16[384,24]{1,0:T(8,128)(2,1)} async-done(((bf16[1536,24]{1,0:T(8,128)(2,1)}), bf16[384,24]{1,0:T(8,128)(2,1)}) %reduce-scatter.7.cloned.1.call-update) | async-done | bytes 18448
  110.9 1.0 copy.186
  112.0 5.8 %psum.7 = f32[24]{0:T(128)S(1)} all-reduce(f32[24]{0:T(128)S(1)} %multiply_reduce_fusion.2), channel_id=1, replica_groups=mesh['req'=8,'tp'=4] {'tp'}, use_global_device_ids=true, to_apply=%region_16.17 | all-reduce | flops 24 | bytes 192 | tf_op jit(solution)/shard_map/psum | solution.py:170
  117.8 5.3 %all_gather.27 = bf16[24,1536]{1,0:T(8,128)(2,1)S(1)} all-gather(bf16[24,384]{1,0:T(8,128)(2,1)S(1)} %multiply_convert_fusion), channel_id=1, replica_groups=mesh['req'=8,'tp'=4] {'tp'}, dimensions={1}, use_global_device_ids=true | all-gather | bytes 92160 | tf_op jit(solution)/shard_map/all_gather | solution.py:174
  123.1 1.3 gather_fusion.3
  124.5 26.1 %all_to_all.10 = bf16[32,8,1536]{2,1,0:T(8,128)(2,1)S(1)} all-to-all(bf16[32,8,1536]{2,1,0:T(8,128)(2,1)S(1)} %bitcast_select_fusion), channel_id=1, replica_groups=mesh['req'=8,'tp'=4] {'req'}, dimensions={0} | all-to-all | bytes 1572864 | tf_op jit(solution)/shard_map/all_to_all | solution.py:191
  150.6 1.4 convolution_maximum_fusion
  152.0 1.4 convolution_maximum_fusion.1
  153.4 1.4 convolution_maximum_fusion.2
  154.7 1.4 convolution_maximum_fusion.3
  156.1 1.9 fusion.6
  158.0 1.9 fusion.7
  159.9 1.9 fusion.8
  161.8 1.9 fusion.9
  163.8 0.9 copy.172
  164.7 3.6 %all-to-all-start.1 = ((bf16[32,8,1536]{2,1,0:T(8,128)(2,1)}), bf16[32,8,1536]{2,1,0:T(8,128)(2,1)S(1)}, u32[]{:S(2)}, u32[]{:S(2)}) async-start(bf16[32,8,1536]{2,1,0:T(8,128)(2,1)} %bitcast.62), calls=%async_computation.1 | async-start | bytes 1572864 | tf_op jit(solution)/shard_map/all_to_all | solution.py:205
  168.6 1.3 gather_fusion.5
  170.4 18.2 %all-to-all-done.1 = bf16[32,8,1536]{2,1,0:T(8,128)(2,1)S(1)} async-done(((bf16[32,8,1536]{2,1,0:T(8,128)(2,1)}), bf16[32,8,1536]{2,1,0:T(8,128)(2,1)S(1)}, u32[]{:S(2)}, u32[]{:S(2)}) %all-to-all-start.1) | async-done | bytes 786464 | tf_op jit(solution)/shard_map/all_to_all | solution.py:205
  188.5 2.3 %gather_fusion.4 = bf16[96,1536]{1,0:T(8,128)(2,1)S(1)} fusion(bf16[1,32,8,1536]{3,2,1,0:T(8,128)(2,1)S(1)} %bitcast.232, s32[96]{0:T(128)S(1)} %reshape.360), kind=kCustom, calls=%fused_computation.4 | custom fusion | bytes 590976 | tf_op jit(solution)/shard_map/gather | solution.py:210
  192.4 19.5 %reduce-scatter.9.cloned.1.call-done = bf16[384,24]{1,0:T(8,128)(2,1)} async-done(((bf16[1536,24]{1,0:T(8,128)(2,1)}), bf16[384,24]{1,0:T(8,128)(2,1)}) %reduce-scatter.9.cloned.1.call-update) | async-done | bytes 18448
  211.9 1.0 copy.188
  (162 shorter events, 15.4 us)
Async XLA Ops:
  6.5 80.7 %copy-start = (bf16[384,1536]{1,0:T(8,128)(2,1)S(1)}, bf16[384,1536]{1,0:T(8,128)(2,1)}, u32[]{:S(2)}) copy-start(bf16[384,1536]{1,0:T(8,128)(2,1)} %param.24) | copy-start | bytes 3538948
  6.5 104.3 %reduce-scatter.7.cloned.1.call-start = ((), (), s32[]{:S(2)}) async-start(), calls=%async_computation.4 | async-start | bytes 491520
  40.8 14.4 %copy-start.1 = (f32[4,24,12]{1,2,0:T(8,128)}, f32[4,24,12]{1,2,0:T(8,128)S(1)}, u32[]{:S(2)}) copy-start(f32[4,24,12]{1,2,0:T(8,128)S(1)} %all-gather.2) | copy-start | bytes 13828
  55.0 0.6 copy-start.2
  76.4 8.2 %copy-start.4 = (bf16[24,2,256]{2,1,0:T(2,128)(2,1)S(1)}, bf16[24,2,256]{2,1,0:T(2,128)(2,1)}, u32[]{:S(2)}) copy-start(bf16[24,2,256]{2,1,0:T(2,128)(2,1)} %param.20) | copy-start | bytes 73732
  76.5 8.8 %slice-start = ((f32[4,24,12]{1,2,0:T(8,128)}), f32[3,24,12]{1,2,0:T(8,128)S(1)}, s32[]{:S(2)}) async-start(f32[4,24,12]{1,2,0:T(8,128)} %copy-done.1), calls=%async_computation.6 | async-start | bytes 49152 | tf_op jit(solution)/shard_map/slice | solution.py:20
  76.5 8.8 %slice-start.1 = ((f32[4,24,12]{1,2,0:T(8,128)}), f32[3,24,12]{1,2,0:T(8,128)S(1)}, s32[]{:S(2)}) async-start(f32[4,24,12]{1,2,0:T(8,128)} %copy-done.2), calls=%async_computation.7 | async-start | bytes 49152 | tf_op jit(solution)/shard_map/slice | solution.py:20
  86.6 2.0 copy-start.5
  86.6 25.2 %copy-start.3 = (bf16[24,384]{1,0:T(8,128)(2,1)S(1)}, bf16[24,384]{1,0:T(8,128)(2,1)}, u32[]{:S(2)}) copy-start(bf16[24,384]{1,0:T(8,128)(2,1)} %param.18) | copy-start | bytes 55300
  164.7 23.8 %all-to-all-start.1 = ((bf16[32,8,1536]{2,1,0:T(8,128)(2,1)}), bf16[32,8,1536]{2,1,0:T(8,128)(2,1)S(1)}, u32[]{:S(2)}, u32[]{:S(2)}) async-start(bf16[32,8,1536]{2,1,0:T(8,128)(2,1)} %bitcast.62), calls=%async_computation.1 | async-start | bytes 1572864 | tf_op jit(solution)/shard_map/all_to_all | solution.py:205
  168.3 43.5 %reduce-scatter.9.cloned.1.call-start = ((), (), s32[]{:S(2)}) async-start(), calls=%async_computation.5 | async-start | bytes 491520
  168.6 1.7 copy-start.6
Sparse Core Ops, SparseCore 0:
  88.7 22.1 reduce-scatter.6
  192.5 19.3 reduce-scatter.8
where the time goes:
time: 221 us; the launch traced here: 220 us
  blocking collectives  62.1 us (28%)
  waiting for transfers between devices  58.7 us (27%)
  local copies, waits for them, and re-layouts  36.2 us (16%)
  other arithmetic  31.7 us (14%)
  between operations  13.9 us (6%)
  matrix products  13.5 us (6%)
  starting transfers between devices  3.68 us (2%)
    unnamed x4, waiting for transfers between devices  40.5 us
    all_to_all x1, blocking collectives, per_device(): lax.all_to_all(outgoing, 'req', split_axis=0, concat_axis=0, tiled=True)  26.1 us
    all_gather x3, blocking collectives, combined_all(): pieces = jax.tree.map(lambda part: lax.all_gather(part, axis), value)  18.7 us
    all_to_all x1, waiting for transfers between devices, per_device(): lax.all_to_all(produced.astype(jnp.bfloat16), 'req', split_axis=0, concat...  18.2 us
    scatter-add x3, other arithmetic, value_block(): jax.ops.segment_sum(weighted.reshape(block_rows, head_count * head_size),...  11.8 us
    dot_general x4, matrix products, per_device(): jnp.dot(activation, down[local_block], preferred_element_type=jnp.float32)  7.51 us
    scatter-add x1, other arithmetic, per_device(): totals_local = jax.ops.segment_sum(weights_local, owners, row_count)  7.27 us
    another operation x1, other arithmetic, per_device(): jax.ops.segment_max(scores, owners, row_count)  7.14 us
  transfers between devices with their start and end apart: 3, of which 3 were waited for; matrix products, arithmetic and copies ran while one was open for 1% of the time, Pallas kernels for 0%

commit v1 on v0

v1 whole, which is shorter than its diff:
```python
import jax
import jax.numpy as jnp
from jax import lax
from jax.sharding import PartitionSpec as P

EXPERTS = 32


rope_base = 1000000.0
norm_eps = 1e-06
neg_floor = -1e30


def apply_rotary_heads(values, positions, head_size):
    half_size = head_size // 2
    exponents = jnp.arange(half_size, dtype=jnp.float32) * (2.0 / head_size)
    inverse_freq = jnp.power(jnp.float32(rope_base), -exponents)
    angles = positions.astype(jnp.float32)[:, None] * inverse_freq[None, :]
    cosine = jnp.cos(angles)[:, None, :]
    sine = jnp.sin(angles)[:, None, :]
    first_half = values[..., :half_size]
    second_half = values[..., half_size:]
    return jnp.concatenate(
        [first_half * cosine - second_half * sine, second_half * cosine + first_half * sine],
        axis=-1,
    )


def per_device(
    hidden_in,
    queries,
    fresh_key_value,
    positions,
    lengths,
    cache,
    out_proj,
    norm_gain,
    expert_ids,
    router_weights,
    gate_up,
    down,
):
    tp_count = lax.axis_size("tp")
    req_count = lax.axis_size("req")
    tp_index = lax.axis_index("tp")
    req_index = lax.axis_index("req")
    row_count = hidden_in.shape[0]
    head_size = cache.shape[3]
    kv_count = cache.shape[2]
    own_heads = queries.shape[1] // head_size
    head_count = own_heads * tp_count
    request_group_size = head_count // kv_count
    score_scaling = head_size ** (-0.5)
    model_width = norm_gain.shape[0]
    own_width = hidden_in.shape[1]
    first_head = tp_index * own_heads
    span_rows = cache.shape[0]

    q_local = apply_rotary_heads(
        queries.reshape(row_count, own_heads, head_size).astype(jnp.float32), positions, head_size
    ).astype(jnp.bfloat16)
    packed = jnp.stack([q_local.reshape(row_count, own_width), hidden_in], axis=0)
    gathered = lax.all_gather(packed, "tp", axis=0)
    q_all = jnp.transpose(gathered[:, 0], (1, 0, 2)).reshape(
        row_count, kv_count, request_group_size, head_size
    )
    hidden_full = jnp.transpose(gathered[:, 1], (1, 0, 2)).reshape(row_count, model_width)

    k_new = apply_rotary_heads(
        fresh_key_value[:, 0].reshape(row_count, kv_count, head_size).astype(jnp.float32),
        positions,
        head_size,
    ).astype(jnp.bfloat16)
    value_fresh = fresh_key_value[:, 1].reshape(row_count, kv_count, head_size)
    own_score = (
        jnp.einsum("rcgd,rcd->rcg", q_all, k_new, preferred_element_type=jnp.float32)
        * score_scaling
    )

    segment_ends = jnp.cumsum(lengths[0], dtype=jnp.int32)
    segment_starts = segment_ends - lengths[0]
    cache_spots = tp_index * span_rows + jnp.arange(span_rows, dtype=jnp.int32)
    mask = (cache_spots[None, :] >= segment_starts[:, None]) & (
        cache_spots[None, :] < segment_ends[:, None]
    )
    mask = mask[:, None, None, :]
    keys = cache[:, 0]
    values = cache[:, 1]
    scores = (
        jnp.einsum("rcgd,jcd->rcgj", q_all, keys, preferred_element_type=jnp.float32)
        * score_scaling
    )
    scores = jnp.where(mask, scores, neg_floor)
    highest_local = jnp.max(scores, axis=3)
    weights = jnp.where(mask, jnp.exp(scores - highest_local[..., None]), 0.0)
    totals_local = jnp.sum(weights, axis=3)
    sums_local = jnp.einsum(
        "rcgj,jcd->rcgd",
        weights,
        values.astype(jnp.float32),
        precision=lax.Precision.HIGHEST,
        preferred_element_type=jnp.float32,
    )
    states = jnp.concatenate(
        [highest_local[..., None], totals_local[..., None], sums_local], axis=3
    ).reshape(row_count, head_count, head_size + 2)
    all_states = lax.all_gather(states, "tp", axis=0)
    all_states = lax.dynamic_slice_in_dim(all_states, first_head, own_heads, 2)
    parts_highest = all_states[..., 0]
    parts_totals = all_states[..., 1]
    parts_sums = all_states[..., 2:]
    own_slice = lax.dynamic_slice_in_dim(own_score.reshape(row_count, head_count), first_head, own_heads, 1)
    top_score = jnp.maximum(jnp.max(parts_highest, axis=0), own_slice)
    factors = jnp.exp(parts_highest - top_score[None])
    own_part = jnp.exp(own_slice - top_score)
    head_kv = (first_head + jnp.arange(own_heads, dtype=jnp.int32)) // request_group_size
    own_values = jnp.take(value_fresh, head_kv, axis=1).astype(jnp.float32)
    totals = jnp.sum(parts_totals * factors, axis=0) + own_part
    summed = jnp.sum(parts_sums * factors[..., None], axis=0) + own_values * own_part[..., None]
    attention_output = (summed / totals[..., None]).astype(jnp.bfloat16).reshape(
        row_count, own_heads * head_size
    )

    partial_proj = jnp.dot(attention_output, out_proj, preferred_element_type=jnp.float32)
    projected = lax.psum(partial_proj, "tp")
    residual = hidden_full.astype(jnp.float32) + projected
    mean_square = jnp.mean(residual * residual, axis=1, keepdims=True)
    normed = (residual * lax.rsqrt(mean_square + norm_eps) * norm_gain[None, :]).astype(jnp.bfloat16)

    local_count = gate_up.shape[0]
    block_total = local_count * req_count
    split_count = max(1, block_total // EXPERTS)
    expert_range = jnp.arange(EXPERTS, dtype=jnp.int32)
    member = jnp.any(expert_ids[:, :, None] == expert_range[None, None, :], axis=1)
    member_int = member.astype(jnp.int32)
    slot_of = jnp.cumsum(member_int, axis=0, dtype=jnp.int32) - member_int
    slot_taken = jnp.take_along_axis(slot_of, expert_ids, axis=1)
    block_taken = (slot_taken % split_count) * EXPERTS + expert_ids
    block_range = jnp.arange(block_total, dtype=jnp.int32)
    block_weights = jnp.sum(
        jnp.where(block_taken[:, :, None] == block_range[None, None, :], router_weights[:, :, None], 0.0),
        axis=1,
    )

    rows_all = lax.all_gather(normed, "req", axis=0, tiled=True)
    weights_all = lax.all_gather(block_weights, "req", axis=0, tiled=True)
    weights_own = lax.dynamic_slice_in_dim(weights_all, req_index * local_count, local_count, 1)

    mixed = jnp.zeros((rows_all.shape[0], model_width), jnp.float32)
    for local_block in range(local_count):
        gate_part = jnp.dot(rows_all, gate_up[local_block, 0], preferred_element_type=jnp.float32)
        up_part = jnp.dot(rows_all, gate_up[local_block, 1], preferred_element_type=jnp.float32)
        activation = (jnp.maximum(gate_part, 0.0) * up_part).astype(jnp.bfloat16)
        produced = jnp.dot(activation, down[local_block], preferred_element_type=jnp.float32)
        produced = produced.astype(jnp.bfloat16).astype(jnp.float32)
        mixed = mixed + weights_own[:, local_block : local_block + 1] * produced

    mixed = mixed.reshape(req_count, row_count, tp_count, own_width)
    mixed = jnp.transpose(mixed, (0, 2, 1, 3)).reshape(req_count * tp_count, row_count, own_width)
    mixed = lax.psum_scatter(mixed, ("req", "tp"), scatter_dimension=0, tiled=True)
    mixed = mixed.reshape(row_count, own_width)
    residual_own = lax.dynamic_slice_in_dim(residual, tp_index * own_width, own_width, 1)
    return (residual_own + mixed).astype(jnp.bfloat16)


def solution(mesh):
    placed = (
        P("req", "tp"),
        P("req", "tp"),
        P("req", None, None),
        P("req"),
        P("req", None),
        P(("req", "tp"), None, None, None),
        P("tp", None),
        P(),
        P("req", None),
        P("req", None),
        P("req", None, None, "tp"),
        P("req", "tp", None),
    )
    return jax.shard_map(
        per_device, mesh=mesh, in_specs=placed, out_specs=P("req", "tp"), check_vma=False
    )
```

time: 221 us -> 227 us (1.027)
  waiting for transfers between devices: 58.7 us -> 98.7 us
  local copies, waits for them, and re-layouts: 36.2 us -> 6.85 us
  other arithmetic: 31.7 us -> 6.41 us
  blocking collectives: 62.1 us -> 80.5 us
  matrix products: 13.5 us -> 20.2 us
  starting transfers between devices: 3.68 us -> 0.04 us
    unnamed x4 -> x3, waiting for transfers between devices: 40.5 us -> 97.7 us
    all_gather x5 -> x4, blocking collectives: 30.2 us -> 80.5 us  [the longest x1 31.8 us: per_device(): rows_all = lax.all_gather(normed, 'req', axis=0, tiled=True)]
    all_to_all x1 -> x0, blocking collectives: 26.1 us -> none  [per_device(): lax.all_to_all(outgoing, 'req', split_axis=0, concat_axis=0, tiled=True)]
    scatter-add x4 -> x0, other arithmetic: 19.1 us -> none  [the longest x3 11.8 us: value_block(): jax.ops.segment_sum(weighted.reshape(block_rows, head_count * head_size),...]
    all_to_all x1 -> x0, waiting for transfers between devices: 18.2 us -> none  [per_device(): lax.all_to_all(produced.astype(jnp.bfloat16), 'req', split_axis=0, concat...]
    gather x12 -> x0, local copies, waits for them, and re-layouts: 10.6 us -> none  [the longest x3 3.79 us: score_block(): q_all[block_owners]]
    dynamic_slice x22 -> x0, local copies, waits for them, and re-layouts: 7.97 us -> none  [the longest x15 7.14 us: per_device(): lax.scan(score_block, jnp.zeros((), jnp.float32), (owner_blocks, cache_bl...]
    another operation x7 -> x5, other arithmetic: 7.65 us -> 1.09 us  [the longest x1 0.73 us: per_device(): jnp.stack([q_local.reshape(row_count, own_width), hidden_in], axis=0)]
  transfers between devices with their start and end apart: 3 -> 2, of which waited for: 3 -> 2; matrix products, arithmetic and copies ran while one was open for 1% -> 0% of each run, Pallas kernels for 0% -> 0%
where the time goes in v1:
time: 227 us; the launch traced here: 226 us
  waiting for transfers between devices  98.7 us (43%)
  blocking collectives  80.5 us (35%)
  matrix products  20.2 us (9%)
  between operations  13.8 us (6%)
  local copies, waits for them, and re-layouts  6.85 us (3%)
  other arithmetic  6.41 us (3%)
    unnamed x3, waiting for transfers between devices  97.7 us
    all_gather x1, blocking collectives, per_device(): rows_all = lax.all_gather(normed, 'req', axis=0, tiled=True)  31.8 us
    all_gather x1, blocking collectives, per_device(): weights_all = lax.all_gather(block_weights, 'req', axis=0, tiled=True)  31 us
    all_gather x1, blocking collectives, per_device(): all_states = lax.all_gather(states, 'tp', axis=0)  11.1 us
    dot_general x4, matrix products, per_device(): jnp.dot(activation, down[local_block], preferred_element_type=jnp.float32)  11 us
    dot_general x4, matrix products, per_device(): jnp.dot(rows_all, gate_up[local_block, 0], preferred_element_type=jnp.flo...  6.93 us
    all_gather x1, blocking collectives, per_device(): gathered = lax.all_gather(packed, 'tp', axis=0)  6.58 us
  transfers between devices with their start and end apart: 2, of which 2 were waited for; matrix products, arithmetic and copies ran while one was open for 0% of the time, Pallas kernels for 0%

profile of v1, /device:TPU:0, one launch (start us, length us, event | category | flops | bytes accessed | tf_op | source)
XLA Modules:
  0.0 226.4 jit_solution(6006693005743040945)
XLA Ops:
  6.6 0.8 convert_element_type.94
  7.4 0.7 reshape.253
  8.1 0.1 multiply_cosine_fusion
  8.3 0.1 subtract_convert_fusion
  8.4 0.1 pad_maximum_fusion.2
  8.5 0.7 pad_maximum_fusion.1
  9.2 6.6 %all-gather = bf16[8,24,384]{2,1,0:T(8,128)(2,1)S(1)} all-gather(bf16[2,24,384]{2,1,0:T(8,128)(2,1)S(1)} %pad_maximum_fusion.1), channel_id=2, replica_groups=mesh['req'=8,'tp'=4] {'tp'}, dimensions={0}, use_global_device_ids=true | all-gather | bytes 184320 | tf_op jit(solution)/shard_map/all_gather | solution.py:63
  16.1 0.1 reduce.1
  16.2 0.5 fusion.74
  16.9 0.5 fusion.76
  17.3 0.1 concatenate.24
  17.5 0.3 fusion.18
  17.8 0.7 fusion.17
  18.5 0.1 concatenate.25
  18.6 0.2 pad_maximum_fusion
  18.9 11.1 %all_gather.17 = f32[4,24,12,130]{3,1,2,0:T(8,128)S(1)} all-gather(f32[1,24,12,130]{3,1,2,0:T(8,128)S(1)} %pad_maximum_fusion), channel_id=1, replica_groups=mesh['req'=8,'tp'=4] {'tp'}, dimensions={0}, use_global_device_ids=true | all-gather | bytes 748800 | tf_op jit(solution)/shard_map/all_gather | solution.py:107
  29.9 0.1 slice_reduce_fusion
  30.0 0.1 subtract_convert_fusion.1
  30.1 0.1 maximum_bitcast_fusion
  30.2 0.2 fusion.58
  30.4 0.1 copy.75
  30.5 0.2 fusion.73
  30.7 0.1 copy.82
  30.8 0.1 constant_dynamic-slice_fusion.1
  30.9 0.3 copy.81
  31.3 0.6 multiply_reduce_fusion
  31.9 0.1 copy.66
  32.0 0.1 copy.83
  32.5 0.6 gather_fusion
  33.3 0.9 fusion.60
  34.4 0.1 select_reduce_fusion
  34.5 31.0 %all_gather.18 = f32[192,32]{1,0:T(8,128)S(1)} all-gather(f32[24,32]{1,0:T(8,128)S(1)} %select_reduce_fusion), channel_id=1, replica_groups=mesh['req'=8,'tp'=4] {'req'}, dimensions={0}, use_global_device_ids=true | all-gather | bytes 27648 | tf_op jit(solution)/shard_map/all_gather | solution.py:146
  65.4 0.4 dynamic-slice_reduce_fusion
  65.8 1.0 all-reduce.3.cloned.1.call-done
  66.8 1.0 multiply_reduce_fusion.1
  68.0 31.8 %all_gather.19 = bf16[192,1536]{1,0:T(8,128)(2,1)S(1)} all-gather(bf16[24,1536]{1,0:T(8,128)(2,1)S(1)} %multiply_convert_fusion), channel_id=1, replica_groups=mesh['req'=8,'tp'=4] {'req'}, dimensions={0}, use_global_device_ids=true | all-gather | bytes 663552 | tf_op jit(solution)/shard_map/all_gather | solution.py:145
  99.8 2.1 convolution_maximum_fusion.3
  101.9 2.1 convolution_maximum_fusion.2
  104.0 1.4 convolution_maximum_fusion.1
  105.4 1.4 convolution_maximum_fusion
  106.8 2.2 fusion.10
  109.0 3.2 %fusion.8 = f32[192,1536]{1,0:T(8,128)} fusion(f32[192,1536]{1,0:T(8,128)S(1)} %fusion.10, f32[192,192]{1,0:T(8,128)} %convolution_maximum_fusion.2, bf16[192,1536]{1,0:T(8,128)(2,1)S(1)} %all_gather.19, bf16[4,192,1536]{2,1,0:T(8,128)(2,1)} %param.23, bf16[4,2,1536,192]{2,3,1,0:T(8,128)(2,1)} %param.22, f32[192]{0:T(256)S(1)} %get-tuple-element.7), kind=kOutput, calls=%fused_computation.12 | convolution fusion | flops 227745792 | bytes 4326144 | tf_op jit(solution)/shard_map/dot_general | solution.py:154
  112.2 2.5 %fusion.5 = f32[192,1536]{1,0:T(8,128)S(1)} fusion(f32[192,1536]{1,0:T(8,128)} %fusion.8, f32[192,192]{1,0:T(8,128)S(1)} %convolution_maximum_fusion.1, bf16[192,1536]{1,0:T(8,128)(2,1)S(1)} %all_gather.19, bf16[4,192,1536]{2,1,0:T(8,128)(2,1)} %param.23, bf16[4,2,1536,192]{2,3,1,0:T(8,128)(2,1)} %param.22, f32[192]{0:T(256)S(1)} %get-tuple-element.6), kind=kOutput, calls=%fused_computation.8 | convolution fusion | flops 227745792 | bytes 4276992 | tf_op jit(solution)/shard_map/dot_general | solution.py:154
  114.7 3.1 %fusion.2 = f32[192,1536]{1,0:T(8,128)} fusion(f32[192,1536]{1,0:T(8,128)S(1)} %fusion.5, f32[192,192]{1,0:T(8,128)S(1)} %convolution_maximum_fusion, bf16[192,1536]{1,0:T(8,128)(2,1)S(1)} %all_gather.19, bf16[4,192,1536]{2,1,0:T(8,128)(2,1)} %param.23, bf16[4,2,1536,192]{2,3,1,0:T(8,128)(2,1)} %param.22, f32[192]{0:T(256)S(1)} %get-tuple-element.5), kind=kOutput, calls=%fused_computation.4 | convolution fusion | flops 227745792 | bytes 4276992 | tf_op jit(solution)/shard_map/dot_general | solution.py:154
  117.8 1.7 reshape.250
  119.5 1.1 copy.71
  120.6 97.6 %reduce-scatter.4.cloned.1.call-done = f32[1,24,384]{2,1,0:T(8,128)} async-done(((f32[32,24,384]{2,1,0:T(8,128)}), f32[1,24,384]{2,1,0:T(8,128)}) %reduce-scatter.4.cloned.1.call-update) | async-done | bytes 36880
  218.2 1.4 fusion.57
  (47 shorter events, 1.2 us)
Async XLA Ops:
  6.5 26.7 %copy-start = (bf16[384,1536]{1,0:T(8,128)(2,1)S(1)}, bf16[384,1536]{1,0:T(8,128)(2,1)}, u32[]{:S(2)}) copy-start(bf16[384,1536]{1,0:T(8,128)(2,1)} %param.18) | copy-start | bytes 3538948
  6.5 9.4 %copy-start.6 = (s32[1,24]{1,0:T(1,128)S(1)}, s32[1,24]{1,0:T(1,128)}, u32[]{:S(2)}) copy-start(s32[1,24]{1,0:T(1,128)} %param.16) | copy-start | bytes 292
  6.5 9.7 %copy-start.1 = (bf16[768,2,2,128]{3,2,1,0:T(2,128)(2,1)S(1)}, bf16[768,2,2,128]{3,2,1,0:T(2,128)(2,1)}, u32[]{:S(2)}) copy-start(bf16[768,2,2,128]{3,2,1,0:T(2,128)(2,1)} %param.17) | copy-start | bytes 2359300
  6.5 60.3 %all-reduce.3.cloned.1.call-start = ((), (), s32[]{:S(2)}) async-start(), calls=%async_computation.1 | async-start | bytes 294912 | tf_op jit(solution)/shard_map/psum | solution.py:125
  18.5 11.4 %copy-start.2 = (bf16[24,2,256]{2,1,0:T(2,128)(2,1)S(1)}, bf16[24,2,256]{2,1,0:T(2,128)(2,1)}, u32[]{:S(2)}) copy-start(bf16[24,2,256]{2,1,0:T(2,128)(2,1)} %param.14) | copy-start | bytes 73732
  33.0 1.3 copy-start.4
  33.1 1.3 copy-start.5
  34.2 33.7 %copy-start.3 = (f32[1536]{0:T(1024)S(1)}, f32[1536]{0:T(1024)}, u32[]{:S(2)}) copy-start(f32[1536]{0:T(1024)} %param.19) | copy-start | bytes 18436
  34.2 184.0 %reduce-scatter.4.cloned.1.call-start = ((), (), s32[]{:S(2)}) async-start(), calls=%async_computation.2 | async-start | bytes 1216512
Sparse Core Ops, SparseCore 0:
  34.3 32.4 all-reduce.2
  120.7 97.4 reduce-scatter.3

commit v2 on v1

--- a/solution.py
+++ b/solution.py
@@ -59,12 +59,10 @@
     q_local = apply_rotary_heads(
         queries.reshape(row_count, own_heads, head_size).astype(jnp.float32), positions, head_size
     ).astype(jnp.bfloat16)
-    packed = jnp.stack([q_local.reshape(row_count, own_width), hidden_in], axis=0)
-    gathered = lax.all_gather(packed, "tp", axis=0)
-    q_all = jnp.transpose(gathered[:, 0], (1, 0, 2)).reshape(
+    gathered = lax.all_gather(q_local.reshape(row_count, own_width), "tp", axis=0)
+    q_all = jnp.transpose(gathered, (1, 0, 2)).reshape(
         row_count, kv_count, request_group_size, head_size
     )
-    hidden_full = jnp.transpose(gathered[:, 1], (1, 0, 2)).reshape(row_count, model_width)
 
     k_new = apply_rotary_heads(
         fresh_key_value[:, 0].reshape(row_count, kv_count, head_size).astype(jnp.float32),
@@ -103,9 +101,10 @@
     )
     states = jnp.concatenate(
         [highest_local[..., None], totals_local[..., None], sums_local], axis=3
-    ).reshape(row_count, head_count, head_size + 2)
-    all_states = lax.all_gather(states, "tp", axis=0)
-    all_states = lax.dynamic_slice_in_dim(all_states, first_head, own_heads, 2)
+    ).reshape(row_count, tp_count, own_heads, head_size + 2)
+    all_states = lax.all_to_all(
+        jnp.transpose(states, (1, 0, 2, 3)), "tp", 0, 0, tiled=True
+    )
     parts_highest = all_states[..., 0]
     parts_totals = all_states[..., 1]
     parts_sums = all_states[..., 2:]
@@ -122,8 +121,10 @@
     )
 
     partial_proj = jnp.dot(attention_output, out_proj, preferred_element_type=jnp.float32)
-    projected = lax.psum(partial_proj, "tp")
-    residual = hidden_full.astype(jnp.float32) + projected
+    partial_proj = jnp.transpose(partial_proj.reshape(row_count, tp_count, own_width), (1, 0, 2))
+    projected = jnp.sum(lax.all_to_all(partial_proj, "tp", 0, 0, tiled=True), axis=0)
+    residual_own = hidden_in.astype(jnp.float32) + projected
+    residual = lax.all_gather(residual_own, "tp", axis=1, tiled=True)
     mean_square = jnp.mean(residual * residual, axis=1, keepdims=True)
     normed = (residual * lax.rsqrt(mean_square + norm_eps) * norm_gain[None, :]).astype(jnp.bfloat16)
 
@@ -142,9 +143,18 @@
         axis=1,
     )
 
-    rows_all = lax.all_gather(normed, "req", axis=0, tiled=True)
     weights_all = lax.all_gather(block_weights, "req", axis=0, tiled=True)
     weights_own = lax.dynamic_slice_in_dim(weights_all, req_index * local_count, local_count, 1)
+    if req_count <= 16:
+        arrived = [normed] + [
+            lax.ppermute(normed, "req", [(i, (i + shift) % req_count) for i in range(req_count)])
+            for shift in range(1, req_count)
+        ]
+        arrived = jnp.stack(arrived, axis=0)
+        order = (req_index - jnp.arange(req_count, dtype=jnp.int32)) % req_count
+        rows_all = jnp.take(arrived, order, axis=0).reshape(req_count * row_count, model_width)
+    else:
+        rows_all = lax.all_gather(normed, "req", axis=0, tiled=True)
 
     mixed = jnp.zeros((rows_all.shape[0], model_width), jnp.float32)
     for local_block in range(local_count):
@@ -155,11 +165,10 @@
         produced = produced.astype(jnp.bfloat16).astype(jnp.float32)
         mixed = mixed + weights_own[:, local_block : local_block + 1] * produced
 
-    mixed = mixed.reshape(req_count, row_count, tp_count, own_width)
+    mixed = mixed.astype(jnp.bfloat16).reshape(req_count, row_count, tp_count, own_width)
     mixed = jnp.transpose(mixed, (0, 2, 1, 3)).reshape(req_count * tp_count, row_count, own_width)
-    mixed = lax.psum_scatter(mixed, ("req", "tp"), scatter_dimension=0, tiled=True)
-    mixed = mixed.reshape(row_count, own_width)
-    residual_own = lax.dynamic_slice_in_dim(residual, tp_index * own_width, own_width, 1)
+    mixed = lax.all_to_all(mixed, ("req", "tp"), 0, 0, tiled=True)
+    mixed = jnp.sum(mixed.astype(jnp.float32), axis=0)
     return (residual_own + mixed).astype(jnp.bfloat16)
 
 

time: 227 us -> 121 us (0.53)
  waiting for transfers between devices: 98.7 us -> 10.1 us
  starting transfers between devices: 0.04 us -> 17.5 us
  blocking collectives: 80.5 us -> 64.5 us
  between operations: 13.8 us -> 0.5 us
  matrix products: 20.2 us -> 17.3 us
    unnamed x3 -> x0, waiting for transfers between devices: 97.7 us -> none
    all_gather x3 -> x2, blocking collectives: 49.5 us -> 11.7 us  [the longest x1 6.21 us: per_device(): lax.all_gather(q_local.reshape(row_count, own_width), 'tp', axis=0)]
    all_to_all x0 -> x1, blocking collectives: none -> 21.4 us  [per_device(): mixed = lax.all_to_all(mixed, ('req', 'tp'), 0, 0, tiled=True)]
    ppermute x0 -> x7, starting transfers between devices: none -> 10.8 us  [per_device(): lax.ppermute(normed, 'req', [(i, (i + shift) % req_count) for i in range(...]
    all_to_all x0 -> x2, starting transfers between devices: none -> 6.78 us  [the longest x1 3.45 us: per_device(): lax.all_to_all(jnp.transpose(states, (1, 0, 2, 3)), 'tp', 0, 0, tiled=True)]
    ppermute x0 -> x7, waiting for transfers between devices: none -> 5.41 us  [per_device(): lax.ppermute(normed, 'req', [(i, (i + shift) % req_count) for i in range(...]
    all_to_all x0 -> x2, waiting for transfers between devices: none -> 4.73 us  [the longest x1 4.73 us: per_device(): lax.all_to_all(partial_proj, 'tp', 0, 0, tiled=True)]
    dot_general x4, matrix products: 11 us -> 8.5 us  [per_device(): jnp.dot(activation, down[local_block], preferred_element_type=jnp.float32)]
  transfers between devices with their start and end apart: 2 -> 9, of which waited for: 2 -> 4; matrix products, arithmetic and copies ran while one was open for 0% -> 2% of each run, Pallas kernels for 0% -> 0%
where the time goes in v2:
time: 121 us; the launch traced here: 120 us
  blocking collectives  64.5 us (53%)
  starting transfers between devices  17.5 us (14%)
  matrix products  17.3 us (14%)
  waiting for transfers between devices  10.1 us (8%)
  local copies, waits for them, and re-layouts  5.31 us (4%)
  other arithmetic  5.16 us (4%)
    all_gather x1, blocking collectives, per_device(): weights_all = lax.all_gather(block_weights, 'req', axis=0, tiled=True)  31.4 us
    all_to_all x1, blocking collectives, per_device(): mixed = lax.all_to_all(mixed, ('req', 'tp'), 0, 0, tiled=True)  21.4 us
    ppermute x7, starting transfers between devices, per_device(): lax.ppermute(normed, 'req', [(i, (i + shift) % req_count) for i in range(...  10.8 us
    dot_general x4, matrix products, per_device(): jnp.dot(activation, down[local_block], preferred_element_type=jnp.float32)  8.5 us
    dot_general x4, matrix products, per_device(): jnp.dot(rows_all, gate_up[local_block, 0], preferred_element_type=jnp.flo...  6.27 us
    all_gather x1, blocking collectives, per_device(): lax.all_gather(q_local.reshape(row_count, own_width), 'tp', axis=0)  6.21 us
    all_gather x1, blocking collectives, per_device(): residual = lax.all_gather(residual_own, 'tp', axis=1, tiled=True)  5.46 us
    ppermute x7, waiting for transfers between devices, per_device(): lax.ppermute(normed, 'req', [(i, (i + shift) % req_count) for i in range(...  5.41 us
  transfers between devices with their start and end apart: 9, of which 4 were waited for; matrix products, arithmetic and copies ran while one was open for 2% of the time, Pallas kernels for 0%

profile of v2, /device:TPU:0, one launch (start us, length us, event | category | flops | bytes accessed | tf_op | source)
XLA Modules:
  0.0 120.4 jit_solution(3855626917030198928)
XLA Ops:
  0.0 0.7 convert_element_type.108
  0.7 0.7 reshape.541
  1.5 0.1 multiply_cosine_fusion
  1.8 6.2 %all_gather.9 = bf16[4,24,384]{2,1,0:T(8,128)(2,1)S(1)} all-gather(bf16[1,24,384]{2,1,0:T(8,128)(2,1)S(1)} %convert_element_type.109), channel_id=1, replica_groups=mesh['req'=8,'tp'=4] {'tp'}, dimensions={0}, use_global_device_ids=true | all-gather | bytes 92160 | tf_op jit(solution)/shard_map/all_gather | solution.py:62
  8.2 0.7 copy.55
  9.1 0.7 bitcast_subtract_fusion.1
  9.7 0.5 fusion.71
  10.4 0.5 fusion.73
  10.8 0.1 concatenate.24
  11.0 0.3 fusion.19
  11.3 0.7 fusion.18
  12.2 0.9 maximum_bitcast_fusion
  13.1 3.5 %all-to-all-start = ((f32[4,24,3,130]{3,1,2,0:T(8,128)}), f32[4,24,3,130]{3,1,2,0:T(8,128)S(1)}, u32[]{:S(2)}, u32[]{:S(2)}) async-start(f32[4,24,3,130]{3,1,2,0:T(8,128)} %maximum_bitcast_fusion), calls=%async_computation | async-start | bytes 589824 | tf_op jit(solution)/shard_map/all_to_all | solution.py:105
  16.9 0.2 fusion.60
  17.3 31.4 %all_gather.10 = f32[192,32]{1,0:T(8,128)S(1)} all-gather(f32[24,32]{1,0:T(8,128)S(1)} %select_reduce_fusion), channel_id=1, replica_groups=mesh['req'=8,'tp'=4] {'req'}, dimensions={0}, use_global_device_ids=true | all-gather | bytes 27648 | tf_op jit(solution)/shard_map/all_gather | solution.py:146
  48.8 0.4 dynamic-slice_reduce_fusion
  49.1 0.7 copy.75
  49.9 0.6 gather_fusion
  50.5 0.1 fusion.72
  50.6 0.1 copy.79
  50.8 0.1 copy.67
  51.0 0.1 fusion.55
  51.3 1.2 convolution_bitcast_fusion
  52.5 3.3 %all-to-all-start.1 = ((f32[4,24,384]{2,1,0:T(8,128)}), f32[4,24,384]{2,1,0:T(8,128)S(1)}, u32[]{:S(2)}, u32[]{:S(2)}) async-start(f32[4,24,384]{2,1,0:T(8,128)} %convolution_bitcast_fusion), calls=%async_computation.1 | async-start | bytes 294912 | tf_op jit(solution)/shard_map/all_to_all | solution.py:125
  55.8 4.7 %all-to-all-done.1 = f32[4,24,384]{2,1,0:T(8,128)S(1)} async-done(((f32[4,24,384]{2,1,0:T(8,128)}), f32[4,24,384]{2,1,0:T(8,128)S(1)}, u32[]{:S(2)}, u32[]{:S(2)}) %all-to-all-start.1) | async-done | bytes 147488 | tf_op jit(solution)/shard_map/all_to_all | solution.py:125
  60.6 5.5 %all_gather.11 = f32[24,1536]{1,0:T(8,128)S(1)} all-gather(f32[24,384]{1,0:T(8,128)S(1)} %convert_add_fusion), channel_id=1, replica_groups=mesh['req'=8,'tp'=4] {'tp'}, dimensions={1}, use_global_device_ids=true | all-gather | bytes 184320 | tf_op jit(solution)/shard_map/all_gather | solution.py:127
  66.1 0.1 multiply_reduce_fusion
  66.3 1.6 %collective-permute-start = (bf16[24,1536]{1,0:T(8,128)(2,1)S(1)}, bf16[24,1536]{1,0:T(8,128)(2,1)S(1)}, u32[]{:S(2)}, u32[]{:S(2)}) collective-permute-start(bf16[24,1536]{1,0:T(8,128)(2,1)S(1)} %get-tuple-element.10), channel_id=1, source_target_pairs={{0,4},{4,8},{8,12},{12,16},{16,20},{20,24},{24,28},{28,0},{1,5},{5... | collective-permute-start | bytes 221192 | tf_op jit(solution)/shard_map/ppermute | solution.py:150
  67.9 1.1 collective-permute-start.2
  69.0 2.8 %collective-permute-start.3 = (bf16[24,1536]{1,0:T(8,128)(2,1)S(1)}, bf16[24,1536]{1,0:T(8,128)(2,1)S(1)}, u32[]{:S(2)}, u32[]{:S(2)}) collective-permute-start(bf16[24,1536]{1,0:T(8,128)(2,1)S(1)} %get-tuple-element.10), channel_id=1, source_target_pairs={{0,16},{4,20},{8,24},{12,28},{16,0},{20,4},{24,8},{28,12},{1,17},{... | collective-permute-start | bytes 221192 | tf_op jit(solution)/shard_map/ppermute | solution.py:150
  71.8 3.8 %collective-permute-start.4 = (bf16[24,1536]{1,0:T(8,128)(2,1)S(1)}, bf16[24,1536]{1,0:T(8,128)(2,1)S(1)}, u32[]{:S(2)}, u32[]{:S(2)}) collective-permute-start(bf16[24,1536]{1,0:T(8,128)(2,1)S(1)} %get-tuple-element.10), channel_id=1, source_target_pairs={{0,20},{4,24},{8,28},{12,0},{16,4},{20,8},{24,12},{28,16},{1,21},{... | collective-permute-start | bytes 221192 | tf_op jit(solution)/shard_map/ppermute | solution.py:150
  75.6 1.5 %collective-permute-start.6 = (bf16[24,1536]{1,0:T(8,128)(2,1)S(1)}, bf16[24,1536]{1,0:T(8,128)(2,1)S(1)}, u32[]{:S(2)}, u32[]{:S(2)}) collective-permute-start(bf16[24,1536]{1,0:T(8,128)(2,1)S(1)} %get-tuple-element.10), channel_id=1, source_target_pairs={{0,28},{4,0},{8,4},{12,8},{16,12},{20,16},{24,20},{28,24},{1,29},{... | collective-permute-start | bytes 221192 | tf_op jit(solution)/shard_map/ppermute | solution.py:150
  77.1 3.0 %collective-permute-done.2 = bf16[24,1536]{1,0:T(8,128)(2,1)S(1)} collective-permute-done((bf16[24,1536]{1,0:T(8,128)(2,1)S(1)}, bf16[24,1536]{1,0:T(8,128)(2,1)S(1)}, u32[]{:S(2)}, u32[]{:S(2)}) %collective-permute-start.2) | collective-permute-done | bytes 73760 | tf_op jit(solution)/shard_map/ppermute | solution.py:150
  80.1 0.4 collective-permute-done.3
  80.5 2.0 %collective-permute-done.5 = bf16[24,1536]{1,0:T(8,128)(2,1)S(1)} collective-permute-done((bf16[24,1536]{1,0:T(8,128)(2,1)S(1)}, bf16[24,1536]{1,0:T(8,128)(2,1)S(1)}, u32[]{:S(2)}, u32[]{:S(2)}) %collective-permute-start.5) | collective-permute-done | bytes 73760 | tf_op jit(solution)/shard_map/ppermute | solution.py:150
  82.6 0.6 gather_fusion.1
  83.2 0.1 broadcast_select_fusion
  83.3 1.4 %convolution_maximum_fusion.3 = f32[192,192]{1,0:T(8,128)S(1)} fusion(bf16[192,1536]{1,0:T(8,128)(2,1)S(1)} %bitcast.140, bf16[4,2,1536,192]{2,3,1,0:T(8,128)(2,1)} %param.22), kind=kOutput, calls=%fused_computation.29 | convolution fusion | flops 113283072 | bytes 1327104 | tf_op jit(solution)/shard_map/dot_general | solution.py:161
  84.7 2.1 %convolution_maximum_fusion.2 = f32[192,192]{1,0:T(8,128)} fusion(bf16[192,1536]{1,0:T(8,128)(2,1)S(1)} %bitcast.141, bf16[4,2,1536,192]{2,3,1,0:T(8,128)(2,1)} %param.22), kind=kOutput, calls=%fused_computation.27 | convolution fusion | flops 113283072 | bytes 1327104 | tf_op jit(solution)/shard_map/dot_general | solution.py:161
  86.8 1.4 %convolution_maximum_fusion.1 = f32[192,192]{1,0:T(8,128)S(1)} fusion(bf16[192,1536]{1,0:T(8,128)(2,1)S(1)} %bitcast.142, bf16[4,2,1536,192]{2,3,1,0:T(8,128)(2,1)} %param.22), kind=kOutput, calls=%fused_computation.25 | convolution fusion | flops 113283072 | bytes 1327104 | tf_op jit(solution)/shard_map/dot_general | solution.py:161
  88.2 1.4 %convolution_maximum_fusion = f32[192,192]{1,0:T(8,128)S(1)} fusion(bf16[192,1536]{1,0:T(8,128)(2,1)S(1)} %bitcast.143, bf16[4,2,1536,192]{2,3,1,0:T(8,128)(2,1)} %param.22), kind=kOutput, calls=%fused_computation.23 | convolution fusion | flops 113283072 | bytes 1327104 | tf_op jit(solution)/shard_map/dot_general | solution.py:161
  89.6 2.1 %fusion.11 = f32[192,1536]{1,0:T(8,128)S(1)} fusion(f32[192,192]{1,0:T(8,128)S(1)} %convolution_maximum_fusion.3, bf16[192,1536]{1,0:T(8,128)(2,1)S(1)} %bitcast.144, bf16[4,192,1536]{2,1,0:T(8,128)(2,1)} %param.23, bf16[4,2,1536,192]{2,3,1,0:T(8,128)(2,1)} %param.22, f32[192]{0:T(256)S(1)} %get-tuple-element.8), kind=kOutput, calls=%fused_computation.17 | convolution fusion | flops 227450880 | bytes 3097344 | tf_op jit(solution)/shard_map/dot_general | solution.py:164
  91.7 2.2 %fusion.9 = f32[192,1536]{1,0:T(8,128)S(1)} fusion(f32[192,1536]{1,0:T(8,128)S(1)} %fusion.11, f32[192,192]{1,0:T(8,128)} %convolution_maximum_fusion.2, bf16[192,1536]{1,0:T(8,128)(2,1)S(1)} %bitcast.145, bf16[4,192,1536]{2,1,0:T(8,128)(2,1)} %param.23, bf16[4,2,1536,192]{2,3,1,0:T(8,128)(2,1)} %param.22, f32[192]{0:T(256)S(1)} %get-tuple-element.7), kind=kOutput, calls=%fused_computation.14 | convolution fusion | flops 227745792 | bytes 4326144 | tf_op jit(solution)/shard_map/dot_general | solution.py:164
  93.9 2.1 %fusion.6 = f32[192,1536]{1,0:T(8,128)S(1)} fusion(f32[192,1536]{1,0:T(8,128)S(1)} %fusion.9, f32[192,192]{1,0:T(8,128)S(1)} %convolution_maximum_fusion.1, bf16[192,1536]{1,0:T(8,128)(2,1)S(1)} %bitcast.146, bf16[4,192,1536]{2,1,0:T(8,128)(2,1)} %param.23, bf16[4,2,1536,192]{2,3,1,0:T(8,128)(2,1)} %param.22, f32[192]{0:T(256)S(1)} %get-tuple-element.6), kind=kOutput, calls=%fused_computation.10 | convolution fusion | flops 227745792 | bytes 4276992 | tf_op jit(solution)/shard_map/dot_general | solution.py:164
  96.0 2.1 %fusion.3 = bf16[192,1536]{1,0:T(8,128)(2,1)S(1)} fusion(f32[192,1536]{1,0:T(8,128)S(1)} %fusion.6, f32[192,192]{1,0:T(8,128)S(1)} %convolution_maximum_fusion, bf16[192,1536]{1,0:T(8,128)(2,1)S(1)} %bitcast.147, bf16[4,192,1536]{2,1,0:T(8,128)(2,1)} %param.23, bf16[4,2,1536,192]{2,3,1,0:T(8,128)(2,1)} %param.22, f32[192]{0:T(256)S(1)} %get-tuple-element.5), kind=kOutput, calls=%fused_computation.6 | convolution fusion | flops 228040704 | bytes 3687168 | tf_op jit(solution)/shard_map/dot_general | solution.py:164
  98.1 0.1 reshape.539
  98.4 21.4 %all_to_all.15 = bf16[32,24,384]{2,1,0:T(8,128)(2,1)S(1)} all-to-all(bf16[32,24,384]{2,1,0:T(8,128)(2,1)S(1)} %bitcast.149), channel_id=1, replica_groups=mesh['req'=8,'tp'=4] {'req','tp'}, dimensions={0} | all-to-all | bytes 1179648 | tf_op jit(solution)/shard_map/all_to_all | solution.py:170
  119.8 0.6 add_convert_fusion.1
  (67 shorter events, 1.9 us)
Async XLA Ops:
  0.0 9.7 %copy-start.1 = (bf16[768,2,2,128]{3,2,1,0:T(2,128)(2,1)S(1)}, bf16[768,2,2,128]{3,2,1,0:T(2,128)(2,1)}, u32[]{:S(2)}) copy-start(bf16[768,2,2,128]{3,2,1,0:T(2,128)(2,1)} %param.17) | copy-start | bytes 2359300
  11.3 5.3 %copy-start.2 = (bf16[24,2,256]{2,1,0:T(2,128)(2,1)S(1)}, bf16[24,2,256]{2,1,0:T(2,128)(2,1)}, u32[]{:S(2)}) copy-start(bf16[24,2,256]{2,1,0:T(2,128)(2,1)} %param.14) | copy-start | bytes 73732
  12.0 5.2 %copy-start.5 = (f32[24,4]{0,1:T(4,128)S(1)}, f32[24,4]{0,1:T(4,128)}, u32[]{:S(2)}) copy-start(f32[24,4]{0,1:T(4,128)} %param.21) | copy-start | bytes 1156
  12.0 5.2 %copy-start.6 = (s32[24,4]{0,1:T(4,128)S(1)}, s32[24,4]{0,1:T(4,128)}, u32[]{:S(2)}) copy-start(s32[24,4]{0,1:T(4,128)} %param.20) | copy-start | bytes 1156
  12.1 37.0 %copy-start = (bf16[384,1536]{1,0:T(8,128)(2,1)S(1)}, bf16[384,1536]{1,0:T(8,128)(2,1)}, u32[]{:S(2)}) copy-start(bf16[384,1536]{1,0:T(8,128)(2,1)} %param.18) | copy-start | bytes 3538948
  13.1 37.4 %all-to-all-start = ((f32[4,24,3,130]{3,1,2,0:T(8,128)}), f32[4,24,3,130]{3,1,2,0:T(8,128)S(1)}, u32[]{:S(2)}, u32[]{:S(2)}) async-start(f32[4,24,3,130]{3,1,2,0:T(8,128)} %maximum_bitcast_fusion), calls=%async_computation | async-start | bytes 589824 | tf_op jit(solution)/shard_map/all_to_all | solution.py:105
  50.7 9.8 %copy-start.3 = (bf16[24,384]{1,0:T(8,128)(2,1)S(1)}, bf16[24,384]{1,0:T(8,128)(2,1)}, u32[]{:S(2)}) copy-start(bf16[24,384]{1,0:T(8,128)(2,1)} %param.12) | copy-start | bytes 55300
  51.2 15.0 %copy-start.4 = (f32[1536]{0:T(1024)S(1)}, f32[1536]{0:T(1024)}, u32[]{:S(2)}) copy-start(f32[1536]{0:T(1024)} %param.19) | copy-start | bytes 18436
  52.5 8.1 %all-to-all-start.1 = ((f32[4,24,384]{2,1,0:T(8,128)}), f32[4,24,384]{2,1,0:T(8,128)S(1)}, u32[]{:S(2)}, u32[]{:S(2)}) async-start(f32[4,24,384]{2,1,0:T(8,128)} %convolution_bitcast_fusion), calls=%async_computation.1 | async-start | bytes 294912 | tf_op jit(solution)/shard_map/all_to_all | solution.py:125
  66.3 9.3 %collective-permute-start = (bf16[24,1536]{1,0:T(8,128)(2,1)S(1)}, bf16[24,1536]{1,0:T(8,128)(2,1)S(1)}, u32[]{:S(2)}, u32[]{:S(2)}) collective-permute-start(bf16[24,1536]{1,0:T(8,128)(2,1)S(1)} %get-tuple-element.10), channel_id=1, source_target_pairs={{0,4},{4,8},{8,12},{12,16},{16,20},{20,24},{24,28},{28,0},{1,5},{5... | collective-permute-start | bytes 221192 | tf_op jit(solution)/shard_map/ppermute | solution.py:150
  67.9 7.7 %collective-permute-start.1 = (bf16[24,1536]{1,0:T(8,128)(2,1)S(1)}, bf16[24,1536]{1,0:T(8,128)(2,1)S(1)}, u32[]{:S(2)}, u32[]{:S(2)}) collective-permute-start(bf16[24,1536]{1,0:T(8,128)(2,1)S(1)} %get-tuple-element.10), channel_id=1, source_target_pairs={{0,8},{4,12},{8,16},{12,20},{16,24},{20,28},{24,0},{28,4},{1,9},{5... | collective-permute-start | bytes 221192 | tf_op jit(solution)/shard_map/ppermute | solution.py:150
  67.9 12.1 %collective-permute-start.2 = (bf16[24,1536]{1,0:T(8,128)(2,1)S(1)}, bf16[24,1536]{1,0:T(8,128)(2,1)S(1)}, u32[]{:S(2)}, u32[]{:S(2)}) collective-permute-start(bf16[24,1536]{1,0:T(8,128)(2,1)S(1)} %get-tuple-element.10), channel_id=1, source_target_pairs={{0,12},{4,16},{8,20},{12,24},{16,28},{20,0},{24,4},{28,8},{1,13},{... | collective-permute-start | bytes 221192 | tf_op jit(solution)/shard_map/ppermute | solution.py:150
  69.0 11.5 %collective-permute-start.3 = (bf16[24,1536]{1,0:T(8,128)(2,1)S(1)}, bf16[24,1536]{1,0:T(8,128)(2,1)S(1)}, u32[]{:S(2)}, u32[]{:S(2)}) collective-permute-start(bf16[24,1536]{1,0:T(8,128)(2,1)S(1)} %get-tuple-element.10), channel_id=1, source_target_pairs={{0,16},{4,20},{8,24},{12,28},{16,0},{20,4},{24,8},{28,12},{1,17},{... | collective-permute-start | bytes 221192 | tf_op jit(solution)/shard_map/ppermute | solution.py:150
  71.8 8.7 %collective-permute-start.4 = (bf16[24,1536]{1,0:T(8,128)(2,1)S(1)}, bf16[24,1536]{1,0:T(8,128)(2,1)S(1)}, u32[]{:S(2)}, u32[]{:S(2)}) collective-permute-start(bf16[24,1536]{1,0:T(8,128)(2,1)S(1)} %get-tuple-element.10), channel_id=1, source_target_pairs={{0,20},{4,24},{8,28},{12,0},{16,4},{20,8},{24,12},{28,16},{1,21},{... | collective-permute-start | bytes 221192 | tf_op jit(solution)/shard_map/ppermute | solution.py:150
  75.6 7.0 %collective-permute-start.5 = (bf16[24,1536]{1,0:T(8,128)(2,1)S(1)}, bf16[24,1536]{1,0:T(8,128)(2,1)S(1)}, u32[]{:S(2)}, u32[]{:S(2)}) collective-permute-start(bf16[24,1536]{1,0:T(8,128)(2,1)S(1)} %get-tuple-element.10), channel_id=1, source_target_pairs={{0,24},{4,28},{8,0},{12,4},{16,8},{20,12},{24,16},{28,20},{1,25},{... | collective-permute-start | bytes 221192 | tf_op jit(solution)/shard_map/ppermute | solution.py:150
  75.6 7.0 %collective-permute-start.6 = (bf16[24,1536]{1,0:T(8,128)(2,1)S(1)}, bf16[24,1536]{1,0:T(8,128)(2,1)S(1)}, u32[]{:S(2)}, u32[]{:S(2)}) collective-permute-start(bf16[24,1536]{1,0:T(8,128)(2,1)S(1)} %get-tuple-element.10), channel_id=1, source_target_pairs={{0,28},{4,0},{8,4},{12,8},{16,12},{20,16},{24,20},{28,24},{1,29},{... | collective-permute-start | bytes 221192 | tf_op jit(solution)/shard_map/ppermute | solution.py:150

commit v3 on v1

--- a/solution.py
+++ b/solution.py
@@ -103,9 +103,10 @@
     )
     states = jnp.concatenate(
         [highest_local[..., None], totals_local[..., None], sums_local], axis=3
-    ).reshape(row_count, head_count, head_size + 2)
-    all_states = lax.all_gather(states, "tp", axis=0)
-    all_states = lax.dynamic_slice_in_dim(all_states, first_head, own_heads, 2)
+    ).reshape(row_count, tp_count, own_heads, head_size + 2)
+    all_states = lax.all_to_all(
+        jnp.transpose(states, (1, 0, 2, 3)), "tp", 0, 0, tiled=True
+    )
     parts_highest = all_states[..., 0]
     parts_totals = all_states[..., 1]
     parts_sums = all_states[..., 2:]
@@ -122,10 +123,11 @@
     )
 
     partial_proj = jnp.dot(attention_output, out_proj, preferred_element_type=jnp.float32)
-    projected = lax.psum(partial_proj, "tp")
+    projected = jnp.sum(lax.all_gather(partial_proj, "tp", axis=0), axis=0)
     residual = hidden_full.astype(jnp.float32) + projected
     mean_square = jnp.mean(residual * residual, axis=1, keepdims=True)
     normed = (residual * lax.rsqrt(mean_square + norm_eps) * norm_gain[None, :]).astype(jnp.bfloat16)
+    residual_own = lax.dynamic_slice_in_dim(residual, tp_index * own_width, own_width, 1)
 
     local_count = gate_up.shape[0]
     block_total = local_count * req_count
@@ -142,8 +144,20 @@
         axis=1,
     )
 
-    rows_all = lax.all_gather(normed, "req", axis=0, tiled=True)
-    weights_all = lax.all_gather(block_weights, "req", axis=0, tiled=True)
+    if req_count <= 16:
+        def gather_req(value):
+            arrived = [value] + [
+                lax.ppermute(value, "req", [(i, (i + shift) % req_count) for i in range(req_count)])
+                for shift in range(1, req_count)
+            ]
+            order = (req_index - jnp.arange(req_count, dtype=jnp.int32)) % req_count
+            arrived = jnp.take(jnp.stack(arrived, axis=0), order, axis=0)
+            return arrived.reshape((req_count * value.shape[0],) + value.shape[1:])
+    else:
+        def gather_req(value):
+            return lax.all_gather(value, "req", axis=0, tiled=True)
+    rows_all = gather_req(normed)
+    weights_all = gather_req(block_weights)
     weights_own = lax.dynamic_slice_in_dim(weights_all, req_index * local_count, local_count, 1)
 
     mixed = jnp.zeros((rows_all.shape[0], model_width), jnp.float32)
@@ -155,11 +169,10 @@
         produced = produced.astype(jnp.bfloat16).astype(jnp.float32)
         mixed = mixed + weights_own[:, local_block : local_block + 1] * produced
 
-    mixed = mixed.reshape(req_count, row_count, tp_count, own_width)
+    mixed = mixed.astype(jnp.bfloat16).reshape(req_count, row_count, tp_count, own_width)
     mixed = jnp.transpose(mixed, (0, 2, 1, 3)).reshape(req_count * tp_count, row_count, own_width)
-    mixed = lax.psum_scatter(mixed, ("req", "tp"), scatter_dimension=0, tiled=True)
-    mixed = mixed.reshape(row_count, own_width)
-    residual_own = lax.dynamic_slice_in_dim(residual, tp_index * own_width, own_width, 1)
+    mixed = lax.all_to_all(mixed, ("req", "tp"), 0, 0, tiled=True)
+    mixed = jnp.sum(mixed.astype(jnp.float32), axis=0)
     return (residual_own + mixed).astype(jnp.bfloat16)
 
 

time: 227 us -> 105 us (0.46)
  waiting for transfers between devices: 98.7 us -> 24.5 us
  blocking collectives: 80.5 us -> 13.5 us
  starting transfers between devices: 0.04 us -> 32.8 us
  between operations: 13.8 us -> 0.52 us
    unnamed x3 -> x0, waiting for transfers between devices: 97.7 us -> none
    all_gather x3 -> x1, blocking collectives: 73.9 us -> 8.01 us  [per_device(): projected = jnp.sum(lax.all_gather(partial_proj, 'tp', axis=0), axis=0)]
    ppermute x0 -> x14, starting transfers between devices: none -> 24.5 us  [gather_req(): lax.ppermute(value, 'req', [(i, (i + shift) % req_count) for i in range(r...]
    all_to_all x0 -> x2, waiting for transfers between devices: none -> 16.8 us  [the longest x1 16.8 us: per_device(): mixed = lax.all_to_all(mixed, ('req', 'tp'), 0, 0, tiled=True)]
    all_to_all x0 -> x2, starting transfers between devices: none -> 8.27 us  [the longest x1 4.82 us: per_device(): mixed = lax.all_to_all(mixed, ('req', 'tp'), 0, 0, tiled=True)]
    ppermute x0 -> x14, waiting for transfers between devices: none -> 7.65 us  [gather_req(): lax.ppermute(value, 'req', [(i, (i + shift) % req_count) for i in range(r...]
  transfers between devices with their start and end apart: 2 -> 16, of which waited for: 2 -> 6; matrix products, arithmetic and copies ran while one was open for 0% -> 10% of each run, Pallas kernels for 0% -> 0%
where the time goes in v3:
time: 105 us
  starting transfers between devices  32.8 us (31%)
  waiting for transfers between devices  24.5 us (23%)
  matrix products  19.1 us (18%)
  blocking collectives  13.5 us (13%)
  local copies, waits for them, and re-layouts  7.48 us (7%)
  other arithmetic  6.69 us (6%)
    ppermute x14, starting transfers between devices, gather_req(): lax.ppermute(value, 'req', [(i, (i + shift) % req_count) for i in range(r...  24.5 us
    all_to_all x1, waiting for transfers between devices, per_device(): mixed = lax.all_to_all(mixed, ('req', 'tp'), 0, 0, tiled=True)  16.8 us
    dot_general x4, matrix products, per_device(): jnp.dot(activation, down[local_block], preferred_element_type=jnp.float32)  11.3 us
    all_gather x1, blocking collectives, per_device(): projected = jnp.sum(lax.all_gather(partial_proj, 'tp', axis=0), axis=0)  8.01 us
    ppermute x14, waiting for transfers between devices, gather_req(): lax.ppermute(value, 'req', [(i, (i + shift) % req_count) for i in range(r...  7.65 us
    dot_general x4, matrix products, per_device(): jnp.dot(rows_all, gate_up[local_block, 0], preferred_element_type=jnp.flo...  6.26 us
    all_gather x1, blocking collectives, per_device(): gathered = lax.all_gather(packed, 'tp', axis=0)  5.45 us
    all_to_all x1, starting transfers between devices, per_device(): mixed = lax.all_to_all(mixed, ('req', 'tp'), 0, 0, tiled=True)  4.82 us
  transfers between devices with their start and end apart: 16, of which 6 were waited for; matrix products, arithmetic and copies ran while one was open for 10% of the time, Pallas kernels for 0%

profile of v3, /device:TPU:0, one launch (start us, length us, event | category | flops | bytes accessed | tf_op | source)
XLA Modules:
  0.0 104.5 jit_solution(5290123499897645492)
XLA Ops:
  0.0 0.9 select_reduce_fusion
  0.9 3.0 %collective-permute-start = (f32[24,32]{1,0:T(8,128)S(1)}, f32[24,32]{1,0:T(8,128)S(1)}, u32[]{:S(2)}, u32[]{:S(2)}) collective-permute-start(f32[24,32]{1,0:T(8,128)S(1)} %select_reduce_fusion), channel_id=1, source_target_pairs={{0,4},{4,8},{8,12},{12,16},{16,20},{20,24},{24,28},{28,0},{1,5},{5... | collective-permute-start | bytes 9224 | tf_op jit(solution)/shard_map/ppermute | solution.py:150
  3.9 1.6 %collective-permute-start.1 = (f32[24,32]{1,0:T(8,128)S(1)}, f32[24,32]{1,0:T(8,128)S(1)}, u32[]{:S(2)}, u32[]{:S(2)}) collective-permute-start(f32[24,32]{1,0:T(8,128)S(1)} %select_reduce_fusion), channel_id=1, source_target_pairs={{0,8},{4,12},{8,16},{12,20},{16,24},{20,28},{24,0},{28,4},{1,9},{5... | collective-permute-start | bytes 9224 | tf_op jit(solution)/shard_map/ppermute | solution.py:150
  5.5 2.5 %collective-permute-start.2 = (f32[24,32]{1,0:T(8,128)S(1)}, f32[24,32]{1,0:T(8,128)S(1)}, u32[]{:S(2)}, u32[]{:S(2)}) collective-permute-start(f32[24,32]{1,0:T(8,128)S(1)} %select_reduce_fusion), channel_id=1, source_target_pairs={{0,12},{4,16},{8,20},{12,24},{16,28},{20,0},{24,4},{28,8},{1,13},{... | collective-permute-start | bytes 9224 | tf_op jit(solution)/shard_map/ppermute | solution.py:150
  8.1 1.2 %collective-permute-start.3 = (f32[24,32]{1,0:T(8,128)S(1)}, f32[24,32]{1,0:T(8,128)S(1)}, u32[]{:S(2)}, u32[]{:S(2)}) collective-permute-start(f32[24,32]{1,0:T(8,128)S(1)} %select_reduce_fusion), channel_id=1, source_target_pairs={{0,16},{4,20},{8,24},{12,28},{16,0},{20,4},{24,8},{28,12},{1,17},{... | collective-permute-start | bytes 9224 | tf_op jit(solution)/shard_map/ppermute | solution.py:150
  9.3 2.6 %collective-permute-start.4 = (f32[24,32]{1,0:T(8,128)S(1)}, f32[24,32]{1,0:T(8,128)S(1)}, u32[]{:S(2)}, u32[]{:S(2)}) collective-permute-start(f32[24,32]{1,0:T(8,128)S(1)} %select_reduce_fusion), channel_id=1, source_target_pairs={{0,20},{4,24},{8,28},{12,0},{16,4},{20,8},{24,12},{28,16},{1,21},{... | collective-permute-start | bytes 9224 | tf_op jit(solution)/shard_map/ppermute | solution.py:150
  11.9 0.7 convert_element_type.128
  12.6 0.7 reshape.581
  13.7 0.7 pad_maximum_fusion
  14.4 5.4 %all-gather = bf16[8,24,384]{2,1,0:T(8,128)(2,1)S(1)} all-gather(bf16[2,24,384]{2,1,0:T(8,128)(2,1)S(1)} %pad_maximum_fusion), channel_id=2, replica_groups=mesh['req'=8,'tp'=4] {'tp'}, dimensions={0}, use_global_device_ids=true | all-gather | bytes 184320 | tf_op jit(solution)/shard_map/all_gather | solution.py:63
  20.0 0.7 copy.84
  20.9 0.7 bitcast_subtract_fusion.1
  21.6 1.7 %fusion.82 = (bf16[768,1,2,128]{3,2,1,0:T(2,128)(2,1)S(1)}, bf16[768,1,2,128]{3,2,1,0:T(2,128)(2,1)S(1)}) fusion(bf16[768,2,2,128]{3,2,1,0:T(2,128)(2,1)} %param.17), kind=kLoop, calls=%fused_computation.166 | loop fusion | bytes 1572864 | tf_op jit(solution)/shard_map/slice | solution.py:88
  23.3 0.5 fusion.84
  24.0 0.3 fusion.19
  24.3 0.7 fusion.18
  25.1 0.9 maximum_bitcast_fusion
  26.0 3.5 %all-to-all-start = ((f32[4,24,3,130]{3,1,2,0:T(8,128)}), f32[4,24,3,130]{3,1,2,0:T(8,128)S(1)}, u32[]{:S(2)}, u32[]{:S(2)}) async-start(f32[4,24,3,130]{3,1,2,0:T(8,128)} %maximum_bitcast_fusion), calls=%async_computation | async-start | bytes 589824 | tf_op jit(solution)/shard_map/all_to_all | solution.py:107
  30.6 0.6 gather_fusion
  31.1 1.4 %collective-permute-start.5 = (f32[24,32]{1,0:T(8,128)S(1)}, f32[24,32]{1,0:T(8,128)S(1)}, u32[]{:S(2)}, u32[]{:S(2)}) collective-permute-start(f32[24,32]{1,0:T(8,128)S(1)} %select_reduce_fusion), channel_id=1, source_target_pairs={{0,24},{4,28},{8,0},{12,4},{16,8},{20,12},{24,16},{28,20},{1,25},{... | collective-permute-start | bytes 9224 | tf_op jit(solution)/shard_map/ppermute | solution.py:150
  32.6 1.4 %collective-permute-start.6 = (f32[24,32]{1,0:T(8,128)S(1)}, f32[24,32]{1,0:T(8,128)S(1)}, u32[]{:S(2)}, u32[]{:S(2)}) collective-permute-start(f32[24,32]{1,0:T(8,128)S(1)} %select_reduce_fusion), channel_id=1, source_target_pairs={{0,28},{4,0},{8,4},{12,8},{16,12},{20,16},{24,20},{28,24},{1,29},{... | collective-permute-start | bytes 9224 | tf_op jit(solution)/shard_map/ppermute | solution.py:150
  34.0 0.9 collective-permute-done.5
  34.9 1.4 %collective-permute-done.6 = f32[24,32]{1,0:T(8,128)S(1)} collective-permute-done((f32[24,32]{1,0:T(8,128)S(1)}, f32[24,32]{1,0:T(8,128)S(1)}, u32[]{:S(2)}, u32[]{:S(2)}) %collective-permute-start.6) | collective-permute-done | bytes 3104 | tf_op jit(solution)/shard_map/ppermute | solution.py:150
  36.3 0.6 gather_fusion.1
  38.1 0.3 fusion.67
  38.3 8.0 %all-gather.1 = f32[96,1536]{1,0:T(8,128)S(1)} all-gather(f32[24,1536]{1,0:T(8,128)S(1)} %fusion.67), channel_id=3, replica_groups=mesh['req'=8,'tp'=4] {'tp'}, dimensions={0}, use_global_device_ids=true | all-gather | bytes 737280 | tf_op jit(solution)/shard_map/all_gather | solution.py:126
  46.6 1.6 %collective-permute-start.7 = (bf16[24,1536]{1,0:T(8,128)(2,1)S(1)}, bf16[24,1536]{1,0:T(8,128)(2,1)S(1)}, u32[]{:S(2)}, u32[]{:S(2)}) collective-permute-start(bf16[24,1536]{1,0:T(8,128)(2,1)S(1)} %get-tuple-element.5), channel_id=1, source_target_pairs={{0,4},{4,8},{8,12},{12,16},{16,20},{20,24},{24,28},{28,0},{1,5},{5... | collective-permute-start | bytes 221192 | tf_op jit(solution)/shard_map/ppermute | solution.py:150
  48.3 2.2 %collective-permute-start.9 = (bf16[24,1536]{1,0:T(8,128)(2,1)S(1)}, bf16[24,1536]{1,0:T(8,128)(2,1)S(1)}, u32[]{:S(2)}, u32[]{:S(2)}) collective-permute-start(bf16[24,1536]{1,0:T(8,128)(2,1)S(1)} %get-tuple-element.5), channel_id=1, source_target_pairs={{0,12},{4,16},{8,20},{12,24},{16,28},{20,0},{24,4},{28,8},{1,13},{... | collective-permute-start | bytes 221192 | tf_op jit(solution)/shard_map/ppermute | solution.py:150
  50.5 2.1 %collective-permute-start.10 = (bf16[24,1536]{1,0:T(8,128)(2,1)S(1)}, bf16[24,1536]{1,0:T(8,128)(2,1)S(1)}, u32[]{:S(2)}, u32[]{:S(2)}) collective-permute-start(bf16[24,1536]{1,0:T(8,128)(2,1)S(1)} %get-tuple-element.5), channel_id=1, source_target_pairs={{0,16},{4,20},{8,24},{12,28},{16,0},{20,4},{24,8},{28,12},{1,17},{... | collective-permute-start | bytes 221192 | tf_op jit(solution)/shard_map/ppermute | solution.py:150
  52.6 3.1 %collective-permute-start.11 = (bf16[24,1536]{1,0:T(8,128)(2,1)S(1)}, bf16[24,1536]{1,0:T(8,128)(2,1)S(1)}, u32[]{:S(2)}, u32[]{:S(2)}) collective-permute-start(bf16[24,1536]{1,0:T(8,128)(2,1)S(1)} %get-tuple-element.5), channel_id=1, source_target_pairs={{0,20},{4,24},{8,28},{12,0},{16,4},{20,8},{24,12},{28,16},{1,21},{... | collective-permute-start | bytes 221192 | tf_op jit(solution)/shard_map/ppermute | solution.py:150
  55.8 0.2 collective-permute-start.12
  56.0 1.4 %collective-permute-start.13 = (bf16[24,1536]{1,0:T(8,128)(2,1)S(1)}, bf16[24,1536]{1,0:T(8,128)(2,1)S(1)}, u32[]{:S(2)}, u32[]{:S(2)}) collective-permute-start(bf16[24,1536]{1,0:T(8,128)(2,1)S(1)} %get-tuple-element.5), channel_id=1, source_target_pairs={{0,28},{4,0},{8,4},{12,8},{16,12},{20,16},{24,20},{28,24},{1,29},{... | collective-permute-start | bytes 221192 | tf_op jit(solution)/shard_map/ppermute | solution.py:150
  57.4 3.0 %collective-permute-done.9 = bf16[24,1536]{1,0:T(8,128)(2,1)S(1)} collective-permute-done((bf16[24,1536]{1,0:T(8,128)(2,1)S(1)}, bf16[24,1536]{1,0:T(8,128)(2,1)S(1)}, u32[]{:S(2)}, u32[]{:S(2)}) %collective-permute-start.9) | collective-permute-done | bytes 73760 | tf_op jit(solution)/shard_map/ppermute | solution.py:150
  60.4 0.3 collective-permute-done.10
  60.8 2.1 %collective-permute-done.12 = bf16[24,1536]{1,0:T(8,128)(2,1)S(1)} collective-permute-done((bf16[24,1536]{1,0:T(8,128)(2,1)S(1)}, bf16[24,1536]{1,0:T(8,128)(2,1)S(1)}, u32[]{:S(2)}, u32[]{:S(2)}) %collective-permute-start.12) | collective-permute-done | bytes 73760 | tf_op jit(solution)/shard_map/ppermute | solution.py:150
  62.9 0.6 gather_fusion.2
  63.6 1.4 %convolution_maximum_fusion.3 = f32[192,192]{1,0:T(8,128)S(1)} fusion(bf16[192,1536]{1,0:T(8,128)(2,1)S(1)} %bitcast.219, bf16[4,2,1536,192]{2,3,1,0:T(8,128)(2,1)} %param.22), kind=kOutput, calls=%fused_computation.30 | convolution fusion | flops 113283072 | bytes 1327104 | tf_op jit(solution)/shard_map/dot_general | solution.py:165
  65.0 2.1 %convolution_maximum_fusion.2 = f32[192,192]{1,0:T(8,128)} fusion(bf16[192,1536]{1,0:T(8,128)(2,1)S(1)} %bitcast.220, bf16[4,2,1536,192]{2,3,1,0:T(8,128)(2,1)} %param.22), kind=kOutput, calls=%fused_computation.28 | convolution fusion | flops 113283072 | bytes 1327104 | tf_op jit(solution)/shard_map/dot_general | solution.py:165
  67.1 1.4 %convolution_maximum_fusion.1 = f32[192,192]{1,0:T(8,128)S(1)} fusion(bf16[192,1536]{1,0:T(8,128)(2,1)S(1)} %bitcast.221, bf16[4,2,1536,192]{2,3,1,0:T(8,128)(2,1)} %param.22), kind=kOutput, calls=%fused_computation.26 | convolution fusion | flops 113283072 | bytes 1327104 | tf_op jit(solution)/shard_map/dot_general | solution.py:165
  68.5 1.4 %convolution_maximum_fusion = f32[192,192]{1,0:T(8,128)S(1)} fusion(bf16[192,1536]{1,0:T(8,128)(2,1)S(1)} %bitcast.222, bf16[4,2,1536,192]{2,3,1,0:T(8,128)(2,1)} %param.22), kind=kOutput, calls=%fused_computation.24 | convolution fusion | flops 113283072 | bytes 1327104 | tf_op jit(solution)/shard_map/dot_general | solution.py:165
  69.9 3.1 %fusion.11 = f32[192,1536]{1,0:T(8,128)} fusion(f32[192,192]{1,0:T(8,128)S(1)} %convolution_maximum_fusion.3, bf16[192,1536]{1,0:T(8,128)(2,1)S(1)} %bitcast.223, bf16[4,192,1536]{2,1,0:T(8,128)(2,1)} %param.23, bf16[4,2,1536,192]{2,3,1,0:T(8,128)(2,1)} %param.22, f32[192]{0:T(256)S(1)} %bitcast.241), kind=kOutput, calls=%fused_computation.18 | convolution fusion | flops 227450880 | bytes 3097344 | tf_op jit(solution)/shard_map/dot_general | solution.py:168
  73.0 2.6 %fusion.9 = f32[192,1536]{1,0:T(8,128)S(1)} fusion(f32[192,1536]{1,0:T(8,128)} %fusion.11, f32[192,192]{1,0:T(8,128)} %convolution_maximum_fusion.2, bf16[192,1536]{1,0:T(8,128)(2,1)S(1)} %bitcast.224, bf16[4,192,1536]{2,1,0:T(8,128)(2,1)} %param.23, bf16[4,2,1536,192]{2,3,1,0:T(8,128)(2,1)} %param.22, f32[192]{0:T(256)S(1)} %bitcast.240), kind=kOutput, calls=%fused_computation.15 | convolution fusion | flops 227745792 | bytes 4326144 | tf_op jit(solution)/shard_map/dot_general | solution.py:168
  75.6 3.1 %fusion.6 = f32[192,1536]{1,0:T(8,128)} fusion(f32[192,1536]{1,0:T(8,128)S(1)} %fusion.9, f32[192,192]{1,0:T(8,128)S(1)} %convolution_maximum_fusion.1, bf16[192,1536]{1,0:T(8,128)(2,1)S(1)} %bitcast.225, bf16[4,192,1536]{2,1,0:T(8,128)(2,1)} %param.23, bf16[4,2,1536,192]{2,3,1,0:T(8,128)(2,1)} %param.22, f32[192]{0:T(256)S(1)} %bitcast.239), kind=kOutput, calls=%fused_computation.11 | convolution fusion | flops 227745792 | bytes 4276992 | tf_op jit(solution)/shard_map/dot_general | solution.py:168
  78.7 2.5 %fusion.3 = bf16[192,1536]{1,0:T(8,128)(2,1)S(1)} fusion(f32[192,1536]{1,0:T(8,128)} %fusion.6, f32[192,192]{1,0:T(8,128)S(1)} %convolution_maximum_fusion, bf16[192,1536]{1,0:T(8,128)(2,1)S(1)} %bitcast.226, bf16[4,192,1536]{2,1,0:T(8,128)(2,1)} %param.23, bf16[4,2,1536,192]{2,3,1,0:T(8,128)(2,1)} %param.22, f32[192]{0:T(256)S(1)} %bitcast.242), kind=kOutput, calls=%fused_computation.7 | convolution fusion | flops 228040704 | bytes 3687168 | tf_op jit(solution)/shard_map/dot_general | solution.py:168
  81.3 0.9 copy.103
  82.2 4.8 %all-to-all-start.1 = ((bf16[32,24,384]{2,1,0:T(8,128)(2,1)}), bf16[32,24,384]{2,1,0:T(8,128)(2,1)S(1)}, u32[]{:S(2)}, u32[]{:S(2)}) async-start(bf16[32,24,384]{2,1,0:T(8,128)(2,1)} %bitcast.65), calls=%async_computation.1 | async-start | bytes 1179648 | tf_op jit(solution)/shard_map/all_to_all | solution.py:174
  87.0 16.8 %all-to-all-done.1 = bf16[32,24,384]{2,1,0:T(8,128)(2,1)S(1)} async-done(((bf16[32,24,384]{2,1,0:T(8,128)(2,1)}), bf16[32,24,384]{2,1,0:T(8,128)(2,1)S(1)}, u32[]{:S(2)}, u32[]{:S(2)}) %all-to-all-start.1) | async-done | bytes 589856 | tf_op jit(solution)/shard_map/all_to_all | solution.py:174
  103.9 0.6 add_convert_fusion.1
  (91 shorter events, 4.0 us)
Async XLA Ops:
  0.0 38.1 %copy-start = (bf16[384,1536]{1,0:T(8,128)(2,1)S(1)}, bf16[384,1536]{1,0:T(8,128)(2,1)}, u32[]{:S(2)}) copy-start(bf16[384,1536]{1,0:T(8,128)(2,1)} %param.18) | copy-start | bytes 3538948
  0.9 30.2 %collective-permute-start = (f32[24,32]{1,0:T(8,128)S(1)}, f32[24,32]{1,0:T(8,128)S(1)}, u32[]{:S(2)}, u32[]{:S(2)}) collective-permute-start(f32[24,32]{1,0:T(8,128)S(1)} %select_reduce_fusion), channel_id=1, source_target_pairs={{0,4},{4,8},{8,12},{12,16},{16,20},{20,24},{24,28},{28,0},{1,5},{5... | collective-permute-start | bytes 9224 | tf_op jit(solution)/shard_map/ppermute | solution.py:150
  3.9 28.6 %collective-permute-start.1 = (f32[24,32]{1,0:T(8,128)S(1)}, f32[24,32]{1,0:T(8,128)S(1)}, u32[]{:S(2)}, u32[]{:S(2)}) collective-permute-start(f32[24,32]{1,0:T(8,128)S(1)} %select_reduce_fusion), channel_id=1, source_target_pairs={{0,8},{4,12},{8,16},{12,20},{16,24},{20,28},{24,0},{28,4},{1,9},{5... | collective-permute-start | bytes 9224 | tf_op jit(solution)/shard_map/ppermute | solution.py:150
  5.5 28.4 %collective-permute-start.2 = (f32[24,32]{1,0:T(8,128)S(1)}, f32[24,32]{1,0:T(8,128)S(1)}, u32[]{:S(2)}, u32[]{:S(2)}) collective-permute-start(f32[24,32]{1,0:T(8,128)S(1)} %select_reduce_fusion), channel_id=1, source_target_pairs={{0,12},{4,16},{8,20},{12,24},{16,28},{20,0},{24,4},{28,8},{1,13},{... | collective-permute-start | bytes 9224 | tf_op jit(solution)/shard_map/ppermute | solution.py:150
  8.1 25.9 %collective-permute-start.3 = (f32[24,32]{1,0:T(8,128)S(1)}, f32[24,32]{1,0:T(8,128)S(1)}, u32[]{:S(2)}, u32[]{:S(2)}) collective-permute-start(f32[24,32]{1,0:T(8,128)S(1)} %select_reduce_fusion), channel_id=1, source_target_pairs={{0,16},{4,20},{8,24},{12,28},{16,0},{20,4},{24,8},{28,12},{1,17},{... | collective-permute-start | bytes 9224 | tf_op jit(solution)/shard_map/ppermute | solution.py:150
  9.3 24.7 %collective-permute-start.4 = (f32[24,32]{1,0:T(8,128)S(1)}, f32[24,32]{1,0:T(8,128)S(1)}, u32[]{:S(2)}, u32[]{:S(2)}) collective-permute-start(f32[24,32]{1,0:T(8,128)S(1)} %select_reduce_fusion), channel_id=1, source_target_pairs={{0,20},{4,24},{8,28},{12,0},{16,4},{20,8},{24,12},{28,16},{1,21},{... | collective-permute-start | bytes 9224 | tf_op jit(solution)/shard_map/ppermute | solution.py:150
  23.8 5.7 %copy-start.1 = (bf16[24,2,256]{2,1,0:T(2,128)(2,1)S(1)}, bf16[24,2,256]{2,1,0:T(2,128)(2,1)}, u32[]{:S(2)}) copy-start(bf16[24,2,256]{2,1,0:T(2,128)(2,1)} %param.14) | copy-start | bytes 73732
  26.0 11.0 %all-to-all-start = ((f32[4,24,3,130]{3,1,2,0:T(8,128)}), f32[4,24,3,130]{3,1,2,0:T(8,128)S(1)}, u32[]{:S(2)}, u32[]{:S(2)}) async-start(f32[4,24,3,130]{3,1,2,0:T(8,128)} %maximum_bitcast_fusion), calls=%async_computation | async-start | bytes 589824 | tf_op jit(solution)/shard_map/all_to_all | solution.py:107
  31.1 3.7 %collective-permute-start.5 = (f32[24,32]{1,0:T(8,128)S(1)}, f32[24,32]{1,0:T(8,128)S(1)}, u32[]{:S(2)}, u32[]{:S(2)}) collective-permute-start(f32[24,32]{1,0:T(8,128)S(1)} %select_reduce_fusion), channel_id=1, source_target_pairs={{0,24},{4,28},{8,0},{12,4},{16,8},{20,12},{24,16},{28,20},{1,25},{... | collective-permute-start | bytes 9224 | tf_op jit(solution)/shard_map/ppermute | solution.py:150
  32.6 3.7 %collective-permute-start.6 = (f32[24,32]{1,0:T(8,128)S(1)}, f32[24,32]{1,0:T(8,128)S(1)}, u32[]{:S(2)}, u32[]{:S(2)}) collective-permute-start(f32[24,32]{1,0:T(8,128)S(1)} %select_reduce_fusion), channel_id=1, source_target_pairs={{0,28},{4,0},{8,4},{12,8},{16,12},{20,16},{24,20},{28,24},{1,29},{... | collective-permute-start | bytes 9224 | tf_op jit(solution)/shard_map/ppermute | solution.py:150
  36.8 9.7 %copy-start.2 = (f32[1536]{0:T(1024)S(1)}, f32[1536]{0:T(1024)}, u32[]{:S(2)}) copy-start(f32[1536]{0:T(1024)} %param.19) | copy-start | bytes 18436
  46.6 9.2 %collective-permute-start.7 = (bf16[24,1536]{1,0:T(8,128)(2,1)S(1)}, bf16[24,1536]{1,0:T(8,128)(2,1)S(1)}, u32[]{:S(2)}, u32[]{:S(2)}) collective-permute-start(bf16[24,1536]{1,0:T(8,128)(2,1)S(1)} %get-tuple-element.5), channel_id=1, source_target_pairs={{0,4},{4,8},{8,12},{12,16},{16,20},{20,24},{24,28},{28,0},{1,5},{5... | collective-permute-start | bytes 221192 | tf_op jit(solution)/shard_map/ppermute | solution.py:150
  48.2 7.8 %collective-permute-start.8 = (bf16[24,1536]{1,0:T(8,128)(2,1)S(1)}, bf16[24,1536]{1,0:T(8,128)(2,1)S(1)}, u32[]{:S(2)}, u32[]{:S(2)}) collective-permute-start(bf16[24,1536]{1,0:T(8,128)(2,1)S(1)} %get-tuple-element.5), channel_id=1, source_target_pairs={{0,8},{4,12},{8,16},{12,20},{16,24},{20,28},{24,0},{28,4},{1,9},{5... | collective-permute-start | bytes 221192 | tf_op jit(solution)/shard_map/ppermute | solution.py:150
  48.3 12.1 %collective-permute-start.9 = (bf16[24,1536]{1,0:T(8,128)(2,1)S(1)}, bf16[24,1536]{1,0:T(8,128)(2,1)S(1)}, u32[]{:S(2)}, u32[]{:S(2)}) collective-permute-start(bf16[24,1536]{1,0:T(8,128)(2,1)S(1)} %get-tuple-element.5), channel_id=1, source_target_pairs={{0,12},{4,16},{8,20},{12,24},{16,28},{20,0},{24,4},{28,8},{1,13},{... | collective-permute-start | bytes 221192 | tf_op jit(solution)/shard_map/ppermute | solution.py:150
  50.5 10.2 %collective-permute-start.10 = (bf16[24,1536]{1,0:T(8,128)(2,1)S(1)}, bf16[24,1536]{1,0:T(8,128)(2,1)S(1)}, u32[]{:S(2)}, u32[]{:S(2)}) collective-permute-start(bf16[24,1536]{1,0:T(8,128)(2,1)S(1)} %get-tuple-element.5), channel_id=1, source_target_pairs={{0,16},{4,20},{8,24},{12,28},{16,0},{20,4},{24,8},{28,12},{1,17},{... | collective-permute-start | bytes 221192 | tf_op jit(solution)/shard_map/ppermute | solution.py:150
  52.6 8.1 %collective-permute-start.11 = (bf16[24,1536]{1,0:T(8,128)(2,1)S(1)}, bf16[24,1536]{1,0:T(8,128)(2,1)S(1)}, u32[]{:S(2)}, u32[]{:S(2)}) collective-permute-start(bf16[24,1536]{1,0:T(8,128)(2,1)S(1)} %get-tuple-element.5), channel_id=1, source_target_pairs={{0,20},{4,24},{8,28},{12,0},{16,4},{20,8},{24,12},{28,16},{1,21},{... | collective-permute-start | bytes 221192 | tf_op jit(solution)/shard_map/ppermute | solution.py:150
  55.8 7.0 %collective-permute-start.12 = (bf16[24,1536]{1,0:T(8,128)(2,1)S(1)}, bf16[24,1536]{1,0:T(8,128)(2,1)S(1)}, u32[]{:S(2)}, u32[]{:S(2)}) collective-permute-start(bf16[24,1536]{1,0:T(8,128)(2,1)S(1)} %get-tuple-element.5), channel_id=1, source_target_pairs={{0,24},{4,28},{8,0},{12,4},{16,8},{20,12},{24,16},{28,20},{1,25},{... | collective-permute-start | bytes 221192 | tf_op jit(solution)/shard_map/ppermute | solution.py:150
  56.0 6.9 %collective-permute-start.13 = (bf16[24,1536]{1,0:T(8,128)(2,1)S(1)}, bf16[24,1536]{1,0:T(8,128)(2,1)S(1)}, u32[]{:S(2)}, u32[]{:S(2)}) collective-permute-start(bf16[24,1536]{1,0:T(8,128)(2,1)S(1)} %get-tuple-element.5), channel_id=1, source_target_pairs={{0,28},{4,0},{8,4},{12,8},{16,12},{20,16},{24,20},{28,24},{1,29},{... | collective-permute-start | bytes 221192 | tf_op jit(solution)/shard_map/ppermute | solution.py:150
  82.2 21.6 %all-to-all-start.1 = ((bf16[32,24,384]{2,1,0:T(8,128)(2,1)}), bf16[32,24,384]{2,1,0:T(8,128)(2,1)S(1)}, u32[]{:S(2)}, u32[]{:S(2)}) async-start(bf16[32,24,384]{2,1,0:T(8,128)(2,1)} %bitcast.65), calls=%async_computation.1 | async-start | bytes 1179648 | tf_op jit(solution)/shard_map/all_to_all | solution.py:174

commit v4 on v3

--- a/solution.py
+++ b/solution.py
@@ -1,6 +1,10 @@
+import math
+
 import jax
 import jax.numpy as jnp
 from jax import lax
+from jax.experimental import pallas as pl
+from jax.experimental.pallas import tpu as pltpu
 from jax.sharding import PartitionSpec as P
 
 EXPERTS = 32
@@ -24,6 +28,47 @@
         [first_half * cosine - second_half * sine, second_half * cosine + first_half * sine],
         axis=-1,
     )
+
+
+def _expert_body(x_ref, gu_ref, dn_ref, w_ref, o_ref, acc_ref):
+    block = pl.program_id(1)
+
+    @pl.when(block == 0)
+    def _():
+        acc_ref[...] = jnp.zeros_like(acc_ref)
+
+    x = x_ref[...]
+    gate_part = jnp.dot(x, gu_ref[0, 0], preferred_element_type=jnp.float32)
+    up_part = jnp.dot(x, gu_ref[0, 1], preferred_element_type=jnp.float32)
+    activation = (jnp.maximum(gate_part, 0.0) * up_part).astype(jnp.bfloat16)
+    produced = jnp.dot(activation, dn_ref[0], preferred_element_type=jnp.float32)
+    produced = produced.astype(jnp.bfloat16).astype(jnp.float32)
+    acc_ref[...] += w_ref[0] * produced
+
+    @pl.when(block == pl.num_programs(1) - 1)
+    def _():
+        o_ref[...] = acc_ref[...].astype(o_ref.dtype)
+
+
+def expert_mix(rows, gate_up, down, weights):
+    row_total, width = rows.shape
+    local_count, _, _, hidden = gate_up.shape
+    tile = math.gcd(row_total, 192)
+    weights_t = jnp.transpose(weights)[:, :, None]
+    return pl.pallas_call(
+        _expert_body,
+        grid=(row_total // tile, local_count),
+        in_specs=[
+            pl.BlockSpec((tile, width), lambda i, b: (i, 0)),
+            pl.BlockSpec((1, 2, width, hidden), lambda i, b: (b, 0, 0, 0)),
+            pl.BlockSpec((1, hidden, width), lambda i, b: (b, 0, 0)),
+            pl.BlockSpec((1, tile, 1), lambda i, b: (b, i, 0)),
+        ],
+        out_specs=pl.BlockSpec((tile, width), lambda i, b: (i, 0)),
+        out_shape=jax.ShapeDtypeStruct((row_total, width), jnp.bfloat16),
+        scratch_shapes=[pltpu.VMEM((tile, width), jnp.float32)],
+        compiler_params=pltpu.CompilerParams(dimension_semantics=("parallel", "arbitrary")),
+    )(rows, gate_up, down, weights_t)
 
 
 def per_device(
@@ -156,20 +201,22 @@
     else:
         def gather_req(value):
             return lax.all_gather(value, "req", axis=0, tiled=True)
-    rows_all = gather_req(normed)
-    weights_all = gather_req(block_weights)
+    weight_high = lax.reduce_precision(block_weights, exponent_bits=8, mantissa_bits=7)
+    weight_rest = block_weights - weight_high
+    weight_mid = lax.reduce_precision(weight_rest, exponent_bits=8, mantissa_bits=7)
+    weight_low = weight_rest - weight_mid
+    message = jnp.concatenate(
+        [normed, weight_high.astype(jnp.bfloat16), weight_mid.astype(jnp.bfloat16), weight_low.astype(jnp.bfloat16)],
+        axis=1,
+    )
+    message_all = gather_req(message)
+    rows_all = message_all[:, :model_width]
+    pieces = message_all[:, model_width:].astype(jnp.float32).reshape(-1, 3, block_total)
+    weights_all = (pieces[:, 0] + pieces[:, 1]) + pieces[:, 2]
     weights_own = lax.dynamic_slice_in_dim(weights_all, req_index * local_count, local_count, 1)
 
-    mixed = jnp.zeros((rows_all.shape[0], model_width), jnp.float32)
-    for local_block in range(local_count):
-        gate_part = jnp.dot(rows_all, gate_up[local_block, 0], preferred_element_type=jnp.float32)
-        up_part = jnp.dot(rows_all, gate_up[local_block, 1], preferred_element_type=jnp.float32)
-        activation = (jnp.maximum(gate_part, 0.0) * up_part).astype(jnp.bfloat16)
-        produced = jnp.dot(activation, down[local_block], preferred_element_type=jnp.float32)
-        produced = produced.astype(jnp.bfloat16).astype(jnp.float32)
-        mixed = mixed + weights_own[:, local_block : local_block + 1] * produced
-
-    mixed = mixed.astype(jnp.bfloat16).reshape(req_count, row_count, tp_count, own_width)
+    mixed = expert_mix(rows_all, gate_up, down, weights_own)
+    mixed = mixed.reshape(req_count, row_count, tp_count, own_width)
     mixed = jnp.transpose(mixed, (0, 2, 1, 3)).reshape(req_count * tp_count, row_count, own_width)
     mixed = lax.all_to_all(mixed, ("req", "tp"), 0, 0, tiled=True)
     mixed = jnp.sum(mixed.astype(jnp.float32), axis=0)

time: 105 us -> 98.3 us (0.936)
  matrix products: 19.1 us -> 1.62 us
  starting transfers between devices: 32.8 us -> 15.9 us
  waiting for transfers between devices: 24.5 us -> 34.9 us
  local copies, waits for them, and re-layouts: 7.48 us -> 17.1 us
  Pallas kernels: 0 us -> 6.88 us
  blocking collectives: 13.5 us -> 14.7 us
    dot_general x8 -> x0, matrix products: 17.5 us -> none  [the longest x4 11.3 us: per_device(): jnp.dot(activation, down[local_block], preferred_element_type=jnp.float32)]
    ppermute x14 -> x7, starting transfers between devices: 24.5 us -> 9.86 us  [gather_req(): lax.ppermute(value, 'req', [(i, (i + shift) % req_count) for i in range(r...]
    ppermute x14 -> x7, waiting for transfers between devices: 7.65 us -> 18.1 us  [gather_req(): lax.ppermute(value, 'req', [(i, (i + shift) % req_count) for i in range(r...]
    unnamed x22, local copies, waits for them, and re-layouts: 0.31 us -> 8.26 us
    pallas_call x0 -> x1, Pallas kernels: none -> 6.88 us  [expert_mix(): pl.pallas_call(_expert_body, grid=(row_total // tile, local_count), in_sp...]
    all_to_all x1, starting transfers between devices: 4.82 us -> 2.61 us  [per_device(): mixed = lax.all_to_all(mixed, ('req', 'tp'), 0, 0, tiled=True)]
    reshape x2 -> x3, local copies, waits for them, and re-layouts: 1.02 us -> 2.56 us  [the longest x2 2.47 us: per_device(): mixed = mixed.reshape(req_count, row_count, tp_count, own_width)]
    all_gather x1, blocking collectives: 5.45 us -> 6.58 us  [per_device(): gathered = lax.all_gather(packed, 'tp', axis=0)]
  transfers between devices with their start and end apart: 16 -> 9, of which waited for: 6 -> 4; matrix products, arithmetic and copies ran while one was open for 10% -> 10% of each run, Pallas kernels for 0% -> 0%
where the time goes in v4:
time: 98.3 us; the launch traced here: 97.6 us
  waiting for transfers between devices  34.9 us (36%)
  local copies, waits for them, and re-layouts  17.1 us (17%)
  starting transfers between devices  15.9 us (16%)
  blocking collectives  14.7 us (15%)
  Pallas kernels  6.88 us (7%)
  other arithmetic  6.01 us (6%)
  matrix products  1.62 us (2%)
    ppermute x7, waiting for transfers between devices, gather_req(): lax.ppermute(value, 'req', [(i, (i + shift) % req_count) for i in range(r...  18.1 us
    all_to_all x1, waiting for transfers between devices, per_device(): mixed = lax.all_to_all(mixed, ('req', 'tp'), 0, 0, tiled=True)  16.8 us
    ppermute x7, starting transfers between devices, gather_req(): lax.ppermute(value, 'req', [(i, (i + shift) % req_count) for i in range(r...  9.86 us
    unnamed x22, local copies, waits for them, and re-layouts  8.26 us
    all_gather x1, blocking collectives, per_device(): projected = jnp.sum(lax.all_gather(partial_proj, 'tp', axis=0), axis=0)  8.15 us
    pallas_call x1, Pallas kernels, expert_mix(): pl.pallas_call(_expert_body, grid=(row_total // tile, local_count), in_sp...  6.88 us
    all_gather x1, blocking collectives, per_device(): gathered = lax.all_gather(packed, 'tp', axis=0)  6.58 us
    all_to_all x1, starting transfers between devices, per_device(): lax.all_to_all(jnp.transpose(states, (1, 0, 2, 3)), 'tp', 0, 0, tiled=True)  3.45 us
  transfers between devices with their start and end apart: 9, of which 4 were waited for; matrix products, arithmetic and copies ran while one was open for 10% of the time, Pallas kernels for 0%

profile of v4, /device:TPU:0, one launch (start us, length us, event | category | flops | bytes accessed | tf_op | source)
XLA Modules:
  0.0 97.6 jit_solution(8491828631785055077)
XLA Ops:
  0.0 0.8 convert_element_type.76
  0.8 0.7 copy.72
  1.6 0.1 reduce.2
  1.7 0.7 bitcast_subtract_fusion.1
  2.4 0.7 reshape.321
  3.1 0.1 multiply_cosine_fusion
  3.3 0.1 subtract_convert_fusion
  3.5 0.7 pad_maximum_fusion
  4.2 6.6 %all-gather = bf16[8,24,384]{2,1,0:T(8,128)(2,1)S(1)} all-gather(bf16[2,24,384]{2,1,0:T(8,128)(2,1)S(1)} %pad_maximum_fusion), channel_id=2, replica_groups=mesh['req'=8,'tp'=4] {'tp'}, dimensions={0}, use_global_device_ids=true | all-gather | bytes 184320 | tf_op jit(solution)/shard_map/all_gather | solution.py:108
  10.9 0.5 fusion.33
  11.6 0.5 fusion.35
  12.1 0.1 concatenate.28
  12.2 0.3 fusion.3
  12.5 0.7 fusion.2
  13.2 0.1 concatenate.29
  13.4 0.9 maximum_bitcast_fusion
  14.3 3.5 %all-to-all-start = ((f32[4,24,3,130]{3,1,2,0:T(8,128)}), f32[4,24,3,130]{3,1,2,0:T(8,128)S(1)}, u32[]{:S(2)}, u32[]{:S(2)}) async-start(f32[4,24,3,130]{3,1,2,0:T(8,128)} %maximum_bitcast_fusion), calls=%async_computation | async-start | bytes 589824 | tf_op jit(solution)/shard_map/all_to_all | solution.py:152
  18.3 0.1 subtract_convert_fusion.1
  18.6 0.2 fusion.14
  18.7 0.1 copy.96
  18.8 8.0 %copy.90.gu_ref = bf16[4,2,1536,192]{3,2,1,0:T(8,128)(2,1)} copy(bf16[4,2,1536,192]{2,3,1,0:T(8,128)(2,1)} %param.22) | data formatting | bytes 9437184 | tf_op args[10]
  26.8 0.6 gather_fusion
  27.4 0.1 slice_reduce_fusion.1
  27.6 0.1 copy.101
  27.7 0.1 copy.86
  28.1 0.1 fusion.10
  28.4 0.3 fusion.16
  28.7 8.1 %all-gather.1 = f32[96,1536]{1,0:T(8,128)S(1)} all-gather(f32[24,1536]{1,0:T(8,128)S(1)} %fusion.16), channel_id=3, replica_groups=mesh['req'=8,'tp'=4] {'tp'}, dimensions={0}, use_global_device_ids=true | all-gather | bytes 737280 | tf_op jit(solution)/shard_map/all_gather | solution.py:171
  36.9 0.1 fusion.9
  37.1 0.1 concatenate.27
  37.2 4.9 %collective-permute-start.6 = (bf16[24,1632]{1,0:T(8,128)(2,1)S(1)}, bf16[24,1632]{1,0:T(8,128)(2,1)S(1)}, u32[]{:S(2)}, u32[]{:S(2)}) collective-permute-start(bf16[24,1632]{1,0:T(8,128)(2,1)S(1)} %concatenate.27), channel_id=1, source_target_pairs={{0,28},{4,0},{8,4},{12,8},{16,12},{20,16},{24,20},{28,24},{1,29},{... | collective-permute-start | bytes 235016 | tf_op jit(solution)/shard_map/ppermute | solution.py:195
  42.1 0.4 collective-permute-start.5
  42.6 3.0 %collective-permute-start.3 = (bf16[24,1632]{1,0:T(8,128)(2,1)S(1)}, bf16[24,1632]{1,0:T(8,128)(2,1)S(1)}, u32[]{:S(2)}, u32[]{:S(2)}) collective-permute-start(bf16[24,1632]{1,0:T(8,128)(2,1)S(1)} %concatenate.27), channel_id=1, source_target_pairs={{0,16},{4,20},{8,24},{12,28},{16,0},{20,4},{24,8},{28,12},{1,17},{... | collective-permute-start | bytes 235016 | tf_op jit(solution)/shard_map/ppermute | solution.py:195
  45.6 1.5 %collective-permute-start = (bf16[24,1632]{1,0:T(8,128)(2,1)S(1)}, bf16[24,1632]{1,0:T(8,128)(2,1)S(1)}, u32[]{:S(2)}, u32[]{:S(2)}) collective-permute-start(bf16[24,1632]{1,0:T(8,128)(2,1)S(1)} %concatenate.27), channel_id=1, source_target_pairs={{0,4},{4,8},{8,12},{12,16},{16,20},{20,24},{24,28},{28,0},{1,5},{5... | collective-permute-start | bytes 235016 | tf_op jit(solution)/shard_map/ppermute | solution.py:195
  47.1 5.7 %collective-permute-done = bf16[24,1632]{1,0:T(8,128)(2,1)S(1)} collective-permute-done((bf16[24,1632]{1,0:T(8,128)(2,1)S(1)}, bf16[24,1632]{1,0:T(8,128)(2,1)S(1)}, u32[]{:S(2)}, u32[]{:S(2)}) %collective-permute-start) | collective-permute-done | bytes 78368 | tf_op jit(solution)/shard_map/ppermute | solution.py:195
  52.8 6.2 %collective-permute-done.1 = bf16[24,1632]{1,0:T(8,128)(2,1)S(1)} collective-permute-done((bf16[24,1632]{1,0:T(8,128)(2,1)S(1)}, bf16[24,1632]{1,0:T(8,128)(2,1)S(1)}, u32[]{:S(2)}, u32[]{:S(2)}) %collective-permute-start.1) | collective-permute-done | bytes 78368 | tf_op jit(solution)/shard_map/ppermute | solution.py:195
  59.0 6.2 %collective-permute-done.2 = bf16[24,1632]{1,0:T(8,128)(2,1)S(1)} collective-permute-done((bf16[24,1632]{1,0:T(8,128)(2,1)S(1)}, bf16[24,1632]{1,0:T(8,128)(2,1)S(1)}, u32[]{:S(2)}, u32[]{:S(2)}) %collective-permute-start.2) | collective-permute-done | bytes 78368 | tf_op jit(solution)/shard_map/ppermute | solution.py:195
  65.4 0.6 gather_fusion.1
  66.0 0.2 bitcast_select_fusion
  66.2 0.9 slice.85.x_ref
  67.2 0.9 copy.91.w_ref
  68.1 6.9 %shard_map.118 = bf16[192,1536]{1,0:T(8,128)(2,1)} custom-call(bf16[192,1536]{1,0:T(8,128)(2,1)} %slice.85.x_ref, bf16[4,2,1536,192]{3,2,1,0:T(8,128)(2,1)} %copy.90.gu_ref, bf16[4,192,1536]{2,1,0:T(8,128)(2,1)} %dn_ref.1, f32[4,192,1]{2,1,0:T(8,128)} %copy.91.w_ref), custom_call_target="tpu_custom_call" | custom-call | tf_op jit(solution)/shard_map/pallas_call | solution.py:58
  75.0 1.6 %reshape.319 = bf16[8,24,4,384]{3,2,1,0:T(4,128)(2,1)S(1)} reshape(bf16[192,1536]{1,0:T(8,128)(2,1)} %shard_map.118) | data formatting | bytes 1179648 | tf_op jit(solution)/shard_map/reshape | solution.py:219
  76.6 0.9 copy.92
  77.5 2.6 %all-to-all-start.1 = ((bf16[32,24,384]{2,1,0:T(8,128)(2,1)}), bf16[32,24,384]{2,1,0:T(8,128)(2,1)S(1)}, u32[]{:S(2)}, u32[]{:S(2)}) async-start(bf16[32,24,384]{2,1,0:T(8,128)(2,1)} %bitcast.44), calls=%async_computation.1 | async-start | bytes 1179648 | tf_op jit(solution)/shard_map/all_to_all | solution.py:221
  80.1 16.8 %all-to-all-done.1 = bf16[32,24,384]{2,1,0:T(8,128)(2,1)S(1)} async-done(((bf16[32,24,384]{2,1,0:T(8,128)(2,1)}), bf16[32,24,384]{2,1,0:T(8,128)(2,1)S(1)}, u32[]{:S(2)}, u32[]{:S(2)}) %all-to-all-start.1) | async-done | bytes 589856 | tf_op jit(solution)/shard_map/all_to_all | solution.py:221
  96.9 0.1 convert_reduce_fusion
  97.0 0.6 add_convert_fusion.1
  (70 shorter events, 1.8 us)
Async XLA Ops:
  0.0 28.4 %copy-start = (bf16[384,1536]{1,0:T(8,128)(2,1)S(1)}, bf16[384,1536]{1,0:T(8,128)(2,1)}, u32[]{:S(2)}) copy-start(bf16[384,1536]{1,0:T(8,128)(2,1)} %param.18) | copy-start | bytes 3538948
  0.0 10.9 %copy-start.1 = (bf16[768,2,2,128]{3,2,1,0:T(2,128)(2,1)S(1)}, bf16[768,2,2,128]{3,2,1,0:T(2,128)(2,1)}, u32[]{:S(2)}) copy-start(bf16[768,2,2,128]{3,2,1,0:T(2,128)(2,1)} %param.17) | copy-start | bytes 2359300
  12.5 5.6 %copy-start.4 = (f32[24,4]{0,1:T(4,128)S(1)}, f32[24,4]{0,1:T(4,128)}, u32[]{:S(2)}) copy-start(f32[24,4]{0,1:T(4,128)} %param.21) | copy-start | bytes 1156
  12.5 5.6 %copy-start.5 = (s32[24,4]{0,1:T(4,128)S(1)}, s32[24,4]{0,1:T(4,128)}, u32[]{:S(2)}) copy-start(s32[24,4]{0,1:T(4,128)} %param.20) | copy-start | bytes 1156
  12.5 5.7 %copy-start.2 = (bf16[24,2,256]{2,1,0:T(2,128)(2,1)S(1)}, bf16[24,2,256]{2,1,0:T(2,128)(2,1)}, u32[]{:S(2)}) copy-start(bf16[24,2,256]{2,1,0:T(2,128)(2,1)} %param.14) | copy-start | bytes 73732
  14.3 13.1 %all-to-all-start = ((f32[4,24,3,130]{3,1,2,0:T(8,128)}), f32[4,24,3,130]{3,1,2,0:T(8,128)S(1)}, u32[]{:S(2)}, u32[]{:S(2)}) async-start(f32[4,24,3,130]{3,1,2,0:T(8,128)} %maximum_bitcast_fusion), calls=%async_computation | async-start | bytes 589824 | tf_op jit(solution)/shard_map/all_to_all | solution.py:152
  28.7 8.3 %copy-start.3 = (f32[1536]{0:T(1024)S(1)}, f32[1536]{0:T(1024)}, u32[]{:S(2)}) copy-start(f32[1536]{0:T(1024)} %param.19) | copy-start | bytes 18436
  37.2 28.1 %collective-permute-start.6 = (bf16[24,1632]{1,0:T(8,128)(2,1)S(1)}, bf16[24,1632]{1,0:T(8,128)(2,1)S(1)}, u32[]{:S(2)}, u32[]{:S(2)}) collective-permute-start(bf16[24,1632]{1,0:T(8,128)(2,1)S(1)} %concatenate.27), channel_id=1, source_target_pairs={{0,28},{4,0},{8,4},{12,8},{16,12},{20,16},{24,20},{28,24},{1,29},{... | collective-permute-start | bytes 235016 | tf_op jit(solution)/shard_map/ppermute | solution.py:195
  42.1 23.2 %collective-permute-start.5 = (bf16[24,1632]{1,0:T(8,128)(2,1)S(1)}, bf16[24,1632]{1,0:T(8,128)(2,1)S(1)}, u32[]{:S(2)}, u32[]{:S(2)}) collective-permute-start(bf16[24,1632]{1,0:T(8,128)(2,1)S(1)} %concatenate.27), channel_id=1, source_target_pairs={{0,24},{4,28},{8,0},{12,4},{16,8},{20,12},{24,16},{28,20},{1,25},{... | collective-permute-start | bytes 235016 | tf_op jit(solution)/shard_map/ppermute | solution.py:195
  42.6 22.7 %collective-permute-start.4 = (bf16[24,1632]{1,0:T(8,128)(2,1)S(1)}, bf16[24,1632]{1,0:T(8,128)(2,1)S(1)}, u32[]{:S(2)}, u32[]{:S(2)}) collective-permute-start(bf16[24,1632]{1,0:T(8,128)(2,1)S(1)} %concatenate.27), channel_id=1, source_target_pairs={{0,20},{4,24},{8,28},{12,0},{16,4},{20,8},{24,12},{28,16},{1,21},{... | collective-permute-start | bytes 235016 | tf_op jit(solution)/shard_map/ppermute | solution.py:195
  42.6 22.7 %collective-permute-start.3 = (bf16[24,1632]{1,0:T(8,128)(2,1)S(1)}, bf16[24,1632]{1,0:T(8,128)(2,1)S(1)}, u32[]{:S(2)}, u32[]{:S(2)}) collective-permute-start(bf16[24,1632]{1,0:T(8,128)(2,1)S(1)} %concatenate.27), channel_id=1, source_target_pairs={{0,16},{4,20},{8,24},{12,28},{16,0},{20,4},{24,8},{28,12},{1,17},{... | collective-permute-start | bytes 235016 | tf_op jit(solution)/shard_map/ppermute | solution.py:195
  45.6 7.2 %collective-permute-start = (bf16[24,1632]{1,0:T(8,128)(2,1)S(1)}, bf16[24,1632]{1,0:T(8,128)(2,1)S(1)}, u32[]{:S(2)}, u32[]{:S(2)}) collective-permute-start(bf16[24,1632]{1,0:T(8,128)(2,1)S(1)} %concatenate.27), channel_id=1, source_target_pairs={{0,4},{4,8},{8,12},{12,16},{16,20},{20,24},{24,28},{28,0},{1,5},{5... | collective-permute-start | bytes 235016 | tf_op jit(solution)/shard_map/ppermute | solution.py:195
  52.8 6.2 %collective-permute-start.1 = (bf16[24,1632]{1,0:T(8,128)(2,1)S(1)}, bf16[24,1632]{1,0:T(8,128)(2,1)S(1)}, u32[]{:S(2)}, u32[]{:S(2)}) collective-permute-start(bf16[24,1632]{1,0:T(8,128)(2,1)S(1)} %concatenate.27), channel_id=1, source_target_pairs={{0,8},{4,12},{8,16},{12,20},{16,24},{20,28},{24,0},{28,4},{1,9},{5... | collective-permute-start | bytes 235016 | tf_op jit(solution)/shard_map/ppermute | solution.py:195
  59.0 6.2 %collective-permute-start.2 = (bf16[24,1632]{1,0:T(8,128)(2,1)S(1)}, bf16[24,1632]{1,0:T(8,128)(2,1)S(1)}, u32[]{:S(2)}, u32[]{:S(2)}) collective-permute-start(bf16[24,1632]{1,0:T(8,128)(2,1)S(1)} %concatenate.27), channel_id=1, source_target_pairs={{0,12},{4,16},{8,20},{12,24},{16,28},{20,0},{24,4},{28,8},{1,13},{... | collective-permute-start | bytes 235016 | tf_op jit(solution)/shard_map/ppermute | solution.py:195
  77.5 19.4 %all-to-all-start.1 = ((bf16[32,24,384]{2,1,0:T(8,128)(2,1)}), bf16[32,24,384]{2,1,0:T(8,128)(2,1)S(1)}, u32[]{:S(2)}, u32[]{:S(2)}) async-start(bf16[32,24,384]{2,1,0:T(8,128)(2,1)} %bitcast.44), calls=%async_computation.1 | async-start | bytes 1179648 | tf_op jit(solution)/shard_map/all_to_all | solution.py:221

commit v5 on v4

--- a/solution.py
+++ b/solution.py
@@ -38,12 +38,16 @@
         acc_ref[...] = jnp.zeros_like(acc_ref)
 
     x = x_ref[...]
-    gate_part = jnp.dot(x, gu_ref[0, 0], preferred_element_type=jnp.float32)
-    up_part = jnp.dot(x, gu_ref[0, 1], preferred_element_type=jnp.float32)
+    contract_rows = (((1,), (1,)), ((), ()))
+    gate_part = lax.dot_general(x, gu_ref[0, 0], contract_rows, preferred_element_type=jnp.float32)
+    up_part = lax.dot_general(x, gu_ref[0, 1], contract_rows, preferred_element_type=jnp.float32)
     activation = (jnp.maximum(gate_part, 0.0) * up_part).astype(jnp.bfloat16)
     produced = jnp.dot(activation, dn_ref[0], preferred_element_type=jnp.float32)
     produced = produced.astype(jnp.bfloat16).astype(jnp.float32)
-    acc_ref[...] += w_ref[0] * produced
+    weights = w_ref[...]
+    lanes = lax.broadcasted_iota(jnp.int32, weights.shape, 1)
+    chosen = jnp.sum(jnp.where(lanes == block, weights, 0.0), axis=1, keepdims=True)
+    acc_ref[...] += chosen * produced
 
     @pl.when(block == pl.num_programs(1) - 1)
     def _():
@@ -54,21 +58,21 @@
     row_total, width = rows.shape
     local_count, _, _, hidden = gate_up.shape
     tile = math.gcd(row_total, 192)
-    weights_t = jnp.transpose(weights)[:, :, None]
+    gate_up_t = jnp.swapaxes(gate_up, 2, 3)
     return pl.pallas_call(
         _expert_body,
         grid=(row_total // tile, local_count),
         in_specs=[
             pl.BlockSpec((tile, width), lambda i, b: (i, 0)),
-            pl.BlockSpec((1, 2, width, hidden), lambda i, b: (b, 0, 0, 0)),
+            pl.BlockSpec((1, 2, hidden, width), lambda i, b: (b, 0, 0, 0)),
             pl.BlockSpec((1, hidden, width), lambda i, b: (b, 0, 0)),
-            pl.BlockSpec((1, tile, 1), lambda i, b: (b, i, 0)),
+            pl.BlockSpec((tile, local_count), lambda i, b: (i, 0)),
         ],
         out_specs=pl.BlockSpec((tile, width), lambda i, b: (i, 0)),
         out_shape=jax.ShapeDtypeStruct((row_total, width), jnp.bfloat16),
         scratch_shapes=[pltpu.VMEM((tile, width), jnp.float32)],
         compiler_params=pltpu.CompilerParams(dimension_semantics=("parallel", "arbitrary")),
-    )(rows, gate_up, down, weights_t)
+    )(rows, gate_up_t, down, weights)
 
 
 def per_device(
@@ -205,13 +209,18 @@
     weight_rest = block_weights - weight_high
     weight_mid = lax.reduce_precision(weight_rest, exponent_bits=8, mantissa_bits=7)
     weight_low = weight_rest - weight_mid
-    message = jnp.concatenate(
-        [normed, weight_high.astype(jnp.bfloat16), weight_mid.astype(jnp.bfloat16), weight_low.astype(jnp.bfloat16)],
+    code = jnp.stack(
+        [weight_high.astype(jnp.bfloat16), weight_mid.astype(jnp.bfloat16), weight_low.astype(jnp.bfloat16)],
         axis=1,
-    )
-    message_all = gather_req(message)
-    rows_all = message_all[:, :model_width]
-    pieces = message_all[:, model_width:].astype(jnp.float32).reshape(-1, 3, block_total)
+    ).reshape(-1)
+    code_rows = -(-code.shape[0] // model_width)
+    code = jnp.pad(code, (0, code_rows * model_width - code.shape[0])).reshape(code_rows, model_width)
+    message = jnp.concatenate([normed, code], axis=0)
+    message_all = gather_req(message).reshape(req_count, row_count + code_rows, model_width)
+    rows_all = message_all[:, :row_count].reshape(req_count * row_count, model_width)
+    pieces = message_all[:, row_count:].reshape(req_count, code_rows * model_width)
+    pieces = pieces[:, : row_count * 3 * block_total].astype(jnp.float32)
+    pieces = pieces.reshape(req_count * row_count, 3, block_total)
     weights_all = (pieces[:, 0] + pieces[:, 1]) + pieces[:, 2]
     weights_own = lax.dynamic_slice_in_dim(weights_all, req_index * local_count, local_count, 1)
 

time: 98.3 us -> 88.6 us (0.901)
  starting transfers between devices: 15.9 us -> 25.4 us
  local copies, waits for them, and re-layouts: 17.1 us -> 7.67 us
  waiting for transfers between devices: 34.9 us -> 26.4 us
  blocking collectives: 14.7 us -> 13.6 us
    ppermute x7, waiting for transfers between devices: 18.1 us -> 4.86 us  [gather_req(): lax.ppermute(value, 'req', [(i, (i + shift) % req_count) for i in range(r...]
    unnamed x22 -> x24, local copies, waits for them, and re-layouts: 8.26 us -> 0.27 us
    all_to_all x1, starting transfers between devices: 2.61 us -> 9.24 us  [per_device(): mixed = lax.all_to_all(mixed, ('req', 'tp'), 0, 0, tiled=True)]
    all_to_all x1, waiting for transfers between devices: 0.01 us -> 4.71 us  [per_device(): lax.all_to_all(jnp.transpose(states, (1, 0, 2, 3)), 'tp', 0, 0, tiled=True)]
    ppermute x7, starting transfers between devices: 9.86 us -> 12.7 us  [gather_req(): lax.ppermute(value, 'req', [(i, (i + shift) % req_count) for i in range(r...]
    add x0 -> x1, other arithmetic: none -> 1.32 us  [per_device(): weights_all = pieces[:, 0] + pieces[:, 1] + pieces[:, 2]]
    all_gather x1, blocking collectives: 8.15 us -> 7 us  [per_device(): projected = jnp.sum(lax.all_gather(partial_proj, 'tp', axis=0), axis=0)]
    broadcast_in_dim x3 -> x0, local copies, waits for them, and re-layouts: 1.1 us -> none  [the longest x1 0.95 us: expert_mix(): weights_t = jnp.transpose(weights)[:, :, None]]
  transfers between devices with their start and end apart: 9 -> 9, of which waited for: 4 -> 5; matrix products, arithmetic and copies ran while one was open for 10% -> 2% of each run, Pallas kernels for 0% -> 0%
where the time goes in v5:
time: 88.6 us; the launch traced here: 88.1 us
  waiting for transfers between devices  26.4 us (30%)
  starting transfers between devices  25.4 us (29%)
  blocking collectives  13.6 us (15%)
  local copies, waits for them, and re-layouts  7.67 us (9%)
  other arithmetic  6.67 us (8%)
  Pallas kernels  6.35 us (7%)
  matrix products  1.62 us (2%)
    all_to_all x1, waiting for transfers between devices, per_device(): mixed = lax.all_to_all(mixed, ('req', 'tp'), 0, 0, tiled=True)  16.8 us
    ppermute x7, starting transfers between devices, gather_req(): lax.ppermute(value, 'req', [(i, (i + shift) % req_count) for i in range(r...  12.7 us
    all_to_all x1, starting transfers between devices, per_device(): mixed = lax.all_to_all(mixed, ('req', 'tp'), 0, 0, tiled=True)  9.24 us
    all_gather x1, blocking collectives, per_device(): projected = jnp.sum(lax.all_gather(partial_proj, 'tp', axis=0), axis=0)  7 us
    all_gather x1, blocking collectives, per_device(): gathered = lax.all_gather(packed, 'tp', axis=0)  6.59 us
    pallas_call x1, Pallas kernels, expert_mix(): pl.pallas_call(_expert_body, grid=(row_total // tile, local_count), in_sp...  6.35 us
    ppermute x7, waiting for transfers between devices, gather_req(): lax.ppermute(value, 'req', [(i, (i + shift) % req_count) for i in range(r...  4.86 us
    all_to_all x1, waiting for transfers between devices, per_device(): lax.all_to_all(jnp.transpose(states, (1, 0, 2, 3)), 'tp', 0, 0, tiled=True)  4.71 us
  transfers between devices with their start and end apart: 9, of which 5 were waited for; matrix products, arithmetic and copies ran while one was open for 2% of the time, Pallas kernels for 0%

profile of v5, /device:TPU:0, one launch (start us, length us, event | category | flops | bytes accessed | tf_op | source)
XLA Modules:
  0.0 88.1 jit_solution(346572710918434665)
XLA Ops:
  0.0 0.8 convert_element_type.99
  0.8 0.7 reshape.367
  1.6 0.1 multiply_cosine_fusion
  1.7 0.1 subtract_convert_fusion
  1.9 0.7 pad_maximum_fusion.1
  2.7 6.6 %all-gather = bf16[8,24,384]{2,1,0:T(8,128)(2,1)S(1)} all-gather(bf16[2,24,384]{2,1,0:T(8,128)(2,1)S(1)} %pad_maximum_fusion.1), channel_id=2, replica_groups=mesh['req'=8,'tp'=4] {'tp'}, dimensions={0}, use_global_device_ids=true | all-gather | bytes 184320 | tf_op jit(solution)/shard_map/all_gather | solution.py:112
  9.5 0.1 reduce.2
  9.7 0.5 fusion.32
  10.3 0.5 fusion.34
  10.8 0.1 concatenate.28
  10.9 0.3 fusion.3
  11.2 0.7 fusion.2
  12.0 0.1 concatenate.29
  12.1 0.9 %maximum_bitcast_fusion = f32[4,24,3,130]{3,1,2,0:T(8,128)} fusion(f32[24,4,3,128]{3,0,2,1:T(8,128)S(1)} %bitcast.165, f32[24,4,3,1]{3,0,2,1:T(8,128)S(1)} %concatenate.29, f32[24,4,3,1]{3,0,2,1:T(8,128)S(1)} %concatenate.28), kind=kLoop, calls=%fused_computation.15 | loop fusion | flops 74880 | bytes 299520 | tf_op jit(solution)/shard_map/transpose | solution.py:157
  13.0 3.5 %all-to-all-start = ((f32[4,24,3,130]{3,1,2,0:T(8,128)}), f32[4,24,3,130]{3,1,2,0:T(8,128)S(1)}, u32[]{:S(2)}, u32[]{:S(2)}) async-start(f32[4,24,3,130]{3,1,2,0:T(8,128)} %maximum_bitcast_fusion), calls=%async_computation | async-start | bytes 589824 | tf_op jit(solution)/shard_map/all_to_all | solution.py:156
  16.7 0.1 subtract_convert_fusion.1
  16.9 0.2 fusion.14
  17.5 0.6 gather_fusion
  18.1 4.7 %all-to-all-done = f32[4,24,3,130]{3,1,2,0:T(8,128)S(1)} async-done(((f32[4,24,3,130]{3,1,2,0:T(8,128)}), f32[4,24,3,130]{3,1,2,0:T(8,128)S(1)}, u32[]{:S(2)}, u32[]{:S(2)}) %all-to-all-start) | async-done | bytes 149792 | tf_op jit(solution)/shard_map/all_to_all | solution.py:156
  22.8 0.1 slice_reduce_fusion.1
  23.0 0.1 copy.89
  23.2 0.1 copy.76
  23.5 0.1 fusion.10
  23.9 0.3 fusion.16
  24.1 7.0 %all-gather.1 = f32[96,1536]{1,0:T(8,128)S(1)} all-gather(f32[24,1536]{1,0:T(8,128)S(1)} %fusion.16), channel_id=3, replica_groups=mesh['req'=8,'tp'=4] {'tp'}, dimensions={0}, use_global_device_ids=true | all-gather | bytes 737280 | tf_op jit(solution)/shard_map/all_gather | solution.py:175
  31.2 0.1 fusion.9
  31.4 1.8 %collective-permute-start = (bf16[26,1536]{1,0:T(8,128)(2,1)S(1)}, bf16[26,1536]{1,0:T(8,128)(2,1)S(1)}, u32[]{:S(2)}, u32[]{:S(2)}) collective-permute-start(bf16[26,1536]{1,0:T(8,128)(2,1)S(1)} %pad_maximum_fusion), channel_id=1, source_target_pairs={{0,4},{4,8},{8,12},{12,16},{16,20},{20,24},{24,28},{28,0},{1,5},{5... | collective-permute-start | bytes 239624 | tf_op jit(solution)/shard_map/ppermute | solution.py:199
  33.3 1.6 %collective-permute-start.1 = (bf16[26,1536]{1,0:T(8,128)(2,1)S(1)}, bf16[26,1536]{1,0:T(8,128)(2,1)S(1)}, u32[]{:S(2)}, u32[]{:S(2)}) collective-permute-start(bf16[26,1536]{1,0:T(8,128)(2,1)S(1)} %pad_maximum_fusion), channel_id=1, source_target_pairs={{0,8},{4,12},{8,16},{12,20},{16,24},{20,28},{24,0},{28,4},{1,9},{5... | collective-permute-start | bytes 239624 | tf_op jit(solution)/shard_map/ppermute | solution.py:199
  34.9 2.5 %collective-permute-start.2 = (bf16[26,1536]{1,0:T(8,128)(2,1)S(1)}, bf16[26,1536]{1,0:T(8,128)(2,1)S(1)}, u32[]{:S(2)}, u32[]{:S(2)}) collective-permute-start(bf16[26,1536]{1,0:T(8,128)(2,1)S(1)} %pad_maximum_fusion), channel_id=1, source_target_pairs={{0,12},{4,16},{8,20},{12,24},{16,28},{20,0},{24,4},{28,8},{1,13},{... | collective-permute-start | bytes 239624 | tf_op jit(solution)/shard_map/ppermute | solution.py:199
  37.4 1.2 %collective-permute-start.3 = (bf16[26,1536]{1,0:T(8,128)(2,1)S(1)}, bf16[26,1536]{1,0:T(8,128)(2,1)S(1)}, u32[]{:S(2)}, u32[]{:S(2)}) collective-permute-start(bf16[26,1536]{1,0:T(8,128)(2,1)S(1)} %pad_maximum_fusion), channel_id=1, source_target_pairs={{0,16},{4,20},{8,24},{12,28},{16,0},{20,4},{24,8},{28,12},{1,17},{... | collective-permute-start | bytes 239624 | tf_op jit(solution)/shard_map/ppermute | solution.py:199
  38.7 2.6 %collective-permute-start.4 = (bf16[26,1536]{1,0:T(8,128)(2,1)S(1)}, bf16[26,1536]{1,0:T(8,128)(2,1)S(1)}, u32[]{:S(2)}, u32[]{:S(2)}) collective-permute-start(bf16[26,1536]{1,0:T(8,128)(2,1)S(1)} %pad_maximum_fusion), channel_id=1, source_target_pairs={{0,20},{4,24},{8,28},{12,0},{16,4},{20,8},{24,12},{28,16},{1,21},{... | collective-permute-start | bytes 239624 | tf_op jit(solution)/shard_map/ppermute | solution.py:199
  41.3 1.3 %collective-permute-start.5 = (bf16[26,1536]{1,0:T(8,128)(2,1)S(1)}, bf16[26,1536]{1,0:T(8,128)(2,1)S(1)}, u32[]{:S(2)}, u32[]{:S(2)}) collective-permute-start(bf16[26,1536]{1,0:T(8,128)(2,1)S(1)} %pad_maximum_fusion), channel_id=1, source_target_pairs={{0,24},{4,28},{8,0},{12,4},{16,8},{20,12},{24,16},{28,20},{1,25},{... | collective-permute-start | bytes 239624 | tf_op jit(solution)/shard_map/ppermute | solution.py:199
  42.7 1.5 %collective-permute-start.6 = (bf16[26,1536]{1,0:T(8,128)(2,1)S(1)}, bf16[26,1536]{1,0:T(8,128)(2,1)S(1)}, u32[]{:S(2)}, u32[]{:S(2)}) collective-permute-start(bf16[26,1536]{1,0:T(8,128)(2,1)S(1)} %pad_maximum_fusion), channel_id=1, source_target_pairs={{0,28},{4,0},{8,4},{12,8},{16,12},{20,16},{24,20},{28,24},{1,29},{... | collective-permute-start | bytes 239624 | tf_op jit(solution)/shard_map/ppermute | solution.py:199
  44.1 4.0 %collective-permute-done.2 = bf16[26,1536]{1,0:T(8,128)(2,1)S(1)} collective-permute-done((bf16[26,1536]{1,0:T(8,128)(2,1)S(1)}, bf16[26,1536]{1,0:T(8,128)(2,1)S(1)}, u32[]{:S(2)}, u32[]{:S(2)}) %collective-permute-start.2) | collective-permute-done | bytes 79904 | tf_op jit(solution)/shard_map/ppermute | solution.py:199
  48.2 0.5 collective-permute-done.3
  48.7 0.4 collective-permute-done.6
  49.1 0.6 gather_fusion.1
  49.7 0.1 broadcast_select_fusion
  49.9 0.8 slice.89
  50.7 0.3 reshape.371
  51.0 0.2 fusion.33
  51.2 1.3 %dynamic-slice_add_fusion = f32[192,1,4]{2,1,0:T(1,128)} fusion(f32[192,1,32]{2,1,0:T(1,128)S(1)} %get-tuple-element.12, s32[]{:T(128)S(6)} %select_n.121, f32[192,1,32]{2,1,0:T(1,128)S(1)} %get-tuple-element.13, f32[192,1,32]{2,1,0:T(1,128)S(1)} %get-tuple-element.11), kind=kLoop, calls=%fused_computation.24 | loop fusion | flops 1536 | bytes 12292 | tf_op jit(solution)/shard_map/add | solution.py:224
  52.5 6.4 %shard_map.118 = bf16[192,1536]{1,0:T(8,128)(2,1)} custom-call(bf16[192,1536]{1,0:T(8,128)(2,1)} %bitcast.153, bf16[4,2,192,1536]{3,2,1,0:T(8,128)(2,1)} %bitcast.152, bf16[4,192,1536]{2,1,0:T(8,128)(2,1)} %dn_ref.1, f32[192,4]{1,0:T(8,128)} %bitcast.159), custom_call_target="tpu_custom_call" | custom-call | tf_op jit(solution)/shard_map/pallas_call | solution.py:62
  58.9 1.6 %reshape.365 = bf16[8,24,4,384]{3,2,1,0:T(4,128)(2,1)S(1)} reshape(bf16[192,1536]{1,0:T(8,128)(2,1)} %shard_map.118) | data formatting | bytes 1179648 | tf_op jit(solution)/shard_map/reshape | solution.py:228
  60.5 0.9 %copy.80 = bf16[8,24,4,384]{3,1,2,0:T(8,128)(2,1)} copy(bf16[8,24,4,384]{3,2,1,0:T(4,128)(2,1)S(1)} %reshape.365) | data formatting | bytes 1179648 | tf_op jit(solution)/shard_map/reshape | solution.py:228
  61.4 9.2 %all-to-all-start.1 = ((bf16[32,24,384]{2,1,0:T(8,128)(2,1)}), bf16[32,24,384]{2,1,0:T(8,128)(2,1)S(1)}, u32[]{:S(2)}, u32[]{:S(2)}) async-start(bf16[32,24,384]{2,1,0:T(8,128)(2,1)} %bitcast.43), calls=%async_computation.1 | async-start | bytes 1179648 | tf_op jit(solution)/shard_map/all_to_all | solution.py:230
  70.6 16.8 %all-to-all-done.1 = bf16[32,24,384]{2,1,0:T(8,128)(2,1)S(1)} async-done(((bf16[32,24,384]{2,1,0:T(8,128)(2,1)}), bf16[32,24,384]{2,1,0:T(8,128)(2,1)S(1)}, u32[]{:S(2)}, u32[]{:S(2)}) %all-to-all-start.1) | async-done | bytes 589856 | tf_op jit(solution)/shard_map/all_to_all | solution.py:230
  87.5 0.6 add_convert_fusion.1
  (75 shorter events, 2.0 us)
Async XLA Ops:
  0.0 23.9 %copy-start = (bf16[384,1536]{1,0:T(8,128)(2,1)S(1)}, bf16[384,1536]{1,0:T(8,128)(2,1)}, u32[]{:S(2)}) copy-start(bf16[384,1536]{1,0:T(8,128)(2,1)} %param.18) | copy-start | bytes 3538948
  0.0 9.4 %copy-start.6 = (s32[1,24]{1,0:T(1,128)S(1)}, s32[1,24]{1,0:T(1,128)}, u32[]{:S(2)}) copy-start(s32[1,24]{1,0:T(1,128)} %param.16) | copy-start | bytes 292
  0.0 9.6 %copy-start.1 = (bf16[768,2,2,128]{3,2,1,0:T(2,128)(2,1)S(1)}, bf16[768,2,2,128]{3,2,1,0:T(2,128)(2,1)}, u32[]{:S(2)}) copy-start(bf16[768,2,2,128]{3,2,1,0:T(2,128)(2,1)} %param.17) | copy-start | bytes 2359300
  11.2 5.3 %copy-start.2 = (bf16[24,2,256]{2,1,0:T(2,128)(2,1)S(1)}, bf16[24,2,256]{2,1,0:T(2,128)(2,1)}, u32[]{:S(2)}) copy-start(bf16[24,2,256]{2,1,0:T(2,128)(2,1)} %param.14) | copy-start | bytes 73732
  11.9 5.3 %copy-start.4 = (f32[24,4]{0,1:T(4,128)S(1)}, f32[24,4]{0,1:T(4,128)}, u32[]{:S(2)}) copy-start(f32[24,4]{0,1:T(4,128)} %param.21) | copy-start | bytes 1156
  11.9 5.3 %copy-start.5 = (s32[24,4]{0,1:T(4,128)S(1)}, s32[24,4]{0,1:T(4,128)}, u32[]{:S(2)}) copy-start(s32[24,4]{0,1:T(4,128)} %param.20) | copy-start | bytes 1156
  13.0 9.8 %all-to-all-start = ((f32[4,24,3,130]{3,1,2,0:T(8,128)}), f32[4,24,3,130]{3,1,2,0:T(8,128)S(1)}, u32[]{:S(2)}, u32[]{:S(2)}) async-start(f32[4,24,3,130]{3,1,2,0:T(8,128)} %maximum_bitcast_fusion), calls=%async_computation | async-start | bytes 589824 | tf_op jit(solution)/shard_map/all_to_all | solution.py:156
  24.1 7.2 %copy-start.3 = (f32[1536]{0:T(1024)S(1)}, f32[1536]{0:T(1024)}, u32[]{:S(2)}) copy-start(f32[1536]{0:T(1024)} %param.19) | copy-start | bytes 18436
  31.4 9.9 %collective-permute-start = (bf16[26,1536]{1,0:T(8,128)(2,1)S(1)}, bf16[26,1536]{1,0:T(8,128)(2,1)S(1)}, u32[]{:S(2)}, u32[]{:S(2)}) collective-permute-start(bf16[26,1536]{1,0:T(8,128)(2,1)S(1)} %pad_maximum_fusion), channel_id=1, source_target_pairs={{0,4},{4,8},{8,12},{12,16},{16,20},{20,24},{24,28},{28,0},{1,5},{5... | collective-permute-start | bytes 239624 | tf_op jit(solution)/shard_map/ppermute | solution.py:199
  33.3 9.4 %collective-permute-start.1 = (bf16[26,1536]{1,0:T(8,128)(2,1)S(1)}, bf16[26,1536]{1,0:T(8,128)(2,1)S(1)}, u32[]{:S(2)}, u32[]{:S(2)}) collective-permute-start(bf16[26,1536]{1,0:T(8,128)(2,1)S(1)} %pad_maximum_fusion), channel_id=1, source_target_pairs={{0,8},{4,12},{8,16},{12,20},{16,24},{20,28},{24,0},{28,4},{1,9},{5... | collective-permute-start | bytes 239624 | tf_op jit(solution)/shard_map/ppermute | solution.py:199
  34.9 13.3 %collective-permute-start.2 = (bf16[26,1536]{1,0:T(8,128)(2,1)S(1)}, bf16[26,1536]{1,0:T(8,128)(2,1)S(1)}, u32[]{:S(2)}, u32[]{:S(2)}) collective-permute-start(bf16[26,1536]{1,0:T(8,128)(2,1)S(1)} %pad_maximum_fusion), channel_id=1, source_target_pairs={{0,12},{4,16},{8,20},{12,24},{16,28},{20,0},{24,4},{28,8},{1,13},{... | collective-permute-start | bytes 239624 | tf_op jit(solution)/shard_map/ppermute | solution.py:199
  37.4 11.2 %collective-permute-start.3 = (bf16[26,1536]{1,0:T(8,128)(2,1)S(1)}, bf16[26,1536]{1,0:T(8,128)(2,1)S(1)}, u32[]{:S(2)}, u32[]{:S(2)}) collective-permute-start(bf16[26,1536]{1,0:T(8,128)(2,1)S(1)} %pad_maximum_fusion), channel_id=1, source_target_pairs={{0,16},{4,20},{8,24},{12,28},{16,0},{20,4},{24,8},{28,12},{1,17},{... | collective-permute-start | bytes 239624 | tf_op jit(solution)/shard_map/ppermute | solution.py:199
  38.7 10.0 %collective-permute-start.4 = (bf16[26,1536]{1,0:T(8,128)(2,1)S(1)}, bf16[26,1536]{1,0:T(8,128)(2,1)S(1)}, u32[]{:S(2)}, u32[]{:S(2)}) collective-permute-start(bf16[26,1536]{1,0:T(8,128)(2,1)S(1)} %pad_maximum_fusion), channel_id=1, source_target_pairs={{0,20},{4,24},{8,28},{12,0},{16,4},{20,8},{24,12},{28,16},{1,21},{... | collective-permute-start | bytes 239624 | tf_op jit(solution)/shard_map/ppermute | solution.py:199
  41.3 7.4 %collective-permute-start.5 = (bf16[26,1536]{1,0:T(8,128)(2,1)S(1)}, bf16[26,1536]{1,0:T(8,128)(2,1)S(1)}, u32[]{:S(2)}, u32[]{:S(2)}) collective-permute-start(bf16[26,1536]{1,0:T(8,128)(2,1)S(1)} %pad_maximum_fusion), channel_id=1, source_target_pairs={{0,24},{4,28},{8,0},{12,4},{16,8},{20,12},{24,16},{28,20},{1,25},{... | collective-permute-start | bytes 239624 | tf_op jit(solution)/shard_map/ppermute | solution.py:199
  42.7 6.4 %collective-permute-start.6 = (bf16[26,1536]{1,0:T(8,128)(2,1)S(1)}, bf16[26,1536]{1,0:T(8,128)(2,1)S(1)}, u32[]{:S(2)}, u32[]{:S(2)}) collective-permute-start(bf16[26,1536]{1,0:T(8,128)(2,1)S(1)} %pad_maximum_fusion), channel_id=1, source_target_pairs={{0,28},{4,0},{8,4},{12,8},{16,12},{20,16},{24,20},{28,24},{1,29},{... | collective-permute-start | bytes 239624 | tf_op jit(solution)/shard_map/ppermute | solution.py:199
  61.4 26.1 %all-to-all-start.1 = ((bf16[32,24,384]{2,1,0:T(8,128)(2,1)}), bf16[32,24,384]{2,1,0:T(8,128)(2,1)S(1)}, u32[]{:S(2)}, u32[]{:S(2)}) async-start(bf16[32,24,384]{2,1,0:T(8,128)(2,1)} %bitcast.43), calls=%async_computation.1 | async-start | bytes 1179648 | tf_op jit(solution)/shard_map/all_to_all | solution.py:230

commit v6 on v5

--- a/solution.py
+++ b/solution.py
@@ -1,3 +1,4 @@
+import functools
 import math
 
 import jax
@@ -30,7 +31,7 @@
     )
 
 
-def _expert_body(x_ref, gu_ref, dn_ref, w_ref, o_ref, acc_ref):
+def _expert_body(x_ref, gu_ref, dn_ref, w_ref, o_ref, acc_ref, *, group_rows, row_count, tp_count):
     block = pl.program_id(1)
 
     @pl.when(block == 0)
@@ -51,25 +52,37 @@
 
     @pl.when(block == pl.num_programs(1) - 1)
     def _():
-        o_ref[...] = acc_ref[...].astype(o_ref.dtype)
-
-
-def expert_mix(rows, gate_up, down, weights):
+        own_width = o_ref.shape[2]
+        for group in range(x_ref.shape[0] // group_rows):
+            for part in range(tp_count):
+                o_ref[group * tp_count + part] = acc_ref[
+                    group * group_rows : group * group_rows + row_count,
+                    part * own_width : (part + 1) * own_width,
+                ].astype(o_ref.dtype)
+
+
+def expert_mix(rows, gate_up, down, weights, group_rows, row_count, tp_count):
     row_total, width = rows.shape
     local_count, _, _, hidden = gate_up.shape
-    tile = math.gcd(row_total, 192)
+    group_total = row_total // group_rows
+    tile_groups = math.gcd(group_total, 8)
+    tile = tile_groups * group_rows
+    own_width = width // tp_count
     gate_up_t = jnp.swapaxes(gate_up, 2, 3)
+    body = functools.partial(
+        _expert_body, group_rows=group_rows, row_count=row_count, tp_count=tp_count
+    )
     return pl.pallas_call(
-        _expert_body,
-        grid=(row_total // tile, local_count),
+        body,
+        grid=(group_total // tile_groups, local_count),
         in_specs=[
             pl.BlockSpec((tile, width), lambda i, b: (i, 0)),
             pl.BlockSpec((1, 2, hidden, width), lambda i, b: (b, 0, 0, 0)),
             pl.BlockSpec((1, hidden, width), lambda i, b: (b, 0, 0)),
             pl.BlockSpec((tile, local_count), lambda i, b: (i, 0)),
         ],
-        out_specs=pl.BlockSpec((tile, width), lambda i, b: (i, 0)),
-        out_shape=jax.ShapeDtypeStruct((row_total, width), jnp.bfloat16),
+        out_specs=pl.BlockSpec((tile_groups * tp_count, row_count, own_width), lambda i, b: (i, 0, 0)),
+        out_shape=jax.ShapeDtypeStruct((group_total * tp_count, row_count, own_width), jnp.bfloat16),
         scratch_shapes=[pltpu.VMEM((tile, width), jnp.float32)],
         compiler_params=pltpu.CompilerParams(dimension_semantics=("parallel", "arbitrary")),
     )(rows, gate_up_t, down, weights)
@@ -211,22 +224,30 @@
     weight_low = weight_rest - weight_mid
     code = jnp.stack(
         [weight_high.astype(jnp.bfloat16), weight_mid.astype(jnp.bfloat16), weight_low.astype(jnp.bfloat16)],
-        axis=1,
+        axis=0,
     ).reshape(-1)
-    code_rows = -(-code.shape[0] // model_width)
+    group_rows = -(-(row_count + -(-code.shape[0] // model_width)) // 16) * 16
+    code_rows = group_rows - row_count
     code = jnp.pad(code, (0, code_rows * model_width - code.shape[0])).reshape(code_rows, model_width)
     message = jnp.concatenate([normed, code], axis=0)
-    message_all = gather_req(message).reshape(req_count, row_count + code_rows, model_width)
-    rows_all = message_all[:, :row_count].reshape(req_count * row_count, model_width)
+    message_all = gather_req(message).reshape(req_count, group_rows, model_width)
     pieces = message_all[:, row_count:].reshape(req_count, code_rows * model_width)
-    pieces = pieces[:, : row_count * 3 * block_total].astype(jnp.float32)
-    pieces = pieces.reshape(req_count * row_count, 3, block_total)
+    pieces = pieces[:, : 3 * row_count * block_total].astype(jnp.float32)
+    pieces = pieces.reshape(req_count, 3, row_count, block_total)
     weights_all = (pieces[:, 0] + pieces[:, 1]) + pieces[:, 2]
-    weights_own = lax.dynamic_slice_in_dim(weights_all, req_index * local_count, local_count, 1)
-
-    mixed = expert_mix(rows_all, gate_up, down, weights_own)
-    mixed = mixed.reshape(req_count, row_count, tp_count, own_width)
-    mixed = jnp.transpose(mixed, (0, 2, 1, 3)).reshape(req_count * tp_count, row_count, own_width)
+    weights_own = lax.dynamic_slice_in_dim(weights_all, req_index * local_count, local_count, 2)
+    weights_own = jnp.pad(weights_own, ((0, 0), (0, code_rows), (0, 0)))
+    weights_own = weights_own.reshape(req_count * group_rows, local_count)
+
+    mixed = expert_mix(
+        message_all.reshape(req_count * group_rows, model_width),
+        gate_up,
+        down,
+        weights_own,
+        group_rows,
+        row_count,
+        tp_count,
+    )
     mixed = lax.all_to_all(mixed, ("req", "tp"), 0, 0, tiled=True)
     mixed = jnp.sum(mixed.astype(jnp.float32), axis=0)
     return (residual_own + mixed).astype(jnp.bfloat16)

time: 88.6 us -> 86 us (0.971)
  local copies, waits for them, and re-layouts: 7.67 us -> 4.92 us
    reshape x3 -> x1, local copies, waits for them, and re-layouts: 2.73 us -> 0.12 us  [per_device(): pieces = pieces.reshape(req_count, 3, row_count, block_total)]
    add x1 -> x0, other arithmetic: 1.32 us -> none  [per_device(): weights_all = pieces[:, 0] + pieces[:, 1] + pieces[:, 2]]
    slice x2 -> x0, local copies, waits for them, and re-layouts: 1.05 us -> none  [the longest x1 0.85 us: per_device(): message_all[:, :row_count].reshape(req_count * row_count, model_width)]
    select_n x2, other arithmetic: 0.15 us -> 1.06 us  [gather_req(): arrived = jnp.take(jnp.stack(arrived, axis=0), order, axis=0)]
where the time goes in v6:
time: 86 us; the launch traced here: 85.5 us
  waiting for transfers between devices  26.2 us (30%)
  starting transfers between devices  25.4 us (30%)
  blocking collectives  13.6 us (16%)
  Pallas kernels  6.88 us (8%)
  other arithmetic  6.47 us (8%)
  local copies, waits for them, and re-layouts  4.92 us (6%)
  matrix products  1.62 us (2%)
    all_to_all x1, waiting for transfers between devices, per_device(): mixed = lax.all_to_all(mixed, ('req', 'tp'), 0, 0, tiled=True)  16.8 us
    ppermute x7, starting transfers between devices, gather_req(): lax.ppermute(value, 'req', [(i, (i + shift) % req_count) for i in range(r...  12.7 us
    all_to_all x1, starting transfers between devices, per_device(): mixed = lax.all_to_all(mixed, ('req', 'tp'), 0, 0, tiled=True)  9.24 us
    all_gather x1, blocking collectives, per_device(): projected = jnp.sum(lax.all_gather(partial_proj, 'tp', axis=0), axis=0)  7 us
    pallas_call x1, Pallas kernels, expert_mix(): pl.pallas_call(body, grid=(group_total // tile_groups, local_count), in_s...  6.88 us
    all_gather x1, blocking collectives, per_device(): gathered = lax.all_gather(packed, 'tp', axis=0)  6.59 us
    ppermute x7, waiting for transfers between devices, gather_req(): lax.ppermute(value, 'req', [(i, (i + shift) % req_count) for i in range(r...  4.87 us
    all_to_all x1, waiting for transfers between devices, per_device(): lax.all_to_all(jnp.transpose(states, (1, 0, 2, 3)), 'tp', 0, 0, tiled=True)  4.52 us
  transfers between devices with their start and end apart: 9, of which 5 were waited for; matrix products, arithmetic and copies ran while one was open for 2% of the time, Pallas kernels for 0%

profile of v6, /device:TPU:0, one launch (start us, length us, event | category | flops | bytes accessed | tf_op | source)
XLA Modules:
  0.0 85.5 jit_solution(10608877749198040971)
XLA Ops:
  0.0 0.8 convert_element_type.101
  0.8 0.7 reshape.361
  1.6 0.1 multiply_cosine_fusion
  1.7 0.1 subtract_convert_fusion
  1.9 0.7 pad_maximum_fusion.1
  2.7 6.6 %all-gather = bf16[8,24,384]{2,1,0:T(8,128)(2,1)S(1)} all-gather(bf16[2,24,384]{2,1,0:T(8,128)(2,1)S(1)} %pad_maximum_fusion.1), channel_id=2, replica_groups=mesh['req'=8,'tp'=4] {'tp'}, dimensions={0}, use_global_device_ids=true | all-gather | bytes 184320 | tf_op jit(solution)/shard_map/all_gather | solution.py:125
  9.5 0.1 reduce.2
  9.7 0.5 fusion.34
  10.3 0.5 fusion.35
  10.8 0.1 concatenate.28
  10.9 0.3 fusion.3
  11.2 0.7 fusion.2
  12.0 0.1 concatenate.29
  12.1 0.9 %maximum_bitcast_fusion = f32[4,24,3,130]{3,1,2,0:T(8,128)} fusion(f32[24,4,3,128]{3,0,2,1:T(8,128)S(1)} %bitcast.170, f32[24,4,3,1]{3,0,2,1:T(8,128)S(1)} %concatenate.29, f32[24,4,3,1]{3,0,2,1:T(8,128)S(1)} %concatenate.28), kind=kLoop, calls=%fused_computation.15 | loop fusion | flops 74880 | bytes 299520 | tf_op jit(solution)/shard_map/transpose | solution.py:170
  13.0 3.5 %all-to-all-start = ((f32[4,24,3,130]{3,1,2,0:T(8,128)}), f32[4,24,3,130]{3,1,2,0:T(8,128)S(1)}, u32[]{:S(2)}, u32[]{:S(2)}) async-start(f32[4,24,3,130]{3,1,2,0:T(8,128)} %maximum_bitcast_fusion), calls=%async_computation | async-start | bytes 589824 | tf_op jit(solution)/shard_map/all_to_all | solution.py:169
  16.7 0.1 subtract_convert_fusion.1
  16.9 0.2 fusion.16
  17.0 0.1 copy.92
  17.3 0.1 select_reduce_fusion
  17.7 0.6 gather_fusion
  18.3 4.5 %all-to-all-done = f32[4,24,3,130]{3,1,2,0:T(8,128)S(1)} async-done(((f32[4,24,3,130]{3,1,2,0:T(8,128)}), f32[4,24,3,130]{3,1,2,0:T(8,128)S(1)}, u32[]{:S(2)}, u32[]{:S(2)}) %all-to-all-start) | async-done | bytes 149792 | tf_op jit(solution)/shard_map/all_to_all | solution.py:169
  22.8 0.1 slice_reduce_fusion.1
  23.0 0.1 copy.97
  23.2 0.1 copy.83
  23.5 0.1 fusion.11
  23.9 0.3 fusion.18
  24.1 7.0 %all-gather.1 = f32[96,1536]{1,0:T(8,128)S(1)} all-gather(f32[24,1536]{1,0:T(8,128)S(1)} %fusion.18), channel_id=3, replica_groups=mesh['req'=8,'tp'=4] {'tp'}, dimensions={0}, use_global_device_ids=true | all-gather | bytes 737280 | tf_op jit(solution)/shard_map/all_gather | solution.py:188
  31.2 0.1 fusion.10
  31.4 1.8 %collective-permute-start = (bf16[32,1536]{1,0:T(8,128)(2,1)S(1)}, bf16[32,1536]{1,0:T(8,128)(2,1)S(1)}, u32[]{:S(2)}, u32[]{:S(2)}) collective-permute-start(bf16[32,1536]{1,0:T(8,128)(2,1)S(1)} %pad_maximum_fusion), channel_id=1, source_target_pairs={{0,4},{4,8},{8,12},{12,16},{16,20},{20,24},{24,28},{28,0},{1,5},{5... | collective-permute-start | bytes 294920 | tf_op jit(solution)/shard_map/ppermute | solution.py:212
  33.3 1.6 %collective-permute-start.1 = (bf16[32,1536]{1,0:T(8,128)(2,1)S(1)}, bf16[32,1536]{1,0:T(8,128)(2,1)S(1)}, u32[]{:S(2)}, u32[]{:S(2)}) collective-permute-start(bf16[32,1536]{1,0:T(8,128)(2,1)S(1)} %pad_maximum_fusion), channel_id=1, source_target_pairs={{0,8},{4,12},{8,16},{12,20},{16,24},{20,28},{24,0},{28,4},{1,9},{5... | collective-permute-start | bytes 294920 | tf_op jit(solution)/shard_map/ppermute | solution.py:212
  34.9 2.5 %collective-permute-start.2 = (bf16[32,1536]{1,0:T(8,128)(2,1)S(1)}, bf16[32,1536]{1,0:T(8,128)(2,1)S(1)}, u32[]{:S(2)}, u32[]{:S(2)}) collective-permute-start(bf16[32,1536]{1,0:T(8,128)(2,1)S(1)} %pad_maximum_fusion), channel_id=1, source_target_pairs={{0,12},{4,16},{8,20},{12,24},{16,28},{20,0},{24,4},{28,8},{1,13},{... | collective-permute-start | bytes 294920 | tf_op jit(solution)/shard_map/ppermute | solution.py:212
  37.4 1.2 %collective-permute-start.3 = (bf16[32,1536]{1,0:T(8,128)(2,1)S(1)}, bf16[32,1536]{1,0:T(8,128)(2,1)S(1)}, u32[]{:S(2)}, u32[]{:S(2)}) collective-permute-start(bf16[32,1536]{1,0:T(8,128)(2,1)S(1)} %pad_maximum_fusion), channel_id=1, source_target_pairs={{0,16},{4,20},{8,24},{12,28},{16,0},{20,4},{24,8},{28,12},{1,17},{... | collective-permute-start | bytes 294920 | tf_op jit(solution)/shard_map/ppermute | solution.py:212
  38.7 2.6 %collective-permute-start.4 = (bf16[32,1536]{1,0:T(8,128)(2,1)S(1)}, bf16[32,1536]{1,0:T(8,128)(2,1)S(1)}, u32[]{:S(2)}, u32[]{:S(2)}) collective-permute-start(bf16[32,1536]{1,0:T(8,128)(2,1)S(1)} %pad_maximum_fusion), channel_id=1, source_target_pairs={{0,20},{4,24},{8,28},{12,0},{16,4},{20,8},{24,12},{28,16},{1,21},{... | collective-permute-start | bytes 294920 | tf_op jit(solution)/shard_map/ppermute | solution.py:212
  41.3 1.3 %collective-permute-start.5 = (bf16[32,1536]{1,0:T(8,128)(2,1)S(1)}, bf16[32,1536]{1,0:T(8,128)(2,1)S(1)}, u32[]{:S(2)}, u32[]{:S(2)}) collective-permute-start(bf16[32,1536]{1,0:T(8,128)(2,1)S(1)} %pad_maximum_fusion), channel_id=1, source_target_pairs={{0,24},{4,28},{8,0},{12,4},{16,8},{20,12},{24,16},{28,20},{1,25},{... | collective-permute-start | bytes 294920 | tf_op jit(solution)/shard_map/ppermute | solution.py:212
  42.7 1.5 %collective-permute-start.6 = (bf16[32,1536]{1,0:T(8,128)(2,1)S(1)}, bf16[32,1536]{1,0:T(8,128)(2,1)S(1)}, u32[]{:S(2)}, u32[]{:S(2)}) collective-permute-start(bf16[32,1536]{1,0:T(8,128)(2,1)S(1)} %pad_maximum_fusion), channel_id=1, source_target_pairs={{0,28},{4,0},{8,4},{12,8},{16,12},{20,16},{24,20},{28,24},{1,29},{... | collective-permute-start | bytes 294920 | tf_op jit(solution)/shard_map/ppermute | solution.py:212
  44.1 4.0 %collective-permute-done.2 = bf16[32,1536]{1,0:T(8,128)(2,1)S(1)} collective-permute-done((bf16[32,1536]{1,0:T(8,128)(2,1)S(1)}, bf16[32,1536]{1,0:T(8,128)(2,1)S(1)}, u32[]{:S(2)}, u32[]{:S(2)}) %collective-permute-start.2) | collective-permute-done | bytes 98336 | tf_op jit(solution)/shard_map/ppermute | solution.py:212
  48.2 0.5 collective-permute-done.3
  48.7 0.4 collective-permute-done.6
  49.1 0.6 gather_fusion.1
  49.9 0.1 reshape.365
  50.0 0.1 fusion.12
  50.2 0.7 pad.9
  50.8 1.0 %bitcast_select_fusion.x_ref = bf16[256,1536]{1,0:T(8,128)(2,1)} fusion(bf16[8,32,1536]{2,1,0:T(8,128)(2,1)S(1)} %gather_fusion.1, pred[256]{0:T(512)(128)(4,1)S(1)} %broadcast_in_dim.102), kind=kLoop, calls=%fused_computation.7 | loop fusion | flops 393216 | bytes 1573120 | tf_op jit(solution)/shard_map/jit(_take)/select_n | solution.py:216
  51.9 6.9 %shard_map.118 = bf16[32,24,384]{2,1,0:T(8,128)(2,1)} custom-call(bf16[256,1536]{1,0:T(8,128)(2,1)} %bitcast_select_fusion.x_ref, bf16[4,2,192,1536]{3,2,1,0:T(8,128)(2,1)} %bitcast.158, bf16[4,192,1536]{2,1,0:T(8,128)(2,1)} %dn_ref.1, f32[256,4]{1,0:T(8,128)} %bitcast.164), custom_call_target="tpu_custom_call" | custom-call | tf_op jit(solution)/shard_map/pallas_call | solution.py:75
  58.8 9.2 %all-to-all-start.1 = ((bf16[32,24,384]{2,1,0:T(8,128)(2,1)}), bf16[32,24,384]{2,1,0:T(8,128)(2,1)S(1)}, u32[]{:S(2)}, u32[]{:S(2)}) async-start(bf16[32,24,384]{2,1,0:T(8,128)(2,1)} %shard_map.118), calls=%async_computation.1 | async-start | bytes 1179648 | tf_op jit(solution)/shard_map/all_to_all | solution.py:251
  68.0 16.8 %all-to-all-done.1 = bf16[32,24,384]{2,1,0:T(8,128)(2,1)S(1)} async-done(((bf16[32,24,384]{2,1,0:T(8,128)(2,1)}), bf16[32,24,384]{2,1,0:T(8,128)(2,1)S(1)}, u32[]{:S(2)}, u32[]{:S(2)}) %all-to-all-start.1) | async-done | bytes 589856 | tf_op jit(solution)/shard_map/all_to_all | solution.py:251
  84.8 0.1 convert_reduce_fusion
  84.9 0.6 add_convert_fusion.1
  (74 shorter events, 2.0 us)
Async XLA Ops:
  0.0 23.9 %copy-start = (bf16[384,1536]{1,0:T(8,128)(2,1)S(1)}, bf16[384,1536]{1,0:T(8,128)(2,1)}, u32[]{:S(2)}) copy-start(bf16[384,1536]{1,0:T(8,128)(2,1)} %param.18) | copy-start | bytes 3538948
  0.0 9.4 %copy-start.6 = (s32[1,24]{1,0:T(1,128)S(1)}, s32[1,24]{1,0:T(1,128)}, u32[]{:S(2)}) copy-start(s32[1,24]{1,0:T(1,128)} %param.16) | copy-start | bytes 292
  0.0 9.6 %copy-start.1 = (bf16[768,2,2,128]{3,2,1,0:T(2,128)(2,1)S(1)}, bf16[768,2,2,128]{3,2,1,0:T(2,128)(2,1)}, u32[]{:S(2)}) copy-start(bf16[768,2,2,128]{3,2,1,0:T(2,128)(2,1)} %param.17) | copy-start | bytes 2359300
  11.2 5.3 %copy-start.2 = (bf16[24,2,256]{2,1,0:T(2,128)(2,1)S(1)}, bf16[24,2,256]{2,1,0:T(2,128)(2,1)}, u32[]{:S(2)}) copy-start(bf16[24,2,256]{2,1,0:T(2,128)(2,1)} %param.14) | copy-start | bytes 73732
  11.9 5.3 %copy-start.4 = (f32[24,4]{0,1:T(4,128)S(1)}, f32[24,4]{0,1:T(4,128)}, u32[]{:S(2)}) copy-start(f32[24,4]{0,1:T(4,128)} %param.21) | copy-start | bytes 1156
  11.9 5.3 %copy-start.5 = (s32[24,4]{0,1:T(4,128)S(1)}, s32[24,4]{0,1:T(4,128)}, u32[]{:S(2)}) copy-start(s32[24,4]{0,1:T(4,128)} %param.20) | copy-start | bytes 1156
  13.0 9.8 %all-to-all-start = ((f32[4,24,3,130]{3,1,2,0:T(8,128)}), f32[4,24,3,130]{3,1,2,0:T(8,128)S(1)}, u32[]{:S(2)}, u32[]{:S(2)}) async-start(f32[4,24,3,130]{3,1,2,0:T(8,128)} %maximum_bitcast_fusion), calls=%async_computation | async-start | bytes 589824 | tf_op jit(solution)/shard_map/all_to_all | solution.py:169
  24.1 7.2 %copy-start.3 = (f32[1536]{0:T(1024)S(1)}, f32[1536]{0:T(1024)}, u32[]{:S(2)}) copy-start(f32[1536]{0:T(1024)} %param.19) | copy-start | bytes 18436
  31.4 9.9 %collective-permute-start = (bf16[32,1536]{1,0:T(8,128)(2,1)S(1)}, bf16[32,1536]{1,0:T(8,128)(2,1)S(1)}, u32[]{:S(2)}, u32[]{:S(2)}) collective-permute-start(bf16[32,1536]{1,0:T(8,128)(2,1)S(1)} %pad_maximum_fusion), channel_id=1, source_target_pairs={{0,4},{4,8},{8,12},{12,16},{16,20},{20,24},{24,28},{28,0},{1,5},{5... | collective-permute-start | bytes 294920 | tf_op jit(solution)/shard_map/ppermute | solution.py:212
  33.3 9.4 %collective-permute-start.1 = (bf16[32,1536]{1,0:T(8,128)(2,1)S(1)}, bf16[32,1536]{1,0:T(8,128)(2,1)S(1)}, u32[]{:S(2)}, u32[]{:S(2)}) collective-permute-start(bf16[32,1536]{1,0:T(8,128)(2,1)S(1)} %pad_maximum_fusion), channel_id=1, source_target_pairs={{0,8},{4,12},{8,16},{12,20},{16,24},{20,28},{24,0},{28,4},{1,9},{5... | collective-permute-start | bytes 294920 | tf_op jit(solution)/shard_map/ppermute | solution.py:212
  34.9 13.3 %collective-permute-start.2 = (bf16[32,1536]{1,0:T(8,128)(2,1)S(1)}, bf16[32,1536]{1,0:T(8,128)(2,1)S(1)}, u32[]{:S(2)}, u32[]{:S(2)}) collective-permute-start(bf16[32,1536]{1,0:T(8,128)(2,1)S(1)} %pad_maximum_fusion), channel_id=1, source_target_pairs={{0,12},{4,16},{8,20},{12,24},{16,28},{20,0},{24,4},{28,8},{1,13},{... | collective-permute-start | bytes 294920 | tf_op jit(solution)/shard_map/ppermute | solution.py:212
  37.4 11.2 %collective-permute-start.3 = (bf16[32,1536]{1,0:T(8,128)(2,1)S(1)}, bf16[32,1536]{1,0:T(8,128)(2,1)S(1)}, u32[]{:S(2)}, u32[]{:S(2)}) collective-permute-start(bf16[32,1536]{1,0:T(8,128)(2,1)S(1)} %pad_maximum_fusion), channel_id=1, source_target_pairs={{0,16},{4,20},{8,24},{12,28},{16,0},{20,4},{24,8},{28,12},{1,17},{... | collective-permute-start | bytes 294920 | tf_op jit(solution)/shard_map/ppermute | solution.py:212
  38.7 10.0 %collective-permute-start.4 = (bf16[32,1536]{1,0:T(8,128)(2,1)S(1)}, bf16[32,1536]{1,0:T(8,128)(2,1)S(1)}, u32[]{:S(2)}, u32[]{:S(2)}) collective-permute-start(bf16[32,1536]{1,0:T(8,128)(2,1)S(1)} %pad_maximum_fusion), channel_id=1, source_target_pairs={{0,20},{4,24},{8,28},{12,0},{16,4},{20,8},{24,12},{28,16},{1,21},{... | collective-permute-start | bytes 294920 | tf_op jit(solution)/shard_map/ppermute | solution.py:212
  41.3 7.4 %collective-permute-start.5 = (bf16[32,1536]{1,0:T(8,128)(2,1)S(1)}, bf16[32,1536]{1,0:T(8,128)(2,1)S(1)}, u32[]{:S(2)}, u32[]{:S(2)}) collective-permute-start(bf16[32,1536]{1,0:T(8,128)(2,1)S(1)} %pad_maximum_fusion), channel_id=1, source_target_pairs={{0,24},{4,28},{8,0},{12,4},{16,8},{20,12},{24,16},{28,20},{1,25},{... | collective-permute-start | bytes 294920 | tf_op jit(solution)/shard_map/ppermute | solution.py:212
  42.7 6.4 %collective-permute-start.6 = (bf16[32,1536]{1,0:T(8,128)(2,1)S(1)}, bf16[32,1536]{1,0:T(8,128)(2,1)S(1)}, u32[]{:S(2)}, u32[]{:S(2)}) collective-permute-start(bf16[32,1536]{1,0:T(8,128)(2,1)S(1)} %pad_maximum_fusion), channel_id=1, source_target_pairs={{0,28},{4,0},{8,4},{12,8},{16,12},{20,16},{24,20},{28,24},{1,29},{... | collective-permute-start | bytes 294920 | tf_op jit(solution)/shard_map/ppermute | solution.py:212
  58.8 26.0 %all-to-all-start.1 = ((bf16[32,24,384]{2,1,0:T(8,128)(2,1)}), bf16[32,24,384]{2,1,0:T(8,128)(2,1)S(1)}, u32[]{:S(2)}, u32[]{:S(2)}) async-start(bf16[32,24,384]{2,1,0:T(8,128)(2,1)} %shard_map.118), calls=%async_computation.1 | async-start | bytes 1179648 | tf_op jit(solution)/shard_map/all_to_all | solution.py:251

commit v7 on v6

--- a/solution.py
+++ b/solution.py
@@ -206,18 +206,30 @@
         axis=1,
     )
 
-    if req_count <= 16:
-        def gather_req(value):
-            arrived = [value] + [
-                lax.ppermute(value, "req", [(i, (i + shift) % req_count) for i in range(req_count)])
-                for shift in range(1, req_count)
-            ]
-            order = (req_index - jnp.arange(req_count, dtype=jnp.int32)) % req_count
-            arrived = jnp.take(jnp.stack(arrived, axis=0), order, axis=0)
-            return arrived.reshape((req_count * value.shape[0],) + value.shape[1:])
-    else:
-        def gather_req(value):
+    def gather_req(value):
+        if req_count > 16 or (req_count - 1) % tp_count != tp_count - 1 or req_count < tp_count:
             return lax.all_gather(value, "req", axis=0, tiled=True)
+        per_tp = (req_count + tp_count - 1) // tp_count
+        fetched = []
+        for slot in range(per_tp):
+            pairs = []
+            for group in range(req_count):
+                for part in range(tp_count):
+                    shift = per_tp * part + slot + 1
+                    if shift < req_count:
+                        source = ((group - shift) % req_count) * tp_count + part
+                        pairs.append((source, group * tp_count + part))
+            moved = lax.ppermute(value, ("req", "tp"), pairs)
+            shift_here = per_tp * tp_index + slot + 1
+            fetched.append(jnp.where(shift_here < req_count, moved, value))
+        shared = lax.all_gather(jnp.stack(fetched, axis=0), "tp", axis=0)
+        shifts = (per_tp * jnp.arange(tp_count, dtype=jnp.int32)[:, None] + jnp.arange(per_tp, dtype=jnp.int32)[None, :] + 1) % req_count
+        shared = shared.reshape((tp_count * per_tp,) + value.shape)
+        groups = ((req_index - shifts.reshape(-1)) % req_count).astype(jnp.int32)
+        order = jnp.argsort(groups)
+        arrived = jnp.take(shared, order, axis=0)
+        return arrived.reshape((req_count * value.shape[0],) + value.shape[1:])
+
     weight_high = lax.reduce_precision(block_weights, exponent_bits=8, mantissa_bits=7)
     weight_rest = block_weights - weight_high
     weight_mid = lax.reduce_precision(weight_rest, exponent_bits=8, mantissa_bits=7)

time: 86 us -> 82 us (0.953)
  starting transfers between devices: 25.4 us -> 12 us
  blocking collectives: 13.6 us -> 22.2 us
  other arithmetic: 6.47 us -> 7.57 us
    all_gather x0 -> x1, blocking collectives: none -> 8.57 us  [gather_req(): shared = lax.all_gather(jnp.stack(fetched, axis=0), 'tp', axis=0)]
    ppermute x7 -> x2, starting transfers between devices: 12.7 us -> 5.31 us  [gather_req(): moved = lax.ppermute(value, ('req', 'tp'), pairs)]
    all_to_all x1, starting transfers between devices: 9.24 us -> 3.24 us  [per_device(): mixed = lax.all_to_all(mixed, ('req', 'tp'), 0, 0, tiled=True)]
    all_to_all x1, waiting for transfers between devices: 4.52 us -> 3.38 us  [per_device(): lax.all_to_all(jnp.transpose(states, (1, 0, 2, 3)), 'tp', 0, 0, tiled=True)]
    sort x0 -> x1, other arithmetic: none -> 0.96 us  [gather_req(): order = jnp.argsort(groups)]
    ppermute x7 -> x2, waiting for transfers between devices: 4.87 us -> 5.73 us  [gather_req(): moved = lax.ppermute(value, ('req', 'tp'), pairs)]
  transfers between devices with their start and end apart: 9 -> 4, of which waited for: 5 -> 4; matrix products, arithmetic and copies ran while one was open for 2% -> 3% of each run, Pallas kernels for 0% -> 0%
where the time goes in v7:
time: 82 us; the launch traced here: 81.6 us
  waiting for transfers between devices  25.9 us (32%)
  blocking collectives  22.2 us (27%)
  starting transfers between devices  12 us (15%)
  other arithmetic  7.57 us (9%)
  Pallas kernels  6.88 us (8%)
  local copies, waits for them, and re-layouts  4.95 us (6%)
  matrix products  1.62 us (2%)
    all_to_all x1, waiting for transfers between devices, per_device(): mixed = lax.all_to_all(mixed, ('req', 'tp'), 0, 0, tiled=True)  16.8 us
    all_gather x1, blocking collectives, gather_req(): shared = lax.all_gather(jnp.stack(fetched, axis=0), 'tp', axis=0)  8.57 us
    all_gather x1, blocking collectives, per_device(): projected = jnp.sum(lax.all_gather(partial_proj, 'tp', axis=0), axis=0)  7 us
    pallas_call x1, Pallas kernels, expert_mix(): pl.pallas_call(body, grid=(group_total // tile_groups, local_count), in_s...  6.88 us
    all_gather x1, blocking collectives, per_device(): gathered = lax.all_gather(packed, 'tp', axis=0)  6.59 us
    ppermute x2, waiting for transfers between devices, gather_req(): moved = lax.ppermute(value, ('req', 'tp'), pairs)  5.73 us
    ppermute x2, starting transfers between devices, gather_req(): moved = lax.ppermute(value, ('req', 'tp'), pairs)  5.31 us
    all_to_all x1, starting transfers between devices, per_device(): lax.all_to_all(jnp.transpose(states, (1, 0, 2, 3)), 'tp', 0, 0, tiled=True)  3.45 us
  transfers between devices with their start and end apart: 4, of which 4 were waited for; matrix products, arithmetic and copies ran while one was open for 3% of the time, Pallas kernels for 0%

profile of v7, /device:TPU:0, one launch (start us, length us, event | category | flops | bytes accessed | tf_op | source)
XLA Modules:
  0.0 81.6 jit_solution(5475546719442662527)
XLA Ops:
  0.0 0.8 convert_element_type.101
  0.8 0.7 reshape.327
  1.6 0.1 multiply_cosine_fusion
  1.7 0.1 subtract_convert_fusion
  1.8 0.1 pad_maximum_fusion.3
  1.9 0.7 pad_maximum_fusion.2
  2.7 6.6 %all-gather = bf16[8,24,384]{2,1,0:T(8,128)(2,1)S(1)} all-gather(bf16[2,24,384]{2,1,0:T(8,128)(2,1)S(1)} %pad_maximum_fusion.2), channel_id=2, replica_groups=mesh['req'=8,'tp'=4] {'tp'}, dimensions={0}, use_global_device_ids=true | all-gather | bytes 184320 | tf_op jit(solution)/shard_map/all_gather | solution.py:125
  9.5 0.1 reduce.2
  9.7 0.5 fusion.34
  10.3 0.5 fusion.35
  10.8 0.1 concatenate.28
  10.9 0.3 fusion.3
  11.2 0.7 fusion.2
  12.0 0.1 concatenate.29
  12.1 0.9 %maximum_bitcast_fusion = f32[4,24,3,130]{3,1,2,0:T(8,128)} fusion(f32[24,4,3,128]{3,0,2,1:T(8,128)S(1)} %bitcast.156, f32[24,4,3,1]{3,0,2,1:T(8,128)S(1)} %concatenate.29, f32[24,4,3,1]{3,0,2,1:T(8,128)S(1)} %concatenate.28), kind=kLoop, calls=%fused_computation.15 | loop fusion | flops 74880 | bytes 299520 | tf_op jit(solution)/shard_map/transpose | solution.py:170
  13.0 3.5 %all-to-all-start = ((f32[4,24,3,130]{3,1,2,0:T(8,128)}), f32[4,24,3,130]{3,1,2,0:T(8,128)S(1)}, u32[]{:S(2)}, u32[]{:S(2)}) async-start(f32[4,24,3,130]{3,1,2,0:T(8,128)} %maximum_bitcast_fusion), calls=%async_computation | async-start | bytes 589824 | tf_op jit(solution)/shard_map/all_to_all | solution.py:169
  16.7 1.0 %sort.17 = (s32[8]{0:T(128)}, s32[8]{0:T(128)S(1)}) sort(s32[8]{0:T(128)S(1)} %and_select_fusion, s32[8]{0:T(128)S(1)} %iota.40), dimensions={0}, to_apply=%region_7.8 | sort | flops 24 | bytes 128 | tf_op jit(solution)/shard_map/jit(argsort)/sort | solution.py:229
  17.8 0.1 subtract_convert_fusion.1
  17.9 0.1 maximum_bitcast_fusion.1
  18.0 0.2 fusion.16
  18.2 0.1 copy.92
  18.3 0.1 select_reduce_fusion
  18.5 0.1 reshape.320
  18.7 0.1 broadcast_in_dim.106
  18.8 0.6 gather_fusion
  19.4 3.4 %all-to-all-done = f32[4,24,3,130]{3,1,2,0:T(8,128)S(1)} async-done(((f32[4,24,3,130]{3,1,2,0:T(8,128)}), f32[4,24,3,130]{3,1,2,0:T(8,128)S(1)}, u32[]{:S(2)}, u32[]{:S(2)}) %all-to-all-start) | async-done | bytes 149792 | tf_op jit(solution)/shard_map/all_to_all | solution.py:169
  22.8 0.1 slice_reduce_fusion.1
  23.0 0.1 copy.97
  23.2 0.1 copy.83
  23.5 0.1 fusion.11
  23.9 0.3 fusion.18
  24.1 7.0 %all-gather.1 = f32[96,1536]{1,0:T(8,128)S(1)} all-gather(f32[24,1536]{1,0:T(8,128)S(1)} %fusion.18), channel_id=3, replica_groups=mesh['req'=8,'tp'=4] {'tp'}, dimensions={0}, use_global_device_ids=true | all-gather | bytes 737280 | tf_op jit(solution)/shard_map/all_gather | solution.py:188
  31.2 0.1 fusion.10
  31.4 1.8 %collective-permute-start = (bf16[32,1536]{1,0:T(8,128)(2,1)S(1)}, bf16[32,1536]{1,0:T(8,128)(2,1)S(1)}, u32[]{:S(2)}, u32[]{:S(2)}) collective-permute-start(bf16[32,1536]{1,0:T(8,128)(2,1)S(1)} %pad_maximum_fusion.1), channel_id=1, source_target_pairs={{28,0},{21,1},{14,2},{7,3},{0,4},{25,5},{18,6},{11,7},{4,8},{29,9}... | collective-permute-start | bytes 294920 | tf_op jit(solution)/shard_map/ppermute | solution.py:222
  33.2 3.5 %collective-permute-start.1 = (bf16[32,1536]{1,0:T(8,128)(2,1)S(1)}, bf16[32,1536]{1,0:T(8,128)(2,1)S(1)}, u32[]{:S(2)}, u32[]{:S(2)}) collective-permute-start(bf16[32,1536]{1,0:T(8,128)(2,1)S(1)} %pad_maximum_fusion.1), channel_id=1, source_target_pairs={{24,0},{17,1},{10,2},{28,4},{21,5},{14,6},{0,8},{25,9},{18,10},{4,... | collective-permute-start | bytes 294920 | tf_op jit(solution)/shard_map/ppermute | solution.py:222
  36.7 2.9 %collective-permute-done = bf16[32,1536]{1,0:T(8,128)(2,1)S(1)} collective-permute-done((bf16[32,1536]{1,0:T(8,128)(2,1)S(1)}, bf16[32,1536]{1,0:T(8,128)(2,1)S(1)}, u32[]{:S(2)}, u32[]{:S(2)}) %collective-permute-start) | collective-permute-done | bytes 98336 | tf_op jit(solution)/shard_map/ppermute | solution.py:222
  39.6 2.8 %collective-permute-done.1 = bf16[32,1536]{1,0:T(8,128)(2,1)S(1)} collective-permute-done((bf16[32,1536]{1,0:T(8,128)(2,1)S(1)}, bf16[32,1536]{1,0:T(8,128)(2,1)S(1)}, u32[]{:S(2)}, u32[]{:S(2)}) %collective-permute-start.1) | collective-permute-done | bytes 98336 | tf_op jit(solution)/shard_map/ppermute | solution.py:222
  42.5 8.6 %all-gather.2 = bf16[8,32,1536]{2,1,0:T(8,128)(2,1)S(1)} all-gather(bf16[2,32,1536]{2,1,0:T(8,128)(2,1)S(1)} %pad_maximum_fusion), channel_id=4, replica_groups=mesh['req'=8,'tp'=4] {'tp'}, dimensions={0}, use_global_device_ids=true | all-gather | bytes 983040 | tf_op jit(solution)/shard_map/all_gather | solution.py:225
  51.1 0.6 gather_fusion.1
  51.9 0.1 reshape.331
  52.1 0.1 fusion.12
  52.2 0.7 pad.9
  52.9 1.0 %bitcast_select_fusion.x_ref = bf16[256,1536]{1,0:T(8,128)(2,1)} fusion(bf16[8,32,1536]{2,1,0:T(8,128)(2,1)S(1)} %gather_fusion.1, pred[256]{0:T(512)(128)(4,1)S(1)} %broadcast_in_dim.106), kind=kLoop, calls=%fused_computation.7 | loop fusion | flops 393216 | bytes 1573120 | tf_op jit(solution)/shard_map/jit(_take)/select_n | solution.py:230
  53.9 6.9 %shard_map.118 = bf16[32,24,384]{2,1,0:T(8,128)(2,1)} custom-call(bf16[256,1536]{1,0:T(8,128)(2,1)} %bitcast_select_fusion.x_ref, bf16[4,2,192,1536]{3,2,1,0:T(8,128)(2,1)} %bitcast.144, bf16[4,192,1536]{2,1,0:T(8,128)(2,1)} %dn_ref.1, f32[256,4]{1,0:T(8,128)} %bitcast.150), custom_call_target="tpu_custom_call" | custom-call | tf_op jit(solution)/shard_map/pallas_call | solution.py:75
  60.8 3.2 %all-to-all-start.1 = ((bf16[32,24,384]{2,1,0:T(8,128)(2,1)}), bf16[32,24,384]{2,1,0:T(8,128)(2,1)S(1)}, u32[]{:S(2)}, u32[]{:S(2)}) async-start(bf16[32,24,384]{2,1,0:T(8,128)(2,1)} %shard_map.118), calls=%async_computation.1 | async-start | bytes 1179648 | tf_op jit(solution)/shard_map/all_to_all | solution.py:263
  64.1 16.8 %all-to-all-done.1 = bf16[32,24,384]{2,1,0:T(8,128)(2,1)S(1)} async-done(((bf16[32,24,384]{2,1,0:T(8,128)(2,1)}), bf16[32,24,384]{2,1,0:T(8,128)(2,1)S(1)}, u32[]{:S(2)}, u32[]{:S(2)}) %all-to-all-start.1) | async-done | bytes 589856 | tf_op jit(solution)/shard_map/all_to_all | solution.py:263
  80.9 0.1 convert_reduce_fusion
  80.9 0.6 add_convert_fusion.1
  (65 shorter events, 1.8 us)
Async XLA Ops:
  0.0 23.9 %copy-start = (bf16[384,1536]{1,0:T(8,128)(2,1)S(1)}, bf16[384,1536]{1,0:T(8,128)(2,1)}, u32[]{:S(2)}) copy-start(bf16[384,1536]{1,0:T(8,128)(2,1)} %param.18) | copy-start | bytes 3538948
  0.0 9.4 %copy-start.6 = (s32[1,24]{1,0:T(1,128)S(1)}, s32[1,24]{1,0:T(1,128)}, u32[]{:S(2)}) copy-start(s32[1,24]{1,0:T(1,128)} %param.16) | copy-start | bytes 292
  0.0 9.6 %copy-start.1 = (bf16[768,2,2,128]{3,2,1,0:T(2,128)(2,1)S(1)}, bf16[768,2,2,128]{3,2,1,0:T(2,128)(2,1)}, u32[]{:S(2)}) copy-start(bf16[768,2,2,128]{3,2,1,0:T(2,128)(2,1)} %param.17) | copy-start | bytes 2359300
  11.2 6.5 %copy-start.2 = (bf16[24,2,256]{2,1,0:T(2,128)(2,1)S(1)}, bf16[24,2,256]{2,1,0:T(2,128)(2,1)}, u32[]{:S(2)}) copy-start(bf16[24,2,256]{2,1,0:T(2,128)(2,1)} %param.14) | copy-start | bytes 73732
  11.9 6.4 %copy-start.4 = (f32[24,4]{0,1:T(4,128)S(1)}, f32[24,4]{0,1:T(4,128)}, u32[]{:S(2)}) copy-start(f32[24,4]{0,1:T(4,128)} %param.21) | copy-start | bytes 1156
  11.9 6.4 %copy-start.5 = (s32[24,4]{0,1:T(4,128)S(1)}, s32[24,4]{0,1:T(4,128)}, u32[]{:S(2)}) copy-start(s32[24,4]{0,1:T(4,128)} %param.20) | copy-start | bytes 1156
  13.0 9.8 %all-to-all-start = ((f32[4,24,3,130]{3,1,2,0:T(8,128)}), f32[4,24,3,130]{3,1,2,0:T(8,128)S(1)}, u32[]{:S(2)}, u32[]{:S(2)}) async-start(f32[4,24,3,130]{3,1,2,0:T(8,128)} %maximum_bitcast_fusion), calls=%async_computation | async-start | bytes 589824 | tf_op jit(solution)/shard_map/all_to_all | solution.py:169
  24.1 7.2 %copy-start.3 = (f32[1536]{0:T(1024)S(1)}, f32[1536]{0:T(1024)}, u32[]{:S(2)}) copy-start(f32[1536]{0:T(1024)} %param.19) | copy-start | bytes 18436
  31.4 8.2 %collective-permute-start = (bf16[32,1536]{1,0:T(8,128)(2,1)S(1)}, bf16[32,1536]{1,0:T(8,128)(2,1)S(1)}, u32[]{:S(2)}, u32[]{:S(2)}) collective-permute-start(bf16[32,1536]{1,0:T(8,128)(2,1)S(1)} %pad_maximum_fusion.1), channel_id=1, source_target_pairs={{28,0},{21,1},{14,2},{7,3},{0,4},{25,5},{18,6},{11,7},{4,8},{29,9}... | collective-permute-start | bytes 294920 | tf_op jit(solution)/shard_map/ppermute | solution.py:222
  33.2 9.2 %collective-permute-start.1 = (bf16[32,1536]{1,0:T(8,128)(2,1)S(1)}, bf16[32,1536]{1,0:T(8,128)(2,1)S(1)}, u32[]{:S(2)}, u32[]{:S(2)}) collective-permute-start(bf16[32,1536]{1,0:T(8,128)(2,1)S(1)} %pad_maximum_fusion.1), channel_id=1, source_target_pairs={{24,0},{17,1},{10,2},{28,4},{21,5},{14,6},{0,8},{25,9},{18,10},{4,... | collective-permute-start | bytes 294920 | tf_op jit(solution)/shard_map/ppermute | solution.py:222
  60.8 20.0 %all-to-all-start.1 = ((bf16[32,24,384]{2,1,0:T(8,128)(2,1)}), bf16[32,24,384]{2,1,0:T(8,128)(2,1)S(1)}, u32[]{:S(2)}, u32[]{:S(2)}) async-start(bf16[32,24,384]{2,1,0:T(8,128)(2,1)} %shard_map.118), calls=%async_computation.1 | async-start | bytes 1179648 | tf_op jit(solution)/shard_map/all_to_all | solution.py:263

commit v8 on v7

--- a/solution.py
+++ b/solution.py
@@ -16,19 +16,29 @@
 neg_floor = -1e30
 
 
-def apply_rotary_heads(values, positions, head_size):
+def apply_rotary_flat(values, positions, head_size):
     half_size = head_size // 2
+    head_total = values.shape[1] // head_size
     exponents = jnp.arange(half_size, dtype=jnp.float32) * (2.0 / head_size)
     inverse_freq = jnp.power(jnp.float32(rope_base), -exponents)
     angles = positions.astype(jnp.float32)[:, None] * inverse_freq[None, :]
-    cosine = jnp.cos(angles)[:, None, :]
-    sine = jnp.sin(angles)[:, None, :]
-    first_half = values[..., :half_size]
-    second_half = values[..., half_size:]
-    return jnp.concatenate(
-        [first_half * cosine - second_half * sine, second_half * cosine + first_half * sine],
-        axis=-1,
-    )
+    cosine = jnp.cos(angles)
+    sine = jnp.sin(angles)
+    cosine_full = jnp.tile(jnp.concatenate([cosine, cosine], axis=1), (1, head_total))
+    sine_full = jnp.tile(jnp.concatenate([-sine, sine], axis=1), (1, head_total))
+    values = values.astype(jnp.float32)
+    swapped = jnp.concatenate(
+        [
+            piece
+            for head in range(head_total)
+            for piece in (
+                values[:, head * head_size + half_size : (head + 1) * head_size],
+                values[:, head * head_size : head * head_size + half_size],
+            )
+        ],
+        axis=1,
+    )
+    return values * cosine_full + swapped * sine_full
 
 
 def _expert_body(x_ref, gu_ref, dn_ref, w_ref, o_ref, acc_ref, *, group_rows, row_count, tp_count):
@@ -118,21 +128,16 @@
     first_head = tp_index * own_heads
     span_rows = cache.shape[0]
 
-    q_local = apply_rotary_heads(
-        queries.reshape(row_count, own_heads, head_size).astype(jnp.float32), positions, head_size
-    ).astype(jnp.bfloat16)
-    packed = jnp.stack([q_local.reshape(row_count, own_width), hidden_in], axis=0)
+    q_local = apply_rotary_flat(queries, positions, head_size).astype(jnp.bfloat16)
+    packed = jnp.stack([q_local, hidden_in], axis=0)
     gathered = lax.all_gather(packed, "tp", axis=0)
     q_all = jnp.transpose(gathered[:, 0], (1, 0, 2)).reshape(
         row_count, kv_count, request_group_size, head_size
     )
     hidden_full = jnp.transpose(gathered[:, 1], (1, 0, 2)).reshape(row_count, model_width)
 
-    k_new = apply_rotary_heads(
-        fresh_key_value[:, 0].reshape(row_count, kv_count, head_size).astype(jnp.float32),
-        positions,
-        head_size,
-    ).astype(jnp.bfloat16)
+    k_new = apply_rotary_flat(fresh_key_value[:, 0], positions, head_size).astype(jnp.bfloat16)
+    k_new = k_new.reshape(row_count, kv_count, head_size)
     value_fresh = fresh_key_value[:, 1].reshape(row_count, kv_count, head_size)
     own_score = (
         jnp.einsum("rcgd,rcd->rcg", q_all, k_new, preferred_element_type=jnp.float32)
@@ -216,17 +221,13 @@
             for group in range(req_count):
                 for part in range(tp_count):
                     shift = per_tp * part + slot + 1
-                    if shift < req_count:
-                        source = ((group - shift) % req_count) * tp_count + part
-                        pairs.append((source, group * tp_count + part))
+                    source = ((group - shift) % req_count) * tp_count + part
+                    pairs.append((source, group * tp_count + part))
             moved = lax.ppermute(value, ("req", "tp"), pairs)
-            shift_here = per_tp * tp_index + slot + 1
-            fetched.append(jnp.where(shift_here < req_count, moved, value))
+            fetched.append(lax.ppermute(value, ("req", "tp"), pairs))
         shared = lax.all_gather(jnp.stack(fetched, axis=0), "tp", axis=0)
-        shifts = (per_tp * jnp.arange(tp_count, dtype=jnp.int32)[:, None] + jnp.arange(per_tp, dtype=jnp.int32)[None, :] + 1) % req_count
         shared = shared.reshape((tp_count * per_tp,) + value.shape)
-        groups = ((req_index - shifts.reshape(-1)) % req_count).astype(jnp.int32)
-        order = jnp.argsort(groups)
+        order = (req_index - jnp.arange(req_count, dtype=jnp.int32) - 1) % req_count
         arrived = jnp.take(shared, order, axis=0)
         return arrived.reshape((req_count * value.shape[0],) + value.shape[1:])
 

time: 82 us -> 82.9 us (1.011)
  waiting for transfers between devices: 25.9 us -> 27 us
    slice x0 -> x3, local copies, waits for them, and re-layouts: none -> 1.16 us  [the longest x1 0.99 us: apply_rotary_flat(): values[:, head * head_size:head * head_size + half_size]]
    all_to_all x1, waiting for transfers between devices: 3.38 us -> 4.47 us  [per_device(): lax.all_to_all(jnp.transpose(states, (1, 0, 2, 3)), 'tp', 0, 0, tiled=True)]
    sort x1 -> x0, other arithmetic: 0.96 us -> none  [gather_req(): order = jnp.argsort(groups)]
  transfers between devices with their start and end apart: 4 -> 4, of which waited for: 4 -> 4; matrix products, arithmetic and copies ran while one was open for 3% -> 2% of each run, Pallas kernels for 0% -> 0%
where the time goes in v8:
time: 82.9 us; the launch traced here: 82.3 us
  waiting for transfers between devices  27 us (33%)
  blocking collectives  22.2 us (27%)
  starting transfers between devices  12 us (14%)
  Pallas kernels  6.88 us (8%)
  other arithmetic  6.82 us (8%)
  local copies, waits for them, and re-layouts  5.4 us (7%)
  matrix products  1.62 us (2%)
    all_to_all x1, waiting for transfers between devices, per_device(): mixed = lax.all_to_all(mixed, ('req', 'tp'), 0, 0, tiled=True)  16.8 us
    all_gather x1, blocking collectives, gather_req(): shared = lax.all_gather(jnp.stack(fetched, axis=0), 'tp', axis=0)  8.57 us
    all_gather x1, blocking collectives, per_device(): projected = jnp.sum(lax.all_gather(partial_proj, 'tp', axis=0), axis=0)  7 us
    pallas_call x1, Pallas kernels, expert_mix(): pl.pallas_call(body, grid=(group_total // tile_groups, local_count), in_s...  6.88 us
    all_gather x1, blocking collectives, per_device(): gathered = lax.all_gather(packed, 'tp', axis=0)  6.59 us
    ppermute x2, waiting for transfers between devices, gather_req(): fetched.append(lax.ppermute(value, ('req', 'tp'), pairs))  5.73 us
    ppermute x2, starting transfers between devices, gather_req(): fetched.append(lax.ppermute(value, ('req', 'tp'), pairs))  5.31 us
    all_to_all x1, waiting for transfers between devices, per_device(): lax.all_to_all(jnp.transpose(states, (1, 0, 2, 3)), 'tp', 0, 0, tiled=True)  4.47 us
  transfers between devices with their start and end apart: 4, of which 4 were waited for; matrix products, arithmetic and copies ran while one was open for 2% of the time, Pallas kernels for 0%

profile of v8, /device:TPU:0, one launch (start us, length us, event | category | flops | bytes accessed | tf_op | source)
XLA Modules:
  0.0 82.3 jit_solution(15305362819337922137)
XLA Ops:
  0.0 1.0 %fusion.42 = (f32[24,64]{1,0:T(8,128)S(1)}, f32[24,64]{1,0:T(8,128)S(1)}, f32[24,64]{1,0:T(8,128)S(1)}, f32[24,64]{1,0:T(8,128)S(1)}, f32[24,64]{1,0:T(8,128)S(1)}, /*index=5*/f32[24,64]{1,0:T(8,128)S(1)}) fusion(bf16[24,384]{1,0:T(8,128)(2,1)} %param.13), kind=kLoop, calls=%fused_computation.116 | loop fusion | bytes 73728 | tf_op jit(solution)/shard_map/slice | solution.py:36
  1.0 0.7 convert_element_type.98
  1.7 0.1 multiply_cosine_fusion
  2.0 0.7 fusion.20
  2.7 0.7 pad_maximum_fusion.2
  3.5 6.6 %all-gather = bf16[8,24,384]{2,1,0:T(8,128)(2,1)S(1)} all-gather(bf16[2,24,384]{2,1,0:T(8,128)(2,1)S(1)} %pad_maximum_fusion.2), channel_id=2, replica_groups=mesh['req'=8,'tp'=4] {'tp'}, dimensions={0}, use_global_device_ids=true | all-gather | bytes 184320 | tf_op jit(solution)/shard_map/all_gather | solution.py:133
  10.2 0.1 copy.71
  10.3 0.1 reduce.2
  10.5 0.5 fusion.40
  11.1 0.5 fusion.43
  11.6 0.1 concatenate.39
  11.7 0.3 fusion.3
  12.0 0.7 fusion.2
  12.8 0.1 concatenate.40
  12.9 0.9 %maximum_bitcast_fusion = f32[4,24,3,130]{3,1,2,0:T(8,128)} fusion(f32[24,4,3,128]{3,0,2,1:T(8,128)S(1)} %bitcast.178, f32[24,4,3,1]{3,0,2,1:T(8,128)S(1)} %concatenate.40, f32[24,4,3,1]{3,0,2,1:T(8,128)S(1)} %concatenate.39), kind=kLoop, calls=%fused_computation.15 | loop fusion | flops 74880 | bytes 299520 | tf_op jit(solution)/shard_map/transpose | solution.py:175
  13.8 3.5 %all-to-all-start = ((f32[4,24,3,130]{3,1,2,0:T(8,128)}), f32[4,24,3,130]{3,1,2,0:T(8,128)S(1)}, u32[]{:S(2)}, u32[]{:S(2)}) async-start(f32[4,24,3,130]{3,1,2,0:T(8,128)} %maximum_bitcast_fusion), calls=%async_computation | async-start | bytes 589824 | tf_op jit(solution)/shard_map/all_to_all | solution.py:174
  17.4 0.1 slice_reduce_fusion
  17.7 0.2 fusion.18
  17.9 0.1 copy.95
  18.1 0.1 select_reduce_fusion
  18.3 0.1 reshape.322
  18.5 0.1 broadcast_in_dim.98
  18.6 0.6 gather_fusion
  19.2 4.5 %all-to-all-done = f32[4,24,3,130]{3,1,2,0:T(8,128)S(1)} async-done(((f32[4,24,3,130]{3,1,2,0:T(8,128)}), f32[4,24,3,130]{3,1,2,0:T(8,128)S(1)}, u32[]{:S(2)}, u32[]{:S(2)}) %all-to-all-start) | async-done | bytes 149792 | tf_op jit(solution)/shard_map/all_to_all | solution.py:174
  23.7 0.1 slice_reduce_fusion.1
  23.8 0.1 copy.100
  24.0 0.1 copy.86
  24.2 0.1 copy.85
  24.3 0.1 fusion.11
  24.7 0.3 fusion.21
  25.0 7.0 %all-gather.1 = f32[96,1536]{1,0:T(8,128)S(1)} all-gather(f32[24,1536]{1,0:T(8,128)S(1)} %fusion.21), channel_id=3, replica_groups=mesh['req'=8,'tp'=4] {'tp'}, dimensions={0}, use_global_device_ids=true | all-gather | bytes 737280 | tf_op jit(solution)/shard_map/all_gather | solution.py:193
  32.0 0.1 fusion.10
  32.2 1.8 %collective-permute-start = (bf16[32,1536]{1,0:T(8,128)(2,1)S(1)}, bf16[32,1536]{1,0:T(8,128)(2,1)S(1)}, u32[]{:S(2)}, u32[]{:S(2)}) collective-permute-start(bf16[32,1536]{1,0:T(8,128)(2,1)S(1)} %pad_maximum_fusion.1), channel_id=1, source_target_pairs={{28,0},{21,1},{14,2},{7,3},{0,4},{25,5},{18,6},{11,7},{4,8},{29,9}... | collective-permute-start | bytes 294920 | tf_op jit(solution)/shard_map/ppermute | solution.py:227
  34.1 3.5 %collective-permute-start.1 = (bf16[32,1536]{1,0:T(8,128)(2,1)S(1)}, bf16[32,1536]{1,0:T(8,128)(2,1)S(1)}, u32[]{:S(2)}, u32[]{:S(2)}) collective-permute-start(bf16[32,1536]{1,0:T(8,128)(2,1)S(1)} %pad_maximum_fusion.1), channel_id=1, source_target_pairs={{24,0},{17,1},{10,2},{3,3},{28,4},{21,5},{14,6},{7,7},{0,8},{25,9}... | collective-permute-start | bytes 294920 | tf_op jit(solution)/shard_map/ppermute | solution.py:227
  37.6 2.9 %collective-permute-done = bf16[32,1536]{1,0:T(8,128)(2,1)S(1)} collective-permute-done((bf16[32,1536]{1,0:T(8,128)(2,1)S(1)}, bf16[32,1536]{1,0:T(8,128)(2,1)S(1)}, u32[]{:S(2)}, u32[]{:S(2)}) %collective-permute-start) | collective-permute-done | bytes 98336 | tf_op jit(solution)/shard_map/ppermute | solution.py:227
  40.5 2.8 %collective-permute-done.1 = bf16[32,1536]{1,0:T(8,128)(2,1)S(1)} collective-permute-done((bf16[32,1536]{1,0:T(8,128)(2,1)S(1)}, bf16[32,1536]{1,0:T(8,128)(2,1)S(1)}, u32[]{:S(2)}, u32[]{:S(2)}) %collective-permute-start.1) | collective-permute-done | bytes 98336 | tf_op jit(solution)/shard_map/ppermute | solution.py:227
  43.3 8.6 %all-gather.2 = bf16[8,32,1536]{2,1,0:T(8,128)(2,1)S(1)} all-gather(bf16[2,32,1536]{2,1,0:T(8,128)(2,1)S(1)} %pad_maximum_fusion), channel_id=4, replica_groups=mesh['req'=8,'tp'=4] {'tp'}, dimensions={0}, use_global_device_ids=true | all-gather | bytes 983040 | tf_op jit(solution)/shard_map/all_gather | solution.py:228
  51.9 0.6 gather_fusion.1
  52.5 0.1 fusion.7
  52.7 0.1 reshape.333
  52.8 0.1 fusion.12
  53.0 0.7 pad.9
  53.7 1.0 %bitcast_select_fusion.x_ref = bf16[256,1536]{1,0:T(8,128)(2,1)} fusion(bf16[8,32,1536]{2,1,0:T(8,128)(2,1)S(1)} %gather_fusion.1, pred[256]{0:T(512)(128)(4,1)S(1)} %broadcast_in_dim.98), kind=kLoop, calls=%fused_computation.7 | loop fusion | flops 393216 | bytes 1573120 | tf_op jit(solution)/shard_map/jit(_take)/select_n | solution.py:231
  54.7 6.9 %shard_map.118 = bf16[32,24,384]{2,1,0:T(8,128)(2,1)} custom-call(bf16[256,1536]{1,0:T(8,128)(2,1)} %bitcast_select_fusion.x_ref, bf16[4,2,192,1536]{3,2,1,0:T(8,128)(2,1)} %bitcast.165, bf16[4,192,1536]{2,1,0:T(8,128)(2,1)} %dn_ref.1, f32[256,4]{1,0:T(8,128)} %bitcast.171), custom_call_target="tpu_custom_call" | custom-call | tf_op jit(solution)/shard_map/pallas_call | solution.py:85
  61.6 3.2 %all-to-all-start.1 = ((bf16[32,24,384]{2,1,0:T(8,128)(2,1)}), bf16[32,24,384]{2,1,0:T(8,128)(2,1)S(1)}, u32[]{:S(2)}, u32[]{:S(2)}) async-start(bf16[32,24,384]{2,1,0:T(8,128)(2,1)} %shard_map.118), calls=%async_computation.1 | async-start | bytes 1179648 | tf_op jit(solution)/shard_map/all_to_all | solution.py:264
  64.8 16.8 %all-to-all-done.1 = bf16[32,24,384]{2,1,0:T(8,128)(2,1)S(1)} async-done(((bf16[32,24,384]{2,1,0:T(8,128)(2,1)}), bf16[32,24,384]{2,1,0:T(8,128)(2,1)S(1)}, u32[]{:S(2)}, u32[]{:S(2)}) %all-to-all-start.1) | async-done | bytes 589856 | tf_op jit(solution)/shard_map/all_to_all | solution.py:264
  81.6 0.1 convert_reduce_fusion
  81.7 0.6 add_convert_fusion
  (64 shorter events, 1.6 us)
Async XLA Ops:
  0.0 24.7 %copy-start = (bf16[384,1536]{1,0:T(8,128)(2,1)S(1)}, bf16[384,1536]{1,0:T(8,128)(2,1)}, u32[]{:S(2)}) copy-start(bf16[384,1536]{1,0:T(8,128)(2,1)} %param.18) | copy-start | bytes 3538948
  0.0 10.2 %copy-start.6 = (s32[1,24]{1,0:T(1,128)S(1)}, s32[1,24]{1,0:T(1,128)}, u32[]{:S(2)}) copy-start(s32[1,24]{1,0:T(1,128)} %param.16) | copy-start | bytes 292
  0.0 10.5 %copy-start.1 = (bf16[768,2,2,128]{3,2,1,0:T(2,128)(2,1)S(1)}, bf16[768,2,2,128]{3,2,1,0:T(2,128)(2,1)}, u32[]{:S(2)}) copy-start(bf16[768,2,2,128]{3,2,1,0:T(2,128)(2,1)} %param.17) | copy-start | bytes 2359300
  12.0 5.3 %copy-start.2 = (bf16[24,2,256]{2,1,0:T(2,128)(2,1)S(1)}, bf16[24,2,256]{2,1,0:T(2,128)(2,1)}, u32[]{:S(2)}) copy-start(bf16[24,2,256]{2,1,0:T(2,128)(2,1)} %param.14) | copy-start | bytes 73732
  12.9 5.2 %copy-start.4 = (f32[24,4]{0,1:T(4,128)S(1)}, f32[24,4]{0,1:T(4,128)}, u32[]{:S(2)}) copy-start(f32[24,4]{0,1:T(4,128)} %param.21) | copy-start | bytes 1156
  12.9 5.2 %copy-start.5 = (s32[24,4]{0,1:T(4,128)S(1)}, s32[24,4]{0,1:T(4,128)}, u32[]{:S(2)}) copy-start(s32[24,4]{0,1:T(4,128)} %param.20) | copy-start | bytes 1156
  13.8 9.8 %all-to-all-start = ((f32[4,24,3,130]{3,1,2,0:T(8,128)}), f32[4,24,3,130]{3,1,2,0:T(8,128)S(1)}, u32[]{:S(2)}, u32[]{:S(2)}) async-start(f32[4,24,3,130]{3,1,2,0:T(8,128)} %maximum_bitcast_fusion), calls=%async_computation | async-start | bytes 589824 | tf_op jit(solution)/shard_map/all_to_all | solution.py:174
  24.9 7.2 %copy-start.3 = (f32[1536]{0:T(1024)S(1)}, f32[1536]{0:T(1024)}, u32[]{:S(2)}) copy-start(f32[1536]{0:T(1024)} %param.19) | copy-start | bytes 18436
  32.2 8.2 %collective-permute-start = (bf16[32,1536]{1,0:T(8,128)(2,1)S(1)}, bf16[32,1536]{1,0:T(8,128)(2,1)S(1)}, u32[]{:S(2)}, u32[]{:S(2)}) collective-permute-start(bf16[32,1536]{1,0:T(8,128)(2,1)S(1)} %pad_maximum_fusion.1), channel_id=1, source_target_pairs={{28,0},{21,1},{14,2},{7,3},{0,4},{25,5},{18,6},{11,7},{4,8},{29,9}... | collective-permute-start | bytes 294920 | tf_op jit(solution)/shard_map/ppermute | solution.py:227
  34.1 9.2 %collective-permute-start.1 = (bf16[32,1536]{1,0:T(8,128)(2,1)S(1)}, bf16[32,1536]{1,0:T(8,128)(2,1)S(1)}, u32[]{:S(2)}, u32[]{:S(2)}) collective-permute-start(bf16[32,1536]{1,0:T(8,128)(2,1)S(1)} %pad_maximum_fusion.1), channel_id=1, source_target_pairs={{24,0},{17,1},{10,2},{3,3},{28,4},{21,5},{14,6},{7,7},{0,8},{25,9}... | collective-permute-start | bytes 294920 | tf_op jit(solution)/shard_map/ppermute | solution.py:227
  61.6 20.0 %all-to-all-start.1 = ((bf16[32,24,384]{2,1,0:T(8,128)(2,1)}), bf16[32,24,384]{2,1,0:T(8,128)(2,1)S(1)}, u32[]{:S(2)}, u32[]{:S(2)}) async-start(bf16[32,24,384]{2,1,0:T(8,128)(2,1)} %shard_map.118), calls=%async_computation.1 | async-start | bytes 1179648 | tf_op jit(solution)/shard_map/all_to_all | solution.py:264

commit v9 on v7

--- a/solution.py
+++ b/solution.py
@@ -31,61 +31,66 @@
     )
 
 
-def _expert_body(x_ref, gu_ref, dn_ref, w_ref, o_ref, acc_ref, *, group_rows, row_count, tp_count):
+def _expert_body(
+    offset_ref, x_ref, gu_ref, dn_ref, o_ref, acc_ref, *, width, block_total, row_count, tp_count
+):
     block = pl.program_id(1)
 
     @pl.when(block == 0)
     def _():
         acc_ref[...] = jnp.zeros_like(acc_ref)
 
-    x = x_ref[...]
+    x = x_ref[:, :width]
     contract_rows = (((1,), (1,)), ((), ()))
     gate_part = lax.dot_general(x, gu_ref[0, 0], contract_rows, preferred_element_type=jnp.float32)
     up_part = lax.dot_general(x, gu_ref[0, 1], contract_rows, preferred_element_type=jnp.float32)
     activation = (jnp.maximum(gate_part, 0.0) * up_part).astype(jnp.bfloat16)
     produced = jnp.dot(activation, dn_ref[0], preferred_element_type=jnp.float32)
     produced = produced.astype(jnp.bfloat16).astype(jnp.float32)
-    weights = w_ref[...]
-    lanes = lax.broadcasted_iota(jnp.int32, weights.shape, 1)
-    chosen = jnp.sum(jnp.where(lanes == block, weights, 0.0), axis=1, keepdims=True)
+    code = x_ref[:, width:].astype(jnp.float32)
+    lanes = lax.broadcasted_iota(jnp.int32, code.shape, 1)
+    column = offset_ref[0] + block
+    chosen = jnp.sum(jnp.where(lanes == column, code, 0.0), axis=1, keepdims=True)
+    chosen = chosen + jnp.sum(jnp.where(lanes == column + block_total, code, 0.0), axis=1, keepdims=True)
+    chosen = chosen + jnp.sum(jnp.where(lanes == column + 2 * block_total, code, 0.0), axis=1, keepdims=True)
     acc_ref[...] += chosen * produced
 
     @pl.when(block == pl.num_programs(1) - 1)
     def _():
         own_width = o_ref.shape[2]
-        for group in range(x_ref.shape[0] // group_rows):
+        for group in range(x_ref.shape[0] // row_count):
             for part in range(tp_count):
                 o_ref[group * tp_count + part] = acc_ref[
-                    group * group_rows : group * group_rows + row_count,
+                    group * row_count : (group + 1) * row_count,
                     part * own_width : (part + 1) * own_width,
                 ].astype(o_ref.dtype)
 
 
-def expert_mix(rows, gate_up, down, weights, group_rows, row_count, tp_count):
-    row_total, width = rows.shape
+def expert_mix(rows, gate_up, down, offset, width, block_total, row_count, tp_count):
+    row_total, message_width = rows.shape
     local_count, _, _, hidden = gate_up.shape
-    group_total = row_total // group_rows
+    group_total = row_total // row_count
     tile_groups = math.gcd(group_total, 8)
-    tile = tile_groups * group_rows
+    tile = tile_groups * row_count
     own_width = width // tp_count
     gate_up_t = jnp.swapaxes(gate_up, 2, 3)
     body = functools.partial(
-        _expert_body, group_rows=group_rows, row_count=row_count, tp_count=tp_count
+        _expert_body, width=width, block_total=block_total, row_count=row_count, tp_count=tp_count
     )
     return pl.pallas_call(
         body,
         grid=(group_total // tile_groups, local_count),
         in_specs=[
-            pl.BlockSpec((tile, width), lambda i, b: (i, 0)),
+            pl.BlockSpec(memory_space=pltpu.SMEM),
+            pl.BlockSpec((tile, message_width), lambda i, b: (i, 0)),
             pl.BlockSpec((1, 2, hidden, width), lambda i, b: (b, 0, 0, 0)),
             pl.BlockSpec((1, hidden, width), lambda i, b: (b, 0, 0)),
-            pl.BlockSpec((tile, local_count), lambda i, b: (i, 0)),
         ],
         out_specs=pl.BlockSpec((tile_groups * tp_count, row_count, own_width), lambda i, b: (i, 0, 0)),
         out_shape=jax.ShapeDtypeStruct((group_total * tp_count, row_count, own_width), jnp.bfloat16),
         scratch_shapes=[pltpu.VMEM((tile, width), jnp.float32)],
         compiler_params=pltpu.CompilerParams(dimension_semantics=("parallel", "arbitrary")),
-    )(rows, gate_up_t, down, weights)
+    )(offset, rows, gate_up_t, down)
 
 
 def per_device(
@@ -176,8 +181,12 @@
     top_score = jnp.maximum(jnp.max(parts_highest, axis=0), own_slice)
     factors = jnp.exp(parts_highest - top_score[None])
     own_part = jnp.exp(own_slice - top_score)
-    head_kv = (first_head + jnp.arange(own_heads, dtype=jnp.int32)) // request_group_size
-    own_values = jnp.take(value_fresh, head_kv, axis=1).astype(jnp.float32)
+    if request_group_size % own_heads == 0:
+        own_values = lax.dynamic_slice_in_dim(value_fresh, first_head // request_group_size, 1, 1)
+        own_values = own_values.astype(jnp.float32)
+    else:
+        head_kv = (first_head + jnp.arange(own_heads, dtype=jnp.int32)) // request_group_size
+        own_values = jnp.take(value_fresh, head_kv, axis=1).astype(jnp.float32)
     totals = jnp.sum(parts_totals * factors, axis=0) + own_part
     summed = jnp.sum(parts_sums * factors[..., None], axis=0) + own_values * own_part[..., None]
     attention_output = (summed / totals[..., None]).astype(jnp.bfloat16).reshape(
@@ -216,17 +225,13 @@
             for group in range(req_count):
                 for part in range(tp_count):
                     shift = per_tp * part + slot + 1
-                    if shift < req_count:
-                        source = ((group - shift) % req_count) * tp_count + part
-                        pairs.append((source, group * tp_count + part))
+                    source = ((group - shift) % req_count) * tp_count + part
+                    pairs.append((source, group * tp_count + part))
             moved = lax.ppermute(value, ("req", "tp"), pairs)
-            shift_here = per_tp * tp_index + slot + 1
-            fetched.append(jnp.where(shift_here < req_count, moved, value))
+            fetched.append(lax.ppermute(value, ("req", "tp"), pairs))
         shared = lax.all_gather(jnp.stack(fetched, axis=0), "tp", axis=0)
-        shifts = (per_tp * jnp.arange(tp_count, dtype=jnp.int32)[:, None] + jnp.arange(per_tp, dtype=jnp.int32)[None, :] + 1) % req_count
         shared = shared.reshape((tp_count * per_tp,) + value.shape)
-        groups = ((req_index - shifts.reshape(-1)) % req_count).astype(jnp.int32)
-        order = jnp.argsort(groups)
+        order = (req_index - jnp.arange(req_count, dtype=jnp.int32) - 1) % req_count
         arrived = jnp.take(shared, order, axis=0)
         return arrived.reshape((req_count * value.shape[0],) + value.shape[1:])
 
@@ -234,31 +239,14 @@
     weight_rest = block_weights - weight_high
     weight_mid = lax.reduce_precision(weight_rest, exponent_bits=8, mantissa_bits=7)
     weight_low = weight_rest - weight_mid
-    code = jnp.stack(
-        [weight_high.astype(jnp.bfloat16), weight_mid.astype(jnp.bfloat16), weight_low.astype(jnp.bfloat16)],
-        axis=0,
-    ).reshape(-1)
-    group_rows = -(-(row_count + -(-code.shape[0] // model_width)) // 16) * 16
-    code_rows = group_rows - row_count
-    code = jnp.pad(code, (0, code_rows * model_width - code.shape[0])).reshape(code_rows, model_width)
-    message = jnp.concatenate([normed, code], axis=0)
-    message_all = gather_req(message).reshape(req_count, group_rows, model_width)
-    pieces = message_all[:, row_count:].reshape(req_count, code_rows * model_width)
-    pieces = pieces[:, : 3 * row_count * block_total].astype(jnp.float32)
-    pieces = pieces.reshape(req_count, 3, row_count, block_total)
-    weights_all = (pieces[:, 0] + pieces[:, 1]) + pieces[:, 2]
-    weights_own = lax.dynamic_slice_in_dim(weights_all, req_index * local_count, local_count, 2)
-    weights_own = jnp.pad(weights_own, ((0, 0), (0, code_rows), (0, 0)))
-    weights_own = weights_own.reshape(req_count * group_rows, local_count)
-
+    code = jnp.concatenate([weight_high, weight_mid, weight_low], axis=1).astype(jnp.bfloat16)
+    code_lanes = -(-code.shape[1] // 128) * 128
+    code = jnp.pad(code, ((0, 0), (0, code_lanes - code.shape[1])))
+    message = jnp.concatenate([normed, code], axis=1)
+    message_all = gather_req(message)
+    offset = (req_index * local_count).astype(jnp.int32).reshape(1)
     mixed = expert_mix(
-        message_all.reshape(req_count * group_rows, model_width),
-        gate_up,
-        down,
-        weights_own,
-        group_rows,
-        row_count,
-        tp_count,
+        message_all, gate_up, down, offset, model_width, block_total, row_count, tp_count
     )
     mixed = lax.all_to_all(mixed, ("req", "tp"), 0, 0, tiled=True)
     mixed = jnp.sum(mixed.astype(jnp.float32), axis=0)

time: 82 us -> 78.4 us (0.956)
  local copies, waits for them, and re-layouts: 4.95 us -> 2.92 us
  blocking collectives: 22.2 us -> 20.7 us
  waiting for transfers between devices: 25.9 us -> 27.4 us
  other arithmetic: 7.57 us -> 6.22 us
    all_to_all x1, waiting for transfers between devices: 3.38 us -> 5.28 us  [per_device(): lax.all_to_all(jnp.transpose(states, (1, 0, 2, 3)), 'tp', 0, 0, tiled=True)]
    all_gather x1, blocking collectives: 8.57 us -> 7.07 us  [gather_req(): shared = lax.all_gather(jnp.stack(fetched, axis=0), 'tp', axis=0)]
    sort x1 -> x0, other arithmetic: 0.96 us -> none  [gather_req(): order = jnp.argsort(groups)]
  transfers between devices with their start and end apart: 4 -> 4, of which waited for: 4 -> 4; matrix products, arithmetic and copies ran while one was open for 3% -> 1% of each run, Pallas kernels for 0% -> 0%
where the time goes in v9:
time: 78.4 us; the launch traced here: 77.9 us
  waiting for transfers between devices  27.4 us (35%)
  blocking collectives  20.7 us (26%)
  starting transfers between devices  12.3 us (16%)
  Pallas kernels  6.38 us (8%)
  other arithmetic  6.22 us (8%)
  local copies, waits for them, and re-layouts  2.92 us (4%)
  matrix products  1.67 us (2%)
    all_to_all x1, waiting for transfers between devices, per_device(): mixed = lax.all_to_all(mixed, ('req', 'tp'), 0, 0, tiled=True)  16.8 us
    all_gather x1, blocking collectives, gather_req(): shared = lax.all_gather(jnp.stack(fetched, axis=0), 'tp', axis=0)  7.07 us
    all_gather x1, blocking collectives, per_device(): projected = jnp.sum(lax.all_gather(partial_proj, 'tp', axis=0), axis=0)  6.99 us
    all_gather x1, blocking collectives, per_device(): gathered = lax.all_gather(packed, 'tp', axis=0)  6.59 us
    pallas_call x1, Pallas kernels, expert_mix(): pl.pallas_call(body, grid=(group_total // tile_groups, local_count), in_s...  6.38 us
    ppermute x2, starting transfers between devices, gather_req(): fetched.append(lax.ppermute(value, ('req', 'tp'), pairs))  5.31 us
    ppermute x2, waiting for transfers between devices, gather_req(): fetched.append(lax.ppermute(value, ('req', 'tp'), pairs))  5.3 us
    all_to_all x1, waiting for transfers between devices, per_device(): lax.all_to_all(jnp.transpose(states, (1, 0, 2, 3)), 'tp', 0, 0, tiled=True)  5.28 us
  transfers between devices with their start and end apart: 4, of which 4 were waited for; matrix products, arithmetic and copies ran while one was open for 1% of the time, Pallas kernels for 0%

profile of v9, /device:TPU:0, one launch (start us, length us, event | category | flops | bytes accessed | tf_op | source)
XLA Modules:
  0.0 77.9 jit_solution(14738285193945330809)
XLA Ops:
  0.0 0.8 %convert_element_type.69 = f32[24]{0:T(128)S(1)} convert(s32[24]{0:T(128)} %param.15) | non-fusion elementwise | flops 24 | bytes 192 | tf_op jit(solution)/shard_map/convert_element_type | solution.py:23
  0.8 0.7 reshape.271
  1.6 0.1 multiply_cosine_fusion
  1.7 0.1 subtract_convert_fusion
  1.8 0.1 pad_maximum_fusion.3
  1.9 0.7 pad_maximum_fusion.2
  2.7 6.6 %all-gather = bf16[8,24,384]{2,1,0:T(8,128)(2,1)S(1)} all-gather(bf16[2,24,384]{2,1,0:T(8,128)(2,1)S(1)} %pad_maximum_fusion.2), channel_id=2, replica_groups=mesh['req'=8,'tp'=4] {'tp'}, dimensions={0}, use_global_device_ids=true | all-gather | bytes 184320 | tf_op jit(solution)/shard_map/all_gather | solution.py:130
  9.4 0.1 copy.70
  9.5 0.1 reduce.2
  9.7 0.5 fusion.32
  10.2 0.1 compare_and_fusion
  10.3 0.5 fusion.33
  10.8 0.1 concatenate.33
  10.9 0.3 fusion.3
  11.2 0.7 fusion.2
  12.0 0.1 concatenate.34
  12.1 0.9 %maximum_bitcast_fusion = f32[4,24,3,130]{3,1,2,0:T(8,128)} fusion(f32[24,4,3,128]{3,0,2,1:T(8,128)S(1)} %bitcast.102, f32[24,4,3,1]{3,0,2,1:T(8,128)S(1)} %concatenate.34, f32[24,4,3,1]{3,0,2,1:T(8,128)S(1)} %concatenate.33), kind=kLoop, calls=%fused_computation.14 | loop fusion | flops 74880 | bytes 299520 | tf_op jit(solution)/shard_map/transpose | solution.py:175
  13.0 3.5 %all-to-all-start = ((f32[4,24,3,130]{3,1,2,0:T(8,128)}), f32[4,24,3,130]{3,1,2,0:T(8,128)S(1)}, u32[]{:S(2)}, u32[]{:S(2)}) async-start(f32[4,24,3,130]{3,1,2,0:T(8,128)} %maximum_bitcast_fusion), calls=%async_computation | async-start | bytes 589824 | tf_op jit(solution)/shard_map/all_to_all | solution.py:174
  16.5 0.1 slice_reduce_fusion
  16.6 0.1 subtract_convert_fusion.1
  16.7 0.1 maximum_bitcast_fusion.1
  16.8 0.2 fusion.12
  17.0 0.1 copy.87
  17.2 0.1 select_reduce_fusion
  17.3 0.1 broadcast_in_dim.79
  17.4 0.1 broadcast_in_dim.80
  17.4 0.1 fusion.23
  17.6 5.3 %all-to-all-done = f32[4,24,3,130]{3,1,2,0:T(8,128)S(1)} async-done(((f32[4,24,3,130]{3,1,2,0:T(8,128)}), f32[4,24,3,130]{3,1,2,0:T(8,128)S(1)}, u32[]{:S(2)}, u32[]{:S(2)}) %all-to-all-start) | async-done | bytes 149792 | tf_op jit(solution)/shard_map/all_to_all | solution.py:174
  22.8 0.1 slice_reduce_fusion.1
  23.0 0.1 copy.92
  23.2 0.1 copy.81
  23.4 0.1 fusion.10
  23.5 0.3 fusion.14
  23.8 7.0 %all-gather.1 = f32[96,1536]{1,0:T(8,128)S(1)} all-gather(f32[24,1536]{1,0:T(8,128)S(1)} %fusion.14), channel_id=3, replica_groups=mesh['req'=8,'tp'=4] {'tp'}, dimensions={0}, use_global_device_ids=true | all-gather | bytes 737280 | tf_op jit(solution)/shard_map/all_gather | solution.py:197
  30.9 0.1 fusion.9
  31.0 0.1 multiply_convert_fusion
  31.1 1.8 %collective-permute-start = (bf16[24,1664]{1,0:T(8,128)(2,1)S(1)}, bf16[24,1664]{1,0:T(8,128)(2,1)S(1)}, u32[]{:S(2)}, u32[]{:S(2)}) collective-permute-start(bf16[24,1664]{1,0:T(8,128)(2,1)S(1)} %pad_maximum_fusion.1), channel_id=1, source_target_pairs={{28,0},{21,1},{14,2},{7,3},{0,4},{25,5},{18,6},{11,7},{4,8},{29,9}... | collective-permute-start | bytes 239624 | tf_op jit(solution)/shard_map/ppermute | solution.py:231
  32.9 3.5 %collective-permute-start.1 = (bf16[24,1664]{1,0:T(8,128)(2,1)S(1)}, bf16[24,1664]{1,0:T(8,128)(2,1)S(1)}, u32[]{:S(2)}, u32[]{:S(2)}) collective-permute-start(bf16[24,1664]{1,0:T(8,128)(2,1)S(1)} %pad_maximum_fusion.1), channel_id=1, source_target_pairs={{24,0},{17,1},{10,2},{3,3},{28,4},{21,5},{14,6},{7,7},{0,8},{25,9}... | collective-permute-start | bytes 239624 | tf_op jit(solution)/shard_map/ppermute | solution.py:231
  36.4 2.5 %collective-permute-done = bf16[24,1664]{1,0:T(8,128)(2,1)S(1)} collective-permute-done((bf16[24,1664]{1,0:T(8,128)(2,1)S(1)}, bf16[24,1664]{1,0:T(8,128)(2,1)S(1)}, u32[]{:S(2)}, u32[]{:S(2)}) %collective-permute-start) | collective-permute-done | bytes 79904 | tf_op jit(solution)/shard_map/ppermute | solution.py:231
  38.9 2.8 %collective-permute-done.1 = bf16[24,1664]{1,0:T(8,128)(2,1)S(1)} collective-permute-done((bf16[24,1664]{1,0:T(8,128)(2,1)S(1)}, bf16[24,1664]{1,0:T(8,128)(2,1)S(1)}, u32[]{:S(2)}, u32[]{:S(2)}) %collective-permute-start.1) | collective-permute-done | bytes 79904 | tf_op jit(solution)/shard_map/ppermute | solution.py:231
  41.8 7.1 %all-gather.2 = bf16[8,24,1664]{2,1,0:T(8,128)(2,1)S(1)} all-gather(bf16[2,24,1664]{2,1,0:T(8,128)(2,1)S(1)} %pad_maximum_fusion), channel_id=4, replica_groups=mesh['req'=8,'tp'=4] {'tp'}, dimensions={0}, use_global_device_ids=true | all-gather | bytes 798720 | tf_op jit(solution)/shard_map/all_gather | solution.py:232
  48.8 0.6 gather_fusion
  49.5 1.0 %bitcast_select_fusion.x_ref = bf16[192,1664]{1,0:T(8,128)(2,1)} fusion(bf16[8,24,1664]{2,1,0:T(8,128)(2,1)S(1)} %gather_fusion, pred[192]{0:T(512)(128)(4,1)S(1)} %broadcast_in_dim.80), kind=kLoop, calls=%fused_computation.8 | loop fusion | flops 319488 | bytes 1278144 | tf_op jit(solution)/shard_map/jit(_take)/select_n | solution.py:235
  50.5 6.4 %shard_map.118 = bf16[32,24,384]{2,1,0:T(8,128)(2,1)} custom-call(s32[1]{0:T(128)} %bitcast.26.offset_ref, bf16[192,1664]{1,0:T(8,128)(2,1)} %bitcast_select_fusion.x_ref, bf16[4,2,192,1536]{3,2,1,0:T(8,128)(2,1)} %bitcast.94, bf16[4,192,1536]{2,1,0:T(8,128)(2,1)} %dn_ref.1), custom_call_target="tpu_custom_call" | custom-call | tf_op jit(solution)/shard_map/pallas_call | solution.py:80
  56.8 3.6 %all-to-all-start.1 = ((bf16[32,24,384]{2,1,0:T(8,128)(2,1)}), bf16[32,24,384]{2,1,0:T(8,128)(2,1)S(1)}, u32[]{:S(2)}, u32[]{:S(2)}) async-start(bf16[32,24,384]{2,1,0:T(8,128)(2,1)} %shard_map.118), calls=%async_computation.1 | async-start | bytes 1179648 | tf_op jit(solution)/shard_map/all_to_all | solution.py:251
  60.4 16.8 %all-to-all-done.1 = bf16[32,24,384]{2,1,0:T(8,128)(2,1)S(1)} async-done(((bf16[32,24,384]{2,1,0:T(8,128)(2,1)}), bf16[32,24,384]{2,1,0:T(8,128)(2,1)S(1)}, u32[]{:S(2)}, u32[]{:S(2)}) %all-to-all-start.1) | async-done | bytes 589856 | tf_op jit(solution)/shard_map/all_to_all | solution.py:251
  77.2 0.1 convert_reduce_fusion
  77.3 0.6 add_convert_fusion.1
  (40 shorter events, 0.5 us)
Async XLA Ops:
  0.0 23.5 %copy-start = (bf16[384,1536]{1,0:T(8,128)(2,1)S(1)}, bf16[384,1536]{1,0:T(8,128)(2,1)}, u32[]{:S(2)}) copy-start(bf16[384,1536]{1,0:T(8,128)(2,1)} %param.18) | copy-start | bytes 3538948
  0.0 9.4 %copy-start.6 = (s32[1,24]{1,0:T(1,128)S(1)}, s32[1,24]{1,0:T(1,128)}, u32[]{:S(2)}) copy-start(s32[1,24]{1,0:T(1,128)} %param.16) | copy-start | bytes 292
  0.0 9.6 %copy-start.1 = (bf16[768,2,2,128]{3,2,1,0:T(2,128)(2,1)S(1)}, bf16[768,2,2,128]{3,2,1,0:T(2,128)(2,1)}, u32[]{:S(2)}) copy-start(bf16[768,2,2,128]{3,2,1,0:T(2,128)(2,1)} %param.17) | copy-start | bytes 2359300
  11.2 5.3 %copy-start.2 = (bf16[24,2,256]{2,1,0:T(2,128)(2,1)S(1)}, bf16[24,2,256]{2,1,0:T(2,128)(2,1)}, u32[]{:S(2)}) copy-start(bf16[24,2,256]{2,1,0:T(2,128)(2,1)} %param.14) | copy-start | bytes 73732
  11.9 5.2 %copy-start.4 = (f32[24,4]{0,1:T(4,128)S(1)}, f32[24,4]{0,1:T(4,128)}, u32[]{:S(2)}) copy-start(f32[24,4]{0,1:T(4,128)} %param.21) | copy-start | bytes 1156
  11.9 5.2 %copy-start.5 = (s32[24,4]{0,1:T(4,128)S(1)}, s32[24,4]{0,1:T(4,128)}, u32[]{:S(2)}) copy-start(s32[24,4]{0,1:T(4,128)} %param.20) | copy-start | bytes 1156
  13.0 9.8 %all-to-all-start = ((f32[4,24,3,130]{3,1,2,0:T(8,128)}), f32[4,24,3,130]{3,1,2,0:T(8,128)S(1)}, u32[]{:S(2)}, u32[]{:S(2)}) async-start(f32[4,24,3,130]{3,1,2,0:T(8,128)} %maximum_bitcast_fusion), calls=%async_computation | async-start | bytes 589824 | tf_op jit(solution)/shard_map/all_to_all | solution.py:174
  23.8 7.2 %copy-start.3 = (f32[1536]{0:T(1024)S(1)}, f32[1536]{0:T(1024)}, u32[]{:S(2)}) copy-start(f32[1536]{0:T(1024)} %param.19) | copy-start | bytes 18436
  31.1 7.8 %collective-permute-start = (bf16[24,1664]{1,0:T(8,128)(2,1)S(1)}, bf16[24,1664]{1,0:T(8,128)(2,1)S(1)}, u32[]{:S(2)}, u32[]{:S(2)}) collective-permute-start(bf16[24,1664]{1,0:T(8,128)(2,1)S(1)} %pad_maximum_fusion.1), channel_id=1, source_target_pairs={{28,0},{21,1},{14,2},{7,3},{0,4},{25,5},{18,6},{11,7},{4,8},{29,9}... | collective-permute-start | bytes 239624 | tf_op jit(solution)/shard_map/ppermute | solution.py:231
  32.9 8.8 %collective-permute-start.1 = (bf16[24,1664]{1,0:T(8,128)(2,1)S(1)}, bf16[24,1664]{1,0:T(8,128)(2,1)S(1)}, u32[]{:S(2)}, u32[]{:S(2)}) collective-permute-start(bf16[24,1664]{1,0:T(8,128)(2,1)S(1)} %pad_maximum_fusion.1), channel_id=1, source_target_pairs={{24,0},{17,1},{10,2},{3,3},{28,4},{21,5},{14,6},{7,7},{0,8},{25,9}... | collective-permute-start | bytes 239624 | tf_op jit(solution)/shard_map/ppermute | solution.py:231
  56.8 20.4 %all-to-all-start.1 = ((bf16[32,24,384]{2,1,0:T(8,128)(2,1)}), bf16[32,24,384]{2,1,0:T(8,128)(2,1)S(1)}, u32[]{:S(2)}, u32[]{:S(2)}) async-start(bf16[32,24,384]{2,1,0:T(8,128)(2,1)} %shard_map.118), calls=%async_computation.1 | async-start | bytes 1179648 | tf_op jit(solution)/shard_map/all_to_all | solution.py:251

commit v10 on v9

--- a/solution.py
+++ b/solution.py
@@ -32,7 +32,7 @@
 
 
 def _expert_body(
-    offset_ref, x_ref, gu_ref, dn_ref, o_ref, acc_ref, *, width, block_total, row_count, tp_count
+    offset_ref, dest_ref, x_ref, gu_ref, dn_ref, o_ref, acc_ref, *, width, block_total, row_count, tp_count
 ):
     block = pl.program_id(1)
 
@@ -58,15 +58,17 @@
     @pl.when(block == pl.num_programs(1) - 1)
     def _():
         own_width = o_ref.shape[2]
-        for group in range(x_ref.shape[0] // row_count):
+        tile_groups = x_ref.shape[0] // row_count
+        for group in range(tile_groups):
+            dest = dest_ref[pl.program_id(0) * tile_groups + group] - pl.program_id(0) * tile_groups
             for part in range(tp_count):
-                o_ref[group * tp_count + part] = acc_ref[
+                o_ref[dest * tp_count + part] = acc_ref[
                     group * row_count : (group + 1) * row_count,
                     part * own_width : (part + 1) * own_width,
                 ].astype(o_ref.dtype)
 
 
-def expert_mix(rows, gate_up, down, offset, width, block_total, row_count, tp_count):
+def expert_mix(rows, gate_up, down, offset, dest, width, block_total, row_count, tp_count):
     row_total, message_width = rows.shape
     local_count, _, _, hidden = gate_up.shape
     group_total = row_total // row_count
@@ -82,6 +84,7 @@
         grid=(group_total // tile_groups, local_count),
         in_specs=[
             pl.BlockSpec(memory_space=pltpu.SMEM),
+            pl.BlockSpec(memory_space=pltpu.SMEM),
             pl.BlockSpec((tile, message_width), lambda i, b: (i, 0)),
             pl.BlockSpec((1, 2, hidden, width), lambda i, b: (b, 0, 0, 0)),
             pl.BlockSpec((1, hidden, width), lambda i, b: (b, 0, 0)),
@@ -90,7 +93,7 @@
         out_shape=jax.ShapeDtypeStruct((group_total * tp_count, row_count, own_width), jnp.bfloat16),
         scratch_shapes=[pltpu.VMEM((tile, width), jnp.float32)],
         compiler_params=pltpu.CompilerParams(dimension_semantics=("parallel", "arbitrary")),
-    )(offset, rows, gate_up_t, down)
+    )(offset, dest, rows, gate_up_t, down)
 
 
 def per_device(
@@ -216,9 +219,10 @@
     )
 
     def gather_req(value):
-        if req_count > 16 or (req_count - 1) % tp_count != tp_count - 1 or req_count < tp_count:
-            return lax.all_gather(value, "req", axis=0, tiled=True)
-        per_tp = (req_count + tp_count - 1) // tp_count
+        if req_count > 8 or req_count % tp_count != 0:
+            gathered = lax.all_gather(value, "req", axis=0, tiled=True)
+            return gathered, jnp.arange(req_count, dtype=jnp.int32)
+        per_tp = req_count // tp_count
         fetched = []
         for slot in range(per_tp):
             pairs = []
@@ -227,13 +231,11 @@
                     shift = per_tp * part + slot + 1
                     source = ((group - shift) % req_count) * tp_count + part
                     pairs.append((source, group * tp_count + part))
-            moved = lax.ppermute(value, ("req", "tp"), pairs)
             fetched.append(lax.ppermute(value, ("req", "tp"), pairs))
         shared = lax.all_gather(jnp.stack(fetched, axis=0), "tp", axis=0)
-        shared = shared.reshape((tp_count * per_tp,) + value.shape)
-        order = (req_index - jnp.arange(req_count, dtype=jnp.int32) - 1) % req_count
-        arrived = jnp.take(shared, order, axis=0)
-        return arrived.reshape((req_count * value.shape[0],) + value.shape[1:])
+        shared = shared.reshape((req_count * value.shape[0],) + value.shape[1:])
+        groups = (req_index - jnp.arange(req_count, dtype=jnp.int32) - 1) % req_count
+        return shared, groups.astype(jnp.int32)
 
     weight_high = lax.reduce_precision(block_weights, exponent_bits=8, mantissa_bits=7)
     weight_rest = block_weights - weight_high
@@ -243,10 +245,10 @@
     code_lanes = -(-code.shape[1] // 128) * 128
     code = jnp.pad(code, ((0, 0), (0, code_lanes - code.shape[1])))
     message = jnp.concatenate([normed, code], axis=1)
-    message_all = gather_req(message)
+    message_all, message_groups = gather_req(message)
     offset = (req_index * local_count).astype(jnp.int32).reshape(1)
     mixed = expert_mix(
-        message_all, gate_up, down, offset, model_width, block_total, row_count, tp_count
+        message_all, gate_up, down, offset, message_groups, model_width, block_total, row_count, tp_count
     )
     mixed = lax.all_to_all(mixed, ("req", "tp"), 0, 0, tiled=True)
     mixed = jnp.sum(mixed.astype(jnp.float32), axis=0)

time: 78.4 us -> 77.3 us (0.986)
  local copies, waits for them, and re-layouts: 2.92 us -> 2.12 us
  transfers between devices with their start and end apart: 4 -> 4, of which waited for: 4 -> 4; matrix products, arithmetic and copies ran while one was open for 1% -> 2% of each run, Pallas kernels for 0% -> 0%
where the time goes in v10:
time: 77.3 us; the launch traced here: 76.8 us
  waiting for transfers between devices  27 us (35%)
  blocking collectives  21.1 us (27%)
  starting transfers between devices  12.3 us (16%)
  Pallas kernels  6.42 us (8%)
  other arithmetic  5.75 us (7%)
  local copies, waits for them, and re-layouts  2.12 us (3%)
  matrix products  1.67 us (2%)
    all_to_all x1, waiting for transfers between devices, per_device(): mixed = lax.all_to_all(mixed, ('req', 'tp'), 0, 0, tiled=True)  16.8 us
    all_gather x1, blocking collectives, gather_req(): shared = lax.all_gather(jnp.stack(fetched, axis=0), 'tp', axis=0)  7.52 us
    all_gather x1, blocking collectives, per_device(): projected = jnp.sum(lax.all_gather(partial_proj, 'tp', axis=0), axis=0)  6.99 us
    all_gather x1, blocking collectives, per_device(): gathered = lax.all_gather(packed, 'tp', axis=0)  6.59 us
    pallas_call x1, Pallas kernels, expert_mix(): pl.pallas_call(body, grid=(group_total // tile_groups, local_count), in_s...  6.42 us
    all_to_all x1, waiting for transfers between devices, per_device(): lax.all_to_all(jnp.transpose(states, (1, 0, 2, 3)), 'tp', 0, 0, tiled=True)  5.48 us
    ppermute x2, starting transfers between devices, gather_req(): fetched.append(lax.ppermute(value, ('req', 'tp'), pairs))  5.31 us
    ppermute x2, waiting for transfers between devices, gather_req(): fetched.append(lax.ppermute(value, ('req', 'tp'), pairs))  4.76 us
  transfers between devices with their start and end apart: 4, of which 4 were waited for; matrix products, arithmetic and copies ran while one was open for 2% of the time, Pallas kernels for 0%

profile of v10, /device:TPU:0, one launch (start us, length us, event | category | flops | bytes accessed | tf_op | source)
XLA Modules:
  0.0 76.8 jit_solution(13144967922101809840)
XLA Ops:
  0.0 0.8 %convert_element_type.69 = f32[24]{0:T(128)S(1)} convert(s32[24]{0:T(128)} %param.15) | non-fusion elementwise | flops 24 | bytes 192 | tf_op jit(solution)/shard_map/convert_element_type | solution.py:23
  0.8 0.7 reshape.211
  1.6 0.1 multiply_cosine_fusion
  1.7 0.1 subtract_convert_fusion
  1.8 0.1 pad_maximum_fusion.3
  1.9 0.7 pad_maximum_fusion.2
  2.7 6.6 %all-gather = bf16[8,24,384]{2,1,0:T(8,128)(2,1)S(1)} all-gather(bf16[2,24,384]{2,1,0:T(8,128)(2,1)S(1)} %pad_maximum_fusion.2), channel_id=2, replica_groups=mesh['req'=8,'tp'=4] {'tp'}, dimensions={0}, use_global_device_ids=true | all-gather | bytes 184320 | tf_op jit(solution)/shard_map/all_gather | solution.py:133
  9.3 0.1 reshape.207
  9.4 0.1 copy.70
  9.5 0.1 reduce.2
  9.7 0.5 fusion.30
  10.2 0.1 compare_and_fusion
  10.3 0.5 fusion.31
  10.8 0.1 concatenate.33
  10.9 0.3 fusion.3
  11.2 0.0 copy-start.2
  11.2 0.7 fusion.2
  11.9 0.0 copy-start.4
  12.0 0.1 concatenate.34
  12.1 0.9 %maximum_bitcast_fusion = f32[4,24,3,130]{3,1,2,0:T(8,128)} fusion(f32[24,4,3,128]{3,0,2,1:T(8,128)S(1)} %bitcast.100, f32[24,4,3,1]{3,0,2,1:T(8,128)S(1)} %concatenate.34, f32[24,4,3,1]{3,0,2,1:T(8,128)S(1)} %concatenate.33), kind=kLoop, calls=%fused_computation.12 | loop fusion | flops 74880 | bytes 299520 | tf_op jit(solution)/shard_map/transpose | solution.py:178
  13.0 3.5 %all-to-all-start = ((f32[4,24,3,130]{3,1,2,0:T(8,128)}), f32[4,24,3,130]{3,1,2,0:T(8,128)S(1)}, u32[]{:S(2)}, u32[]{:S(2)}) async-start(f32[4,24,3,130]{3,1,2,0:T(8,128)} %maximum_bitcast_fusion), calls=%async_computation | async-start | bytes 589824 | tf_op jit(solution)/shard_map/all_to_all | solution.py:177
  16.5 0.1 slice_reduce_fusion
  16.6 0.1 subtract_convert_fusion.1
  16.7 0.1 maximum_bitcast_fusion.1
  16.8 0.2 fusion.12
  17.0 0.1 copy.87
  17.1 0.1 select_reduce_fusion
  17.3 0.1 fusion.23
  17.4 5.5 %all-to-all-done = f32[4,24,3,130]{3,1,2,0:T(8,128)S(1)} async-done(((f32[4,24,3,130]{3,1,2,0:T(8,128)}), f32[4,24,3,130]{3,1,2,0:T(8,128)S(1)}, u32[]{:S(2)}, u32[]{:S(2)}) %all-to-all-start) | async-done | bytes 149792 | tf_op jit(solution)/shard_map/all_to_all | solution.py:177
  22.8 0.1 slice_reduce_fusion.1
  23.0 0.1 copy.92
  23.2 0.1 copy.81
  23.4 0.1 fusion.10
  23.5 0.3 fusion.14
  23.8 7.0 %all-gather.1 = f32[96,1536]{1,0:T(8,128)S(1)} all-gather(f32[24,1536]{1,0:T(8,128)S(1)} %fusion.14), channel_id=3, replica_groups=mesh['req'=8,'tp'=4] {'tp'}, dimensions={0}, use_global_device_ids=true | all-gather | bytes 737280 | tf_op jit(solution)/shard_map/all_gather | solution.py:200
  30.9 0.1 fusion.9
  31.0 0.1 multiply_convert_fusion
  31.1 1.8 %collective-permute-start = (bf16[24,1664]{1,0:T(8,128)(2,1)S(1)}, bf16[24,1664]{1,0:T(8,128)(2,1)S(1)}, u32[]{:S(2)}, u32[]{:S(2)}) collective-permute-start(bf16[24,1664]{1,0:T(8,128)(2,1)S(1)} %pad_maximum_fusion.1), channel_id=1, source_target_pairs={{28,0},{21,1},{14,2},{7,3},{0,4},{25,5},{18,6},{11,7},{4,8},{29,9}... | collective-permute-start | bytes 239624 | tf_op jit(solution)/shard_map/ppermute | solution.py:234
  32.9 3.5 %collective-permute-start.1 = (bf16[24,1664]{1,0:T(8,128)(2,1)S(1)}, bf16[24,1664]{1,0:T(8,128)(2,1)S(1)}, u32[]{:S(2)}, u32[]{:S(2)}) collective-permute-start(bf16[24,1664]{1,0:T(8,128)(2,1)S(1)} %pad_maximum_fusion.1), channel_id=1, source_target_pairs={{24,0},{17,1},{10,2},{3,3},{28,4},{21,5},{14,6},{7,7},{0,8},{25,9}... | collective-permute-start | bytes 239624 | tf_op jit(solution)/shard_map/ppermute | solution.py:234
  36.4 0.5 and_select_fusion.dest_ref
  37.0 1.9 %collective-permute-done = bf16[24,1664]{1,0:T(8,128)(2,1)S(1)} collective-permute-done((bf16[24,1664]{1,0:T(8,128)(2,1)S(1)}, bf16[24,1664]{1,0:T(8,128)(2,1)S(1)}, u32[]{:S(2)}, u32[]{:S(2)}) %collective-permute-start) | collective-permute-done | bytes 79904 | tf_op jit(solution)/shard_map/ppermute | solution.py:234
  38.9 2.8 %collective-permute-done.1 = bf16[24,1664]{1,0:T(8,128)(2,1)S(1)} collective-permute-done((bf16[24,1664]{1,0:T(8,128)(2,1)S(1)}, bf16[24,1664]{1,0:T(8,128)(2,1)S(1)}, u32[]{:S(2)}, u32[]{:S(2)}) %collective-permute-start.1) | collective-permute-done | bytes 79904 | tf_op jit(solution)/shard_map/ppermute | solution.py:234
  41.8 7.5 %all-gather.2 = bf16[8,24,1664]{2,1,0:T(8,128)(2,1)} all-gather(bf16[2,24,1664]{2,1,0:T(8,128)(2,1)S(1)} %pad_maximum_fusion), channel_id=4, replica_groups=mesh['req'=8,'tp'=4] {'tp'}, dimensions={0}, use_global_device_ids=true | all-gather | bytes 798720 | tf_op jit(solution)/shard_map/all_gather | solution.py:235
  49.3 6.4 %shard_map.118 = bf16[32,24,384]{2,1,0:T(8,128)(2,1)} custom-call(s32[1]{0:T(128)} %bitcast.26.offset_ref, s32[8]{0:T(128)} %and_select_fusion.dest_ref, bf16[192,1664]{1,0:T(8,128)(2,1)} %bitcast.92, bf16[4,2,192,1536]{3,2,1,0:T(8,128)(2,1)} %bitcast.91, bf16[4,192,1536]{2,1,0:T(8,128)(2,1)} %dn_ref.1), custom_call_target="tpu_custom_call" | custom-call | tf_op jit(solution)/shard_map/pallas_call | solution.py:82
  55.7 3.6 %all-to-all-start.1 = ((bf16[32,24,384]{2,1,0:T(8,128)(2,1)}), bf16[32,24,384]{2,1,0:T(8,128)(2,1)S(1)}, u32[]{:S(2)}, u32[]{:S(2)}) async-start(bf16[32,24,384]{2,1,0:T(8,128)(2,1)} %shard_map.118), calls=%async_computation.1 | async-start | bytes 1179648 | tf_op jit(solution)/shard_map/all_to_all | solution.py:253
  59.3 16.8 %all-to-all-done.1 = bf16[32,24,384]{2,1,0:T(8,128)(2,1)S(1)} async-done(((bf16[32,24,384]{2,1,0:T(8,128)(2,1)}), bf16[32,24,384]{2,1,0:T(8,128)(2,1)S(1)}, u32[]{:S(2)}, u32[]{:S(2)}) %all-to-all-start.1) | async-done | bytes 589856 | tf_op jit(solution)/shard_map/all_to_all | solution.py:253
  76.1 0.1 convert_reduce_fusion
  76.2 0.6 add_convert_fusion.1
  (34 shorter events, 0.4 us)
Async XLA Ops:
  0.0 23.5 %copy-start = (bf16[384,1536]{1,0:T(8,128)(2,1)S(1)}, bf16[384,1536]{1,0:T(8,128)(2,1)}, u32[]{:S(2)}) copy-start(bf16[384,1536]{1,0:T(8,128)(2,1)} %param.18) | copy-start | bytes 3538948
  0.0 9.4 %copy-start.6 = (s32[1,24]{1,0:T(1,128)S(1)}, s32[1,24]{1,0:T(1,128)}, u32[]{:S(2)}) copy-start(s32[1,24]{1,0:T(1,128)} %param.16) | copy-start | bytes 292
  0.0 9.6 %copy-start.1 = (bf16[768,2,2,128]{3,2,1,0:T(2,128)(2,1)S(1)}, bf16[768,2,2,128]{3,2,1,0:T(2,128)(2,1)}, u32[]{:S(2)}) copy-start(bf16[768,2,2,128]{3,2,1,0:T(2,128)(2,1)} %param.17) | copy-start | bytes 2359300
  11.2 5.3 %copy-start.2 = (bf16[24,2,256]{2,1,0:T(2,128)(2,1)S(1)}, bf16[24,2,256]{2,1,0:T(2,128)(2,1)}, u32[]{:S(2)}) copy-start(bf16[24,2,256]{2,1,0:T(2,128)(2,1)} %param.14) | copy-start | bytes 73732
  11.9 5.2 %copy-start.4 = (f32[24,4]{0,1:T(4,128)S(1)}, f32[24,4]{0,1:T(4,128)}, u32[]{:S(2)}) copy-start(f32[24,4]{0,1:T(4,128)} %param.21) | copy-start | bytes 1156
  11.9 5.2 %copy-start.5 = (s32[24,4]{0,1:T(4,128)S(1)}, s32[24,4]{0,1:T(4,128)}, u32[]{:S(2)}) copy-start(s32[24,4]{0,1:T(4,128)} %param.20) | copy-start | bytes 1156
  13.0 9.8 %all-to-all-start = ((f32[4,24,3,130]{3,1,2,0:T(8,128)}), f32[4,24,3,130]{3,1,2,0:T(8,128)S(1)}, u32[]{:S(2)}, u32[]{:S(2)}) async-start(f32[4,24,3,130]{3,1,2,0:T(8,128)} %maximum_bitcast_fusion), calls=%async_computation | async-start | bytes 589824 | tf_op jit(solution)/shard_map/all_to_all | solution.py:177
  23.8 7.2 %copy-start.3 = (f32[1536]{0:T(1024)S(1)}, f32[1536]{0:T(1024)}, u32[]{:S(2)}) copy-start(f32[1536]{0:T(1024)} %param.19) | copy-start | bytes 18436
  31.1 7.8 %collective-permute-start = (bf16[24,1664]{1,0:T(8,128)(2,1)S(1)}, bf16[24,1664]{1,0:T(8,128)(2,1)S(1)}, u32[]{:S(2)}, u32[]{:S(2)}) collective-permute-start(bf16[24,1664]{1,0:T(8,128)(2,1)S(1)} %pad_maximum_fusion.1), channel_id=1, source_target_pairs={{28,0},{21,1},{14,2},{7,3},{0,4},{25,5},{18,6},{11,7},{4,8},{29,9}... | collective-permute-start | bytes 239624 | tf_op jit(solution)/shard_map/ppermute | solution.py:234
  32.9 8.8 %collective-permute-start.1 = (bf16[24,1664]{1,0:T(8,128)(2,1)S(1)}, bf16[24,1664]{1,0:T(8,128)(2,1)S(1)}, u32[]{:S(2)}, u32[]{:S(2)}) collective-permute-start(bf16[24,1664]{1,0:T(8,128)(2,1)S(1)} %pad_maximum_fusion.1), channel_id=1, source_target_pairs={{24,0},{17,1},{10,2},{3,3},{28,4},{21,5},{14,6},{7,7},{0,8},{25,9}... | collective-permute-start | bytes 239624 | tf_op jit(solution)/shard_map/ppermute | solution.py:234
  55.7 20.4 %all-to-all-start.1 = ((bf16[32,24,384]{2,1,0:T(8,128)(2,1)}), bf16[32,24,384]{2,1,0:T(8,128)(2,1)S(1)}, u32[]{:S(2)}, u32[]{:S(2)}) async-start(bf16[32,24,384]{2,1,0:T(8,128)(2,1)} %shard_map.118), calls=%async_computation.1 | async-start | bytes 1179648 | tf_op jit(solution)/shard_map/all_to_all | solution.py:253

commit v11 on v10

--- a/solution.py
+++ b/solution.py
@@ -174,9 +174,15 @@
     states = jnp.concatenate(
         [highest_local[..., None], totals_local[..., None], sums_local], axis=3
     ).reshape(row_count, tp_count, own_heads, head_size + 2)
-    all_states = lax.all_to_all(
-        jnp.transpose(states, (1, 0, 2, 3)), "tp", 0, 0, tiled=True
-    )
+    states = jnp.transpose(states, (1, 0, 2, 3))
+    own_part_states = lax.dynamic_index_in_dim(states, tp_index, 0, keepdims=False)
+    all_states = [own_part_states]
+    for shift in range(1, tp_count):
+        outgoing = lax.dynamic_index_in_dim(states, (tp_index + shift) % tp_count, 0, keepdims=False)
+        all_states.append(
+            lax.ppermute(outgoing, "tp", [(i, (i + shift) % tp_count) for i in range(tp_count)])
+        )
+    all_states = jnp.stack(all_states, axis=0)
     parts_highest = all_states[..., 0]
     parts_totals = all_states[..., 1]
     parts_sums = all_states[..., 2:]

time: 77.3 us -> 73.6 us (0.952)
  waiting for transfers between devices: 27 us -> 22.9 us
  blocking collectives: 21.1 us -> 22.3 us
    all_to_all x1 -> x0, waiting for transfers between devices: 5.48 us -> none  [per_device(): lax.all_to_all(jnp.transpose(states, (1, 0, 2, 3)), 'tp', 0, 0, tiled=True)]
    all_to_all x1 -> x0, starting transfers between devices: 3.45 us -> none  [per_device(): lax.all_to_all(jnp.transpose(states, (1, 0, 2, 3)), 'tp', 0, 0, tiled=True)]
    ppermute x0 -> x3, starting transfers between devices: none -> 3.35 us  [per_device(): lax.ppermute(outgoing, 'tp', [(i, (i + shift) % tp_count) for i in range(...]
    ppermute x0 -> x3, waiting for transfers between devices: none -> 1.34 us  [per_device(): lax.ppermute(outgoing, 'tp', [(i, (i + shift) % tp_count) for i in range(...]
    all_gather x1, blocking collectives: 6.99 us -> 8.02 us  [per_device(): projected = jnp.sum(lax.all_gather(partial_proj, 'tp', axis=0), axis=0)]
    transpose x1 -> x0, other arithmetic: 0.93 us -> none  [per_device(): jnp.transpose(states, (1, 0, 2, 3))]
  transfers between devices with their start and end apart: 4 -> 6, of which waited for: 4 -> 5; matrix products, arithmetic and copies ran while one was open for 2% -> 2% of each run, Pallas kernels for 0% -> 0%
where the time goes in v11:
time: 73.6 us; the launch traced here: 73.2 us
  waiting for transfers between devices  22.9 us (31%)
  blocking collectives  22.3 us (30%)
  starting transfers between devices  12.3 us (17%)
  Pallas kernels  6.42 us (9%)
  other arithmetic  5.07 us (7%)
  local copies, waits for them, and re-layouts  2.15 us (3%)
  matrix products  1.67 us (2%)
    all_to_all x1, waiting for transfers between devices, per_device(): mixed = lax.all_to_all(mixed, ('req', 'tp'), 0, 0, tiled=True)  16.8 us
    all_gather x1, blocking collectives, per_device(): projected = jnp.sum(lax.all_gather(partial_proj, 'tp', axis=0), axis=0)  8.02 us
    all_gather x1, blocking collectives, gather_req(): shared = lax.all_gather(jnp.stack(fetched, axis=0), 'tp', axis=0)  7.65 us
    all_gather x1, blocking collectives, per_device(): gathered = lax.all_gather(packed, 'tp', axis=0)  6.62 us
    pallas_call x1, Pallas kernels, expert_mix(): pl.pallas_call(body, grid=(group_total // tile_groups, local_count), in_s...  6.42 us
    ppermute x2, starting transfers between devices, gather_req(): fetched.append(lax.ppermute(value, ('req', 'tp'), pairs))  5.38 us
    ppermute x2, waiting for transfers between devices, gather_req(): fetched.append(lax.ppermute(value, ('req', 'tp'), pairs))  4.76 us
    all_to_all x1, starting transfers between devices, per_device(): mixed = lax.all_to_all(mixed, ('req', 'tp'), 0, 0, tiled=True)  3.58 us
  transfers between devices with their start and end apart: 6, of which 5 were waited for; matrix products, arithmetic and copies ran while one was open for 2% of the time, Pallas kernels for 0%

profile of v11, /device:TPU:0, one launch (start us, length us, event | category | flops | bytes accessed | tf_op | source)
XLA Modules:
  0.0 73.2 jit_solution(7179018690762048858)
XLA Ops:
  0.0 0.8 %convert_element_type.69 = f32[24]{0:T(128)S(1)} convert(s32[24]{0:T(128)} %param.15) | non-fusion elementwise | flops 24 | bytes 192 | tf_op jit(solution)/shard_map/convert_element_type | solution.py:23
  0.8 0.7 %reshape.218 = f32[24,3,128]{2,1,0:T(4,128)S(1)} reshape(bf16[24,384]{1,0:T(8,128)(2,1)} %param.13) | data formatting | bytes 55296 | tf_op jit(solution)/shard_map/convert_element_type | solution.py:130
  1.6 0.1 multiply_cosine_fusion
  1.7 0.1 subtract_convert_fusion
  1.8 0.1 pad_maximum_fusion.5
  1.9 0.7 %pad_maximum_fusion.4 = bf16[2,24,384]{2,1,0:T(8,128)(2,1)S(1)} fusion(bf16[1,24,384]{2,1,0:T(8,128)(2,1)} %bitcast.116, bf16[1,24,384]{2,1,0:T(8,128)(2,1)S(1)} %convert_element_type.70), kind=kLoop, calls=%fused_computation.36 | loop fusion | flops 18432 | bytes 73728 | tf_op jit(solution)/shard_map/stack | solution.py:132
  2.7 6.6 %all-gather = bf16[8,24,384]{2,1,0:T(8,128)(2,1)S(1)} all-gather(bf16[2,24,384]{2,1,0:T(8,128)(2,1)S(1)} %pad_maximum_fusion.4), channel_id=2, replica_groups=mesh['req'=8,'tp'=4] {'tp'}, dimensions={0}, use_global_device_ids=true | all-gather | bytes 184320 | tf_op jit(solution)/shard_map/all_gather | solution.py:133
  9.4 0.1 copy.119
  9.6 0.1 reduce.2
  9.7 0.5 fusion.31
  10.2 0.1 compare_and_fusion
  10.3 0.5 fusion.32
  10.8 0.1 concatenate.33
  10.9 0.3 fusion.3
  11.3 0.7 fusion.2
  12.0 0.1 concatenate.34
  12.1 0.2 pad_maximum_fusion
  12.4 0.4 collective-permute-start
  12.8 1.8 %collective-permute-start.1 = (f32[24,3,130]{2,0,1:T(8,128)S(1)}, f32[24,3,130]{2,0,1:T(8,128)S(1)}, u32[]{:S(2)}, u32[]{:S(2)}) collective-permute-start(f32[24,3,130]{2,0,1:T(8,128)S(1)} %get-tuple-element.16), channel_id=1, source_target_pairs={{0,2},{1,3},{2,0},{3,1},{4,6},{5,7},{6,4},{7,5},{8,10},{9,11},{10,... | collective-permute-start | bytes 112328 | tf_op jit(solution)/shard_map/ppermute | solution.py:183
  14.6 1.1 %collective-permute-start.2 = (f32[24,3,130]{2,0,1:T(8,128)S(1)}, f32[24,3,130]{2,0,1:T(8,128)S(1)}, u32[]{:S(2)}, u32[]{:S(2)}) collective-permute-start(f32[24,3,130]{2,0,1:T(8,128)S(1)} %get-tuple-element.15), channel_id=1, source_target_pairs={{0,3},{1,0},{2,1},{3,2},{4,7},{5,4},{6,5},{7,6},{8,11},{9,8},{10,9... | collective-permute-start | bytes 112328 | tf_op jit(solution)/shard_map/ppermute | solution.py:183
  15.7 0.1 slice_reduce_fusion
  15.8 0.1 subtract_convert_fusion.1
  15.9 0.1 maximum_bitcast_fusion
  16.0 0.2 fusion.12
  16.2 0.1 copy.134
  16.3 0.1 select_reduce_fusion
  16.5 0.1 fusion.23
  16.6 0.7 collective-permute-done.1
  17.3 0.6 collective-permute-done.2
  18.0 0.1 slice_reduce_fusion.1
  18.1 0.1 copy.138
  18.3 0.1 fusion.10
  18.4 0.1 copy.128
  18.6 0.3 fusion.14
  19.0 8.0 %all-gather.1 = f32[96,1536]{1,0:T(8,128)S(1)} all-gather(f32[24,1536]{1,0:T(8,128)S(1)} %fusion.14), channel_id=3, replica_groups=mesh['req'=8,'tp'=4] {'tp'}, dimensions={0}, use_global_device_ids=true | all-gather | bytes 737280 | tf_op jit(solution)/shard_map/all_gather | solution.py:206
  27.0 0.1 fusion.9
  27.2 0.1 multiply_convert_fusion
  27.3 1.9 %collective-permute-start.3 = (bf16[24,1664]{1,0:T(8,128)(2,1)S(1)}, bf16[24,1664]{1,0:T(8,128)(2,1)S(1)}, u32[]{:S(2)}, u32[]{:S(2)}) collective-permute-start(bf16[24,1664]{1,0:T(8,128)(2,1)S(1)} %pad_maximum_fusion.3), channel_id=1, source_target_pairs={{28,0},{21,1},{14,2},{7,3},{0,4},{25,5},{18,6},{11,7},{4,8},{29,9}... | collective-permute-start | bytes 239624 | tf_op jit(solution)/shard_map/ppermute | solution.py:240
  29.2 3.5 %collective-permute-start.4 = (bf16[24,1664]{1,0:T(8,128)(2,1)S(1)}, bf16[24,1664]{1,0:T(8,128)(2,1)S(1)}, u32[]{:S(2)}, u32[]{:S(2)}) collective-permute-start(bf16[24,1664]{1,0:T(8,128)(2,1)S(1)} %pad_maximum_fusion.3), channel_id=1, source_target_pairs={{24,0},{17,1},{10,2},{3,3},{28,4},{21,5},{14,6},{7,7},{0,8},{25,9}... | collective-permute-start | bytes 239624 | tf_op jit(solution)/shard_map/ppermute | solution.py:240
  32.7 0.5 and_select_fusion.dest_ref
  33.2 1.9 %collective-permute-done.3 = bf16[24,1664]{1,0:T(8,128)(2,1)S(1)} collective-permute-done((bf16[24,1664]{1,0:T(8,128)(2,1)S(1)}, bf16[24,1664]{1,0:T(8,128)(2,1)S(1)}, u32[]{:S(2)}, u32[]{:S(2)}) %collective-permute-start.3) | collective-permute-done | bytes 79904 | tf_op jit(solution)/shard_map/ppermute | solution.py:240
  35.1 2.8 %collective-permute-done.4 = bf16[24,1664]{1,0:T(8,128)(2,1)S(1)} collective-permute-done((bf16[24,1664]{1,0:T(8,128)(2,1)S(1)}, bf16[24,1664]{1,0:T(8,128)(2,1)S(1)}, u32[]{:S(2)}, u32[]{:S(2)}) %collective-permute-start.4) | collective-permute-done | bytes 79904 | tf_op jit(solution)/shard_map/ppermute | solution.py:240
  38.0 7.7 %all-gather.2 = bf16[8,24,1664]{2,1,0:T(8,128)(2,1)} all-gather(bf16[2,24,1664]{2,1,0:T(8,128)(2,1)S(1)} %pad_maximum_fusion.2), channel_id=4, replica_groups=mesh['req'=8,'tp'=4] {'tp'}, dimensions={0}, use_global_device_ids=true | all-gather | bytes 798720 | tf_op jit(solution)/shard_map/all_gather | solution.py:241
  45.6 6.4 %shard_map.118 = bf16[32,24,384]{2,1,0:T(8,128)(2,1)} custom-call(s32[1]{0:T(128)} %bitcast.32.offset_ref, s32[8]{0:T(128)} %and_select_fusion.dest_ref, bf16[192,1664]{1,0:T(8,128)(2,1)} %bitcast.101, bf16[4,2,192,1536]{3,2,1,0:T(8,128)(2,1)} %bitcast.100, bf16[4,192,1536]{2,1,0:T(8,128)(2,1)} %dn_ref.1), custom_call_target="tpu_custom_call" | custom-call | tf_op jit(solution)/shard_map/pallas_call | solution.py:82
  52.1 3.6 %all-to-all-start = ((bf16[32,24,384]{2,1,0:T(8,128)(2,1)}), bf16[32,24,384]{2,1,0:T(8,128)(2,1)S(1)}, u32[]{:S(2)}, u32[]{:S(2)}) async-start(bf16[32,24,384]{2,1,0:T(8,128)(2,1)} %shard_map.118), calls=%async_computation | async-start | bytes 1179648 | tf_op jit(solution)/shard_map/all_to_all | solution.py:259
  55.7 16.8 %all-to-all-done = bf16[32,24,384]{2,1,0:T(8,128)(2,1)S(1)} async-done(((bf16[32,24,384]{2,1,0:T(8,128)(2,1)}), bf16[32,24,384]{2,1,0:T(8,128)(2,1)S(1)}, u32[]{:S(2)}, u32[]{:S(2)}) %all-to-all-start) | async-done | bytes 589856 | tf_op jit(solution)/shard_map/all_to_all | solution.py:259
  72.5 0.1 convert_reduce_fusion
  72.5 0.6 add_convert_fusion.1
  (40 shorter events, 0.5 us)
Async XLA Ops:
  0.0 18.6 %copy-start = (bf16[384,1536]{1,0:T(8,128)(2,1)S(1)}, bf16[384,1536]{1,0:T(8,128)(2,1)}, u32[]{:S(2)}) copy-start(bf16[384,1536]{1,0:T(8,128)(2,1)} %param.18) | copy-start | bytes 3538948
  0.0 9.4 %copy-start.6 = (s32[1,24]{1,0:T(1,128)S(1)}, s32[1,24]{1,0:T(1,128)}, u32[]{:S(2)}) copy-start(s32[1,24]{1,0:T(1,128)} %param.16) | copy-start | bytes 292
  0.0 9.7 %copy-start.1 = (bf16[768,2,2,128]{3,2,1,0:T(2,128)(2,1)S(1)}, bf16[768,2,2,128]{3,2,1,0:T(2,128)(2,1)}, u32[]{:S(2)}) copy-start(bf16[768,2,2,128]{3,2,1,0:T(2,128)(2,1)} %param.17) | copy-start | bytes 2359300
  11.2 4.5 %copy-start.2 = (bf16[24,2,256]{2,1,0:T(2,128)(2,1)S(1)}, bf16[24,2,256]{2,1,0:T(2,128)(2,1)}, u32[]{:S(2)}) copy-start(bf16[24,2,256]{2,1,0:T(2,128)(2,1)} %param.14) | copy-start | bytes 73732
  12.0 4.4 %copy-start.4 = (f32[24,4]{0,1:T(4,128)S(1)}, f32[24,4]{0,1:T(4,128)}, u32[]{:S(2)}) copy-start(f32[24,4]{0,1:T(4,128)} %param.21) | copy-start | bytes 1156
  12.0 4.4 %copy-start.5 = (s32[24,4]{0,1:T(4,128)S(1)}, s32[24,4]{0,1:T(4,128)}, u32[]{:S(2)}) copy-start(s32[24,4]{0,1:T(4,128)} %param.20) | copy-start | bytes 1156
  12.4 4.2 %collective-permute-start = (f32[24,3,130]{2,0,1:T(8,128)S(1)}, f32[24,3,130]{2,0,1:T(8,128)S(1)}, u32[]{:S(2)}, u32[]{:S(2)}) collective-permute-start(f32[24,3,130]{2,0,1:T(8,128)S(1)} %get-tuple-element.17), channel_id=1, source_target_pairs={{0,1},{1,2},{2,3},{3,0},{4,5},{5,6},{6,7},{7,4},{8,9},{9,10},{10,1... | collective-permute-start | bytes 112328 | tf_op jit(solution)/shard_map/ppermute | solution.py:183
  12.8 4.5 %collective-permute-start.1 = (f32[24,3,130]{2,0,1:T(8,128)S(1)}, f32[24,3,130]{2,0,1:T(8,128)S(1)}, u32[]{:S(2)}, u32[]{:S(2)}) collective-permute-start(f32[24,3,130]{2,0,1:T(8,128)S(1)} %get-tuple-element.16), channel_id=1, source_target_pairs={{0,2},{1,3},{2,0},{3,1},{4,6},{5,7},{6,4},{7,5},{8,10},{9,11},{10,... | collective-permute-start | bytes 112328 | tf_op jit(solution)/shard_map/ppermute | solution.py:183
  14.6 3.3 %collective-permute-start.2 = (f32[24,3,130]{2,0,1:T(8,128)S(1)}, f32[24,3,130]{2,0,1:T(8,128)S(1)}, u32[]{:S(2)}, u32[]{:S(2)}) collective-permute-start(f32[24,3,130]{2,0,1:T(8,128)S(1)} %get-tuple-element.15), channel_id=1, source_target_pairs={{0,3},{1,0},{2,1},{3,2},{4,7},{5,4},{6,5},{7,6},{8,11},{9,8},{10,9... | collective-permute-start | bytes 112328 | tf_op jit(solution)/shard_map/ppermute | solution.py:183
  19.0 8.2 %copy-start.3 = (f32[1536]{0:T(1024)S(1)}, f32[1536]{0:T(1024)}, u32[]{:S(2)}) copy-start(f32[1536]{0:T(1024)} %param.19) | copy-start | bytes 18436
  27.3 7.9 %collective-permute-start.3 = (bf16[24,1664]{1,0:T(8,128)(2,1)S(1)}, bf16[24,1664]{1,0:T(8,128)(2,1)S(1)}, u32[]{:S(2)}, u32[]{:S(2)}) collective-permute-start(bf16[24,1664]{1,0:T(8,128)(2,1)S(1)} %pad_maximum_fusion.3), channel_id=1, source_target_pairs={{28,0},{21,1},{14,2},{7,3},{0,4},{25,5},{18,6},{11,7},{4,8},{29,9}... | collective-permute-start | bytes 239624 | tf_op jit(solution)/shard_map/ppermute | solution.py:240
  29.2 8.8 %collective-permute-start.4 = (bf16[24,1664]{1,0:T(8,128)(2,1)S(1)}, bf16[24,1664]{1,0:T(8,128)(2,1)S(1)}, u32[]{:S(2)}, u32[]{:S(2)}) collective-permute-start(bf16[24,1664]{1,0:T(8,128)(2,1)S(1)} %pad_maximum_fusion.3), channel_id=1, source_target_pairs={{24,0},{17,1},{10,2},{3,3},{28,4},{21,5},{14,6},{7,7},{0,8},{25,9}... | collective-permute-start | bytes 239624 | tf_op jit(solution)/shard_map/ppermute | solution.py:240
  52.1 20.4 %all-to-all-start = ((bf16[32,24,384]{2,1,0:T(8,128)(2,1)}), bf16[32,24,384]{2,1,0:T(8,128)(2,1)S(1)}, u32[]{:S(2)}, u32[]{:S(2)}) async-start(bf16[32,24,384]{2,1,0:T(8,128)(2,1)} %shard_map.118), calls=%async_computation | async-start | bytes 1179648 | tf_op jit(solution)/shard_map/all_to_all | solution.py:259

commit v12 on v11

--- a/solution.py
+++ b/solution.py
@@ -130,7 +130,13 @@
         queries.reshape(row_count, own_heads, head_size).astype(jnp.float32), positions, head_size
     ).astype(jnp.bfloat16)
     packed = jnp.stack([q_local.reshape(row_count, own_width), hidden_in], axis=0)
-    gathered = lax.all_gather(packed, "tp", axis=0)
+    arrivals = [packed] + [
+        lax.ppermute(packed, "tp", [(i, (i + shift) % tp_count) for i in range(tp_count)])
+        for shift in range(1, tp_count)
+    ]
+    arrivals = jnp.stack(arrivals, axis=0)
+    order = (tp_index - jnp.arange(tp_count, dtype=jnp.int32)) % tp_count
+    gathered = jnp.take(arrivals, order, axis=0, mode="clip")
     q_all = jnp.transpose(gathered[:, 0], (1, 0, 2)).reshape(
         row_count, kv_count, request_group_size, head_size
     )

time: 73.6 us -> 74.1 us (level)
  blocking collectives: 22.3 us -> 15.4 us
  starting transfers between devices: 12.3 us -> 14.7 us
  local copies, waits for them, and re-layouts: 2.15 us -> 4.52 us
  waiting for transfers between devices: 22.9 us -> 24.7 us
    all_gather x1 -> x0, blocking collectives: 6.62 us -> none  [per_device(): gathered = lax.all_gather(packed, 'tp', axis=0)]
    ppermute x0 -> x3, starting transfers between devices: none -> 4.48 us  [per_device(): lax.ppermute(packed, 'tp', [(i, (i + shift) % tp_count) for i in range(tp...]
    ppermute x3, waiting for transfers between devices: 1.34 us -> 3.16 us  [per_device(): lax.ppermute(outgoing, 'tp', [(i, (i + shift) % tp_count) for i in range(...]
    ppermute x3, starting transfers between devices: 3.35 us -> 1.79 us  [per_device(): lax.ppermute(outgoing, 'tp', [(i, (i + shift) % tp_count) for i in range(...]
    slice x1, local copies, waits for them, and re-layouts: 0.54 us -> 1.65 us  [per_device(): values = cache[:, 1]]
  transfers between devices with their start and end apart: 6 -> 9, of which waited for: 5 -> 5; matrix products, arithmetic and copies ran while one was open for 2% -> 6% of each run, Pallas kernels for 0% -> 0%
where the time goes in v12:
time: 74.1 us; the launch traced here: 73.6 us
  waiting for transfers between devices  24.7 us (33%)
  blocking collectives  15.4 us (21%)
  starting transfers between devices  14.7 us (20%)
  Pallas kernels  6.42 us (9%)
  other arithmetic  5.74 us (8%)
  local copies, waits for them, and re-layouts  4.52 us (6%)
  matrix products  1.67 us (2%)
    all_to_all x1, waiting for transfers between devices, per_device(): mixed = lax.all_to_all(mixed, ('req', 'tp'), 0, 0, tiled=True)  16.8 us
    all_gather x1, blocking collectives, per_device(): projected = jnp.sum(lax.all_gather(partial_proj, 'tp', axis=0), axis=0)  8.16 us
    all_gather x1, blocking collectives, gather_req(): shared = lax.all_gather(jnp.stack(fetched, axis=0), 'tp', axis=0)  7.27 us
    pallas_call x1, Pallas kernels, expert_mix(): pl.pallas_call(body, grid=(group_total // tile_groups, local_count), in_s...  6.42 us
    ppermute x2, starting transfers between devices, gather_req(): fetched.append(lax.ppermute(value, ('req', 'tp'), pairs))  5.04 us
    ppermute x2, waiting for transfers between devices, gather_req(): fetched.append(lax.ppermute(value, ('req', 'tp'), pairs))  4.76 us
    ppermute x3, starting transfers between devices, per_device(): lax.ppermute(packed, 'tp', [(i, (i + shift) % tp_count) for i in range(tp...  4.48 us
    all_to_all x1, starting transfers between devices, per_device(): mixed = lax.all_to_all(mixed, ('req', 'tp'), 0, 0, tiled=True)  3.38 us
  transfers between devices with their start and end apart: 9, of which 5 were waited for; matrix products, arithmetic and copies ran while one was open for 6% of the time, Pallas kernels for 0%

profile of v12, /device:TPU:0, one launch (start us, length us, event | category | flops | bytes accessed | tf_op | source)
XLA Modules:
  0.0 73.6 jit_solution(3415447791084341573)
XLA Ops:
  0.0 0.8 %convert_element_type.69 = f32[24]{0:T(128)S(1)} convert(s32[24]{0:T(128)} %param.15) | non-fusion elementwise | flops 24 | bytes 192 | tf_op jit(solution)/shard_map/convert_element_type | solution.py:23
  0.8 0.8 %reshape.258 = f32[24,3,128]{2,1,0:T(4,128)S(1)} reshape(bf16[24,384]{1,0:T(8,128)(2,1)} %param.13) | data formatting | bytes 55296 | tf_op jit(solution)/shard_map/convert_element_type | solution.py:130
  1.5 0.1 multiply_cosine_fusion
  1.7 0.1 subtract_convert_fusion
  1.8 0.1 pad_maximum_fusion.6
  1.9 0.7 fusion.32
  2.6 0.5 collective-permute-start
  3.2 2.6 %collective-permute-start.1 = (bf16[2,24,384]{2,1,0:T(8,128)(2,1)S(1)}, bf16[2,24,384]{2,1,0:T(8,128)(2,1)S(1)}, u32[]{:S(2)}, u32[]{:S(2)}) collective-permute-start(bf16[2,24,384]{2,1,0:T(8,128)(2,1)S(1)} %get-tuple-element.25), channel_id=1, source_target_pairs={{0,2},{1,3},{2,0},{3,1},{4,6},{5,7},{6,4},{7,5},{8,10},{9,11},{10,... | collective-permute-start | bytes 110600 | tf_op jit(solution)/shard_map/ppermute | solution.py:134
  5.7 1.4 %collective-permute-start.2 = (bf16[2,24,384]{2,1,0:T(8,128)(2,1)S(1)}, bf16[2,24,384]{2,1,0:T(8,128)(2,1)S(1)}, u32[]{:S(2)}, u32[]{:S(2)}) collective-permute-start(bf16[2,24,384]{2,1,0:T(8,128)(2,1)S(1)} %get-tuple-element.25), channel_id=1, source_target_pairs={{0,3},{1,0},{2,1},{3,2},{4,7},{5,4},{6,5},{7,6},{8,11},{9,8},{10,9... | collective-permute-start | bytes 110600 | tf_op jit(solution)/shard_map/ppermute | solution.py:134
  7.1 0.7 copy.118
  7.9 0.1 reduce.2
  8.0 0.7 bitcast_subtract_fusion.1
  8.7 1.7 %fusion.34 = (bf16[768,1,2,128]{3,2,1,0:T(2,128)(2,1)S(1)}, bf16[768,1,2,128]{3,2,1,0:T(2,128)(2,1)S(1)}) fusion(bf16[768,2,2,128]{3,2,1,0:T(2,128)(2,1)} %param.17), kind=kLoop, calls=%fused_computation.94 | loop fusion | bytes 1572864 | tf_op jit(solution)/shard_map/slice | solution.py:164
  10.4 0.1 slice_reduce_fusion
  10.5 0.1 subtract_convert_fusion.1
  10.6 0.1 select_reduce_fusion
  10.8 0.1 maximum_bitcast_fusion
  11.1 0.6 gather_fusion
  11.9 0.5 fusion.35
  12.3 0.1 concatenate.33
  12.5 0.3 fusion.3
  12.8 0.7 fusion.2
  13.5 0.1 concatenate.34
  13.6 0.2 pad_maximum_fusion
  13.9 0.4 collective-permute-start.4
  14.3 1.3 %collective-permute-start.5 = (f32[24,3,130]{2,0,1:T(8,128)S(1)}, f32[24,3,130]{2,0,1:T(8,128)S(1)}, u32[]{:S(2)}, u32[]{:S(2)}) collective-permute-start(f32[24,3,130]{2,0,1:T(8,128)S(1)} %get-tuple-element.15), channel_id=1, source_target_pairs={{0,3},{1,0},{2,1},{3,2},{4,7},{5,4},{6,5},{7,6},{8,11},{9,8},{10,9... | collective-permute-start | bytes 112328 | tf_op jit(solution)/shard_map/ppermute | solution.py:189
  15.7 0.2 fusion.12
  15.8 0.1 copy.133
  16.0 1.9 %collective-permute-done.3 = f32[24,3,130]{2,0,1:T(8,128)S(1)} collective-permute-done((f32[24,3,130]{2,0,1:T(8,128)S(1)}, f32[24,3,130]{2,0,1:T(8,128)S(1)}, u32[]{:S(2)}, u32[]{:S(2)}) %collective-permute-start.3) | collective-permute-done | bytes 37472 | tf_op jit(solution)/shard_map/ppermute | solution.py:189
  17.8 1.3 %collective-permute-done.4 = f32[24,3,130]{2,0,1:T(8,128)S(1)} collective-permute-done((f32[24,3,130]{2,0,1:T(8,128)S(1)}, f32[24,3,130]{2,0,1:T(8,128)S(1)}, u32[]{:S(2)}, u32[]{:S(2)}) %collective-permute-start.4) | collective-permute-done | bytes 37472 | tf_op jit(solution)/shard_map/ppermute | solution.py:189
  19.2 0.1 slice_reduce_fusion.1
  19.3 0.1 copy.136
  19.5 0.1 fusion.10
  19.7 0.1 copy.127
  19.9 0.3 fusion.14
  20.2 8.2 %all-gather = f32[96,1536]{1,0:T(8,128)S(1)} all-gather(f32[24,1536]{1,0:T(8,128)S(1)} %fusion.14), channel_id=2, replica_groups=mesh['req'=8,'tp'=4] {'tp'}, dimensions={0}, use_global_device_ids=true | all-gather | bytes 737280 | tf_op jit(solution)/shard_map/all_gather | solution.py:212
  28.4 0.1 fusion.9
  28.6 1.6 %collective-permute-start.6 = (bf16[24,1664]{1,0:T(8,128)(2,1)S(1)}, bf16[24,1664]{1,0:T(8,128)(2,1)S(1)}, u32[]{:S(2)}, u32[]{:S(2)}) collective-permute-start(bf16[24,1664]{1,0:T(8,128)(2,1)S(1)} %pad_maximum_fusion.4), channel_id=1, source_target_pairs={{28,0},{21,1},{14,2},{7,3},{0,4},{25,5},{18,6},{11,7},{4,8},{29,9}... | collective-permute-start | bytes 239624 | tf_op jit(solution)/shard_map/ppermute | solution.py:246
  30.2 3.5 %collective-permute-start.7 = (bf16[24,1664]{1,0:T(8,128)(2,1)S(1)}, bf16[24,1664]{1,0:T(8,128)(2,1)S(1)}, u32[]{:S(2)}, u32[]{:S(2)}) collective-permute-start(bf16[24,1664]{1,0:T(8,128)(2,1)S(1)} %pad_maximum_fusion.4), channel_id=1, source_target_pairs={{24,0},{17,1},{10,2},{3,3},{28,4},{21,5},{14,6},{7,7},{0,8},{25,9}... | collective-permute-start | bytes 239624 | tf_op jit(solution)/shard_map/ppermute | solution.py:246
  33.7 0.5 and_select_fusion.dest_ref
  34.2 1.9 %collective-permute-done.6 = bf16[24,1664]{1,0:T(8,128)(2,1)S(1)} collective-permute-done((bf16[24,1664]{1,0:T(8,128)(2,1)S(1)}, bf16[24,1664]{1,0:T(8,128)(2,1)S(1)}, u32[]{:S(2)}, u32[]{:S(2)}) %collective-permute-start.6) | collective-permute-done | bytes 79904 | tf_op jit(solution)/shard_map/ppermute | solution.py:246
  36.2 2.8 %collective-permute-done.7 = bf16[24,1664]{1,0:T(8,128)(2,1)S(1)} collective-permute-done((bf16[24,1664]{1,0:T(8,128)(2,1)S(1)}, bf16[24,1664]{1,0:T(8,128)(2,1)S(1)}, u32[]{:S(2)}, u32[]{:S(2)}) %collective-permute-start.7) | collective-permute-done | bytes 79904 | tf_op jit(solution)/shard_map/ppermute | solution.py:246
  39.0 7.3 %all-gather.1 = bf16[8,24,1664]{2,1,0:T(8,128)(2,1)} all-gather(bf16[2,24,1664]{2,1,0:T(8,128)(2,1)S(1)} %pad_maximum_fusion.2), channel_id=3, replica_groups=mesh['req'=8,'tp'=4] {'tp'}, dimensions={0}, use_global_device_ids=true | all-gather | bytes 798720 | tf_op jit(solution)/shard_map/all_gather | solution.py:247
  46.3 6.4 %shard_map.118 = bf16[32,24,384]{2,1,0:T(8,128)(2,1)} custom-call(s32[1]{0:T(128)} %bitcast.36.offset_ref, s32[8]{0:T(128)} %and_select_fusion.dest_ref, bf16[192,1664]{1,0:T(8,128)(2,1)} %bitcast.106, bf16[4,2,192,1536]{3,2,1,0:T(8,128)(2,1)} %bitcast.105, bf16[4,192,1536]{2,1,0:T(8,128)(2,1)} %dn_ref.1), custom_call_target="tpu_custom_call" | custom-call | tf_op jit(solution)/shard_map/pallas_call | solution.py:82
  52.7 3.4 %all-to-all-start = ((bf16[32,24,384]{2,1,0:T(8,128)(2,1)}), bf16[32,24,384]{2,1,0:T(8,128)(2,1)S(1)}, u32[]{:S(2)}, u32[]{:S(2)}) async-start(bf16[32,24,384]{2,1,0:T(8,128)(2,1)} %shard_map.118), calls=%async_computation | async-start | bytes 1179648 | tf_op jit(solution)/shard_map/all_to_all | solution.py:265
  56.1 16.8 %all-to-all-done = bf16[32,24,384]{2,1,0:T(8,128)(2,1)S(1)} async-done(((bf16[32,24,384]{2,1,0:T(8,128)(2,1)}), bf16[32,24,384]{2,1,0:T(8,128)(2,1)S(1)}, u32[]{:S(2)}, u32[]{:S(2)}) %all-to-all-start) | async-done | bytes 589856 | tf_op jit(solution)/shard_map/all_to_all | solution.py:265
  72.9 0.1 convert_reduce_fusion
  73.0 0.6 add_convert_fusion.1
  (45 shorter events, 0.9 us)
Async XLA Ops:
  0.0 19.9 %copy-start = (bf16[384,1536]{1,0:T(8,128)(2,1)S(1)}, bf16[384,1536]{1,0:T(8,128)(2,1)}, u32[]{:S(2)}) copy-start(bf16[384,1536]{1,0:T(8,128)(2,1)} %param.18) | copy-start | bytes 3538948
  0.0 10.4 %copy-start.1 = (bf16[24,2,256]{2,1,0:T(2,128)(2,1)S(1)}, bf16[24,2,256]{2,1,0:T(2,128)(2,1)}, u32[]{:S(2)}) copy-start(bf16[24,2,256]{2,1,0:T(2,128)(2,1)} %param.14) | copy-start | bytes 73732
  0.8 9.8 %copy-start.3 = (f32[24,4]{0,1:T(4,128)S(1)}, f32[24,4]{0,1:T(4,128)}, u32[]{:S(2)}) copy-start(f32[24,4]{0,1:T(4,128)} %param.21) | copy-start | bytes 1156
  0.8 9.8 %copy-start.4 = (s32[24,4]{0,1:T(4,128)S(1)}, s32[24,4]{0,1:T(4,128)}, u32[]{:S(2)}) copy-start(s32[24,4]{0,1:T(4,128)} %param.20) | copy-start | bytes 1156
  2.6 8.4 %collective-permute-start = (bf16[2,24,384]{2,1,0:T(8,128)(2,1)S(1)}, bf16[2,24,384]{2,1,0:T(8,128)(2,1)S(1)}, u32[]{:S(2)}, u32[]{:S(2)}) collective-permute-start(bf16[2,24,384]{2,1,0:T(8,128)(2,1)S(1)} %get-tuple-element.25), channel_id=1, source_target_pairs={{0,1},{1,2},{2,3},{3,0},{4,5},{5,6},{6,7},{7,4},{8,9},{9,10},{10,1... | collective-permute-start | bytes 110600 | tf_op jit(solution)/shard_map/ppermute | solution.py:134
  3.2 7.9 %collective-permute-start.1 = (bf16[2,24,384]{2,1,0:T(8,128)(2,1)S(1)}, bf16[2,24,384]{2,1,0:T(8,128)(2,1)S(1)}, u32[]{:S(2)}, u32[]{:S(2)}) collective-permute-start(bf16[2,24,384]{2,1,0:T(8,128)(2,1)S(1)} %get-tuple-element.25), channel_id=1, source_target_pairs={{0,2},{1,3},{2,0},{3,1},{4,6},{5,7},{6,4},{7,5},{8,10},{9,11},{10,... | collective-permute-start | bytes 110600 | tf_op jit(solution)/shard_map/ppermute | solution.py:134
  5.7 5.4 %collective-permute-start.2 = (bf16[2,24,384]{2,1,0:T(8,128)(2,1)S(1)}, bf16[2,24,384]{2,1,0:T(8,128)(2,1)S(1)}, u32[]{:S(2)}, u32[]{:S(2)}) collective-permute-start(bf16[2,24,384]{2,1,0:T(8,128)(2,1)S(1)} %get-tuple-element.25), channel_id=1, source_target_pairs={{0,3},{1,0},{2,1},{3,2},{4,7},{5,4},{6,5},{7,6},{8,11},{9,8},{10,9... | collective-permute-start | bytes 110600 | tf_op jit(solution)/shard_map/ppermute | solution.py:134
  13.9 4.0 %collective-permute-start.3 = (f32[24,3,130]{2,0,1:T(8,128)S(1)}, f32[24,3,130]{2,0,1:T(8,128)S(1)}, u32[]{:S(2)}, u32[]{:S(2)}) collective-permute-start(f32[24,3,130]{2,0,1:T(8,128)S(1)} %get-tuple-element.17), channel_id=1, source_target_pairs={{0,1},{1,2},{2,3},{3,0},{4,5},{5,6},{6,7},{7,4},{8,9},{9,10},{10,1... | collective-permute-start | bytes 112328 | tf_op jit(solution)/shard_map/ppermute | solution.py:189
  13.9 5.2 %collective-permute-start.4 = (f32[24,3,130]{2,0,1:T(8,128)S(1)}, f32[24,3,130]{2,0,1:T(8,128)S(1)}, u32[]{:S(2)}, u32[]{:S(2)}) collective-permute-start(f32[24,3,130]{2,0,1:T(8,128)S(1)} %get-tuple-element.16), channel_id=1, source_target_pairs={{0,2},{1,3},{2,0},{3,1},{4,6},{5,7},{6,4},{7,5},{8,10},{9,11},{10,... | collective-permute-start | bytes 112328 | tf_op jit(solution)/shard_map/ppermute | solution.py:189
  14.3 4.8 %collective-permute-start.5 = (f32[24,3,130]{2,0,1:T(8,128)S(1)}, f32[24,3,130]{2,0,1:T(8,128)S(1)}, u32[]{:S(2)}, u32[]{:S(2)}) collective-permute-start(f32[24,3,130]{2,0,1:T(8,128)S(1)} %get-tuple-element.15), channel_id=1, source_target_pairs={{0,3},{1,0},{2,1},{3,2},{4,7},{5,4},{6,5},{7,6},{8,11},{9,8},{10,9... | collective-permute-start | bytes 112328 | tf_op jit(solution)/shard_map/ppermute | solution.py:189
  20.2 8.3 %copy-start.2 = (f32[1536]{0:T(1024)S(1)}, f32[1536]{0:T(1024)}, u32[]{:S(2)}) copy-start(f32[1536]{0:T(1024)} %param.19) | copy-start | bytes 18436
  28.6 7.5 %collective-permute-start.6 = (bf16[24,1664]{1,0:T(8,128)(2,1)S(1)}, bf16[24,1664]{1,0:T(8,128)(2,1)S(1)}, u32[]{:S(2)}, u32[]{:S(2)}) collective-permute-start(bf16[24,1664]{1,0:T(8,128)(2,1)S(1)} %pad_maximum_fusion.4), channel_id=1, source_target_pairs={{28,0},{21,1},{14,2},{7,3},{0,4},{25,5},{18,6},{11,7},{4,8},{29,9}... | collective-permute-start | bytes 239624 | tf_op jit(solution)/shard_map/ppermute | solution.py:246
  30.2 8.8 %collective-permute-start.7 = (bf16[24,1664]{1,0:T(8,128)(2,1)S(1)}, bf16[24,1664]{1,0:T(8,128)(2,1)S(1)}, u32[]{:S(2)}, u32[]{:S(2)}) collective-permute-start(bf16[24,1664]{1,0:T(8,128)(2,1)S(1)} %pad_maximum_fusion.4), channel_id=1, source_target_pairs={{24,0},{17,1},{10,2},{3,3},{28,4},{21,5},{14,6},{7,7},{0,8},{25,9}... | collective-permute-start | bytes 239624 | tf_op jit(solution)/shard_map/ppermute | solution.py:246
  52.7 20.2 %all-to-all-start = ((bf16[32,24,384]{2,1,0:T(8,128)(2,1)}), bf16[32,24,384]{2,1,0:T(8,128)(2,1)S(1)}, u32[]{:S(2)}, u32[]{:S(2)}) async-start(bf16[32,24,384]{2,1,0:T(8,128)(2,1)} %shard_map.118), calls=%async_computation | async-start | bytes 1179648 | tf_op jit(solution)/shard_map/all_to_all | solution.py:265

commit v13 on v11

--- a/solution.py
+++ b/solution.py
@@ -203,7 +203,9 @@
     )
 
     partial_proj = jnp.dot(attention_output, out_proj, preferred_element_type=jnp.float32)
-    projected = jnp.sum(lax.all_gather(partial_proj, "tp", axis=0), axis=0)
+    projected = jnp.sum(
+        lax.all_gather(partial_proj.astype(jnp.bfloat16), "tp", axis=0).astype(jnp.float32), axis=0
+    )
     residual = hidden_full.astype(jnp.float32) + projected
     mean_square = jnp.mean(residual * residual, axis=1, keepdims=True)
     normed = (residual * lax.rsqrt(mean_square + norm_eps) * norm_gain[None, :]).astype(jnp.bfloat16)

time: 73.6 us -> 71.8 us (0.976)
  blocking collectives: 22.3 us -> 20.6 us
    all_gather x1, blocking collectives: 8.02 us -> 6.29 us  [per_device(): lax.all_gather(partial_proj.astype(jnp.bfloat16), 'tp', axis=0)]
where the time goes in v13:
time: 71.8 us; the launch traced here: 71.4 us
  waiting for transfers between devices  22.9 us (32%)
  blocking collectives  20.6 us (29%)
  starting transfers between devices  12.3 us (17%)
  Pallas kernels  6.41 us (9%)
  other arithmetic  5.08 us (7%)
  local copies, waits for them, and re-layouts  2.16 us (3%)
  matrix products  1.67 us (2%)
    all_to_all x1, waiting for transfers between devices, per_device(): mixed = lax.all_to_all(mixed, ('req', 'tp'), 0, 0, tiled=True)  16.8 us
    all_gather x1, blocking collectives, gather_req(): shared = lax.all_gather(jnp.stack(fetched, axis=0), 'tp', axis=0)  7.65 us
    all_gather x1, blocking collectives, per_device(): gathered = lax.all_gather(packed, 'tp', axis=0)  6.62 us
    pallas_call x1, Pallas kernels, expert_mix(): pl.pallas_call(body, grid=(group_total // tile_groups, local_count), in_s...  6.41 us
    all_gather x1, blocking collectives, per_device(): lax.all_gather(partial_proj.astype(jnp.bfloat16), 'tp', axis=0)  6.29 us
    ppermute x2, starting transfers between devices, gather_req(): fetched.append(lax.ppermute(value, ('req', 'tp'), pairs))  5.38 us
    ppermute x2, waiting for transfers between devices, gather_req(): fetched.append(lax.ppermute(value, ('req', 'tp'), pairs))  4.76 us
    all_to_all x1, starting transfers between devices, per_device(): mixed = lax.all_to_all(mixed, ('req', 'tp'), 0, 0, tiled=True)  3.57 us
  transfers between devices with their start and end apart: 6, of which 5 were waited for; matrix products, arithmetic and copies ran while one was open for 2% of the time, Pallas kernels for 0%

profile of v13, /device:TPU:0, one launch (start us, length us, event | category | flops | bytes accessed | tf_op | source)
XLA Modules:
  0.0 71.4 jit_solution(597635214783435380)
XLA Ops:
  0.0 0.8 %convert_element_type.75 = f32[24]{0:T(128)S(1)} convert(s32[24]{0:T(128)} %param.15) | non-fusion elementwise | flops 24 | bytes 192 | tf_op jit(solution)/shard_map/convert_element_type | solution.py:23
  0.8 0.7 %reshape.218 = f32[24,3,128]{2,1,0:T(4,128)S(1)} reshape(bf16[24,384]{1,0:T(8,128)(2,1)} %param.13) | data formatting | bytes 55296 | tf_op jit(solution)/shard_map/convert_element_type | solution.py:130
  1.6 0.1 multiply_cosine_fusion
  1.7 0.1 subtract_convert_fusion
  1.8 0.1 pad_maximum_fusion.5
  1.9 0.7 %pad_maximum_fusion.4 = bf16[2,24,384]{2,1,0:T(8,128)(2,1)S(1)} fusion(bf16[1,24,384]{2,1,0:T(8,128)(2,1)} %bitcast.117, bf16[1,24,384]{2,1,0:T(8,128)(2,1)S(1)} %convert_element_type.76), kind=kLoop, calls=%fused_computation.38 | loop fusion | flops 18432 | bytes 73728 | tf_op jit(solution)/shard_map/stack | solution.py:132
  2.7 6.6 %all-gather = bf16[8,24,384]{2,1,0:T(8,128)(2,1)S(1)} all-gather(bf16[2,24,384]{2,1,0:T(8,128)(2,1)S(1)} %pad_maximum_fusion.4), channel_id=2, replica_groups=mesh['req'=8,'tp'=4] {'tp'}, dimensions={0}, use_global_device_ids=true | all-gather | bytes 184320 | tf_op jit(solution)/shard_map/all_gather | solution.py:133
  9.4 0.1 copy.119
  9.6 0.1 reduce.2
  9.7 0.5 fusion.30
  10.2 0.1 compare_and_fusion
  10.3 0.5 fusion.31
  10.8 0.1 concatenate.33
  10.9 0.3 fusion.3
  11.3 0.7 fusion.2
  12.0 0.1 concatenate.34
  12.1 0.2 pad_maximum_fusion
  12.4 0.4 collective-permute-start
  12.8 1.8 %collective-permute-start.1 = (f32[24,3,130]{2,0,1:T(8,128)S(1)}, f32[24,3,130]{2,0,1:T(8,128)S(1)}, u32[]{:S(2)}, u32[]{:S(2)}) collective-permute-start(f32[24,3,130]{2,0,1:T(8,128)S(1)} %get-tuple-element.16), channel_id=1, source_target_pairs={{0,2},{1,3},{2,0},{3,1},{4,6},{5,7},{6,4},{7,5},{8,10},{9,11},{10,... | collective-permute-start | bytes 112328 | tf_op jit(solution)/shard_map/ppermute | solution.py:183
  14.6 1.1 %collective-permute-start.2 = (f32[24,3,130]{2,0,1:T(8,128)S(1)}, f32[24,3,130]{2,0,1:T(8,128)S(1)}, u32[]{:S(2)}, u32[]{:S(2)}) collective-permute-start(f32[24,3,130]{2,0,1:T(8,128)S(1)} %get-tuple-element.15), channel_id=1, source_target_pairs={{0,3},{1,0},{2,1},{3,2},{4,7},{5,4},{6,5},{7,6},{8,11},{9,8},{10,9... | collective-permute-start | bytes 112328 | tf_op jit(solution)/shard_map/ppermute | solution.py:183
  15.7 0.1 slice_reduce_fusion
  15.8 0.1 subtract_convert_fusion.1
  15.9 0.1 maximum_bitcast_fusion
  16.0 0.2 fusion.12
  16.2 0.1 copy.134
  16.3 0.1 select_reduce_fusion
  16.5 0.1 fusion.22
  16.6 0.7 collective-permute-done.1
  17.3 0.6 collective-permute-done.2
  18.0 0.1 slice_reduce_fusion.1
  18.1 0.1 copy.138
  18.3 0.1 fusion.10
  18.4 0.1 copy.128
  18.7 0.3 convolution_convert_fusion
  19.0 6.3 %all-gather.1 = bf16[96,1536]{1,0:T(8,128)(2,1)S(1)} all-gather(bf16[24,1536]{1,0:T(8,128)(2,1)S(1)} %convolution_convert_fusion), channel_id=3, replica_groups=mesh['req'=8,'tp'=4] {'tp'}, dimensions={0}, use_global_device_ids=true | all-gather | bytes 368640 | tf_op jit(solution)/shard_map/all_gather | solution.py:207
  25.3 0.1 fusion.9
  25.5 0.1 multiply_convert_fusion
  25.6 1.9 %collective-permute-start.3 = (bf16[24,1664]{1,0:T(8,128)(2,1)S(1)}, bf16[24,1664]{1,0:T(8,128)(2,1)S(1)}, u32[]{:S(2)}, u32[]{:S(2)}) collective-permute-start(bf16[24,1664]{1,0:T(8,128)(2,1)S(1)} %pad_maximum_fusion.3), channel_id=1, source_target_pairs={{28,0},{21,1},{14,2},{7,3},{0,4},{25,5},{18,6},{11,7},{4,8},{29,9}... | collective-permute-start | bytes 239624 | tf_op jit(solution)/shard_map/ppermute | solution.py:242
  27.5 3.5 %collective-permute-start.4 = (bf16[24,1664]{1,0:T(8,128)(2,1)S(1)}, bf16[24,1664]{1,0:T(8,128)(2,1)S(1)}, u32[]{:S(2)}, u32[]{:S(2)}) collective-permute-start(bf16[24,1664]{1,0:T(8,128)(2,1)S(1)} %pad_maximum_fusion.3), channel_id=1, source_target_pairs={{24,0},{17,1},{10,2},{3,3},{28,4},{21,5},{14,6},{7,7},{0,8},{25,9}... | collective-permute-start | bytes 239624 | tf_op jit(solution)/shard_map/ppermute | solution.py:242
  30.9 0.5 and_select_fusion.dest_ref
  31.5 1.9 %collective-permute-done.3 = bf16[24,1664]{1,0:T(8,128)(2,1)S(1)} collective-permute-done((bf16[24,1664]{1,0:T(8,128)(2,1)S(1)}, bf16[24,1664]{1,0:T(8,128)(2,1)S(1)}, u32[]{:S(2)}, u32[]{:S(2)}) %collective-permute-start.3) | collective-permute-done | bytes 79904 | tf_op jit(solution)/shard_map/ppermute | solution.py:242
  33.4 2.8 %collective-permute-done.4 = bf16[24,1664]{1,0:T(8,128)(2,1)S(1)} collective-permute-done((bf16[24,1664]{1,0:T(8,128)(2,1)S(1)}, bf16[24,1664]{1,0:T(8,128)(2,1)S(1)}, u32[]{:S(2)}, u32[]{:S(2)}) %collective-permute-start.4) | collective-permute-done | bytes 79904 | tf_op jit(solution)/shard_map/ppermute | solution.py:242
  36.3 7.7 %all-gather.2 = bf16[8,24,1664]{2,1,0:T(8,128)(2,1)} all-gather(bf16[2,24,1664]{2,1,0:T(8,128)(2,1)S(1)} %pad_maximum_fusion.2), channel_id=4, replica_groups=mesh['req'=8,'tp'=4] {'tp'}, dimensions={0}, use_global_device_ids=true | all-gather | bytes 798720 | tf_op jit(solution)/shard_map/all_gather | solution.py:243
  43.9 6.4 %shard_map.118 = bf16[32,24,384]{2,1,0:T(8,128)(2,1)} custom-call(s32[1]{0:T(128)} %bitcast.32.offset_ref, s32[8]{0:T(128)} %and_select_fusion.dest_ref, bf16[192,1664]{1,0:T(8,128)(2,1)} %bitcast.102, bf16[4,2,192,1536]{3,2,1,0:T(8,128)(2,1)} %bitcast.101, bf16[4,192,1536]{2,1,0:T(8,128)(2,1)} %dn_ref.1), custom_call_target="tpu_custom_call" | custom-call | tf_op jit(solution)/shard_map/pallas_call | solution.py:82
  50.4 3.6 %all-to-all-start = ((bf16[32,24,384]{2,1,0:T(8,128)(2,1)}), bf16[32,24,384]{2,1,0:T(8,128)(2,1)S(1)}, u32[]{:S(2)}, u32[]{:S(2)}) async-start(bf16[32,24,384]{2,1,0:T(8,128)(2,1)} %shard_map.118), calls=%async_computation | async-start | bytes 1179648 | tf_op jit(solution)/shard_map/all_to_all | solution.py:261
  53.9 16.8 %all-to-all-done = bf16[32,24,384]{2,1,0:T(8,128)(2,1)S(1)} async-done(((bf16[32,24,384]{2,1,0:T(8,128)(2,1)}), bf16[32,24,384]{2,1,0:T(8,128)(2,1)S(1)}, u32[]{:S(2)}, u32[]{:S(2)}) %all-to-all-start) | async-done | bytes 589856 | tf_op jit(solution)/shard_map/all_to_all | solution.py:261
  70.7 0.1 convert_reduce_fusion
  70.8 0.6 add_convert_fusion.1
  (40 shorter events, 0.5 us)
Async XLA Ops:
  0.0 18.7 %copy-start = (bf16[384,1536]{1,0:T(8,128)(2,1)S(1)}, bf16[384,1536]{1,0:T(8,128)(2,1)}, u32[]{:S(2)}) copy-start(bf16[384,1536]{1,0:T(8,128)(2,1)} %param.18) | copy-start | bytes 3538948
  0.0 9.4 %copy-start.6 = (s32[1,24]{1,0:T(1,128)S(1)}, s32[1,24]{1,0:T(1,128)}, u32[]{:S(2)}) copy-start(s32[1,24]{1,0:T(1,128)} %param.16) | copy-start | bytes 292
  0.0 9.7 %copy-start.1 = (bf16[768,2,2,128]{3,2,1,0:T(2,128)(2,1)S(1)}, bf16[768,2,2,128]{3,2,1,0:T(2,128)(2,1)}, u32[]{:S(2)}) copy-start(bf16[768,2,2,128]{3,2,1,0:T(2,128)(2,1)} %param.17) | copy-start | bytes 2359300
  11.2 4.5 %copy-start.2 = (bf16[24,2,256]{2,1,0:T(2,128)(2,1)S(1)}, bf16[24,2,256]{2,1,0:T(2,128)(2,1)}, u32[]{:S(2)}) copy-start(bf16[24,2,256]{2,1,0:T(2,128)(2,1)} %param.14) | copy-start | bytes 73732
  12.0 4.4 %copy-start.4 = (f32[24,4]{0,1:T(4,128)S(1)}, f32[24,4]{0,1:T(4,128)}, u32[]{:S(2)}) copy-start(f32[24,4]{0,1:T(4,128)} %param.21) | copy-start | bytes 1156
  12.0 4.4 %copy-start.5 = (s32[24,4]{0,1:T(4,128)S(1)}, s32[24,4]{0,1:T(4,128)}, u32[]{:S(2)}) copy-start(s32[24,4]{0,1:T(4,128)} %param.20) | copy-start | bytes 1156
  12.4 4.2 %collective-permute-start = (f32[24,3,130]{2,0,1:T(8,128)S(1)}, f32[24,3,130]{2,0,1:T(8,128)S(1)}, u32[]{:S(2)}, u32[]{:S(2)}) collective-permute-start(f32[24,3,130]{2,0,1:T(8,128)S(1)} %get-tuple-element.17), channel_id=1, source_target_pairs={{0,1},{1,2},{2,3},{3,0},{4,5},{5,6},{6,7},{7,4},{8,9},{9,10},{10,1... | collective-permute-start | bytes 112328 | tf_op jit(solution)/shard_map/ppermute | solution.py:183
  12.8 4.5 %collective-permute-start.1 = (f32[24,3,130]{2,0,1:T(8,128)S(1)}, f32[24,3,130]{2,0,1:T(8,128)S(1)}, u32[]{:S(2)}, u32[]{:S(2)}) collective-permute-start(f32[24,3,130]{2,0,1:T(8,128)S(1)} %get-tuple-element.16), channel_id=1, source_target_pairs={{0,2},{1,3},{2,0},{3,1},{4,6},{5,7},{6,4},{7,5},{8,10},{9,11},{10,... | collective-permute-start | bytes 112328 | tf_op jit(solution)/shard_map/ppermute | solution.py:183
  14.6 3.3 %collective-permute-start.2 = (f32[24,3,130]{2,0,1:T(8,128)S(1)}, f32[24,3,130]{2,0,1:T(8,128)S(1)}, u32[]{:S(2)}, u32[]{:S(2)}) collective-permute-start(f32[24,3,130]{2,0,1:T(8,128)S(1)} %get-tuple-element.15), channel_id=1, source_target_pairs={{0,3},{1,0},{2,1},{3,2},{4,7},{5,4},{6,5},{7,6},{8,11},{9,8},{10,9... | collective-permute-start | bytes 112328 | tf_op jit(solution)/shard_map/ppermute | solution.py:183
  18.6 6.8 %copy-start.3 = (f32[1536]{0:T(1024)S(1)}, f32[1536]{0:T(1024)}, u32[]{:S(2)}) copy-start(f32[1536]{0:T(1024)} %param.19) | copy-start | bytes 18436
  25.6 7.9 %collective-permute-start.3 = (bf16[24,1664]{1,0:T(8,128)(2,1)S(1)}, bf16[24,1664]{1,0:T(8,128)(2,1)S(1)}, u32[]{:S(2)}, u32[]{:S(2)}) collective-permute-start(bf16[24,1664]{1,0:T(8,128)(2,1)S(1)} %pad_maximum_fusion.3), channel_id=1, source_target_pairs={{28,0},{21,1},{14,2},{7,3},{0,4},{25,5},{18,6},{11,7},{4,8},{29,9}... | collective-permute-start | bytes 239624 | tf_op jit(solution)/shard_map/ppermute | solution.py:242
  27.5 8.8 %collective-permute-start.4 = (bf16[24,1664]{1,0:T(8,128)(2,1)S(1)}, bf16[24,1664]{1,0:T(8,128)(2,1)S(1)}, u32[]{:S(2)}, u32[]{:S(2)}) collective-permute-start(bf16[24,1664]{1,0:T(8,128)(2,1)S(1)} %pad_maximum_fusion.3), channel_id=1, source_target_pairs={{24,0},{17,1},{10,2},{3,3},{28,4},{21,5},{14,6},{7,7},{0,8},{25,9}... | collective-permute-start | bytes 239624 | tf_op jit(solution)/shard_map/ppermute | solution.py:242
  50.4 20.4 %all-to-all-start = ((bf16[32,24,384]{2,1,0:T(8,128)(2,1)}), bf16[32,24,384]{2,1,0:T(8,128)(2,1)S(1)}, u32[]{:S(2)}, u32[]{:S(2)}) async-start(bf16[32,24,384]{2,1,0:T(8,128)(2,1)} %shard_map.118), calls=%async_computation | async-start | bytes 1179648 | tf_op jit(solution)/shard_map/all_to_all | solution.py:261

commit v14 on v13

--- a/solution.py
+++ b/solution.py
@@ -42,8 +42,11 @@
 
     x = x_ref[:, :width]
     contract_rows = (((1,), (1,)), ((), ()))
-    gate_part = lax.dot_general(x, gu_ref[0, 0], contract_rows, preferred_element_type=jnp.float32)
-    up_part = lax.dot_general(x, gu_ref[0, 1], contract_rows, preferred_element_type=jnp.float32)
+    hidden = gu_ref.shape[2]
+    both = gu_ref[0].reshape(2 * hidden, gu_ref.shape[3])
+    both_part = lax.dot_general(x, both, contract_rows, preferred_element_type=jnp.float32)
+    gate_part = both_part[:, :hidden]
+    up_part = both_part[:, hidden:]
     activation = (jnp.maximum(gate_part, 0.0) * up_part).astype(jnp.bfloat16)
     produced = jnp.dot(activation, dn_ref[0], preferred_element_type=jnp.float32)
     produced = produced.astype(jnp.bfloat16).astype(jnp.float32)

time: 71.8 us -> 72.5 us (level)
  no operation moved by 1% of the time
where the time goes in v14:
time: 72.5 us; the launch traced here: 72.1 us
  waiting for transfers between devices  22.9 us (32%)
  blocking collectives  20.6 us (28%)
  starting transfers between devices  12.3 us (17%)
  Pallas kernels  7.06 us (10%)
  other arithmetic  5.08 us (7%)
  local copies, waits for them, and re-layouts  2.16 us (3%)
  matrix products  1.67 us (2%)
    all_to_all x1, waiting for transfers between devices, per_device(): mixed = lax.all_to_all(mixed, ('req', 'tp'), 0, 0, tiled=True)  16.8 us
    all_gather x1, blocking collectives, gather_req(): shared = lax.all_gather(jnp.stack(fetched, axis=0), 'tp', axis=0)  7.65 us
    pallas_call x1, Pallas kernels, expert_mix(): pl.pallas_call(body, grid=(group_total // tile_groups, local_count), in_s...  7.06 us
    all_gather x1, blocking collectives, per_device(): gathered = lax.all_gather(packed, 'tp', axis=0)  6.62 us
    all_gather x1, blocking collectives, per_device(): lax.all_gather(partial_proj.astype(jnp.bfloat16), 'tp', axis=0)  6.29 us
    ppermute x2, starting transfers between devices, gather_req(): fetched.append(lax.ppermute(value, ('req', 'tp'), pairs))  5.38 us
    ppermute x2, waiting for transfers between devices, gather_req(): fetched.append(lax.ppermute(value, ('req', 'tp'), pairs))  4.76 us
    all_to_all x1, starting transfers between devices, per_device(): mixed = lax.all_to_all(mixed, ('req', 'tp'), 0, 0, tiled=True)  3.56 us
  transfers between devices with their start and end apart: 6, of which 5 were waited for; matrix products, arithmetic and copies ran while one was open for 2% of the time, Pallas kernels for 0%

profile of v14, /device:TPU:0, one launch (start us, length us, event | category | flops | bytes accessed | tf_op | source)
XLA Modules:
  0.0 72.1 jit_solution(14939948601365242641)
XLA Ops:
  0.0 0.8 %convert_element_type.75 = f32[24]{0:T(128)S(1)} convert(s32[24]{0:T(128)} %param.15) | non-fusion elementwise | flops 24 | bytes 192 | tf_op jit(solution)/shard_map/convert_element_type | solution.py:23
  0.8 0.7 %reshape.218 = f32[24,3,128]{2,1,0:T(4,128)S(1)} reshape(bf16[24,384]{1,0:T(8,128)(2,1)} %param.13) | data formatting | bytes 55296 | tf_op jit(solution)/shard_map/convert_element_type | solution.py:133
  1.6 0.1 multiply_cosine_fusion
  1.7 0.1 subtract_convert_fusion
  1.8 0.1 pad_maximum_fusion.5
  1.9 0.7 %pad_maximum_fusion.4 = bf16[2,24,384]{2,1,0:T(8,128)(2,1)S(1)} fusion(bf16[1,24,384]{2,1,0:T(8,128)(2,1)} %bitcast.117, bf16[1,24,384]{2,1,0:T(8,128)(2,1)S(1)} %convert_element_type.76), kind=kLoop, calls=%fused_computation.38 | loop fusion | flops 18432 | bytes 73728 | tf_op jit(solution)/shard_map/stack | solution.py:135
  2.7 6.6 %all-gather = bf16[8,24,384]{2,1,0:T(8,128)(2,1)S(1)} all-gather(bf16[2,24,384]{2,1,0:T(8,128)(2,1)S(1)} %pad_maximum_fusion.4), channel_id=2, replica_groups=mesh['req'=8,'tp'=4] {'tp'}, dimensions={0}, use_global_device_ids=true | all-gather | bytes 184320 | tf_op jit(solution)/shard_map/all_gather | solution.py:136
  9.4 0.1 copy.119
  9.6 0.1 reduce.2
  9.7 0.5 fusion.30
  10.2 0.1 compare_and_fusion
  10.3 0.5 fusion.31
  10.8 0.1 concatenate.33
  10.9 0.3 fusion.3
  11.3 0.7 fusion.2
  12.0 0.1 concatenate.34
  12.1 0.2 pad_maximum_fusion
  12.4 0.4 collective-permute-start
  12.8 1.8 %collective-permute-start.1 = (f32[24,3,130]{2,0,1:T(8,128)S(1)}, f32[24,3,130]{2,0,1:T(8,128)S(1)}, u32[]{:S(2)}, u32[]{:S(2)}) collective-permute-start(f32[24,3,130]{2,0,1:T(8,128)S(1)} %get-tuple-element.16), channel_id=1, source_target_pairs={{0,2},{1,3},{2,0},{3,1},{4,6},{5,7},{6,4},{7,5},{8,10},{9,11},{10,... | collective-permute-start | bytes 112328 | tf_op jit(solution)/shard_map/ppermute | solution.py:186
  14.6 1.1 %collective-permute-start.2 = (f32[24,3,130]{2,0,1:T(8,128)S(1)}, f32[24,3,130]{2,0,1:T(8,128)S(1)}, u32[]{:S(2)}, u32[]{:S(2)}) collective-permute-start(f32[24,3,130]{2,0,1:T(8,128)S(1)} %get-tuple-element.15), channel_id=1, source_target_pairs={{0,3},{1,0},{2,1},{3,2},{4,7},{5,4},{6,5},{7,6},{8,11},{9,8},{10,9... | collective-permute-start | bytes 112328 | tf_op jit(solution)/shard_map/ppermute | solution.py:186
  15.7 0.1 slice_reduce_fusion
  15.8 0.1 subtract_convert_fusion.1
  15.9 0.1 maximum_bitcast_fusion
  16.0 0.2 fusion.12
  16.2 0.1 copy.134
  16.3 0.1 select_reduce_fusion
  16.5 0.1 fusion.22
  16.6 0.7 collective-permute-done.1
  17.3 0.6 collective-permute-done.2
  18.0 0.1 slice_reduce_fusion.1
  18.1 0.1 copy.138
  18.3 0.1 fusion.10
  18.4 0.1 copy.128
  18.7 0.3 convolution_convert_fusion
  19.0 6.3 %all-gather.1 = bf16[96,1536]{1,0:T(8,128)(2,1)S(1)} all-gather(bf16[24,1536]{1,0:T(8,128)(2,1)S(1)} %convolution_convert_fusion), channel_id=3, replica_groups=mesh['req'=8,'tp'=4] {'tp'}, dimensions={0}, use_global_device_ids=true | all-gather | bytes 368640 | tf_op jit(solution)/shard_map/all_gather | solution.py:210
  25.3 0.1 fusion.9
  25.5 0.1 multiply_convert_fusion
  25.6 1.9 %collective-permute-start.3 = (bf16[24,1664]{1,0:T(8,128)(2,1)S(1)}, bf16[24,1664]{1,0:T(8,128)(2,1)S(1)}, u32[]{:S(2)}, u32[]{:S(2)}) collective-permute-start(bf16[24,1664]{1,0:T(8,128)(2,1)S(1)} %pad_maximum_fusion.3), channel_id=1, source_target_pairs={{28,0},{21,1},{14,2},{7,3},{0,4},{25,5},{18,6},{11,7},{4,8},{29,9}... | collective-permute-start | bytes 239624 | tf_op jit(solution)/shard_map/ppermute | solution.py:245
  27.5 3.5 %collective-permute-start.4 = (bf16[24,1664]{1,0:T(8,128)(2,1)S(1)}, bf16[24,1664]{1,0:T(8,128)(2,1)S(1)}, u32[]{:S(2)}, u32[]{:S(2)}) collective-permute-start(bf16[24,1664]{1,0:T(8,128)(2,1)S(1)} %pad_maximum_fusion.3), channel_id=1, source_target_pairs={{24,0},{17,1},{10,2},{3,3},{28,4},{21,5},{14,6},{7,7},{0,8},{25,9}... | collective-permute-start | bytes 239624 | tf_op jit(solution)/shard_map/ppermute | solution.py:245
  30.9 0.5 and_select_fusion.dest_ref
  31.5 1.9 %collective-permute-done.3 = bf16[24,1664]{1,0:T(8,128)(2,1)S(1)} collective-permute-done((bf16[24,1664]{1,0:T(8,128)(2,1)S(1)}, bf16[24,1664]{1,0:T(8,128)(2,1)S(1)}, u32[]{:S(2)}, u32[]{:S(2)}) %collective-permute-start.3) | collective-permute-done | bytes 79904 | tf_op jit(solution)/shard_map/ppermute | solution.py:245
  33.4 2.8 %collective-permute-done.4 = bf16[24,1664]{1,0:T(8,128)(2,1)S(1)} collective-permute-done((bf16[24,1664]{1,0:T(8,128)(2,1)S(1)}, bf16[24,1664]{1,0:T(8,128)(2,1)S(1)}, u32[]{:S(2)}, u32[]{:S(2)}) %collective-permute-start.4) | collective-permute-done | bytes 79904 | tf_op jit(solution)/shard_map/ppermute | solution.py:245
  36.3 7.7 %all-gather.2 = bf16[8,24,1664]{2,1,0:T(8,128)(2,1)} all-gather(bf16[2,24,1664]{2,1,0:T(8,128)(2,1)S(1)} %pad_maximum_fusion.2), channel_id=4, replica_groups=mesh['req'=8,'tp'=4] {'tp'}, dimensions={0}, use_global_device_ids=true | all-gather | bytes 798720 | tf_op jit(solution)/shard_map/all_gather | solution.py:246
  43.9 7.1 %shard_map.118 = bf16[32,24,384]{2,1,0:T(8,128)(2,1)} custom-call(s32[1]{0:T(128)} %bitcast.32.offset_ref, s32[8]{0:T(128)} %and_select_fusion.dest_ref, bf16[192,1664]{1,0:T(8,128)(2,1)} %bitcast.102, bf16[4,2,192,1536]{3,2,1,0:T(8,128)(2,1)} %bitcast.101, bf16[4,192,1536]{2,1,0:T(8,128)(2,1)} %dn_ref.1), custom_call_target="tpu_custom_call" | custom-call | tf_op jit(solution)/shard_map/pallas_call | solution.py:85
  51.0 3.6 %all-to-all-start = ((bf16[32,24,384]{2,1,0:T(8,128)(2,1)}), bf16[32,24,384]{2,1,0:T(8,128)(2,1)S(1)}, u32[]{:S(2)}, u32[]{:S(2)}) async-start(bf16[32,24,384]{2,1,0:T(8,128)(2,1)} %shard_map.118), calls=%async_computation | async-start | bytes 1179648 | tf_op jit(solution)/shard_map/all_to_all | solution.py:264
  54.6 16.8 %all-to-all-done = bf16[32,24,384]{2,1,0:T(8,128)(2,1)S(1)} async-done(((bf16[32,24,384]{2,1,0:T(8,128)(2,1)}), bf16[32,24,384]{2,1,0:T(8,128)(2,1)S(1)}, u32[]{:S(2)}, u32[]{:S(2)}) %all-to-all-start) | async-done | bytes 589856 | tf_op jit(solution)/shard_map/all_to_all | solution.py:264
  71.4 0.1 convert_reduce_fusion
  71.5 0.6 add_convert_fusion.1
  (40 shorter events, 0.5 us)
Async XLA Ops:
  0.0 18.7 %copy-start = (bf16[384,1536]{1,0:T(8,128)(2,1)S(1)}, bf16[384,1536]{1,0:T(8,128)(2,1)}, u32[]{:S(2)}) copy-start(bf16[384,1536]{1,0:T(8,128)(2,1)} %param.18) | copy-start | bytes 3538948
  0.0 9.4 %copy-start.6 = (s32[1,24]{1,0:T(1,128)S(1)}, s32[1,24]{1,0:T(1,128)}, u32[]{:S(2)}) copy-start(s32[1,24]{1,0:T(1,128)} %param.16) | copy-start | bytes 292
  0.0 9.7 %copy-start.1 = (bf16[768,2,2,128]{3,2,1,0:T(2,128)(2,1)S(1)}, bf16[768,2,2,128]{3,2,1,0:T(2,128)(2,1)}, u32[]{:S(2)}) copy-start(bf16[768,2,2,128]{3,2,1,0:T(2,128)(2,1)} %param.17) | copy-start | bytes 2359300
  11.2 4.5 %copy-start.2 = (bf16[24,2,256]{2,1,0:T(2,128)(2,1)S(1)}, bf16[24,2,256]{2,1,0:T(2,128)(2,1)}, u32[]{:S(2)}) copy-start(bf16[24,2,256]{2,1,0:T(2,128)(2,1)} %param.14) | copy-start | bytes 73732
  12.0 4.4 %copy-start.4 = (f32[24,4]{0,1:T(4,128)S(1)}, f32[24,4]{0,1:T(4,128)}, u32[]{:S(2)}) copy-start(f32[24,4]{0,1:T(4,128)} %param.21) | copy-start | bytes 1156
  12.0 4.4 %copy-start.5 = (s32[24,4]{0,1:T(4,128)S(1)}, s32[24,4]{0,1:T(4,128)}, u32[]{:S(2)}) copy-start(s32[24,4]{0,1:T(4,128)} %param.20) | copy-start | bytes 1156
  12.4 4.2 %collective-permute-start = (f32[24,3,130]{2,0,1:T(8,128)S(1)}, f32[24,3,130]{2,0,1:T(8,128)S(1)}, u32[]{:S(2)}, u32[]{:S(2)}) collective-permute-start(f32[24,3,130]{2,0,1:T(8,128)S(1)} %get-tuple-element.17), channel_id=1, source_target_pairs={{0,1},{1,2},{2,3},{3,0},{4,5},{5,6},{6,7},{7,4},{8,9},{9,10},{10,1... | collective-permute-start | bytes 112328 | tf_op jit(solution)/shard_map/ppermute | solution.py:186
  12.8 4.5 %collective-permute-start.1 = (f32[24,3,130]{2,0,1:T(8,128)S(1)}, f32[24,3,130]{2,0,1:T(8,128)S(1)}, u32[]{:S(2)}, u32[]{:S(2)}) collective-permute-start(f32[24,3,130]{2,0,1:T(8,128)S(1)} %get-tuple-element.16), channel_id=1, source_target_pairs={{0,2},{1,3},{2,0},{3,1},{4,6},{5,7},{6,4},{7,5},{8,10},{9,11},{10,... | collective-permute-start | bytes 112328 | tf_op jit(solution)/shard_map/ppermute | solution.py:186
  14.6 3.3 %collective-permute-start.2 = (f32[24,3,130]{2,0,1:T(8,128)S(1)}, f32[24,3,130]{2,0,1:T(8,128)S(1)}, u32[]{:S(2)}, u32[]{:S(2)}) collective-permute-start(f32[24,3,130]{2,0,1:T(8,128)S(1)} %get-tuple-element.15), channel_id=1, source_target_pairs={{0,3},{1,0},{2,1},{3,2},{4,7},{5,4},{6,5},{7,6},{8,11},{9,8},{10,9... | collective-permute-start | bytes 112328 | tf_op jit(solution)/shard_map/ppermute | solution.py:186
  18.6 6.8 %copy-start.3 = (f32[1536]{0:T(1024)S(1)}, f32[1536]{0:T(1024)}, u32[]{:S(2)}) copy-start(f32[1536]{0:T(1024)} %param.19) | copy-start | bytes 18436
  25.6 7.9 %collective-permute-start.3 = (bf16[24,1664]{1,0:T(8,128)(2,1)S(1)}, bf16[24,1664]{1,0:T(8,128)(2,1)S(1)}, u32[]{:S(2)}, u32[]{:S(2)}) collective-permute-start(bf16[24,1664]{1,0:T(8,128)(2,1)S(1)} %pad_maximum_fusion.3), channel_id=1, source_target_pairs={{28,0},{21,1},{14,2},{7,3},{0,4},{25,5},{18,6},{11,7},{4,8},{29,9}... | collective-permute-start | bytes 239624 | tf_op jit(solution)/shard_map/ppermute | solution.py:245
  27.5 8.8 %collective-permute-start.4 = (bf16[24,1664]{1,0:T(8,128)(2,1)S(1)}, bf16[24,1664]{1,0:T(8,128)(2,1)S(1)}, u32[]{:S(2)}, u32[]{:S(2)}) collective-permute-start(bf16[24,1664]{1,0:T(8,128)(2,1)S(1)} %pad_maximum_fusion.3), channel_id=1, source_target_pairs={{24,0},{17,1},{10,2},{3,3},{28,4},{21,5},{14,6},{7,7},{0,8},{25,9}... | collective-permute-start | bytes 239624 | tf_op jit(solution)/shard_map/ppermute | solution.py:245
  51.0 20.4 %all-to-all-start = ((bf16[32,24,384]{2,1,0:T(8,128)(2,1)}), bf16[32,24,384]{2,1,0:T(8,128)(2,1)S(1)}, u32[]{:S(2)}, u32[]{:S(2)}) async-start(bf16[32,24,384]{2,1,0:T(8,128)(2,1)} %shard_map.118), calls=%async_computation | async-start | bytes 1179648 | tf_op jit(solution)/shard_map/all_to_all | solution.py:264

commit v15 on v13

--- a/solution.py
+++ b/solution.py
@@ -126,14 +126,11 @@
     first_head = tp_index * own_heads
     span_rows = cache.shape[0]
 
-    q_local = apply_rotary_heads(
-        queries.reshape(row_count, own_heads, head_size).astype(jnp.float32), positions, head_size
-    ).astype(jnp.bfloat16)
-    packed = jnp.stack([q_local.reshape(row_count, own_width), hidden_in], axis=0)
+    packed = jnp.stack([queries, hidden_in], axis=0)
     gathered = lax.all_gather(packed, "tp", axis=0)
-    q_all = jnp.transpose(gathered[:, 0], (1, 0, 2)).reshape(
-        row_count, kv_count, request_group_size, head_size
-    )
+    q_raw = jnp.transpose(gathered[:, 0], (1, 0, 2)).reshape(row_count, head_count, head_size)
+    q_all = apply_rotary_heads(q_raw.astype(jnp.float32), positions, head_size).astype(jnp.bfloat16)
+    q_all = q_all.reshape(row_count, kv_count, request_group_size, head_size)
     hidden_full = jnp.transpose(gathered[:, 1], (1, 0, 2)).reshape(row_count, model_width)
 
     k_new = apply_rotary_heads(

time: 71.8 us -> 70.7 us (0.985)
    convert_element_type x1, other arithmetic: 0.8 us -> 0.01 us  [apply_rotary_heads(): angles = positions.astype(jnp.float32)[:, None] * inverse_freq[None, :]]
where the time goes in v15:
time: 70.7 us; the launch traced here: 70.4 us
  waiting for transfers between devices  22.9 us (32%)
  blocking collectives  20.7 us (29%)
  starting transfers between devices  12.3 us (17%)
  Pallas kernels  6.42 us (9%)
  other arithmetic  4.44 us (6%)
  matrix products  1.68 us (2%)
  local copies, waits for them, and re-layouts  1.58 us (2%)
    all_to_all x1, waiting for transfers between devices, per_device(): mixed = lax.all_to_all(mixed, ('req', 'tp'), 0, 0, tiled=True)  16.8 us
    all_gather x1, blocking collectives, gather_req(): shared = lax.all_gather(jnp.stack(fetched, axis=0), 'tp', axis=0)  7.65 us
    all_gather x1, blocking collectives, per_device(): gathered = lax.all_gather(packed, 'tp', axis=0)  6.74 us
    pallas_call x1, Pallas kernels, expert_mix(): pl.pallas_call(body, grid=(group_total // tile_groups, local_count), in_s...  6.42 us
    all_gather x1, blocking collectives, per_device(): lax.all_gather(partial_proj.astype(jnp.bfloat16), 'tp', axis=0)  6.29 us
    ppermute x2, starting transfers between devices, gather_req(): fetched.append(lax.ppermute(value, ('req', 'tp'), pairs))  5.38 us
    ppermute x2, waiting for transfers between devices, gather_req(): fetched.append(lax.ppermute(value, ('req', 'tp'), pairs))  4.77 us
    all_to_all x1, starting transfers between devices, per_device(): mixed = lax.all_to_all(mixed, ('req', 'tp'), 0, 0, tiled=True)  3.57 us
  transfers between devices with their start and end apart: 6, of which 5 were waited for; matrix products, arithmetic and copies ran while one was open for 2% of the time, Pallas kernels for 0%

profile of v15, /device:TPU:0, one launch (start us, length us, event | category | flops | bytes accessed | tf_op | source)
XLA Modules:
  0.0 70.4 jit_solution(3306688894863418140)
XLA Ops:
  0.0 0.8 %pad_maximum_fusion.5 = bf16[2,24,384]{2,1,0:T(8,128)(2,1)S(1)} fusion(bf16[1,24,384]{2,1,0:T(8,128)(2,1)} %bitcast.125, bf16[1,24,384]{2,1,0:T(8,128)(2,1)} %bitcast.126), kind=kLoop, calls=%fused_computation.41 | loop fusion | flops 18432 | bytes 73728 | tf_op jit(solution)/shard_map/stack | solution.py:129
  0.9 6.7 %all-gather = bf16[8,24,384]{2,1,0:T(8,128)(2,1)S(1)} all-gather(bf16[2,24,384]{2,1,0:T(8,128)(2,1)S(1)} %pad_maximum_fusion.5), channel_id=2, replica_groups=mesh['req'=8,'tp'=4] {'tp'}, dimensions={0}, use_global_device_ids=true | all-gather | bytes 184320 | tf_op jit(solution)/shard_map/all_gather | solution.py:130
  7.7 0.1 reshape.211
  7.8 0.1 multiply_cosine_fusion
  7.9 0.1 subtract_convert_fusion
  8.1 0.1 copy.123
  8.3 0.1 reduce.2
  8.4 0.1 copy-done.2
  8.5 0.5 fusion.30
  9.0 0.1 pad_maximum_fusion.4
  9.1 0.1 compare_and_fusion
  9.2 0.5 fusion.31
  9.7 0.1 concatenate.40
  9.9 0.3 fusion.3
  10.2 0.7 %fusion.2 = f32[2,24,6,128]{3,1,2,0:T(8,128)S(1)} fusion(f32[24,2,6,768]{3,0,2,1:T(8,128)S(1)} %get-tuple-element.32, f32[24,2,6]{0,2,1:T(8,128)S(1)} %get-tuple-element.31, pred[24,768]{1,0:T(8,128)(4,1)S(1)} %compare_and_fusion, bf16[768,1,2,128]{3,2,1,0:T(2,128)(2,1)S(1)} %get-tuple-element.9), kind=kOutput, calls=%fused_computation.6 | convolution fusion | flops 340180992 | bytes 1444992 | tf_op jit(solution)/shard_map/rcgj,jcd->rcgd/dot_general | solution.py:164
  10.9 0.1 concatenate.41
  11.1 0.2 pad_maximum_fusion
  11.3 0.4 collective-permute-start
  11.7 1.8 %collective-permute-start.1 = (f32[24,3,130]{2,0,1:T(8,128)S(1)}, f32[24,3,130]{2,0,1:T(8,128)S(1)}, u32[]{:S(2)}, u32[]{:S(2)}) collective-permute-start(f32[24,3,130]{2,0,1:T(8,128)S(1)} %get-tuple-element.16), channel_id=1, source_target_pairs={{0,2},{1,3},{2,0},{3,1},{4,6},{5,7},{6,4},{7,5},{8,10},{9,11},{10,... | collective-permute-start | bytes 112328 | tf_op jit(solution)/shard_map/ppermute | solution.py:180
  13.6 1.1 %collective-permute-start.2 = (f32[24,3,130]{2,0,1:T(8,128)S(1)}, f32[24,3,130]{2,0,1:T(8,128)S(1)}, u32[]{:S(2)}, u32[]{:S(2)}) collective-permute-start(f32[24,3,130]{2,0,1:T(8,128)S(1)} %get-tuple-element.15), channel_id=1, source_target_pairs={{0,3},{1,0},{2,1},{3,2},{4,7},{5,4},{6,5},{7,6},{8,11},{9,8},{10,9... | collective-permute-start | bytes 112328 | tf_op jit(solution)/shard_map/ppermute | solution.py:180
  14.7 0.1 slice_reduce_fusion
  14.8 0.1 subtract_convert_fusion.1
  14.9 0.1 maximum_bitcast_fusion
  15.0 0.2 fusion.11
  15.2 0.1 copy.140
  15.3 0.1 select_reduce_fusion
  15.4 0.1 fusion.22
  15.5 0.7 collective-permute-done.1
  16.2 0.6 collective-permute-done.2
  16.9 0.1 slice_reduce_fusion.1
  17.0 0.1 copy.144
  17.2 0.1 fusion.10
  17.4 0.1 copy.133
  17.6 0.3 convolution_convert_fusion
  17.9 6.3 %all-gather.1 = bf16[96,1536]{1,0:T(8,128)(2,1)S(1)} all-gather(bf16[24,1536]{1,0:T(8,128)(2,1)S(1)} %convolution_convert_fusion), channel_id=3, replica_groups=mesh['req'=8,'tp'=4] {'tp'}, dimensions={0}, use_global_device_ids=true | all-gather | bytes 368640 | tf_op jit(solution)/shard_map/all_gather | solution.py:204
  24.2 0.1 fusion.9
  24.4 0.1 multiply_convert_fusion
  24.5 1.9 %collective-permute-start.3 = (bf16[24,1664]{1,0:T(8,128)(2,1)S(1)}, bf16[24,1664]{1,0:T(8,128)(2,1)S(1)}, u32[]{:S(2)}, u32[]{:S(2)}) collective-permute-start(bf16[24,1664]{1,0:T(8,128)(2,1)S(1)} %pad_maximum_fusion.3), channel_id=1, source_target_pairs={{28,0},{21,1},{14,2},{7,3},{0,4},{25,5},{18,6},{11,7},{4,8},{29,9}... | collective-permute-start | bytes 239624 | tf_op jit(solution)/shard_map/ppermute | solution.py:239
  26.4 3.5 %collective-permute-start.4 = (bf16[24,1664]{1,0:T(8,128)(2,1)S(1)}, bf16[24,1664]{1,0:T(8,128)(2,1)S(1)}, u32[]{:S(2)}, u32[]{:S(2)}) collective-permute-start(bf16[24,1664]{1,0:T(8,128)(2,1)S(1)} %pad_maximum_fusion.3), channel_id=1, source_target_pairs={{24,0},{17,1},{10,2},{3,3},{28,4},{21,5},{14,6},{7,7},{0,8},{25,9}... | collective-permute-start | bytes 239624 | tf_op jit(solution)/shard_map/ppermute | solution.py:239
  29.9 0.5 and_select_fusion.dest_ref
  30.4 1.9 %collective-permute-done.3 = bf16[24,1664]{1,0:T(8,128)(2,1)S(1)} collective-permute-done((bf16[24,1664]{1,0:T(8,128)(2,1)S(1)}, bf16[24,1664]{1,0:T(8,128)(2,1)S(1)}, u32[]{:S(2)}, u32[]{:S(2)}) %collective-permute-start.3) | collective-permute-done | bytes 79904 | tf_op jit(solution)/shard_map/ppermute | solution.py:239
  32.3 2.8 %collective-permute-done.4 = bf16[24,1664]{1,0:T(8,128)(2,1)S(1)} collective-permute-done((bf16[24,1664]{1,0:T(8,128)(2,1)S(1)}, bf16[24,1664]{1,0:T(8,128)(2,1)S(1)}, u32[]{:S(2)}, u32[]{:S(2)}) %collective-permute-start.4) | collective-permute-done | bytes 79904 | tf_op jit(solution)/shard_map/ppermute | solution.py:239
  35.2 7.6 %all-gather.2 = bf16[8,24,1664]{2,1,0:T(8,128)(2,1)} all-gather(bf16[2,24,1664]{2,1,0:T(8,128)(2,1)S(1)} %pad_maximum_fusion.2), channel_id=4, replica_groups=mesh['req'=8,'tp'=4] {'tp'}, dimensions={0}, use_global_device_ids=true | all-gather | bytes 798720 | tf_op jit(solution)/shard_map/all_gather | solution.py:240
  42.9 6.4 %shard_map.118 = bf16[32,24,384]{2,1,0:T(8,128)(2,1)} custom-call(s32[1]{0:T(128)} %bitcast.35.offset_ref, s32[8]{0:T(128)} %and_select_fusion.dest_ref, bf16[192,1664]{1,0:T(8,128)(2,1)} %bitcast.108, bf16[4,2,192,1536]{3,2,1,0:T(8,128)(2,1)} %bitcast.107, bf16[4,192,1536]{2,1,0:T(8,128)(2,1)} %dn_ref.1), custom_call_target="tpu_custom_call" | custom-call | tf_op jit(solution)/shard_map/pallas_call | solution.py:82
  49.3 3.6 %all-to-all-start = ((bf16[32,24,384]{2,1,0:T(8,128)(2,1)}), bf16[32,24,384]{2,1,0:T(8,128)(2,1)S(1)}, u32[]{:S(2)}, u32[]{:S(2)}) async-start(bf16[32,24,384]{2,1,0:T(8,128)(2,1)} %shard_map.118), calls=%async_computation | async-start | bytes 1179648 | tf_op jit(solution)/shard_map/all_to_all | solution.py:258
  52.9 16.8 %all-to-all-done = bf16[32,24,384]{2,1,0:T(8,128)(2,1)S(1)} async-done(((bf16[32,24,384]{2,1,0:T(8,128)(2,1)}), bf16[32,24,384]{2,1,0:T(8,128)(2,1)S(1)}, u32[]{:S(2)}, u32[]{:S(2)}) %all-to-all-start) | async-done | bytes 589856 | tf_op jit(solution)/shard_map/all_to_all | solution.py:258
  69.7 0.1 convert_reduce_fusion
  69.8 0.6 add_convert_fusion.1
  (46 shorter events, 0.5 us)
Async XLA Ops:
  0.0 17.6 %copy-start = (bf16[384,1536]{1,0:T(8,128)(2,1)S(1)}, bf16[384,1536]{1,0:T(8,128)(2,1)}, u32[]{:S(2)}) copy-start(bf16[384,1536]{1,0:T(8,128)(2,1)} %param.18) | copy-start | bytes 3538948
  0.0 7.7 %copy-start.9 = (s32[24]{0:T(128)S(1)}, s32[24]{0:T(128)}, u32[]{:S(2)}) copy-start(s32[24]{0:T(128)} %param.15) | copy-start | bytes 292
  0.0 8.1 %copy-start.8 = (s32[1,24]{1,0:T(1,128)S(1)}, s32[1,24]{1,0:T(1,128)}, u32[]{:S(2)}) copy-start(s32[1,24]{1,0:T(1,128)} %param.16) | copy-start | bytes 292
  0.9 7.6 %copy-start.1 = (bf16[768,2,2,128]{3,2,1,0:T(2,128)(2,1)S(1)}, bf16[768,2,2,128]{3,2,1,0:T(2,128)(2,1)}, u32[]{:S(2)}) copy-start(bf16[768,2,2,128]{3,2,1,0:T(2,128)(2,1)} %param.17) | copy-start | bytes 2359300
  7.9 0.6 copy-start.2
  10.2 4.5 %copy-start.4 = (bf16[24,2,256]{2,1,0:T(2,128)(2,1)S(1)}, bf16[24,2,256]{2,1,0:T(2,128)(2,1)}, u32[]{:S(2)}) copy-start(bf16[24,2,256]{2,1,0:T(2,128)(2,1)} %param.14) | copy-start | bytes 73732
  10.9 3.9 %copy-start.3 = (f32[24,64]{1,0:T(8,128)S(1)}, f32[24,64]{1,0:T(8,128)}, u32[]{:S(2)}) copy-start(f32[24,64]{1,0:T(8,128)} %copy-done.2) | copy-start | bytes 18436
  10.9 4.4 %copy-start.6 = (f32[24,4]{0,1:T(4,128)S(1)}, f32[24,4]{0,1:T(4,128)}, u32[]{:S(2)}) copy-start(f32[24,4]{0,1:T(4,128)} %param.21) | copy-start | bytes 1156
  10.9 4.4 %copy-start.7 = (s32[24,4]{0,1:T(4,128)S(1)}, s32[24,4]{0,1:T(4,128)}, u32[]{:S(2)}) copy-start(s32[24,4]{0,1:T(4,128)} %param.20) | copy-start | bytes 1156
  11.3 4.2 %collective-permute-start = (f32[24,3,130]{2,0,1:T(8,128)S(1)}, f32[24,3,130]{2,0,1:T(8,128)S(1)}, u32[]{:S(2)}, u32[]{:S(2)}) collective-permute-start(f32[24,3,130]{2,0,1:T(8,128)S(1)} %get-tuple-element.17), channel_id=1, source_target_pairs={{0,1},{1,2},{2,3},{3,0},{4,5},{5,6},{6,7},{7,4},{8,9},{9,10},{10,1... | collective-permute-start | bytes 112328 | tf_op jit(solution)/shard_map/ppermute | solution.py:180
  11.7 4.5 %collective-permute-start.1 = (f32[24,3,130]{2,0,1:T(8,128)S(1)}, f32[24,3,130]{2,0,1:T(8,128)S(1)}, u32[]{:S(2)}, u32[]{:S(2)}) collective-permute-start(f32[24,3,130]{2,0,1:T(8,128)S(1)} %get-tuple-element.16), channel_id=1, source_target_pairs={{0,2},{1,3},{2,0},{3,1},{4,6},{5,7},{6,4},{7,5},{8,10},{9,11},{10,... | collective-permute-start | bytes 112328 | tf_op jit(solution)/shard_map/ppermute | solution.py:180
  13.6 3.3 %collective-permute-start.2 = (f32[24,3,130]{2,0,1:T(8,128)S(1)}, f32[24,3,130]{2,0,1:T(8,128)S(1)}, u32[]{:S(2)}, u32[]{:S(2)}) collective-permute-start(f32[24,3,130]{2,0,1:T(8,128)S(1)} %get-tuple-element.15), channel_id=1, source_target_pairs={{0,3},{1,0},{2,1},{3,2},{4,7},{5,4},{6,5},{7,6},{8,11},{9,8},{10,9... | collective-permute-start | bytes 112328 | tf_op jit(solution)/shard_map/ppermute | solution.py:180
  17.5 6.8 %copy-start.5 = (f32[1536]{0:T(1024)S(1)}, f32[1536]{0:T(1024)}, u32[]{:S(2)}) copy-start(f32[1536]{0:T(1024)} %param.19) | copy-start | bytes 18436
  24.5 7.9 %collective-permute-start.3 = (bf16[24,1664]{1,0:T(8,128)(2,1)S(1)}, bf16[24,1664]{1,0:T(8,128)(2,1)S(1)}, u32[]{:S(2)}, u32[]{:S(2)}) collective-permute-start(bf16[24,1664]{1,0:T(8,128)(2,1)S(1)} %pad_maximum_fusion.3), channel_id=1, source_target_pairs={{28,0},{21,1},{14,2},{7,3},{0,4},{25,5},{18,6},{11,7},{4,8},{29,9}... | collective-permute-start | bytes 239624 | tf_op jit(solution)/shard_map/ppermute | solution.py:239
  26.4 8.8 %collective-permute-start.4 = (bf16[24,1664]{1,0:T(8,128)(2,1)S(1)}, bf16[24,1664]{1,0:T(8,128)(2,1)S(1)}, u32[]{:S(2)}, u32[]{:S(2)}) collective-permute-start(bf16[24,1664]{1,0:T(8,128)(2,1)S(1)} %pad_maximum_fusion.3), channel_id=1, source_target_pairs={{24,0},{17,1},{10,2},{3,3},{28,4},{21,5},{14,6},{7,7},{0,8},{25,9}... | collective-permute-start | bytes 239624 | tf_op jit(solution)/shard_map/ppermute | solution.py:239
  49.3 20.4 %all-to-all-start = ((bf16[32,24,384]{2,1,0:T(8,128)(2,1)}), bf16[32,24,384]{2,1,0:T(8,128)(2,1)S(1)}, u32[]{:S(2)}, u32[]{:S(2)}) async-start(bf16[32,24,384]{2,1,0:T(8,128)(2,1)} %shard_map.118), calls=%async_computation | async-start | bytes 1179648 | tf_op jit(solution)/shard_map/all_to_all | solution.py:258

commit v16 on v15

--- a/solution.py
+++ b/solution.py
@@ -32,7 +32,7 @@
 
 
 def _expert_body(
-    offset_ref, dest_ref, x_ref, gu_ref, dn_ref, o_ref, acc_ref, *, width, block_total, row_count, tp_count
+    index_ref, x_ref, gu_ref, dn_ref, o_ref, acc_ref, *, width, block_total, row_count, tp_count, arrival_order
 ):
     block = pl.program_id(1)
 
@@ -49,7 +49,8 @@
     produced = produced.astype(jnp.bfloat16).astype(jnp.float32)
     code = x_ref[:, width:].astype(jnp.float32)
     lanes = lax.broadcasted_iota(jnp.int32, code.shape, 1)
-    column = offset_ref[0] + block
+    local_count = pl.num_programs(1)
+    column = index_ref[0] * local_count + block
     chosen = jnp.sum(jnp.where(lanes == column, code, 0.0), axis=1, keepdims=True)
     chosen = chosen + jnp.sum(jnp.where(lanes == column + block_total, code, 0.0), axis=1, keepdims=True)
     chosen = chosen + jnp.sum(jnp.where(lanes == column + 2 * block_total, code, 0.0), axis=1, keepdims=True)
@@ -60,7 +61,11 @@
         own_width = o_ref.shape[2]
         tile_groups = x_ref.shape[0] // row_count
         for group in range(tile_groups):
-            dest = dest_ref[pl.program_id(0) * tile_groups + group] - pl.program_id(0) * tile_groups
+            if arrival_order:
+                group_total = o_ref.shape[0] // tp_count
+                dest = (index_ref[0] + 2 * group_total - group - 1) % group_total
+            else:
+                dest = group
             for part in range(tp_count):
                 o_ref[dest * tp_count + part] = acc_ref[
                     group * row_count : (group + 1) * row_count,
@@ -68,7 +73,7 @@
                 ].astype(o_ref.dtype)
 
 
-def expert_mix(rows, gate_up, down, offset, dest, width, block_total, row_count, tp_count):
+def expert_mix(rows, gate_up, down, req_index, arrival_order, width, block_total, row_count, tp_count):
     row_total, message_width = rows.shape
     local_count, _, _, hidden = gate_up.shape
     group_total = row_total // row_count
@@ -77,13 +82,17 @@
     own_width = width // tp_count
     gate_up_t = jnp.swapaxes(gate_up, 2, 3)
     body = functools.partial(
-        _expert_body, width=width, block_total=block_total, row_count=row_count, tp_count=tp_count
+        _expert_body,
+        width=width,
+        block_total=block_total,
+        row_count=row_count,
+        tp_count=tp_count,
+        arrival_order=arrival_order,
     )
     return pl.pallas_call(
         body,
         grid=(group_total // tile_groups, local_count),
         in_specs=[
-            pl.BlockSpec(memory_space=pltpu.SMEM),
             pl.BlockSpec(memory_space=pltpu.SMEM),
             pl.BlockSpec((tile, message_width), lambda i, b: (i, 0)),
             pl.BlockSpec((1, 2, hidden, width), lambda i, b: (b, 0, 0, 0)),
@@ -93,7 +102,7 @@
         out_shape=jax.ShapeDtypeStruct((group_total * tp_count, row_count, own_width), jnp.bfloat16),
         scratch_shapes=[pltpu.VMEM((tile, width), jnp.float32)],
         compiler_params=pltpu.CompilerParams(dimension_semantics=("parallel", "arbitrary")),
-    )(offset, dest, rows, gate_up_t, down)
+    )(req_index, rows, gate_up_t, down)
 
 
 def per_device(
@@ -126,12 +135,10 @@
     first_head = tp_index * own_heads
     span_rows = cache.shape[0]
 
-    packed = jnp.stack([queries, hidden_in], axis=0)
-    gathered = lax.all_gather(packed, "tp", axis=0)
-    q_raw = jnp.transpose(gathered[:, 0], (1, 0, 2)).reshape(row_count, head_count, head_size)
+    gathered = lax.all_gather(queries, "tp", axis=0)
+    q_raw = jnp.transpose(gathered, (1, 0, 2)).reshape(row_count, head_count, head_size)
     q_all = apply_rotary_heads(q_raw.astype(jnp.float32), positions, head_size).astype(jnp.bfloat16)
     q_all = q_all.reshape(row_count, kv_count, request_group_size, head_size)
-    hidden_full = jnp.transpose(gathered[:, 1], (1, 0, 2)).reshape(row_count, model_width)
 
     k_new = apply_rotary_heads(
         fresh_key_value[:, 0].reshape(row_count, kv_count, head_size).astype(jnp.float32),
@@ -200,9 +207,10 @@
     )
 
     partial_proj = jnp.dot(attention_output, out_proj, preferred_element_type=jnp.float32)
-    projected = jnp.sum(
-        lax.all_gather(partial_proj.astype(jnp.bfloat16), "tp", axis=0).astype(jnp.float32), axis=0
-    )
+    proj_message = jnp.concatenate([partial_proj.astype(jnp.bfloat16), hidden_in], axis=1)
+    proj_all = lax.all_gather(proj_message, "tp", axis=0)
+    projected = jnp.sum(proj_all[:, :, :model_width].astype(jnp.float32), axis=0)
+    hidden_full = jnp.transpose(proj_all[:, :, model_width:], (1, 0, 2)).reshape(row_count, model_width)
     residual = hidden_full.astype(jnp.float32) + projected
     mean_square = jnp.mean(residual * residual, axis=1, keepdims=True)
     normed = (residual * lax.rsqrt(mean_square + norm_eps) * norm_gain[None, :]).astype(jnp.bfloat16)
@@ -224,9 +232,8 @@
     )
 
     def gather_req(value):
-        if req_count > 8 or req_count % tp_count != 0:
-            gathered = lax.all_gather(value, "req", axis=0, tiled=True)
-            return gathered, jnp.arange(req_count, dtype=jnp.int32)
+        if req_count > 8 or 8 % req_count != 0 or req_count % tp_count != 0:
+            return lax.all_gather(value, "req", axis=0, tiled=True), False
         per_tp = req_count // tp_count
         fetched = []
         for slot in range(per_tp):
@@ -239,8 +246,7 @@
             fetched.append(lax.ppermute(value, ("req", "tp"), pairs))
         shared = lax.all_gather(jnp.stack(fetched, axis=0), "tp", axis=0)
         shared = shared.reshape((req_count * value.shape[0],) + value.shape[1:])
-        groups = (req_index - jnp.arange(req_count, dtype=jnp.int32) - 1) % req_count
-        return shared, groups.astype(jnp.int32)
+        return shared, True
 
     weight_high = lax.reduce_precision(block_weights, exponent_bits=8, mantissa_bits=7)
     weight_rest = block_weights - weight_high
@@ -250,10 +256,10 @@
     code_lanes = -(-code.shape[1] // 128) * 128
     code = jnp.pad(code, ((0, 0), (0, code_lanes - code.shape[1])))
     message = jnp.concatenate([normed, code], axis=1)
-    message_all, message_groups = gather_req(message)
-    offset = (req_index * local_count).astype(jnp.int32).reshape(1)
+    message_all, arrival_order = gather_req(message)
+    index_scalar = req_index.astype(jnp.int32).reshape(1)
     mixed = expert_mix(
-        message_all, gate_up, down, offset, message_groups, model_width, block_total, row_count, tp_count
+        message_all, gate_up, down, index_scalar, arrival_order, model_width, block_total, row_count, tp_count
     )
     mixed = lax.all_to_all(mixed, ("req", "tp"), 0, 0, tiled=True)
     mixed = jnp.sum(mixed.astype(jnp.float32), axis=0)

time: 70.7 us -> 72.1 us (1.020)
    another operation x6 -> x5, other arithmetic: 1.25 us -> 0.41 us  [the longest x1 0.84 us: per_device(): packed = jnp.stack([queries, hidden_in], axis=0)]
    another operation x3, local copies, waits for them, and re-layouts: 0.13 us -> 0.91 us
  transfers between devices with their start and end apart: 6 -> 6, of which waited for: 5 -> 5; matrix products, arithmetic and copies ran while one was open for 2% -> 1% of each run, Pallas kernels for 0% -> 0%
where the time goes in v16:
time: 72.1 us; the launch traced here: 71.7 us
  waiting for transfers between devices  23.5 us (33%)
  blocking collectives  20.8 us (29%)
  starting transfers between devices  12.5 us (17%)
  Pallas kernels  6.38 us (9%)
  other arithmetic  4.37 us (6%)
  local copies, waits for them, and re-layouts  2.23 us (3%)
  matrix products  1.68 us (2%)
    all_to_all x1, waiting for transfers between devices, per_device(): mixed = lax.all_to_all(mixed, ('req', 'tp'), 0, 0, tiled=True)  16.8 us
    all_gather x1, blocking collectives, gather_req(): shared = lax.all_gather(jnp.stack(fetched, axis=0), 'tp', axis=0)  7.65 us
    all_gather x1, blocking collectives, per_device(): proj_all = lax.all_gather(proj_message, 'tp', axis=0)  6.66 us
    all_gather x1, blocking collectives, per_device(): gathered = lax.all_gather(queries, 'tp', axis=0)  6.46 us
    pallas_call x1, Pallas kernels, expert_mix(): pl.pallas_call(body, grid=(group_total // tile_groups, local_count), in_s...  6.38 us
    ppermute x2, starting transfers between devices, gather_req(): fetched.append(lax.ppermute(value, ('req', 'tp'), pairs))  5.41 us
    ppermute x2, waiting for transfers between devices, gather_req(): fetched.append(lax.ppermute(value, ('req', 'tp'), pairs))  5.31 us
    all_to_all x1, starting transfers between devices, per_device(): mixed = lax.all_to_all(mixed, ('req', 'tp'), 0, 0, tiled=True)  3.57 us
  transfers between devices with their start and end apart: 6, of which 5 were waited for; matrix products, arithmetic and copies ran while one was open for 1% of the time, Pallas kernels for 0%

profile of v16, /device:TPU:0, one launch (start us, length us, event | category | flops | bytes accessed | tf_op | source)
XLA Modules:
  0.0 71.7 jit_solution(15806400113530077416)
XLA Ops:
  0.0 0.9 %copy.125 = s32[24,1]{1,0:T(8,128)S(1)} copy(s32[24,1]{0,1:T(1,128)} %bitcast.112) | data formatting | bytes 192 | tf_op jit(solution)/shard_map/reshape.170
  0.9 0.1 reduce.2
  1.1 0.7 bitcast_subtract_fusion.1
  1.7 0.7 convert_element_type.66
  2.4 6.5 %all-gather = bf16[96,384]{1,0:T(8,128)(2,1)S(1)} all-gather(bf16[24,384]{1,0:T(8,128)(2,1)} %param.13), channel_id=2, replica_groups=mesh['req'=8,'tp'=4] {'tp'}, dimensions={0}, use_global_device_ids=true | all-gather | bytes 92160 | tf_op jit(solution)/shard_map/all_gather | solution.py:138
  8.9 0.1 reshape.204
  9.0 0.1 multiply_cosine_fusion
  9.1 0.1 subtract_convert_fusion
  9.3 0.5 fusion.29
  9.8 0.1 compare_and_fusion
  9.9 0.1 pad_maximum_fusion.5
  10.0 0.5 fusion.30
  10.5 0.1 concatenate.44
  10.6 0.3 fusion.3
  11.0 0.7 fusion.2
  11.7 0.1 concatenate.45
  11.8 0.2 pad_maximum_fusion
  12.1 0.4 collective-permute-start
  12.5 2.0 %collective-permute-start.1 = (f32[24,3,130]{2,0,1:T(8,128)S(1)}, f32[24,3,130]{2,0,1:T(8,128)S(1)}, u32[]{:S(2)}, u32[]{:S(2)}) collective-permute-start(f32[24,3,130]{2,0,1:T(8,128)S(1)} %get-tuple-element.16), channel_id=1, source_target_pairs={{0,2},{1,3},{2,0},{3,1},{4,6},{5,7},{6,4},{7,5},{8,10},{9,11},{10,... | collective-permute-start | bytes 112328 | tf_op jit(solution)/shard_map/ppermute | solution.py:187
  14.5 1.1 %collective-permute-start.2 = (f32[24,3,130]{2,0,1:T(8,128)S(1)}, f32[24,3,130]{2,0,1:T(8,128)S(1)}, u32[]{:S(2)}, u32[]{:S(2)}) collective-permute-start(f32[24,3,130]{2,0,1:T(8,128)S(1)} %get-tuple-element.15), channel_id=1, source_target_pairs={{0,3},{1,0},{2,1},{3,2},{4,7},{5,4},{6,5},{7,6},{8,11},{9,8},{10,9... | collective-permute-start | bytes 112328 | tf_op jit(solution)/shard_map/ppermute | solution.py:187
  15.6 0.1 slice_reduce_fusion
  15.7 0.1 subtract_convert_fusion.1
  15.8 0.1 maximum_bitcast_fusion
  15.9 0.2 fusion.11
  16.1 0.1 copy.143
  16.2 0.1 select_reduce_fusion
  16.3 0.1 fusion.22
  16.4 0.6 collective-permute-done.1
  17.0 0.8 %collective-permute-done.2 = f32[24,3,130]{2,0,1:T(8,128)S(1)} collective-permute-done((f32[24,3,130]{2,0,1:T(8,128)S(1)}, f32[24,3,130]{2,0,1:T(8,128)S(1)}, u32[]{:S(2)}, u32[]{:S(2)}) %collective-permute-start.2) | collective-permute-done | bytes 37472 | tf_op jit(solution)/shard_map/ppermute | solution.py:187
  17.8 0.1 slice_reduce_fusion.1
  18.0 0.1 copy.146
  18.1 0.1 fusion.10
  18.3 0.1 copy.135
  18.5 0.3 convolution_convert_fusion
  18.8 0.0 copy-done.3
  18.9 6.7 %all-gather.1 = bf16[96,1920]{1,0:T(8,128)(2,1)S(1)} all-gather(bf16[24,1920]{1,0:T(8,128)(2,1)S(1)} %pad_maximum_fusion.3), channel_id=3, replica_groups=mesh['req'=8,'tp'=4] {'tp'}, dimensions={0}, use_global_device_ids=true | all-gather | bytes 460800 | tf_op jit(solution)/shard_map/all_gather | solution.py:211
  25.6 0.1 fusion.9
  25.7 0.1 multiply_convert_fusion
  25.9 1.9 %collective-permute-start.3 = (bf16[24,1664]{1,0:T(8,128)(2,1)S(1)}, bf16[24,1664]{1,0:T(8,128)(2,1)S(1)}, u32[]{:S(2)}, u32[]{:S(2)}) collective-permute-start(bf16[24,1664]{1,0:T(8,128)(2,1)S(1)} %pad_maximum_fusion.4), channel_id=1, source_target_pairs={{28,0},{21,1},{14,2},{7,3},{0,4},{25,5},{18,6},{11,7},{4,8},{29,9}... | collective-permute-start | bytes 239624 | tf_op jit(solution)/shard_map/ppermute | solution.py:246
  27.8 3.5 %collective-permute-start.4 = (bf16[24,1664]{1,0:T(8,128)(2,1)S(1)}, bf16[24,1664]{1,0:T(8,128)(2,1)S(1)}, u32[]{:S(2)}, u32[]{:S(2)}) collective-permute-start(bf16[24,1664]{1,0:T(8,128)(2,1)S(1)} %pad_maximum_fusion.4), channel_id=1, source_target_pairs={{24,0},{17,1},{10,2},{3,3},{28,4},{21,5},{14,6},{7,7},{0,8},{25,9}... | collective-permute-start | bytes 239624 | tf_op jit(solution)/shard_map/ppermute | solution.py:246
  31.3 2.5 %collective-permute-done.3 = bf16[24,1664]{1,0:T(8,128)(2,1)S(1)} collective-permute-done((bf16[24,1664]{1,0:T(8,128)(2,1)S(1)}, bf16[24,1664]{1,0:T(8,128)(2,1)S(1)}, u32[]{:S(2)}, u32[]{:S(2)}) %collective-permute-start.3) | collective-permute-done | bytes 79904 | tf_op jit(solution)/shard_map/ppermute | solution.py:246
  33.7 2.8 %collective-permute-done.4 = bf16[24,1664]{1,0:T(8,128)(2,1)S(1)} collective-permute-done((bf16[24,1664]{1,0:T(8,128)(2,1)S(1)}, bf16[24,1664]{1,0:T(8,128)(2,1)S(1)}, u32[]{:S(2)}, u32[]{:S(2)}) %collective-permute-start.4) | collective-permute-done | bytes 79904 | tf_op jit(solution)/shard_map/ppermute | solution.py:246
  36.6 7.6 %all-gather.2 = bf16[8,24,1664]{2,1,0:T(8,128)(2,1)} all-gather(bf16[2,24,1664]{2,1,0:T(8,128)(2,1)S(1)} %pad_maximum_fusion.2), channel_id=4, replica_groups=mesh['req'=8,'tp'=4] {'tp'}, dimensions={0}, use_global_device_ids=true | all-gather | bytes 798720 | tf_op jit(solution)/shard_map/all_gather | solution.py:247
  44.3 6.4 %shard_map.118 = bf16[32,24,384]{2,1,0:T(8,128)(2,1)} custom-call(s32[1]{0:T(128)} %bitcast.31.index_ref, bf16[192,1664]{1,0:T(8,128)(2,1)} %bitcast.94, bf16[4,2,192,1536]{3,2,1,0:T(8,128)(2,1)} %bitcast.93, bf16[4,192,1536]{2,1,0:T(8,128)(2,1)} %dn_ref.1), custom_call_target="tpu_custom_call" | custom-call | tf_op jit(solution)/shard_map/pallas_call | solution.py:92
  50.6 3.6 %all-to-all-start = ((bf16[32,24,384]{2,1,0:T(8,128)(2,1)}), bf16[32,24,384]{2,1,0:T(8,128)(2,1)S(1)}, u32[]{:S(2)}, u32[]{:S(2)}) async-start(bf16[32,24,384]{2,1,0:T(8,128)(2,1)} %shard_map.118), calls=%async_computation | async-start | bytes 1179648 | tf_op jit(solution)/shard_map/all_to_all | solution.py:264
  54.2 16.8 %all-to-all-done = bf16[32,24,384]{2,1,0:T(8,128)(2,1)S(1)} async-done(((bf16[32,24,384]{2,1,0:T(8,128)(2,1)}), bf16[32,24,384]{2,1,0:T(8,128)(2,1)S(1)}, u32[]{:S(2)}, u32[]{:S(2)}) %all-to-all-start) | async-done | bytes 589856 | tf_op jit(solution)/shard_map/all_to_all | solution.py:264
  71.0 0.1 convert_reduce_fusion
  71.1 0.6 add_convert_fusion.1
  (39 shorter events, 0.5 us)
Async XLA Ops:
  0.0 18.5 %copy-start = (bf16[384,1536]{1,0:T(8,128)(2,1)S(1)}, bf16[384,1536]{1,0:T(8,128)(2,1)}, u32[]{:S(2)}) copy-start(bf16[384,1536]{1,0:T(8,128)(2,1)} %param.18) | copy-start | bytes 3538948
  0.0 9.3 %copy-start.1 = (bf16[768,2,2,128]{3,2,1,0:T(2,128)(2,1)S(1)}, bf16[768,2,2,128]{3,2,1,0:T(2,128)(2,1)}, u32[]{:S(2)}) copy-start(bf16[768,2,2,128]{3,2,1,0:T(2,128)(2,1)} %param.17) | copy-start | bytes 2359300
  10.9 4.6 %copy-start.2 = (bf16[24,2,256]{2,1,0:T(2,128)(2,1)S(1)}, bf16[24,2,256]{2,1,0:T(2,128)(2,1)}, u32[]{:S(2)}) copy-start(bf16[24,2,256]{2,1,0:T(2,128)(2,1)} %param.14) | copy-start | bytes 73732
  11.7 4.5 %copy-start.5 = (f32[24,4]{0,1:T(4,128)S(1)}, f32[24,4]{0,1:T(4,128)}, u32[]{:S(2)}) copy-start(f32[24,4]{0,1:T(4,128)} %param.21) | copy-start | bytes 1156
  11.7 4.5 %copy-start.6 = (s32[24,4]{0,1:T(4,128)S(1)}, s32[24,4]{0,1:T(4,128)}, u32[]{:S(2)}) copy-start(s32[24,4]{0,1:T(4,128)} %param.20) | copy-start | bytes 1156
  12.1 4.3 %collective-permute-start = (f32[24,3,130]{2,0,1:T(8,128)S(1)}, f32[24,3,130]{2,0,1:T(8,128)S(1)}, u32[]{:S(2)}, u32[]{:S(2)}) collective-permute-start(f32[24,3,130]{2,0,1:T(8,128)S(1)} %get-tuple-element.17), channel_id=1, source_target_pairs={{0,1},{1,2},{2,3},{3,0},{4,5},{5,6},{6,7},{7,4},{8,9},{9,10},{10,1... | collective-permute-start | bytes 112328 | tf_op jit(solution)/shard_map/ppermute | solution.py:187
  12.5 4.5 %collective-permute-start.1 = (f32[24,3,130]{2,0,1:T(8,128)S(1)}, f32[24,3,130]{2,0,1:T(8,128)S(1)}, u32[]{:S(2)}, u32[]{:S(2)}) collective-permute-start(f32[24,3,130]{2,0,1:T(8,128)S(1)} %get-tuple-element.16), channel_id=1, source_target_pairs={{0,2},{1,3},{2,0},{3,1},{4,6},{5,7},{6,4},{7,5},{8,10},{9,11},{10,... | collective-permute-start | bytes 112328 | tf_op jit(solution)/shard_map/ppermute | solution.py:187
  14.5 3.3 %collective-permute-start.2 = (f32[24,3,130]{2,0,1:T(8,128)S(1)}, f32[24,3,130]{2,0,1:T(8,128)S(1)}, u32[]{:S(2)}, u32[]{:S(2)}) collective-permute-start(f32[24,3,130]{2,0,1:T(8,128)S(1)} %get-tuple-element.15), channel_id=1, source_target_pairs={{0,3},{1,0},{2,1},{3,2},{4,7},{5,4},{6,5},{7,6},{8,11},{9,8},{10,9... | collective-permute-start | bytes 112328 | tf_op jit(solution)/shard_map/ppermute | solution.py:187
  17.8 1.0 %copy-start.3 = (bf16[24,384]{1,0:T(8,128)(2,1)S(1)}, bf16[24,384]{1,0:T(8,128)(2,1)}, u32[]{:S(2)}) copy-start(bf16[24,384]{1,0:T(8,128)(2,1)} %param.12) | copy-start | bytes 55300
  18.8 6.9 %copy-start.4 = (f32[1536]{0:T(1024)S(1)}, f32[1536]{0:T(1024)}, u32[]{:S(2)}) copy-start(f32[1536]{0:T(1024)} %param.19) | copy-start | bytes 18436
  25.9 7.9 %collective-permute-start.3 = (bf16[24,1664]{1,0:T(8,128)(2,1)S(1)}, bf16[24,1664]{1,0:T(8,128)(2,1)S(1)}, u32[]{:S(2)}, u32[]{:S(2)}) collective-permute-start(bf16[24,1664]{1,0:T(8,128)(2,1)S(1)} %pad_maximum_fusion.4), channel_id=1, source_target_pairs={{28,0},{21,1},{14,2},{7,3},{0,4},{25,5},{18,6},{11,7},{4,8},{29,9}... | collective-permute-start | bytes 239624 | tf_op jit(solution)/shard_map/ppermute | solution.py:246
  27.8 8.8 %collective-permute-start.4 = (bf16[24,1664]{1,0:T(8,128)(2,1)S(1)}, bf16[24,1664]{1,0:T(8,128)(2,1)S(1)}, u32[]{:S(2)}, u32[]{:S(2)}) collective-permute-start(bf16[24,1664]{1,0:T(8,128)(2,1)S(1)} %pad_maximum_fusion.4), channel_id=1, source_target_pairs={{24,0},{17,1},{10,2},{3,3},{28,4},{21,5},{14,6},{7,7},{0,8},{25,9}... | collective-permute-start | bytes 239624 | tf_op jit(solution)/shard_map/ppermute | solution.py:246
  50.6 20.4 %all-to-all-start = ((bf16[32,24,384]{2,1,0:T(8,128)(2,1)}), bf16[32,24,384]{2,1,0:T(8,128)(2,1)S(1)}, u32[]{:S(2)}, u32[]{:S(2)}) async-start(bf16[32,24,384]{2,1,0:T(8,128)(2,1)} %shard_map.118), calls=%async_computation | async-start | bytes 1179648 | tf_op jit(solution)/shard_map/all_to_all | solution.py:264

commit v17 on v16

--- a/solution.py
+++ b/solution.py
@@ -135,10 +135,12 @@
     first_head = tp_index * own_heads
     span_rows = cache.shape[0]
 
-    gathered = lax.all_gather(queries, "tp", axis=0)
-    q_raw = jnp.transpose(gathered, (1, 0, 2)).reshape(row_count, head_count, head_size)
+    packed = jnp.stack([queries, hidden_in], axis=0)
+    gathered = lax.all_gather(packed, "tp", axis=0)
+    q_raw = jnp.transpose(gathered[:, 0], (1, 0, 2)).reshape(row_count, head_count, head_size)
     q_all = apply_rotary_heads(q_raw.astype(jnp.float32), positions, head_size).astype(jnp.bfloat16)
     q_all = q_all.reshape(row_count, kv_count, request_group_size, head_size)
+    hidden_full = jnp.transpose(gathered[:, 1], (1, 0, 2)).reshape(row_count, model_width)
 
     k_new = apply_rotary_heads(
         fresh_key_value[:, 0].reshape(row_count, kv_count, head_size).astype(jnp.float32),
@@ -207,10 +209,9 @@
     )
 
     partial_proj = jnp.dot(attention_output, out_proj, preferred_element_type=jnp.float32)
-    proj_message = jnp.concatenate([partial_proj.astype(jnp.bfloat16), hidden_in], axis=1)
-    proj_all = lax.all_gather(proj_message, "tp", axis=0)
-    projected = jnp.sum(proj_all[:, :, :model_width].astype(jnp.float32), axis=0)
-    hidden_full = jnp.transpose(proj_all[:, :, model_width:], (1, 0, 2)).reshape(row_count, model_width)
+    projected = jnp.sum(
+        lax.all_gather(partial_proj.astype(jnp.bfloat16), "tp", axis=0).astype(jnp.float32), axis=0
+    )
     residual = hidden_full.astype(jnp.float32) + projected
     mean_square = jnp.mean(residual * residual, axis=1, keepdims=True)
     normed = (residual * lax.rsqrt(mean_square + norm_eps) * norm_gain[None, :]).astype(jnp.bfloat16)

time: 72.1 us -> 70.7 us (0.981)
    another operation x5 -> x6, other arithmetic: 0.41 us -> 1.25 us  [the longest x1 0.84 us: per_device(): packed = jnp.stack([queries, hidden_in], axis=0)]
    another operation x3, local copies, waits for them, and re-layouts: 0.91 us -> 0.13 us
where the time goes in v17:
time: 70.7 us; the launch traced here: 70.3 us
  waiting for transfers between devices  23.4 us (33%)
  blocking collectives  20.7 us (29%)
  starting transfers between devices  12.3 us (17%)
  Pallas kernels  6.39 us (9%)
  other arithmetic  3.89 us (6%)
  matrix products  1.68 us (2%)
  local copies, waits for them, and re-layouts  1.58 us (2%)
    all_to_all x1, waiting for transfers between devices, per_device(): mixed = lax.all_to_all(mixed, ('req', 'tp'), 0, 0, tiled=True)  16.8 us
    all_gather x1, blocking collectives, gather_req(): shared = lax.all_gather(jnp.stack(fetched, axis=0), 'tp', axis=0)  7.65 us
    all_gather x1, blocking collectives, per_device(): gathered = lax.all_gather(packed, 'tp', axis=0)  6.74 us
    pallas_call x1, Pallas kernels, expert_mix(): pl.pallas_call(body, grid=(group_total // tile_groups, local_count), in_s...  6.39 us
    all_gather x1, blocking collectives, per_device(): lax.all_gather(partial_proj.astype(jnp.bfloat16), 'tp', axis=0)  6.29 us
    ppermute x2, starting transfers between devices, gather_req(): fetched.append(lax.ppermute(value, ('req', 'tp'), pairs))  5.38 us
    ppermute x2, waiting for transfers between devices, gather_req(): fetched.append(lax.ppermute(value, ('req', 'tp'), pairs))  5.31 us
    all_to_all x1, starting transfers between devices, per_device(): mixed = lax.all_to_all(mixed, ('req', 'tp'), 0, 0, tiled=True)  3.56 us
  transfers between devices with their start and end apart: 6, of which 5 were waited for; matrix products, arithmetic and copies ran while one was open for 1% of the time, Pallas kernels for 0%

profile of v17, /device:TPU:0, one launch (start us, length us, event | category | flops | bytes accessed | tf_op | source)
XLA Modules:
  0.0 70.3 jit_solution(393733027100913206)
XLA Ops:
  0.0 0.8 %pad_maximum_fusion.5 = bf16[2,24,384]{2,1,0:T(8,128)(2,1)S(1)} fusion(bf16[1,24,384]{2,1,0:T(8,128)(2,1)} %bitcast.125, bf16[1,24,384]{2,1,0:T(8,128)(2,1)} %bitcast.126), kind=kLoop, calls=%fused_computation.41 | loop fusion | flops 18432 | bytes 73728 | tf_op jit(solution)/shard_map/stack | solution.py:138
  0.9 6.7 %all-gather = bf16[8,24,384]{2,1,0:T(8,128)(2,1)S(1)} all-gather(bf16[2,24,384]{2,1,0:T(8,128)(2,1)S(1)} %pad_maximum_fusion.5), channel_id=2, replica_groups=mesh['req'=8,'tp'=4] {'tp'}, dimensions={0}, use_global_device_ids=true | all-gather | bytes 184320 | tf_op jit(solution)/shard_map/all_gather | solution.py:139
  7.7 0.1 reshape.211
  7.8 0.1 multiply_cosine_fusion
  7.9 0.0 copy-start.2
  7.9 0.1 subtract_convert_fusion
  8.1 0.1 copy.123
  8.3 0.1 reduce.2
  8.4 0.1 copy-done.2
  8.5 0.5 fusion.29
  9.0 0.1 pad_maximum_fusion.4
  9.1 0.1 compare_and_fusion
  9.2 0.5 fusion.30
  9.7 0.1 concatenate.40
  9.9 0.3 fusion.3
  10.2 0.7 %fusion.2 = f32[2,24,6,128]{3,1,2,0:T(8,128)S(1)} fusion(f32[24,2,6,768]{3,0,2,1:T(8,128)S(1)} %get-tuple-element.32, f32[24,2,6]{0,2,1:T(8,128)S(1)} %get-tuple-element.31, pred[24,768]{1,0:T(8,128)(4,1)S(1)} %compare_and_fusion, bf16[768,1,2,128]{3,2,1,0:T(2,128)(2,1)S(1)} %get-tuple-element.9), kind=kOutput, calls=%fused_computation.6 | convolution fusion | flops 340180992 | bytes 1444992 | tf_op jit(solution)/shard_map/rcgj,jcd->rcgd/dot_general | solution.py:173
  10.9 0.1 concatenate.41
  11.1 0.2 pad_maximum_fusion
  11.3 0.4 collective-permute-start
  11.7 1.8 %collective-permute-start.1 = (f32[24,3,130]{2,0,1:T(8,128)S(1)}, f32[24,3,130]{2,0,1:T(8,128)S(1)}, u32[]{:S(2)}, u32[]{:S(2)}) collective-permute-start(f32[24,3,130]{2,0,1:T(8,128)S(1)} %get-tuple-element.16), channel_id=1, source_target_pairs={{0,2},{1,3},{2,0},{3,1},{4,6},{5,7},{6,4},{7,5},{8,10},{9,11},{10,... | collective-permute-start | bytes 112328 | tf_op jit(solution)/shard_map/ppermute | solution.py:189
  13.6 1.1 %collective-permute-start.2 = (f32[24,3,130]{2,0,1:T(8,128)S(1)}, f32[24,3,130]{2,0,1:T(8,128)S(1)}, u32[]{:S(2)}, u32[]{:S(2)}) collective-permute-start(f32[24,3,130]{2,0,1:T(8,128)S(1)} %get-tuple-element.15), channel_id=1, source_target_pairs={{0,3},{1,0},{2,1},{3,2},{4,7},{5,4},{6,5},{7,6},{8,11},{9,8},{10,9... | collective-permute-start | bytes 112328 | tf_op jit(solution)/shard_map/ppermute | solution.py:189
  14.7 0.1 slice_reduce_fusion
  14.8 0.1 subtract_convert_fusion.1
  14.9 0.1 maximum_bitcast_fusion
  15.0 0.2 fusion.11
  15.2 0.1 copy.140
  15.3 0.1 select_reduce_fusion
  15.4 0.1 fusion.22
  15.5 0.7 collective-permute-done.1
  16.2 0.6 collective-permute-done.2
  16.9 0.1 slice_reduce_fusion.1
  17.0 0.1 copy.144
  17.2 0.1 fusion.10
  17.4 0.1 copy.133
  17.6 0.3 convolution_convert_fusion
  17.9 6.3 %all-gather.1 = bf16[96,1536]{1,0:T(8,128)(2,1)S(1)} all-gather(bf16[24,1536]{1,0:T(8,128)(2,1)S(1)} %convolution_convert_fusion), channel_id=3, replica_groups=mesh['req'=8,'tp'=4] {'tp'}, dimensions={0}, use_global_device_ids=true | all-gather | bytes 368640 | tf_op jit(solution)/shard_map/all_gather | solution.py:213
  24.2 0.1 fusion.9
  24.4 0.1 multiply_convert_fusion
  24.5 1.9 %collective-permute-start.3 = (bf16[24,1664]{1,0:T(8,128)(2,1)S(1)}, bf16[24,1664]{1,0:T(8,128)(2,1)S(1)}, u32[]{:S(2)}, u32[]{:S(2)}) collective-permute-start(bf16[24,1664]{1,0:T(8,128)(2,1)S(1)} %pad_maximum_fusion.3), channel_id=1, source_target_pairs={{28,0},{21,1},{14,2},{7,3},{0,4},{25,5},{18,6},{11,7},{4,8},{29,9}... | collective-permute-start | bytes 239624 | tf_op jit(solution)/shard_map/ppermute | solution.py:247
  26.4 3.5 %collective-permute-start.4 = (bf16[24,1664]{1,0:T(8,128)(2,1)S(1)}, bf16[24,1664]{1,0:T(8,128)(2,1)S(1)}, u32[]{:S(2)}, u32[]{:S(2)}) collective-permute-start(bf16[24,1664]{1,0:T(8,128)(2,1)S(1)} %pad_maximum_fusion.3), channel_id=1, source_target_pairs={{24,0},{17,1},{10,2},{3,3},{28,4},{21,5},{14,6},{7,7},{0,8},{25,9}... | collective-permute-start | bytes 239624 | tf_op jit(solution)/shard_map/ppermute | solution.py:247
  29.9 2.5 %collective-permute-done.3 = bf16[24,1664]{1,0:T(8,128)(2,1)S(1)} collective-permute-done((bf16[24,1664]{1,0:T(8,128)(2,1)S(1)}, bf16[24,1664]{1,0:T(8,128)(2,1)S(1)}, u32[]{:S(2)}, u32[]{:S(2)}) %collective-permute-start.3) | collective-permute-done | bytes 79904 | tf_op jit(solution)/shard_map/ppermute | solution.py:247
  32.3 2.8 %collective-permute-done.4 = bf16[24,1664]{1,0:T(8,128)(2,1)S(1)} collective-permute-done((bf16[24,1664]{1,0:T(8,128)(2,1)S(1)}, bf16[24,1664]{1,0:T(8,128)(2,1)S(1)}, u32[]{:S(2)}, u32[]{:S(2)}) %collective-permute-start.4) | collective-permute-done | bytes 79904 | tf_op jit(solution)/shard_map/ppermute | solution.py:247
  35.2 7.6 %all-gather.2 = bf16[8,24,1664]{2,1,0:T(8,128)(2,1)} all-gather(bf16[2,24,1664]{2,1,0:T(8,128)(2,1)S(1)} %pad_maximum_fusion.2), channel_id=4, replica_groups=mesh['req'=8,'tp'=4] {'tp'}, dimensions={0}, use_global_device_ids=true | all-gather | bytes 798720 | tf_op jit(solution)/shard_map/all_gather | solution.py:248
  42.9 6.4 %shard_map.118 = bf16[32,24,384]{2,1,0:T(8,128)(2,1)} custom-call(s32[1]{0:T(128)} %bitcast.35.index_ref, bf16[192,1664]{1,0:T(8,128)(2,1)} %bitcast.108, bf16[4,2,192,1536]{3,2,1,0:T(8,128)(2,1)} %bitcast.107, bf16[4,192,1536]{2,1,0:T(8,128)(2,1)} %dn_ref.1), custom_call_target="tpu_custom_call" | custom-call | tf_op jit(solution)/shard_map/pallas_call | solution.py:92
  49.3 3.6 %all-to-all-start = ((bf16[32,24,384]{2,1,0:T(8,128)(2,1)}), bf16[32,24,384]{2,1,0:T(8,128)(2,1)S(1)}, u32[]{:S(2)}, u32[]{:S(2)}) async-start(bf16[32,24,384]{2,1,0:T(8,128)(2,1)} %shard_map.118), calls=%async_computation | async-start | bytes 1179648 | tf_op jit(solution)/shard_map/all_to_all | solution.py:265
  52.8 16.8 %all-to-all-done = bf16[32,24,384]{2,1,0:T(8,128)(2,1)S(1)} async-done(((bf16[32,24,384]{2,1,0:T(8,128)(2,1)}), bf16[32,24,384]{2,1,0:T(8,128)(2,1)S(1)}, u32[]{:S(2)}, u32[]{:S(2)}) %all-to-all-start) | async-done | bytes 589856 | tf_op jit(solution)/shard_map/all_to_all | solution.py:265
  69.6 0.1 convert_reduce_fusion
  69.7 0.6 add_convert_fusion.1
  (45 shorter events, 0.5 us)
Async XLA Ops:
  0.0 17.6 %copy-start = (bf16[384,1536]{1,0:T(8,128)(2,1)S(1)}, bf16[384,1536]{1,0:T(8,128)(2,1)}, u32[]{:S(2)}) copy-start(bf16[384,1536]{1,0:T(8,128)(2,1)} %param.18) | copy-start | bytes 3538948
  0.0 7.7 %copy-start.9 = (s32[24]{0:T(128)S(1)}, s32[24]{0:T(128)}, u32[]{:S(2)}) copy-start(s32[24]{0:T(128)} %param.15) | copy-start | bytes 292
  0.0 8.1 %copy-start.8 = (s32[1,24]{1,0:T(1,128)S(1)}, s32[1,24]{1,0:T(1,128)}, u32[]{:S(2)}) copy-start(s32[1,24]{1,0:T(1,128)} %param.16) | copy-start | bytes 292
  0.9 7.6 %copy-start.1 = (bf16[768,2,2,128]{3,2,1,0:T(2,128)(2,1)S(1)}, bf16[768,2,2,128]{3,2,1,0:T(2,128)(2,1)}, u32[]{:S(2)}) copy-start(bf16[768,2,2,128]{3,2,1,0:T(2,128)(2,1)} %param.17) | copy-start | bytes 2359300
  7.9 0.6 copy-start.2
  10.2 4.5 %copy-start.4 = (bf16[24,2,256]{2,1,0:T(2,128)(2,1)S(1)}, bf16[24,2,256]{2,1,0:T(2,128)(2,1)}, u32[]{:S(2)}) copy-start(bf16[24,2,256]{2,1,0:T(2,128)(2,1)} %param.14) | copy-start | bytes 73732
  10.9 3.9 %copy-start.3 = (f32[24,64]{1,0:T(8,128)S(1)}, f32[24,64]{1,0:T(8,128)}, u32[]{:S(2)}) copy-start(f32[24,64]{1,0:T(8,128)} %copy-done.2) | copy-start | bytes 18436
  10.9 4.4 %copy-start.6 = (f32[24,4]{0,1:T(4,128)S(1)}, f32[24,4]{0,1:T(4,128)}, u32[]{:S(2)}) copy-start(f32[24,4]{0,1:T(4,128)} %param.21) | copy-start | bytes 1156
  10.9 4.4 %copy-start.7 = (s32[24,4]{0,1:T(4,128)S(1)}, s32[24,4]{0,1:T(4,128)}, u32[]{:S(2)}) copy-start(s32[24,4]{0,1:T(4,128)} %param.20) | copy-start | bytes 1156
  11.3 4.2 %collective-permute-start = (f32[24,3,130]{2,0,1:T(8,128)S(1)}, f32[24,3,130]{2,0,1:T(8,128)S(1)}, u32[]{:S(2)}, u32[]{:S(2)}) collective-permute-start(f32[24,3,130]{2,0,1:T(8,128)S(1)} %get-tuple-element.17), channel_id=1, source_target_pairs={{0,1},{1,2},{2,3},{3,0},{4,5},{5,6},{6,7},{7,4},{8,9},{9,10},{10,1... | collective-permute-start | bytes 112328 | tf_op jit(solution)/shard_map/ppermute | solution.py:189
  11.7 4.5 %collective-permute-start.1 = (f32[24,3,130]{2,0,1:T(8,128)S(1)}, f32[24,3,130]{2,0,1:T(8,128)S(1)}, u32[]{:S(2)}, u32[]{:S(2)}) collective-permute-start(f32[24,3,130]{2,0,1:T(8,128)S(1)} %get-tuple-element.16), channel_id=1, source_target_pairs={{0,2},{1,3},{2,0},{3,1},{4,6},{5,7},{6,4},{7,5},{8,10},{9,11},{10,... | collective-permute-start | bytes 112328 | tf_op jit(solution)/shard_map/ppermute | solution.py:189
  13.6 3.3 %collective-permute-start.2 = (f32[24,3,130]{2,0,1:T(8,128)S(1)}, f32[24,3,130]{2,0,1:T(8,128)S(1)}, u32[]{:S(2)}, u32[]{:S(2)}) collective-permute-start(f32[24,3,130]{2,0,1:T(8,128)S(1)} %get-tuple-element.15), channel_id=1, source_target_pairs={{0,3},{1,0},{2,1},{3,2},{4,7},{5,4},{6,5},{7,6},{8,11},{9,8},{10,9... | collective-permute-start | bytes 112328 | tf_op jit(solution)/shard_map/ppermute | solution.py:189
  17.5 6.8 %copy-start.5 = (f32[1536]{0:T(1024)S(1)}, f32[1536]{0:T(1024)}, u32[]{:S(2)}) copy-start(f32[1536]{0:T(1024)} %param.19) | copy-start | bytes 18436
  24.5 7.9 %collective-permute-start.3 = (bf16[24,1664]{1,0:T(8,128)(2,1)S(1)}, bf16[24,1664]{1,0:T(8,128)(2,1)S(1)}, u32[]{:S(2)}, u32[]{:S(2)}) collective-permute-start(bf16[24,1664]{1,0:T(8,128)(2,1)S(1)} %pad_maximum_fusion.3), channel_id=1, source_target_pairs={{28,0},{21,1},{14,2},{7,3},{0,4},{25,5},{18,6},{11,7},{4,8},{29,9}... | collective-permute-start | bytes 239624 | tf_op jit(solution)/shard_map/ppermute | solution.py:247
  26.4 8.8 %collective-permute-start.4 = (bf16[24,1664]{1,0:T(8,128)(2,1)S(1)}, bf16[24,1664]{1,0:T(8,128)(2,1)S(1)}, u32[]{:S(2)}, u32[]{:S(2)}) collective-permute-start(bf16[24,1664]{1,0:T(8,128)(2,1)S(1)} %pad_maximum_fusion.3), channel_id=1, source_target_pairs={{24,0},{17,1},{10,2},{3,3},{28,4},{21,5},{14,6},{7,7},{0,8},{25,9}... | collective-permute-start | bytes 239624 | tf_op jit(solution)/shard_map/ppermute | solution.py:247
  49.3 20.4 %all-to-all-start = ((bf16[32,24,384]{2,1,0:T(8,128)(2,1)}), bf16[32,24,384]{2,1,0:T(8,128)(2,1)S(1)}, u32[]{:S(2)}, u32[]{:S(2)}) async-start(bf16[32,24,384]{2,1,0:T(8,128)(2,1)} %shard_map.118), calls=%async_computation | async-start | bytes 1179648 | tf_op jit(solution)/shard_map/all_to_all | solution.py:265

commit v18 on v17

--- a/solution.py
+++ b/solution.py
@@ -177,10 +177,17 @@
         precision=lax.Precision.HIGHEST,
         preferred_element_type=jnp.float32,
     )
-    states = jnp.concatenate(
-        [highest_local[..., None], totals_local[..., None], sums_local], axis=3
-    ).reshape(row_count, tp_count, own_heads, head_size + 2)
-    states = jnp.transpose(states, (1, 0, 2, 3))
+    sums_heads = sums_local.reshape(row_count, tp_count, own_heads * head_size)
+    stats = jnp.concatenate(
+        [
+            highest_local.reshape(row_count, tp_count, own_heads),
+            totals_local.reshape(row_count, tp_count, own_heads),
+        ],
+        axis=2,
+    )
+    stats_lanes = -(-stats.shape[2] // 128) * 128
+    stats = jnp.pad(stats, ((0, 0), (0, 0), (0, stats_lanes - stats.shape[2])))
+    states = jnp.transpose(jnp.concatenate([sums_heads, stats], axis=2), (1, 0, 2))
     own_part_states = lax.dynamic_index_in_dim(states, tp_index, 0, keepdims=False)
     all_states = [own_part_states]
     for shift in range(1, tp_count):
@@ -189,9 +196,10 @@
             lax.ppermute(outgoing, "tp", [(i, (i + shift) % tp_count) for i in range(tp_count)])
         )
     all_states = jnp.stack(all_states, axis=0)
-    parts_highest = all_states[..., 0]
-    parts_totals = all_states[..., 1]
-    parts_sums = all_states[..., 2:]
+    sums_width = own_heads * head_size
+    parts_sums = all_states[:, :, :sums_width].reshape(tp_count, row_count, own_heads, head_size)
+    parts_highest = all_states[:, :, sums_width : sums_width + own_heads]
+    parts_totals = all_states[:, :, sums_width + own_heads : sums_width + 2 * own_heads]
     own_slice = lax.dynamic_slice_in_dim(own_score.reshape(row_count, head_count), first_head, own_heads, 1)
     top_score = jnp.maximum(jnp.max(parts_highest, axis=0), own_slice)
     factors = jnp.exp(parts_highest - top_score[None])

time: 70.7 us -> 70.1 us (level)
  no operation moved by 1% of the time
where the time goes in v18:
time: 70.1 us; the launch traced here: 69.8 us
  waiting for transfers between devices  22.9 us (33%)
  blocking collectives  20.7 us (30%)
  starting transfers between devices  12.2 us (17%)
  Pallas kernels  6.38 us (9%)
  other arithmetic  3.82 us (5%)
  local copies, waits for them, and re-layouts  1.82 us (3%)
  matrix products  1.63 us (2%)
    all_to_all x1, waiting for transfers between devices, per_device(): mixed = lax.all_to_all(mixed, ('req', 'tp'), 0, 0, tiled=True)  16.8 us
    all_gather x1, blocking collectives, gather_req(): shared = lax.all_gather(jnp.stack(fetched, axis=0), 'tp', axis=0)  7.78 us
    all_gather x1, blocking collectives, per_device(): gathered = lax.all_gather(packed, 'tp', axis=0)  6.74 us
    pallas_call x1, Pallas kernels, expert_mix(): pl.pallas_call(body, grid=(group_total // tile_groups, local_count), in_s...  6.38 us
    all_gather x1, blocking collectives, per_device(): lax.all_gather(partial_proj.astype(jnp.bfloat16), 'tp', axis=0)  6.16 us
    ppermute x2, waiting for transfers between devices, gather_req(): fetched.append(lax.ppermute(value, ('req', 'tp'), pairs))  5.3 us
    ppermute x2, starting transfers between devices, gather_req(): fetched.append(lax.ppermute(value, ('req', 'tp'), pairs))  5.24 us
    all_to_all x1, starting transfers between devices, per_device(): mixed = lax.all_to_all(mixed, ('req', 'tp'), 0, 0, tiled=True)  3.57 us
  transfers between devices with their start and end apart: 6, of which 5 were waited for; matrix products, arithmetic and copies ran while one was open for 1% of the time, Pallas kernels for 0%

profile of v18, /device:TPU:0, one launch (start us, length us, event | category | flops | bytes accessed | tf_op | source)
XLA Modules:
  0.0 69.8 jit_solution(16096152927381677350)
XLA Ops:
  0.0 0.8 %pad_maximum_fusion.5 = bf16[2,24,384]{2,1,0:T(8,128)(2,1)S(1)} fusion(bf16[1,24,384]{2,1,0:T(8,128)(2,1)} %bitcast.134, bf16[1,24,384]{2,1,0:T(8,128)(2,1)} %bitcast.135), kind=kLoop, calls=%fused_computation.61 | loop fusion | flops 18432 | bytes 73728 | tf_op jit(solution)/shard_map/stack | solution.py:138
  0.9 6.7 %all-gather = bf16[8,24,384]{2,1,0:T(8,128)(2,1)S(1)} all-gather(bf16[2,24,384]{2,1,0:T(8,128)(2,1)S(1)} %pad_maximum_fusion.5), channel_id=2, replica_groups=mesh['req'=8,'tp'=4] {'tp'}, dimensions={0}, use_global_device_ids=true | all-gather | bytes 184320 | tf_op jit(solution)/shard_map/all_gather | solution.py:139
  7.8 0.1 multiply_cosine_fusion
  7.9 0.1 subtract_convert_fusion
  8.1 0.1 copy.51
  8.3 0.1 reduce.2
  8.4 0.1 copy-done.2
  8.5 0.5 fusion.29
  9.0 0.1 pad_maximum_fusion.3
  9.1 0.1 compare_and_fusion
  9.2 0.5 fusion.30
  9.7 0.3 fusion.2
  10.1 0.1 copy.59
  10.2 0.1 copy.58
  10.3 0.7 %convolution_bitcast_fusion = f32[24,2,6,128]{3,0,2,1:T(8,128)S(1)} fusion(f32[24,2,6,768]{3,0,2,1:T(8,128)S(1)} %get-tuple-element.31, f32[24,2,6]{0,2,1:T(8,128)S(1)} %get-tuple-element.30, pred[24,768]{1,0:T(8,128)(4,1)S(1)} %compare_and_fusion, bf16[768,1,2,128]{3,2,1,0:T(2,128)(2,1)S(1)} %get-tuple-element.9), kind=kOutput, calls=%fused_computation.5 | convolution fusion | flops 340180992 | bytes 1444992 | tf_op jit(solution)/shard_map/rcgj,jcd->rcgd/dot_general | solution.py:173
  11.2 0.1 select_maximum_fusion
  11.3 0.2 fusion.13
  11.5 0.4 collective-permute-start
  11.9 1.8 %collective-permute-start.1 = (f32[24,512]{1,0:T(8,128)S(1)}, f32[24,512]{1,0:T(8,128)S(1)}, u32[]{:S(2)}, u32[]{:S(2)}) collective-permute-start(f32[24,512]{1,0:T(8,128)S(1)} %bitcast.132), channel_id=1, source_target_pairs={{0,2},{1,3},{2,0},{3,1},{4,6},{5,7},{6,4},{7,5},{8,10},{9,11},{10,... | collective-permute-start | bytes 147464 | tf_op jit(solution)/shard_map/ppermute | solution.py:196
  13.7 1.1 %collective-permute-start.2 = (f32[24,512]{1,0:T(8,128)S(1)}, f32[24,512]{1,0:T(8,128)S(1)}, u32[]{:S(2)}, u32[]{:S(2)}) collective-permute-start(f32[24,512]{1,0:T(8,128)S(1)} %bitcast.133), channel_id=1, source_target_pairs={{0,3},{1,0},{2,1},{3,2},{4,7},{5,4},{6,5},{7,6},{8,11},{9,8},{10,9... | collective-permute-start | bytes 147464 | tf_op jit(solution)/shard_map/ppermute | solution.py:196
  14.9 0.1 slice_reduce_fusion
  15.0 0.1 subtract_convert_fusion.1
  15.1 0.1 maximum_bitcast_fusion
  15.2 0.2 fusion.10
  15.3 0.1 copy.66
  15.5 0.1 select_reduce_fusion
  15.7 0.1 copy.74
  15.8 0.2 collective-permute-done.1
  16.0 0.6 collective-permute-done.2
  16.7 0.1 subtract_exponential_fusion
  16.8 0.2 mul.193
  16.9 0.1 mul.194
  17.1 0.1 broadcast_multiply_fusion
  17.2 0.1 div.19
  17.3 0.3 convolution_convert_fusion
  17.5 6.2 %all-gather.1 = bf16[96,1536]{1,0:T(8,128)(2,1)S(1)} all-gather(bf16[24,1536]{1,0:T(8,128)(2,1)S(1)} %convolution_convert_fusion), channel_id=3, replica_groups=mesh['req'=8,'tp'=4] {'tp'}, dimensions={0}, use_global_device_ids=true | all-gather | bytes 368640 | tf_op jit(solution)/shard_map/all_gather | solution.py:221
  23.7 0.1 fusion.8
  23.9 0.1 multiply_convert_fusion
  24.0 1.8 %collective-permute-start.3 = (bf16[24,1664]{1,0:T(8,128)(2,1)S(1)}, bf16[24,1664]{1,0:T(8,128)(2,1)S(1)}, u32[]{:S(2)}, u32[]{:S(2)}) collective-permute-start(bf16[24,1664]{1,0:T(8,128)(2,1)S(1)} %pad_maximum_fusion.2), channel_id=1, source_target_pairs={{28,0},{21,1},{14,2},{7,3},{0,4},{25,5},{18,6},{11,7},{4,8},{29,9}... | collective-permute-start | bytes 239624 | tf_op jit(solution)/shard_map/ppermute | solution.py:255
  25.7 3.5 %collective-permute-start.4 = (bf16[24,1664]{1,0:T(8,128)(2,1)S(1)}, bf16[24,1664]{1,0:T(8,128)(2,1)S(1)}, u32[]{:S(2)}, u32[]{:S(2)}) collective-permute-start(bf16[24,1664]{1,0:T(8,128)(2,1)S(1)} %pad_maximum_fusion.2), channel_id=1, source_target_pairs={{24,0},{17,1},{10,2},{3,3},{28,4},{21,5},{14,6},{7,7},{0,8},{25,9}... | collective-permute-start | bytes 239624 | tf_op jit(solution)/shard_map/ppermute | solution.py:255
  29.2 2.5 %collective-permute-done.3 = bf16[24,1664]{1,0:T(8,128)(2,1)S(1)} collective-permute-done((bf16[24,1664]{1,0:T(8,128)(2,1)S(1)}, bf16[24,1664]{1,0:T(8,128)(2,1)S(1)}, u32[]{:S(2)}, u32[]{:S(2)}) %collective-permute-start.3) | collective-permute-done | bytes 79904 | tf_op jit(solution)/shard_map/ppermute | solution.py:255
  31.7 2.8 %collective-permute-done.4 = bf16[24,1664]{1,0:T(8,128)(2,1)S(1)} collective-permute-done((bf16[24,1664]{1,0:T(8,128)(2,1)S(1)}, bf16[24,1664]{1,0:T(8,128)(2,1)S(1)}, u32[]{:S(2)}, u32[]{:S(2)}) %collective-permute-start.4) | collective-permute-done | bytes 79904 | tf_op jit(solution)/shard_map/ppermute | solution.py:255
  34.6 7.8 %all-gather.2 = bf16[8,24,1664]{2,1,0:T(8,128)(2,1)} all-gather(bf16[2,24,1664]{2,1,0:T(8,128)(2,1)S(1)} %pad_maximum_fusion.1), channel_id=4, replica_groups=mesh['req'=8,'tp'=4] {'tp'}, dimensions={0}, use_global_device_ids=true | all-gather | bytes 798720 | tf_op jit(solution)/shard_map/all_gather | solution.py:256
  42.3 6.4 %shard_map.118 = bf16[32,24,384]{2,1,0:T(8,128)(2,1)} custom-call(s32[1]{0:T(128)} %bitcast.27.index_ref, bf16[192,1664]{1,0:T(8,128)(2,1)} %bitcast.104, bf16[4,2,192,1536]{3,2,1,0:T(8,128)(2,1)} %bitcast.103, bf16[4,192,1536]{2,1,0:T(8,128)(2,1)} %dn_ref.1), custom_call_target="tpu_custom_call" | custom-call | tf_op jit(solution)/shard_map/pallas_call | solution.py:92
  48.7 3.6 %all-to-all-start = ((bf16[32,24,384]{2,1,0:T(8,128)(2,1)}), bf16[32,24,384]{2,1,0:T(8,128)(2,1)S(1)}, u32[]{:S(2)}, u32[]{:S(2)}) async-start(bf16[32,24,384]{2,1,0:T(8,128)(2,1)} %shard_map.118), calls=%async_computation | async-start | bytes 1179648 | tf_op jit(solution)/shard_map/all_to_all | solution.py:273
  52.3 16.8 %all-to-all-done = bf16[32,24,384]{2,1,0:T(8,128)(2,1)S(1)} async-done(((bf16[32,24,384]{2,1,0:T(8,128)(2,1)}), bf16[32,24,384]{2,1,0:T(8,128)(2,1)S(1)}, u32[]{:S(2)}, u32[]{:S(2)}) %all-to-all-start) | async-done | bytes 589856 | tf_op jit(solution)/shard_map/all_to_all | solution.py:273
  69.1 0.1 convert_reduce_fusion
  69.2 0.6 add_convert_fusion.1
  (55 shorter events, 0.7 us)
Async XLA Ops:
  0.0 17.2 %copy-start = (bf16[384,1536]{1,0:T(8,128)(2,1)S(1)}, bf16[384,1536]{1,0:T(8,128)(2,1)}, u32[]{:S(2)}) copy-start(bf16[384,1536]{1,0:T(8,128)(2,1)} %param.18) | copy-start | bytes 3538948
  0.0 7.7 %copy-start.9 = (s32[24]{0:T(128)S(1)}, s32[24]{0:T(128)}, u32[]{:S(2)}) copy-start(s32[24]{0:T(128)} %param.15) | copy-start | bytes 292
  0.0 8.1 %copy-start.8 = (s32[1,24]{1,0:T(1,128)S(1)}, s32[1,24]{1,0:T(1,128)}, u32[]{:S(2)}) copy-start(s32[1,24]{1,0:T(1,128)} %param.16) | copy-start | bytes 292
  0.9 7.6 %copy-start.1 = (bf16[768,2,2,128]{3,2,1,0:T(2,128)(2,1)S(1)}, bf16[768,2,2,128]{3,2,1,0:T(2,128)(2,1)}, u32[]{:S(2)}) copy-start(bf16[768,2,2,128]{3,2,1,0:T(2,128)(2,1)} %param.17) | copy-start | bytes 2359300
  7.9 0.6 copy-start.2
  10.3 4.6 %copy-start.4 = (bf16[24,2,256]{2,1,0:T(2,128)(2,1)S(1)}, bf16[24,2,256]{2,1,0:T(2,128)(2,1)}, u32[]{:S(2)}) copy-start(bf16[24,2,256]{2,1,0:T(2,128)(2,1)} %param.14) | copy-start | bytes 73732
  11.0 4.0 %copy-start.3 = (f32[24,64]{1,0:T(8,128)S(1)}, f32[24,64]{1,0:T(8,128)}, u32[]{:S(2)}) copy-start(f32[24,64]{1,0:T(8,128)} %copy-done.2) | copy-start | bytes 18436
  11.0 4.5 %copy-start.6 = (f32[24,4]{0,1:T(4,128)S(1)}, f32[24,4]{0,1:T(4,128)}, u32[]{:S(2)}) copy-start(f32[24,4]{0,1:T(4,128)} %param.21) | copy-start | bytes 1156
  11.0 4.4 %copy-start.7 = (s32[24,4]{0,1:T(4,128)S(1)}, s32[24,4]{0,1:T(4,128)}, u32[]{:S(2)}) copy-start(s32[24,4]{0,1:T(4,128)} %param.20) | copy-start | bytes 1156
  11.5 4.3 %collective-permute-start = (f32[24,512]{1,0:T(8,128)S(1)}, f32[24,512]{1,0:T(8,128)S(1)}, u32[]{:S(2)}, u32[]{:S(2)}) collective-permute-start(f32[24,512]{1,0:T(8,128)S(1)} %bitcast.131), channel_id=1, source_target_pairs={{0,1},{1,2},{2,3},{3,0},{4,5},{5,6},{6,7},{7,4},{8,9},{9,10},{10,1... | collective-permute-start | bytes 147464 | tf_op jit(solution)/shard_map/ppermute | solution.py:196
  11.9 4.1 %collective-permute-start.1 = (f32[24,512]{1,0:T(8,128)S(1)}, f32[24,512]{1,0:T(8,128)S(1)}, u32[]{:S(2)}, u32[]{:S(2)}) collective-permute-start(f32[24,512]{1,0:T(8,128)S(1)} %bitcast.132), channel_id=1, source_target_pairs={{0,2},{1,3},{2,0},{3,1},{4,6},{5,7},{6,4},{7,5},{8,10},{9,11},{10,... | collective-permute-start | bytes 147464 | tf_op jit(solution)/shard_map/ppermute | solution.py:196
  13.7 2.9 %collective-permute-start.2 = (f32[24,512]{1,0:T(8,128)S(1)}, f32[24,512]{1,0:T(8,128)S(1)}, u32[]{:S(2)}, u32[]{:S(2)}) collective-permute-start(f32[24,512]{1,0:T(8,128)S(1)} %bitcast.133), channel_id=1, source_target_pairs={{0,3},{1,0},{2,1},{3,2},{4,7},{5,4},{6,5},{7,6},{8,11},{9,8},{10,9... | collective-permute-start | bytes 147464 | tf_op jit(solution)/shard_map/ppermute | solution.py:196
  17.2 6.6 %copy-start.5 = (f32[1536]{0:T(1024)S(1)}, f32[1536]{0:T(1024)}, u32[]{:S(2)}) copy-start(f32[1536]{0:T(1024)} %param.19) | copy-start | bytes 18436
  24.0 7.7 %collective-permute-start.3 = (bf16[24,1664]{1,0:T(8,128)(2,1)S(1)}, bf16[24,1664]{1,0:T(8,128)(2,1)S(1)}, u32[]{:S(2)}, u32[]{:S(2)}) collective-permute-start(bf16[24,1664]{1,0:T(8,128)(2,1)S(1)} %pad_maximum_fusion.2), channel_id=1, source_target_pairs={{28,0},{21,1},{14,2},{7,3},{0,4},{25,5},{18,6},{11,7},{4,8},{29,9}... | collective-permute-start | bytes 239624 | tf_op jit(solution)/shard_map/ppermute | solution.py:255
  25.7 8.8 %collective-permute-start.4 = (bf16[24,1664]{1,0:T(8,128)(2,1)S(1)}, bf16[24,1664]{1,0:T(8,128)(2,1)S(1)}, u32[]{:S(2)}, u32[]{:S(2)}) collective-permute-start(bf16[24,1664]{1,0:T(8,128)(2,1)S(1)} %pad_maximum_fusion.2), channel_id=1, source_target_pairs={{24,0},{17,1},{10,2},{3,3},{28,4},{21,5},{14,6},{7,7},{0,8},{25,9}... | collective-permute-start | bytes 239624 | tf_op jit(solution)/shard_map/ppermute | solution.py:255
  48.7 20.4 %all-to-all-start = ((bf16[32,24,384]{2,1,0:T(8,128)(2,1)}), bf16[32,24,384]{2,1,0:T(8,128)(2,1)S(1)}, u32[]{:S(2)}, u32[]{:S(2)}) async-start(bf16[32,24,384]{2,1,0:T(8,128)(2,1)} %shard_map.118), calls=%async_computation | async-start | bytes 1179648 | tf_op jit(solution)/shard_map/all_to_all | solution.py:273

commit v19 on v18

--- a/solution.py
+++ b/solution.py
@@ -63,7 +63,10 @@
         for group in range(tile_groups):
             if arrival_order:
                 group_total = o_ref.shape[0] // tp_count
-                dest = (index_ref[0] + 2 * group_total - group - 1) % group_total
+                per_tp = group_total // tp_count
+                source_tp = (index_ref[1] + tp_count - group // per_tp) % tp_count
+                message = source_tp * per_tp + group % per_tp
+                dest = (index_ref[0] + 2 * group_total - message - 1) % group_total
             else:
                 dest = group
             for part in range(tp_count):
@@ -253,7 +256,12 @@
                     source = ((group - shift) % req_count) * tp_count + part
                     pairs.append((source, group * tp_count + part))
             fetched.append(lax.ppermute(value, ("req", "tp"), pairs))
-        shared = lax.all_gather(jnp.stack(fetched, axis=0), "tp", axis=0)
+        fetched = jnp.stack(fetched, axis=0)
+        shared = [fetched] + [
+            lax.ppermute(fetched, "tp", [(i, (i + shift) % tp_count) for i in range(tp_count)])
+            for shift in range(1, tp_count)
+        ]
+        shared = jnp.stack(shared, axis=0)
         shared = shared.reshape((req_count * value.shape[0],) + value.shape[1:])
         return shared, True
 
@@ -266,7 +274,7 @@
     code = jnp.pad(code, ((0, 0), (0, code_lanes - code.shape[1])))
     message = jnp.concatenate([normed, code], axis=1)
     message_all, arrival_order = gather_req(message)
-    index_scalar = req_index.astype(jnp.int32).reshape(1)
+    index_scalar = jnp.stack([req_index, tp_index]).astype(jnp.int32)
     mixed = expert_mix(
         message_all, gate_up, down, index_scalar, arrival_order, model_width, block_total, row_count, tp_count
     )

time: 70.1 us -> 73.1 us (1.043)
  blocking collectives: 20.7 us -> 12.9 us
  waiting for transfers between devices: 22.9 us -> 28.2 us
  starting transfers between devices: 12.2 us -> 16 us
  other arithmetic: 3.82 us -> 5.33 us
    all_gather x1 -> x0, blocking collectives: 7.78 us -> none  [gather_req(): shared = lax.all_gather(jnp.stack(fetched, axis=0), 'tp', axis=0)]
    ppermute x0 -> x3, waiting for transfers between devices: none -> 5.31 us  [gather_req(): lax.ppermute(fetched, 'tp', [(i, (i + shift) % tp_count) for i in range(t...]
    ppermute x0 -> x3, starting transfers between devices: none -> 2.54 us  [gather_req(): lax.ppermute(fetched, 'tp', [(i, (i + shift) % tp_count) for i in range(t...]
    another operation x6 -> x8, other arithmetic: 0.43 us -> 1.93 us  [the longest x2 0.95 us: gather_req(): shared = jnp.stack(shared, axis=0)]
    all_to_all x1, starting transfers between devices: 3.57 us -> 4.92 us  [per_device(): mixed = lax.all_to_all(mixed, ('req', 'tp'), 0, 0, tiled=True)]
  transfers between devices with their start and end apart: 6 -> 9, of which waited for: 5 -> 8; matrix products, arithmetic and copies ran while one was open for 1% -> 2% of each run, Pallas kernels for 0% -> 0%
where the time goes in v19:
time: 73.1 us; the launch traced here: 72.8 us
  waiting for transfers between devices  28.2 us (39%)
  starting transfers between devices  16 us (22%)
  blocking collectives  12.9 us (18%)
  Pallas kernels  6.42 us (9%)
  other arithmetic  5.33 us (7%)
  local copies, waits for them, and re-layouts  1.82 us (2%)
  matrix products  1.63 us (2%)
    all_to_all x1, waiting for transfers between devices, per_device(): mixed = lax.all_to_all(mixed, ('req', 'tp'), 0, 0, tiled=True)  16.8 us
    all_gather x1, blocking collectives, per_device(): gathered = lax.all_gather(packed, 'tp', axis=0)  6.74 us
    pallas_call x1, Pallas kernels, expert_mix(): pl.pallas_call(body, grid=(group_total // tile_groups, local_count), in_s...  6.42 us
    all_gather x1, blocking collectives, per_device(): lax.all_gather(partial_proj.astype(jnp.bfloat16), 'tp', axis=0)  6.16 us
    ppermute x3, waiting for transfers between devices, gather_req(): lax.ppermute(fetched, 'tp', [(i, (i + shift) % tp_count) for i in range(t...  5.31 us
    ppermute x2, waiting for transfers between devices, gather_req(): fetched.append(lax.ppermute(value, ('req', 'tp'), pairs))  5.31 us
    ppermute x2, starting transfers between devices, gather_req(): fetched.append(lax.ppermute(value, ('req', 'tp'), pairs))  5.24 us
    all_to_all x1, starting transfers between devices, per_device(): mixed = lax.all_to_all(mixed, ('req', 'tp'), 0, 0, tiled=True)  4.92 us
  transfers between devices with their start and end apart: 9, of which 8 were waited for; matrix products, arithmetic and copies ran while one was open for 2% of the time, Pallas kernels for 0%

profile of v19, /device:TPU:0, one launch (start us, length us, event | category | flops | bytes accessed | tf_op | source)
XLA Modules:
  0.0 72.8 jit_solution(8634156348961343970)
XLA Ops:
  0.0 0.8 %pad_maximum_fusion.6 = bf16[2,24,384]{2,1,0:T(8,128)(2,1)S(1)} fusion(bf16[1,24,384]{2,1,0:T(8,128)(2,1)} %bitcast.143, bf16[1,24,384]{2,1,0:T(8,128)(2,1)} %bitcast.144), kind=kLoop, calls=%fused_computation.62 | loop fusion | flops 18432 | bytes 73728 | tf_op jit(solution)/shard_map/stack | solution.py:141
  0.9 6.7 %all-gather = bf16[8,24,384]{2,1,0:T(8,128)(2,1)S(1)} all-gather(bf16[2,24,384]{2,1,0:T(8,128)(2,1)S(1)} %pad_maximum_fusion.6), channel_id=2, replica_groups=mesh['req'=8,'tp'=4] {'tp'}, dimensions={0}, use_global_device_ids=true | all-gather | bytes 184320 | tf_op jit(solution)/shard_map/all_gather | solution.py:142
  7.8 0.1 multiply_cosine_fusion
  7.9 0.1 subtract_convert_fusion
  8.3 0.1 reduce.2
  8.4 0.1 copy-done.2
  8.5 0.5 fusion.30
  9.0 0.1 pad_maximum_fusion.4
  9.2 0.5 fusion.31
  9.7 0.3 fusion.2
  10.1 0.1 copy.59
  10.2 0.1 copy.58
  10.3 0.7 convolution_bitcast_fusion
  11.2 0.1 select_maximum_fusion
  11.3 0.2 fusion.13
  11.5 0.4 collective-permute-start
  11.9 1.8 %collective-permute-start.1 = (f32[24,512]{1,0:T(8,128)S(1)}, f32[24,512]{1,0:T(8,128)S(1)}, u32[]{:S(2)}, u32[]{:S(2)}) collective-permute-start(f32[24,512]{1,0:T(8,128)S(1)} %bitcast.141), channel_id=1, source_target_pairs={{0,2},{1,3},{2,0},{3,1},{4,6},{5,7},{6,4},{7,5},{8,10},{9,11},{10,... | collective-permute-start | bytes 147464 | tf_op jit(solution)/shard_map/ppermute | solution.py:199
  13.7 1.1 %collective-permute-start.2 = (f32[24,512]{1,0:T(8,128)S(1)}, f32[24,512]{1,0:T(8,128)S(1)}, u32[]{:S(2)}, u32[]{:S(2)}) collective-permute-start(f32[24,512]{1,0:T(8,128)S(1)} %bitcast.142), channel_id=1, source_target_pairs={{0,3},{1,0},{2,1},{3,2},{4,7},{5,4},{6,5},{7,6},{8,11},{9,8},{10,9... | collective-permute-start | bytes 147464 | tf_op jit(solution)/shard_map/ppermute | solution.py:199
  15.0 0.1 subtract_convert_fusion.1
  15.1 0.1 maximum_bitcast_fusion
  15.2 0.2 fusion.10
  15.3 0.1 copy.66
  15.5 0.1 select_reduce_fusion
  15.8 0.2 collective-permute-done.1
  16.0 0.6 collective-permute-done.2
  16.7 0.1 subtract_exponential_fusion
  16.8 0.2 mul.193
  17.1 0.1 broadcast_multiply_fusion
  17.3 0.3 convolution_convert_fusion
  17.5 6.2 %all-gather.1 = bf16[96,1536]{1,0:T(8,128)(2,1)S(1)} all-gather(bf16[24,1536]{1,0:T(8,128)(2,1)S(1)} %convolution_convert_fusion), channel_id=3, replica_groups=mesh['req'=8,'tp'=4] {'tp'}, dimensions={0}, use_global_device_ids=true | all-gather | bytes 368640 | tf_op jit(solution)/shard_map/all_gather | solution.py:224
  23.7 0.1 fusion.8
  23.9 0.1 multiply_convert_fusion
  24.0 1.8 %collective-permute-start.3 = (bf16[24,1664]{1,0:T(8,128)(2,1)S(1)}, bf16[24,1664]{1,0:T(8,128)(2,1)S(1)}, u32[]{:S(2)}, u32[]{:S(2)}) collective-permute-start(bf16[24,1664]{1,0:T(8,128)(2,1)S(1)} %pad_maximum_fusion.3), channel_id=1, source_target_pairs={{28,0},{21,1},{14,2},{7,3},{0,4},{25,5},{18,6},{11,7},{4,8},{29,9}... | collective-permute-start | bytes 239624 | tf_op jit(solution)/shard_map/ppermute | solution.py:258
  25.7 3.5 %collective-permute-start.4 = (bf16[24,1664]{1,0:T(8,128)(2,1)S(1)}, bf16[24,1664]{1,0:T(8,128)(2,1)S(1)}, u32[]{:S(2)}, u32[]{:S(2)}) collective-permute-start(bf16[24,1664]{1,0:T(8,128)(2,1)S(1)} %pad_maximum_fusion.3), channel_id=1, source_target_pairs={{24,0},{17,1},{10,2},{3,3},{28,4},{21,5},{14,6},{7,7},{0,8},{25,9}... | collective-permute-start | bytes 239624 | tf_op jit(solution)/shard_map/ppermute | solution.py:258
  29.2 2.5 %collective-permute-done.3 = bf16[24,1664]{1,0:T(8,128)(2,1)S(1)} collective-permute-done((bf16[24,1664]{1,0:T(8,128)(2,1)S(1)}, bf16[24,1664]{1,0:T(8,128)(2,1)S(1)}, u32[]{:S(2)}, u32[]{:S(2)}) %collective-permute-start.3) | collective-permute-done | bytes 79904 | tf_op jit(solution)/shard_map/ppermute | solution.py:258
  31.7 2.8 %collective-permute-done.4 = bf16[24,1664]{1,0:T(8,128)(2,1)S(1)} collective-permute-done((bf16[24,1664]{1,0:T(8,128)(2,1)S(1)}, bf16[24,1664]{1,0:T(8,128)(2,1)S(1)}, u32[]{:S(2)}, u32[]{:S(2)}) %collective-permute-start.4) | collective-permute-done | bytes 79904 | tf_op jit(solution)/shard_map/ppermute | solution.py:258
  34.6 1.1 %collective-permute-start.6 = (bf16[2,24,1664]{2,1,0:T(8,128)(2,1)S(1)}, bf16[2,24,1664]{2,1,0:T(8,128)(2,1)S(1)}, u32[]{:S(2)}, u32[]{:S(2)}) collective-permute-start(bf16[2,24,1664]{2,1,0:T(8,128)(2,1)S(1)} %get-tuple-element.20), channel_id=1, source_target_pairs={{0,2},{1,3},{2,0},{3,1},{4,6},{5,7},{6,4},{7,5},{8,10},{9,11},{10,... | collective-permute-start | bytes 479240 | tf_op jit(solution)/shard_map/ppermute | solution.py:261
  35.7 1.4 %collective-permute-start.7 = (bf16[2,24,1664]{2,1,0:T(8,128)(2,1)S(1)}, bf16[2,24,1664]{2,1,0:T(8,128)(2,1)S(1)}, u32[]{:S(2)}, u32[]{:S(2)}) collective-permute-start(bf16[2,24,1664]{2,1,0:T(8,128)(2,1)S(1)} %get-tuple-element.20), channel_id=1, source_target_pairs={{0,3},{1,0},{2,1},{3,2},{4,7},{5,4},{6,5},{7,6},{8,11},{9,8},{10,9... | collective-permute-start | bytes 479240 | tf_op jit(solution)/shard_map/ppermute | solution.py:261
  37.1 0.6 pad_add_fusion.index_ref
  37.7 2.7 %collective-permute-done.5 = bf16[2,24,1664]{2,1,0:T(8,128)(2,1)S(1)} collective-permute-done((bf16[2,24,1664]{2,1,0:T(8,128)(2,1)S(1)}, bf16[2,24,1664]{2,1,0:T(8,128)(2,1)S(1)}, u32[]{:S(2)}, u32[]{:S(2)}) %collective-permute-start.5) | collective-permute-done | bytes 159776 | tf_op jit(solution)/shard_map/ppermute | solution.py:261
  40.4 1.3 %collective-permute-done.6 = bf16[2,24,1664]{2,1,0:T(8,128)(2,1)S(1)} collective-permute-done((bf16[2,24,1664]{2,1,0:T(8,128)(2,1)S(1)}, bf16[2,24,1664]{2,1,0:T(8,128)(2,1)S(1)}, u32[]{:S(2)}, u32[]{:S(2)}) %collective-permute-start.6) | collective-permute-done | bytes 159776 | tf_op jit(solution)/shard_map/ppermute | solution.py:261
  41.7 1.3 %collective-permute-done.7 = bf16[2,24,1664]{2,1,0:T(8,128)(2,1)S(1)} collective-permute-done((bf16[2,24,1664]{2,1,0:T(8,128)(2,1)S(1)}, bf16[2,24,1664]{2,1,0:T(8,128)(2,1)S(1)}, u32[]{:S(2)}, u32[]{:S(2)}) %collective-permute-start.7) | collective-permute-done | bytes 159776 | tf_op jit(solution)/shard_map/ppermute | solution.py:261
  43.0 0.9 %pad_maximum_fusion = bf16[4,2,24,1664]{3,2,1,0:T(8,128)(2,1)} fusion(bf16[1,2,24,1664]{3,2,1,0:T(8,128)(2,1)S(1)} %bitcast.134, bf16[1,2,24,1664]{3,2,1,0:T(8,128)(2,1)S(1)} %bitcast.133, bf16[1,2,24,1664]{3,2,1,0:T(8,128)(2,1)S(1)} %bitcast.132, bf16[1,2,24,1664]{3,2,1,0:T(8,128)(2,1)S(1)} %get-tuple-element.19), kind=kLoop, calls=%fused_computation.8 | loop fusion | flops 958464 | bytes 1277952 | tf_op jit(solution)/shard_map/stack | solution.py:264
  43.9 6.4 %shard_map.118 = bf16[32,24,384]{2,1,0:T(8,128)(2,1)} custom-call(s32[2]{0:T(128)} %pad_add_fusion.index_ref, bf16[192,1664]{1,0:T(8,128)(2,1)} %bitcast.110, bf16[4,2,192,1536]{3,2,1,0:T(8,128)(2,1)} %bitcast.109, bf16[4,192,1536]{2,1,0:T(8,128)(2,1)} %dn_ref.1), custom_call_target="tpu_custom_call" | custom-call | tf_op jit(solution)/shard_map/pallas_call | solution.py:95
  50.4 4.9 %all-to-all-start = ((bf16[32,24,384]{2,1,0:T(8,128)(2,1)}), bf16[32,24,384]{2,1,0:T(8,128)(2,1)S(1)}, u32[]{:S(2)}, u32[]{:S(2)}) async-start(bf16[32,24,384]{2,1,0:T(8,128)(2,1)} %shard_map.118), calls=%async_computation | async-start | bytes 1179648 | tf_op jit(solution)/shard_map/all_to_all | solution.py:281
  55.3 16.8 %all-to-all-done = bf16[32,24,384]{2,1,0:T(8,128)(2,1)S(1)} async-done(((bf16[32,24,384]{2,1,0:T(8,128)(2,1)}), bf16[32,24,384]{2,1,0:T(8,128)(2,1)S(1)}, u32[]{:S(2)}, u32[]{:S(2)}) %all-to-all-start) | async-done | bytes 589856 | tf_op jit(solution)/shard_map/all_to_all | solution.py:281
  72.1 0.1 convert_reduce_fusion
  72.2 0.6 add_convert_fusion.1
  (62 shorter events, 1.3 us)
Async XLA Ops:
  0.0 17.2 %copy-start = (bf16[384,1536]{1,0:T(8,128)(2,1)S(1)}, bf16[384,1536]{1,0:T(8,128)(2,1)}, u32[]{:S(2)}) copy-start(bf16[384,1536]{1,0:T(8,128)(2,1)} %param.18) | copy-start | bytes 3538948
  0.0 7.7 %copy-start.9 = (s32[24]{0:T(128)S(1)}, s32[24]{0:T(128)}, u32[]{:S(2)}) copy-start(s32[24]{0:T(128)} %param.15) | copy-start | bytes 292
  0.0 8.1 %copy-start.8 = (s32[1,24]{1,0:T(1,128)S(1)}, s32[1,24]{1,0:T(1,128)}, u32[]{:S(2)}) copy-start(s32[1,24]{1,0:T(1,128)} %param.16) | copy-start | bytes 292
  0.9 7.6 %copy-start.1 = (bf16[768,2,2,128]{3,2,1,0:T(2,128)(2,1)S(1)}, bf16[768,2,2,128]{3,2,1,0:T(2,128)(2,1)}, u32[]{:S(2)}) copy-start(bf16[768,2,2,128]{3,2,1,0:T(2,128)(2,1)} %param.17) | copy-start | bytes 2359300
  7.9 0.6 copy-start.2
  10.3 4.6 %copy-start.4 = (bf16[24,2,256]{2,1,0:T(2,128)(2,1)S(1)}, bf16[24,2,256]{2,1,0:T(2,128)(2,1)}, u32[]{:S(2)}) copy-start(bf16[24,2,256]{2,1,0:T(2,128)(2,1)} %param.14) | copy-start | bytes 73732
  11.0 4.0 %copy-start.3 = (f32[24,64]{1,0:T(8,128)S(1)}, f32[24,64]{1,0:T(8,128)}, u32[]{:S(2)}) copy-start(f32[24,64]{1,0:T(8,128)} %copy-done.2) | copy-start | bytes 18436
  11.0 4.5 %copy-start.6 = (f32[24,4]{0,1:T(4,128)S(1)}, f32[24,4]{0,1:T(4,128)}, u32[]{:S(2)}) copy-start(f32[24,4]{0,1:T(4,128)} %param.21) | copy-start | bytes 1156
  11.0 4.4 %copy-start.7 = (s32[24,4]{0,1:T(4,128)S(1)}, s32[24,4]{0,1:T(4,128)}, u32[]{:S(2)}) copy-start(s32[24,4]{0,1:T(4,128)} %param.20) | copy-start | bytes 1156
  11.5 4.3 %collective-permute-start = (f32[24,512]{1,0:T(8,128)S(1)}, f32[24,512]{1,0:T(8,128)S(1)}, u32[]{:S(2)}, u32[]{:S(2)}) collective-permute-start(f32[24,512]{1,0:T(8,128)S(1)} %bitcast.140), channel_id=1, source_target_pairs={{0,1},{1,2},{2,3},{3,0},{4,5},{5,6},{6,7},{7,4},{8,9},{9,10},{10,1... | collective-permute-start | bytes 147464 | tf_op jit(solution)/shard_map/ppermute | solution.py:199
  11.9 4.1 %collective-permute-start.1 = (f32[24,512]{1,0:T(8,128)S(1)}, f32[24,512]{1,0:T(8,128)S(1)}, u32[]{:S(2)}, u32[]{:S(2)}) collective-permute-start(f32[24,512]{1,0:T(8,128)S(1)} %bitcast.141), channel_id=1, source_target_pairs={{0,2},{1,3},{2,0},{3,1},{4,6},{5,7},{6,4},{7,5},{8,10},{9,11},{10,... | collective-permute-start | bytes 147464 | tf_op jit(solution)/shard_map/ppermute | solution.py:199
  13.7 2.9 %collective-permute-start.2 = (f32[24,512]{1,0:T(8,128)S(1)}, f32[24,512]{1,0:T(8,128)S(1)}, u32[]{:S(2)}, u32[]{:S(2)}) collective-permute-start(f32[24,512]{1,0:T(8,128)S(1)} %bitcast.142), channel_id=1, source_target_pairs={{0,3},{1,0},{2,1},{3,2},{4,7},{5,4},{6,5},{7,6},{8,11},{9,8},{10,9... | collective-permute-start | bytes 147464 | tf_op jit(solution)/shard_map/ppermute | solution.py:199
  17.2 6.6 %copy-start.5 = (f32[1536]{0:T(1024)S(1)}, f32[1536]{0:T(1024)}, u32[]{:S(2)}) copy-start(f32[1536]{0:T(1024)} %param.19) | copy-start | bytes 18436
  24.0 7.7 %collective-permute-start.3 = (bf16[24,1664]{1,0:T(8,128)(2,1)S(1)}, bf16[24,1664]{1,0:T(8,128)(2,1)S(1)}, u32[]{:S(2)}, u32[]{:S(2)}) collective-permute-start(bf16[24,1664]{1,0:T(8,128)(2,1)S(1)} %pad_maximum_fusion.3), channel_id=1, source_target_pairs={{28,0},{21,1},{14,2},{7,3},{0,4},{25,5},{18,6},{11,7},{4,8},{29,9}... | collective-permute-start | bytes 239624 | tf_op jit(solution)/shard_map/ppermute | solution.py:258
  25.7 8.8 %collective-permute-start.4 = (bf16[24,1664]{1,0:T(8,128)(2,1)S(1)}, bf16[24,1664]{1,0:T(8,128)(2,1)S(1)}, u32[]{:S(2)}, u32[]{:S(2)}) collective-permute-start(bf16[24,1664]{1,0:T(8,128)(2,1)S(1)} %pad_maximum_fusion.3), channel_id=1, source_target_pairs={{24,0},{17,1},{10,2},{3,3},{28,4},{21,5},{14,6},{7,7},{0,8},{25,9}... | collective-permute-start | bytes 239624 | tf_op jit(solution)/shard_map/ppermute | solution.py:258
  34.6 5.8 %collective-permute-start.5 = (bf16[2,24,1664]{2,1,0:T(8,128)(2,1)S(1)}, bf16[2,24,1664]{2,1,0:T(8,128)(2,1)S(1)}, u32[]{:S(2)}, u32[]{:S(2)}) collective-permute-start(bf16[2,24,1664]{2,1,0:T(8,128)(2,1)S(1)} %get-tuple-element.20), channel_id=1, source_target_pairs={{0,1},{1,2},{2,3},{3,0},{4,5},{5,6},{6,7},{7,4},{8,9},{9,10},{10,1... | collective-permute-start | bytes 479240 | tf_op jit(solution)/shard_map/ppermute | solution.py:261
  34.6 7.1 %collective-permute-start.6 = (bf16[2,24,1664]{2,1,0:T(8,128)(2,1)S(1)}, bf16[2,24,1664]{2,1,0:T(8,128)(2,1)S(1)}, u32[]{:S(2)}, u32[]{:S(2)}) collective-permute-start(bf16[2,24,1664]{2,1,0:T(8,128)(2,1)S(1)} %get-tuple-element.20), channel_id=1, source_target_pairs={{0,2},{1,3},{2,0},{3,1},{4,6},{5,7},{6,4},{7,5},{8,10},{9,11},{10,... | collective-permute-start | bytes 479240 | tf_op jit(solution)/shard_map/ppermute | solution.py:261
  35.7 7.3 %collective-permute-start.7 = (bf16[2,24,1664]{2,1,0:T(8,128)(2,1)S(1)}, bf16[2,24,1664]{2,1,0:T(8,128)(2,1)S(1)}, u32[]{:S(2)}, u32[]{:S(2)}) collective-permute-start(bf16[2,24,1664]{2,1,0:T(8,128)(2,1)S(1)} %get-tuple-element.20), channel_id=1, source_target_pairs={{0,3},{1,0},{2,1},{3,2},{4,7},{5,4},{6,5},{7,6},{8,11},{9,8},{10,9... | collective-permute-start | bytes 479240 | tf_op jit(solution)/shard_map/ppermute | solution.py:261
  50.4 21.7 %all-to-all-start = ((bf16[32,24,384]{2,1,0:T(8,128)(2,1)}), bf16[32,24,384]{2,1,0:T(8,128)(2,1)S(1)}, u32[]{:S(2)}, u32[]{:S(2)}) async-start(bf16[32,24,384]{2,1,0:T(8,128)(2,1)} %shard_map.118), calls=%async_computation | async-start | bytes 1179648 | tf_op jit(solution)/shard_map/all_to_all | solution.py:281

commit v20 on v18

--- a/solution.py
+++ b/solution.py
@@ -63,7 +63,9 @@
         for group in range(tile_groups):
             if arrival_order:
                 group_total = o_ref.shape[0] // tp_count
-                dest = (index_ref[0] + 2 * group_total - group - 1) % group_total
+                per_tp = group_total // tp_count
+                shift = (group % per_tp) * tp_count + group // per_tp + 1
+                dest = (index_ref[0] + 2 * group_total - shift) % group_total
             else:
                 dest = group
             for part in range(tp_count):
@@ -249,7 +251,7 @@
             pairs = []
             for group in range(req_count):
                 for part in range(tp_count):
-                    shift = per_tp * part + slot + 1
+                    shift = slot * tp_count + part + 1
                     source = ((group - shift) % req_count) * tp_count + part
                     pairs.append((source, group * tp_count + part))
             fetched.append(lax.ppermute(value, ("req", "tp"), pairs))

time: 70.1 us -> 71.2 us (1.016)
  starting transfers between devices: 12.2 us -> 15.9 us
  waiting for transfers between devices: 22.9 us -> 19.8 us
    ppermute x2, waiting for transfers between devices: 5.3 us -> 2.21 us  [gather_req(): fetched.append(lax.ppermute(value, ('req', 'tp'), pairs))]
    ppermute x2, starting transfers between devices: 5.24 us -> 7.22 us  [gather_req(): fetched.append(lax.ppermute(value, ('req', 'tp'), pairs))]
    all_to_all x1, starting transfers between devices: 3.57 us -> 5.38 us  [per_device(): mixed = lax.all_to_all(mixed, ('req', 'tp'), 0, 0, tiled=True)]
where the time goes in v20:
time: 71.2 us; the launch traced here: 70.9 us
  blocking collectives  21 us (29%)
  waiting for transfers between devices  19.8 us (28%)
  starting transfers between devices  15.9 us (22%)
  Pallas kernels  6.39 us (9%)
  other arithmetic  3.82 us (5%)
  local copies, waits for them, and re-layouts  1.82 us (3%)
  matrix products  1.63 us (2%)
    all_to_all x1, waiting for transfers between devices, per_device(): mixed = lax.all_to_all(mixed, ('req', 'tp'), 0, 0, tiled=True)  16.8 us
    all_gather x1, blocking collectives, gather_req(): shared = lax.all_gather(jnp.stack(fetched, axis=0), 'tp', axis=0)  8.13 us
    ppermute x2, starting transfers between devices, gather_req(): fetched.append(lax.ppermute(value, ('req', 'tp'), pairs))  7.22 us
    all_gather x1, blocking collectives, per_device(): gathered = lax.all_gather(packed, 'tp', axis=0)  6.74 us
    pallas_call x1, Pallas kernels, expert_mix(): pl.pallas_call(body, grid=(group_total // tile_groups, local_count), in_s...  6.39 us
    all_gather x1, blocking collectives, per_device(): lax.all_gather(partial_proj.astype(jnp.bfloat16), 'tp', axis=0)  6.16 us
    all_to_all x1, starting transfers between devices, per_device(): mixed = lax.all_to_all(mixed, ('req', 'tp'), 0, 0, tiled=True)  5.38 us
    ppermute x3, starting transfers between devices, per_device(): lax.ppermute(outgoing, 'tp', [(i, (i + shift) % tp_count) for i in range(...  3.34 us
  transfers between devices with their start and end apart: 6, of which 5 were waited for; matrix products, arithmetic and copies ran while one was open for 1% of the time, Pallas kernels for 0%

profile of v20, /device:TPU:0, one launch (start us, length us, event | category | flops | bytes accessed | tf_op | source)
XLA Modules:
  0.0 70.9 jit_solution(5201679525917059805)
XLA Ops:
  0.0 0.8 %pad_maximum_fusion.5 = bf16[2,24,384]{2,1,0:T(8,128)(2,1)S(1)} fusion(bf16[1,24,384]{2,1,0:T(8,128)(2,1)} %bitcast.134, bf16[1,24,384]{2,1,0:T(8,128)(2,1)} %bitcast.135), kind=kLoop, calls=%fused_computation.61 | loop fusion | flops 18432 | bytes 73728 | tf_op jit(solution)/shard_map/stack | solution.py:140
  0.9 6.7 %all-gather = bf16[8,24,384]{2,1,0:T(8,128)(2,1)S(1)} all-gather(bf16[2,24,384]{2,1,0:T(8,128)(2,1)S(1)} %pad_maximum_fusion.5), channel_id=2, replica_groups=mesh['req'=8,'tp'=4] {'tp'}, dimensions={0}, use_global_device_ids=true | all-gather | bytes 184320 | tf_op jit(solution)/shard_map/all_gather | solution.py:141
  7.8 0.1 multiply_cosine_fusion
  7.9 0.1 subtract_convert_fusion
  8.1 0.1 copy.51
  8.3 0.1 reduce.2
  8.4 0.1 copy-done.2
  8.5 0.5 fusion.29
  9.0 0.1 pad_maximum_fusion.3
  9.1 0.1 compare_and_fusion
  9.2 0.5 fusion.30
  9.7 0.3 fusion.2
  10.1 0.1 copy.59
  10.2 0.1 copy.58
  10.3 0.7 convolution_bitcast_fusion
  11.2 0.1 select_maximum_fusion
  11.3 0.2 fusion.13
  11.5 0.4 collective-permute-start
  11.9 1.8 %collective-permute-start.1 = (f32[24,512]{1,0:T(8,128)S(1)}, f32[24,512]{1,0:T(8,128)S(1)}, u32[]{:S(2)}, u32[]{:S(2)}) collective-permute-start(f32[24,512]{1,0:T(8,128)S(1)} %bitcast.132), channel_id=1, source_target_pairs={{0,2},{1,3},{2,0},{3,1},{4,6},{5,7},{6,4},{7,5},{8,10},{9,11},{10,... | collective-permute-start | bytes 147464 | tf_op jit(solution)/shard_map/ppermute | solution.py:198
  13.7 1.1 %collective-permute-start.2 = (f32[24,512]{1,0:T(8,128)S(1)}, f32[24,512]{1,0:T(8,128)S(1)}, u32[]{:S(2)}, u32[]{:S(2)}) collective-permute-start(f32[24,512]{1,0:T(8,128)S(1)} %bitcast.133), channel_id=1, source_target_pairs={{0,3},{1,0},{2,1},{3,2},{4,7},{5,4},{6,5},{7,6},{8,11},{9,8},{10,9... | collective-permute-start | bytes 147464 | tf_op jit(solution)/shard_map/ppermute | solution.py:198
  14.9 0.1 slice_reduce_fusion
  15.0 0.1 subtract_convert_fusion.1
  15.1 0.1 maximum_bitcast_fusion
  15.2 0.2 fusion.10
  15.3 0.1 copy.66
  15.5 0.1 select_reduce_fusion
  15.7 0.1 copy.74
  15.8 0.2 collective-permute-done.1
  16.0 0.6 collective-permute-done.2
  16.7 0.1 subtract_exponential_fusion
  16.8 0.2 mul.193
  16.9 0.1 mul.194
  17.1 0.1 broadcast_multiply_fusion
  17.2 0.1 div.19
  17.3 0.3 convolution_convert_fusion
  17.5 6.2 %all-gather.1 = bf16[96,1536]{1,0:T(8,128)(2,1)S(1)} all-gather(bf16[24,1536]{1,0:T(8,128)(2,1)S(1)} %convolution_convert_fusion), channel_id=3, replica_groups=mesh['req'=8,'tp'=4] {'tp'}, dimensions={0}, use_global_device_ids=true | all-gather | bytes 368640 | tf_op jit(solution)/shard_map/all_gather | solution.py:223
  23.7 0.1 fusion.8
  23.9 0.1 multiply_convert_fusion
  24.0 1.8 %collective-permute-start.3 = (bf16[24,1664]{1,0:T(8,128)(2,1)S(1)}, bf16[24,1664]{1,0:T(8,128)(2,1)S(1)}, u32[]{:S(2)}, u32[]{:S(2)}) collective-permute-start(bf16[24,1664]{1,0:T(8,128)(2,1)S(1)} %pad_maximum_fusion.2), channel_id=1, source_target_pairs={{28,0},{25,1},{22,2},{19,3},{0,4},{29,5},{26,6},{23,7},{4,8},{1,9}... | collective-permute-start | bytes 239624 | tf_op jit(solution)/shard_map/ppermute | solution.py:257
  25.7 5.4 %collective-permute-start.4 = (bf16[24,1664]{1,0:T(8,128)(2,1)S(1)}, bf16[24,1664]{1,0:T(8,128)(2,1)S(1)}, u32[]{:S(2)}, u32[]{:S(2)}) collective-permute-start(bf16[24,1664]{1,0:T(8,128)(2,1)S(1)} %pad_maximum_fusion.2), channel_id=1, source_target_pairs={{12,0},{9,1},{6,2},{3,3},{16,4},{13,5},{10,6},{7,7},{20,8},{17,9},... | collective-permute-start | bytes 239624 | tf_op jit(solution)/shard_map/ppermute | solution.py:257
  31.2 0.5 collective-permute-done.3
  31.7 1.7 %collective-permute-done.4 = bf16[24,1664]{1,0:T(8,128)(2,1)S(1)} collective-permute-done((bf16[24,1664]{1,0:T(8,128)(2,1)S(1)}, bf16[24,1664]{1,0:T(8,128)(2,1)S(1)}, u32[]{:S(2)}, u32[]{:S(2)}) %collective-permute-start.4) | collective-permute-done | bytes 79904 | tf_op jit(solution)/shard_map/ppermute | solution.py:257
  33.4 8.1 %all-gather.2 = bf16[8,24,1664]{2,1,0:T(8,128)(2,1)} all-gather(bf16[2,24,1664]{2,1,0:T(8,128)(2,1)S(1)} %pad_maximum_fusion.1), channel_id=4, replica_groups=mesh['req'=8,'tp'=4] {'tp'}, dimensions={0}, use_global_device_ids=true | all-gather | bytes 798720 | tf_op jit(solution)/shard_map/all_gather | solution.py:258
  41.6 6.4 %shard_map.118 = bf16[32,24,384]{2,1,0:T(8,128)(2,1)} custom-call(s32[1]{0:T(128)} %bitcast.27.index_ref, bf16[192,1664]{1,0:T(8,128)(2,1)} %bitcast.104, bf16[4,2,192,1536]{3,2,1,0:T(8,128)(2,1)} %bitcast.103, bf16[4,192,1536]{2,1,0:T(8,128)(2,1)} %dn_ref.1), custom_call_target="tpu_custom_call" | custom-call | tf_op jit(solution)/shard_map/pallas_call | solution.py:94
  48.0 5.4 %all-to-all-start = ((bf16[32,24,384]{2,1,0:T(8,128)(2,1)}), bf16[32,24,384]{2,1,0:T(8,128)(2,1)S(1)}, u32[]{:S(2)}, u32[]{:S(2)}) async-start(bf16[32,24,384]{2,1,0:T(8,128)(2,1)} %shard_map.118), calls=%async_computation | async-start | bytes 1179648 | tf_op jit(solution)/shard_map/all_to_all | solution.py:275
  53.3 16.8 %all-to-all-done = bf16[32,24,384]{2,1,0:T(8,128)(2,1)S(1)} async-done(((bf16[32,24,384]{2,1,0:T(8,128)(2,1)}), bf16[32,24,384]{2,1,0:T(8,128)(2,1)S(1)}, u32[]{:S(2)}, u32[]{:S(2)}) %all-to-all-start) | async-done | bytes 589856 | tf_op jit(solution)/shard_map/all_to_all | solution.py:275
  70.1 0.1 convert_reduce_fusion
  70.2 0.6 add_convert_fusion.1
  (55 shorter events, 0.7 us)
Async XLA Ops:
  0.0 17.2 %copy-start = (bf16[384,1536]{1,0:T(8,128)(2,1)S(1)}, bf16[384,1536]{1,0:T(8,128)(2,1)}, u32[]{:S(2)}) copy-start(bf16[384,1536]{1,0:T(8,128)(2,1)} %param.18) | copy-start | bytes 3538948
  0.0 7.7 %copy-start.9 = (s32[24]{0:T(128)S(1)}, s32[24]{0:T(128)}, u32[]{:S(2)}) copy-start(s32[24]{0:T(128)} %param.15) | copy-start | bytes 292
  0.0 8.1 %copy-start.8 = (s32[1,24]{1,0:T(1,128)S(1)}, s32[1,24]{1,0:T(1,128)}, u32[]{:S(2)}) copy-start(s32[1,24]{1,0:T(1,128)} %param.16) | copy-start | bytes 292
  0.9 7.6 %copy-start.1 = (bf16[768,2,2,128]{3,2,1,0:T(2,128)(2,1)S(1)}, bf16[768,2,2,128]{3,2,1,0:T(2,128)(2,1)}, u32[]{:S(2)}) copy-start(bf16[768,2,2,128]{3,2,1,0:T(2,128)(2,1)} %param.17) | copy-start | bytes 2359300
  7.9 0.6 copy-start.2
  10.3 4.6 %copy-start.4 = (bf16[24,2,256]{2,1,0:T(2,128)(2,1)S(1)}, bf16[24,2,256]{2,1,0:T(2,128)(2,1)}, u32[]{:S(2)}) copy-start(bf16[24,2,256]{2,1,0:T(2,128)(2,1)} %param.14) | copy-start | bytes 73732
  11.0 4.0 %copy-start.3 = (f32[24,64]{1,0:T(8,128)S(1)}, f32[24,64]{1,0:T(8,128)}, u32[]{:S(2)}) copy-start(f32[24,64]{1,0:T(8,128)} %copy-done.2) | copy-start | bytes 18436
  11.0 4.5 %copy-start.6 = (f32[24,4]{0,1:T(4,128)S(1)}, f32[24,4]{0,1:T(4,128)}, u32[]{:S(2)}) copy-start(f32[24,4]{0,1:T(4,128)} %param.21) | copy-start | bytes 1156
  11.0 4.4 %copy-start.7 = (s32[24,4]{0,1:T(4,128)S(1)}, s32[24,4]{0,1:T(4,128)}, u32[]{:S(2)}) copy-start(s32[24,4]{0,1:T(4,128)} %param.20) | copy-start | bytes 1156
  11.5 4.3 %collective-permute-start = (f32[24,512]{1,0:T(8,128)S(1)}, f32[24,512]{1,0:T(8,128)S(1)}, u32[]{:S(2)}, u32[]{:S(2)}) collective-permute-start(f32[24,512]{1,0:T(8,128)S(1)} %bitcast.131), channel_id=1, source_target_pairs={{0,1},{1,2},{2,3},{3,0},{4,5},{5,6},{6,7},{7,4},{8,9},{9,10},{10,1... | collective-permute-start | bytes 147464 | tf_op jit(solution)/shard_map/ppermute | solution.py:198
  11.9 4.1 %collective-permute-start.1 = (f32[24,512]{1,0:T(8,128)S(1)}, f32[24,512]{1,0:T(8,128)S(1)}, u32[]{:S(2)}, u32[]{:S(2)}) collective-permute-start(f32[24,512]{1,0:T(8,128)S(1)} %bitcast.132), channel_id=1, source_target_pairs={{0,2},{1,3},{2,0},{3,1},{4,6},{5,7},{6,4},{7,5},{8,10},{9,11},{10,... | collective-permute-start | bytes 147464 | tf_op jit(solution)/shard_map/ppermute | solution.py:198
  13.7 2.9 %collective-permute-start.2 = (f32[24,512]{1,0:T(8,128)S(1)}, f32[24,512]{1,0:T(8,128)S(1)}, u32[]{:S(2)}, u32[]{:S(2)}) collective-permute-start(f32[24,512]{1,0:T(8,128)S(1)} %bitcast.133), channel_id=1, source_target_pairs={{0,3},{1,0},{2,1},{3,2},{4,7},{5,4},{6,5},{7,6},{8,11},{9,8},{10,9... | collective-permute-start | bytes 147464 | tf_op jit(solution)/shard_map/ppermute | solution.py:198
  17.2 6.6 %copy-start.5 = (f32[1536]{0:T(1024)S(1)}, f32[1536]{0:T(1024)}, u32[]{:S(2)}) copy-start(f32[1536]{0:T(1024)} %param.19) | copy-start | bytes 18436
  24.0 7.8 %collective-permute-start.3 = (bf16[24,1664]{1,0:T(8,128)(2,1)S(1)}, bf16[24,1664]{1,0:T(8,128)(2,1)S(1)}, u32[]{:S(2)}, u32[]{:S(2)}) collective-permute-start(bf16[24,1664]{1,0:T(8,128)(2,1)S(1)} %pad_maximum_fusion.2), channel_id=1, source_target_pairs={{28,0},{25,1},{22,2},{19,3},{0,4},{29,5},{26,6},{23,7},{4,8},{1,9}... | collective-permute-start | bytes 239624 | tf_op jit(solution)/shard_map/ppermute | solution.py:257
  25.7 7.7 %collective-permute-start.4 = (bf16[24,1664]{1,0:T(8,128)(2,1)S(1)}, bf16[24,1664]{1,0:T(8,128)(2,1)S(1)}, u32[]{:S(2)}, u32[]{:S(2)}) collective-permute-start(bf16[24,1664]{1,0:T(8,128)(2,1)S(1)} %pad_maximum_fusion.2), channel_id=1, source_target_pairs={{12,0},{9,1},{6,2},{3,3},{16,4},{13,5},{10,6},{7,7},{20,8},{17,9},... | collective-permute-start | bytes 239624 | tf_op jit(solution)/shard_map/ppermute | solution.py:257
  48.0 22.2 %all-to-all-start = ((bf16[32,24,384]{2,1,0:T(8,128)(2,1)}), bf16[32,24,384]{2,1,0:T(8,128)(2,1)S(1)}, u32[]{:S(2)}, u32[]{:S(2)}) async-start(bf16[32,24,384]{2,1,0:T(8,128)(2,1)} %shard_map.118), calls=%async_computation | async-start | bytes 1179648 | tf_op jit(solution)/shard_map/all_to_all | solution.py:275
